TPU v7x, 32 devices: a whole 2x2x4 slice. The times are simulated.
32 devices in a mesh: groups: 2 (over y), ty: 16 (over z, x, core).
Axes of the slice: x: 2, y: 2, z: 4, core: 2. Of those that a mesh axis runs over, the one named last changes fastest.
Arguments:
- image: float32 [2048, 2048], P(('groups', 'ty')), parts along dimension 0, may hold values from -6 to 6
- band_row: int32 [64], P(('groups', 'ty')), parts along dimension 0, may hold values from 0 to 32, as said below
- col_block: int32 [64], P(('groups', 'ty')), parts along dimension 0, may hold values from 0 to 15
- cell_index: int32 [64], P(('groups', 'ty')), parts along dimension 0, may hold values from 0 to 255
- offset_y: float32 [64, 128], P(('groups', 'ty')), parts along dimension 0, may hold values from 0 to 32
- offset_x: float32 [64, 128], P(('groups', 'ty')), parts along dimension 0, may hold values from 0 to 128
- flux_start: float32 [64, 128], P(('groups', 'ty')), parts along dimension 0, may hold values from 0.5 to 3
- psf_coef: float32 [9, 256], replicated, may hold values from -0.25 to 1.4
Outputs:
- fluxes: float32 [64, 128], P(('groups', 'ty')), parts along dimension 0
- residual: float32 [2048, 2048], P(('groups', 'ty')), parts along dimension 0
There are 2 independent parts, one for each index of `groups`. A program takes and returns all parts, laid end to end along the dimension named above; an argument that names none is the same for every part. Nothing has to cross between parts.
Inputs may be any that keep to these rules, and one draw needn't show every extreme that they name: `band_row`: on every tile row, one of its 2 star blocks starts at row 0 and the other at row 32.
All inputs are finite; a program needn't handle non-finite values.
Results may differ from a plain program's by a relative error of at most 0.0003.
Values sent between devices are 32-bit elements; how exact they have to be, the bound alone decides.
No kernel may reach another device: no remote copies, remote signals or barrier semaphores. Data moves between devices by JAX's collectives and lax.ppermute only.
A program may use at most 64 MiB of HBM per device.

v0:
```python
import jax
import jax.numpy as jnp
from jax import lax
from jax.sharding import PartitionSpec as P

REACH = 15
ITERS = 2


HIGHEST = lax.Precision.HIGHEST


def from_behind(shard, axis, by):
    devices = lax.axis_size(axis)
    pairs = [(i, i + by) for i in range(devices) if 0 <= i + by < devices]
    return lax.ppermute(shard, axis, pairs)


def padded_2(block, sides, width):
    for axis, dim in sides:
        count = lax.axis_size(axis)
        forward = [(i, i + 1) for i in range(count - 1)]
        backward = [(target, source) for source, target in forward]
        low = lax.ppermute(
            lax.slice_in_dim(block, block.shape[dim] - width, None, axis=dim), axis, forward
        )
        high = lax.ppermute(lax.slice_in_dim(block, 0, width, axis=dim), axis, backward)
        block = jnp.concatenate([low, block, high], axis=dim)
    return block


def profile(dist):
    tapered = jnp.maximum(0.0, 1.0 - dist / 15.5 * (dist / 15.5))
    scaled = dist / 1.7
    core_part = jnp.exp(-0.5 * scaled * scaled) * tapered
    wing_part = jnp.exp(-dist * dist / 72.0) * tapered
    return jnp.stack([core_part, scaled * core_part, wing_part], axis=-2)


def placement(col_ids, col_count, dtype):
    slot_ids = jnp.arange(col_count + 1)
    left_hit = (slot_ids[None, :] == col_ids[:, None]).astype(dtype)
    right_hit = (slot_ids[None, :] == col_ids[:, None] + 1).astype(dtype)
    return jnp.stack([left_hit, right_hit])


def block_coefs(psf_coef, cell_index):
    cell_ids = jnp.arange(psf_coef.shape[1])
    picker = (cell_ids[:, None] == cell_index[None, :]).astype(psf_coef.dtype)
    return jnp.dot(psf_coef, picker, precision=HIGHEST)


def norms(ylocal, xoff, coefs):
    block_count = ylocal.shape[0]
    offsets = jnp.arange(-15, 17).astype(ylocal.dtype)
    rows_profile = profile(
        jnp.floor(ylocal)[:, None, :] + offsets[None, :, None] - ylocal[:, None, :]
    )
    cols_profile = profile(jnp.floor(xoff)[:, None, :] + offsets[None, :, None] - xoff[:, None, :])
    gram_rows = jnp.einsum("jkas,jkcs->acjs", rows_profile, rows_profile, precision=HIGHEST)
    gram_cols = jnp.einsum("jkbs,jkds->bdjs", cols_profile, cols_profile, precision=HIGHEST)
    shaped = coefs.reshape(3, 3, block_count)
    return jnp.einsum(
        "abj,cdj,acjs,bdjs->js", shaped, shaped, gram_rows, gram_cols, precision=HIGHEST
    )


def render(rows_profile, cols_profile, coefs, fluxes, col_ids, col_count):
    block_count, row_count, _, star_count = rows_profile.shape
    mixed = jnp.einsum(
        "abj,jwbs->jwas", coefs.reshape(3, 3, block_count), cols_profile, precision=HIGHEST
    )
    mixed = mixed * fluxes[:, None, None, :]
    stamps = jnp.einsum(
        "jhk,jwk->jhw",
        rows_profile.reshape(block_count, row_count, 3 * star_count),
        mixed.reshape(block_count, 256, 3 * star_count),
        precision=HIGHEST,
    )
    placed = placement(col_ids, col_count, stamps.dtype)
    canvas = jnp.einsum(
        "pjc,jhpw->hcw", placed, stamps.reshape(block_count, row_count, 2, 128), precision=HIGHEST
    )
    return canvas.reshape(row_count, (col_count + 1) * 128)[:, 64 : 64 + 128 * col_count]


def fit_terms(resid_ext, rows_profile, cols_profile, coefs, col_ids, col_count):
    block_count, row_count, _, star_count = rows_profile.shape
    padded = jnp.pad(resid_ext, ((0, 0), (64, 64))).reshape(row_count, col_count + 1, 128)
    placed = placement(col_ids, col_count, resid_ext.dtype)
    windows = jnp.einsum("pjc,hcw->jhpw", placed, padded, precision=HIGHEST).reshape(
        block_count, row_count, 256
    )
    across = jnp.einsum(
        "jhw,jwk->jhk",
        windows,
        cols_profile.reshape(block_count, 256, 3 * star_count),
        precision=HIGHEST,
    ).reshape(block_count, row_count, 3, star_count)
    paired = jnp.einsum("jhas,jhbs->jabs", rows_profile, across, precision=HIGHEST)
    return jnp.einsum("abj,jabs->js", coefs.reshape(3, 3, block_count), paired, precision=HIGHEST)


def local(image, band_row, col_block, cell_index, offset_y, offset_x, flux_start, psf_coef):
    strip_rows, strip_width = image.shape
    col_count = strip_width // 128
    block_count = band_row.shape[0]
    coefs = block_coefs(psf_coef, cell_index)
    ylocal = band_row.astype(jnp.float32)[:, None] + offset_y
    weight = norms(ylocal, offset_x, coefs)
    ext_ids = jnp.arange(-REACH, strip_rows + REACH).astype(jnp.float32)
    own_ids = jnp.arange(strip_rows).astype(jnp.float32)
    columns = jnp.arange(256).astype(jnp.float32) - 64.0
    rows_ext = profile(ext_ids[None, :, None] - ylocal[:, None, :])
    cols_profile = profile(columns[None, :, None] - offset_x[:, None, :])
    edge_count = max(1, block_count // 4)
    band_kind = jnp.where(band_row < 16, 0, jnp.where(band_row > strip_rows - 48, 2, 1))
    ranking = jnp.argsort(band_kind * block_count + jnp.arange(block_count))
    top_ids = ranking[:edge_count]
    bottom_ids = ranking[block_count - edge_count :]
    star_meta = jnp.concatenate([coefs, col_block.astype(jnp.float32)[None, :]], axis=0)

    def model_of(fluxes):
        star_values = jnp.stack([ylocal, offset_x, fluxes])
        upper_vals, upper_meta = from_behind(
            (star_values[:, bottom_ids], star_meta[:, bottom_ids]), "ty", 1
        )
        lower_vals, lower_meta = from_behind(
            (star_values[:, top_ids], star_meta[:, top_ids]), "ty", -1
        )
        all_y = jnp.concatenate(
            [ylocal, upper_vals[0] - strip_rows, lower_vals[0] + strip_rows], axis=0
        )
        all_x = jnp.concatenate([offset_x, upper_vals[1], lower_vals[1]], axis=0)
        all_flux = jnp.concatenate([fluxes, upper_vals[2], lower_vals[2]], axis=0)
        all_coefs = jnp.concatenate([coefs, upper_meta[:9], lower_meta[:9]], axis=1)
        all_cols = jnp.concatenate(
            [col_block, upper_meta[9].astype(jnp.int32), lower_meta[9].astype(jnp.int32)], axis=0
        )
        return render(
            profile(own_ids[None, :, None] - all_y[:, None, :]),
            profile(columns[None, :, None] - all_x[:, None, :]),
            all_coefs,
            all_flux,
            all_cols,
            col_count,
        )

    fluxes = flux_start
    for iteration in range(ITERS):
        residue = image - model_of(fluxes)
        resid_ext = padded_2(residue, (("ty", 0),), REACH)
        fluxes = (
            fluxes
            + 0.5
            * fit_terms(resid_ext, rows_ext, cols_profile, coefs, col_block, col_count)
            / weight
        )
    residual = image - model_of(fluxes)
    return (fluxes, residual)


def solution(mesh):
    return jax.shard_map(
        local,
        mesh=mesh,
        in_specs=(
            P(("groups", "ty"), None),
            P(("groups", "ty")),
            P(("groups", "ty")),
            P(("groups", "ty")),
            P(("groups", "ty"), None),
            P(("groups", "ty"), None),
            P(("groups", "ty"), None),
            P(),
        ),
        out_specs=(P(("groups", "ty"), None), P(("groups", "ty"), None)),
        check_vma=False,
    )
```

profile of v0, /device:TPU:11, one launch (start us, length us, event | category | flops | bytes accessed | tf_op | source)
XLA Modules:
  0.0 109.2 jit_solution(11240024817080600241)
XLA Ops:
  7.9 2.6 %collective-permute-start.1 = (f32[3,1,128]{2,1,0:T(1,128)S(1)}, f32[3,1,128]{2,1,0:T(1,128)S(1)}, u32[]{:S(2)}, u32[]{:S(2)}) collective-permute-start(f32[3,1,128]{2,1,0:T(1,128)S(1)} %get-tuple-element.114), channel_id=1, source_target_pairs={{1,0},{2,1},{3,2},{4,3},{5,4},{6,5},{7,6},{8,7},{9,8},{10,9},{11,1... | collective-permute-start | bytes 4616 | tf_op jit(solution)/shard_map/ppermute | solution.py:16
  10.5 3.9 %collective-permute-start = (f32[3,1,128]{2,1,0:T(1,128)S(1)}, f32[3,1,128]{2,1,0:T(1,128)S(1)}, u32[]{:S(2)}, u32[]{:S(2)}) collective-permute-start(f32[3,1,128]{2,1,0:T(1,128)S(1)} %get-tuple-element.113), channel_id=1, source_target_pairs={{0,1},{1,2},{2,3},{3,4},{4,5},{5,6},{6,7},{7,8},{8,9},{9,10},{10,1... | collective-permute-start | bytes 4616 | tf_op jit(solution)/shard_map/ppermute | solution.py:16
  15.2 0.8 convolution_bitcast_fusion.6
  16.2 1.9 %collective-permute-start.3 = (f32[10,1]{0,1:T(1,128)S(1)}, f32[10,1]{0,1:T(1,128)S(1)}, u32[]{:S(2)}, u32[]{:S(2)}) collective-permute-start(f32[10,1]{0,1:T(1,128)S(1)} %get-tuple-element.155), channel_id=1, source_target_pairs={{1,0},{2,1},{3,2},{4,3},{5,4},{6,5},{7,6},{8,7},{9,8},{10,9},{11,1... | collective-permute-start | bytes 128 | tf_op jit(solution)/shard_map/ppermute | solution.py:16
  18.1 4.5 %collective-permute-start.2 = (f32[10,1]{0,1:T(1,128)S(1)}, f32[10,1]{0,1:T(1,128)S(1)}, u32[]{:S(2)}, u32[]{:S(2)}) collective-permute-start(f32[10,1]{0,1:T(1,128)S(1)} %get-tuple-element.154), channel_id=1, source_target_pairs={{0,1},{1,2},{2,3},{3,4},{4,5},{5,6},{6,7},{7,8},{8,9},{9,10},{10,1... | collective-permute-start | bytes 128 | tf_op jit(solution)/shard_map/ppermute | solution.py:16
  24.6 1.8 %convolution_bitcast_fusion.1 = f32[3,3,2,128]{0,1,3,2:T(4,128)S(1)} fusion(f32[2,32,3,128]{1,2,3,0:T(4,128)S(1)} %copy.41), kind=kOutput, calls=%fused_computation.30 | convolution fusion | flops 884736 | bytes 107520 | tf_op jit(solution)/shard_map/jkbs,jkds->bdjs/dot_general | solution.py:61
  26.9 1.8 %convolution_bitcast_fusion.2 = f32[3,3,2,128]{0,1,3,2:T(4,128)S(1)} fusion(f32[2,32,3,128]{1,2,3,0:T(4,128)S(1)} %copy.37), kind=kOutput, calls=%fused_computation.31 | convolution fusion | flops 884736 | bytes 107520 | tf_op jit(solution)/shard_map/jkas,jkcs->acjs/dot_general | solution.py:60
  28.7 1.1 %fusion.62 = (f32[2,256,1,128]{1,3,2,0:T(8,128)}, f32[2,256,1,128]{1,3,2,0:T(8,128)}, f32[2,256,1,128]{1,3,2,0:T(8,128)}) fusion(f32[2,128]{1,0:T(2,128)S(1)} %copy-done.7, f32[256]{0:T(256)S(1)} %convert_add_fusion), kind=kLoop, calls=%fused_computation.123 | loop fusion | flops 917504 | bytes 788480 | tf_op jit(solution)/shard_map/mul | solution.py:35
  30.3 1.0 copy.36
  35.4 4.4 %multiply_bitcast_fusion.2 = f32[4,256,3,128]{3,2,1,0:T(4,128)S(1)} fusion(f32[4,128]{1,0:T(4,128)S(1)} %pad_maximum_fusion.18, f32[3,3,4,1]{1,0,2,3:T(4,128)S(1)} %reshape.1038, f32[4,256,3,128]{3,1,2,0:T(8,128)S(1)} %pad_maximum_fusion), kind=kOutput, calls=%fused_computation.8 | convolution fusion | flops 14548992 | bytes 3147920 | tf_op jit(solution)/shard_map/abj,jwbs->jwas/dot_general | solution.py:70
  39.7 1.6 %copy.31 = f32[4,256,3,128]{1,3,2,0:T(8,128)} copy(f32[4,256,3,128]{3,2,1,0:T(4,128)S(1)} %multiply_bitcast_fusion.2) | data formatting | bytes 3145728 | tf_op jit(solution)/shard_map/mul | solution.py:73
  41.5 2.5 %fusion.55 = f32[4,64,256]{2,1,0:T(8,128)S(1)} fusion(f32[4,256,384]{1,2,0:T(8,128)} %bitcast.207, f32[4,64,1,128]{3,1,2,0:T(8,128)S(1)} %get-tuple-element.122, f32[4,64,1,128]{3,1,2,0:T(8,128)S(1)} %get-tuple-element.123, f32[4,64,1,128]{3,1,2,0:T(8,128)S(1)} %get-tuple-element.121), kind=kOutput, calls=%fused_computation.97 | convolution fusion | flops 302186496 | bytes 2228224 | tf_op jit(solution)/shard_map/jhk,jwk->jhw/dot_general | solution.py:74
  45.3 1.9 %collective-permute-start.5 = (f32[15,2048]{1,0:T(8,128)S(1)}, f32[15,2048]{1,0:T(8,128)S(1)}, u32[]{:S(2)}, u32[]{:S(2)}) collective-permute-start(f32[15,2048]{1,0:T(8,128)S(1)} %get-tuple-element.99), channel_id=1, source_target_pairs={{1,0},{2,1},{3,2},{4,3},{5,4},{6,5},{7,6},{8,7},{9,8},{10,9},{11,1... | collective-permute-start | bytes 368648 | tf_op jit(solution)/shard_map/ppermute | solution.py:27
  47.2 4.7 %collective-permute-start.4 = (f32[15,2048]{1,0:T(8,128)S(1)}, f32[15,2048]{1,0:T(8,128)S(1)}, u32[]{:S(2)}, u32[]{:S(2)}) collective-permute-start(f32[15,2048]{1,0:T(8,128)S(1)} %get-tuple-element.98), channel_id=1, source_target_pairs={{0,1},{1,2},{2,3},{3,4},{4,5},{5,6},{6,7},{7,8},{8,9},{9,10},{10,1... | collective-permute-start | bytes 368648 | tf_op jit(solution)/shard_map/ppermute | solution.py:24
  52.6 1.1 %collective-permute-done.4 = f32[15,2048]{1,0:T(8,128)S(1)} collective-permute-done((f32[15,2048]{1,0:T(8,128)S(1)}, f32[15,2048]{1,0:T(8,128)S(1)}, u32[]{:S(2)}, u32[]{:S(2)}) %collective-permute-start.4) | collective-permute-done | bytes 122912 | tf_op jit(solution)/shard_map/ppermute | solution.py:24
  56.2 1.8 %convolution_bitcast_fusion.3 = f32[2,3,3,128]{1,2,3,0:T(4,128)S(1)} fusion(f32[2,94,3,128]{1,2,3,0:T(4,128)S(1)} %copy.35, f32[2,94,3,128]{1,2,3,0:T(4,128)S(1)} %copy-done.2), kind=kOutput, calls=%fused_computation.32 | convolution fusion | flops 2598912 | bytes 586752 | tf_op jit(solution)/shard_map/jhas,jhbs->jabs/dot_general | solution.py:100
  58.5 2.0 %collective-permute-start.7 = (f32[3,1,128]{2,1,0:T(1,128)S(1)}, f32[3,1,128]{2,1,0:T(1,128)S(1)}, u32[]{:S(2)}, u32[]{:S(2)}) collective-permute-start(f32[3,1,128]{2,1,0:T(1,128)S(1)} %get-tuple-element.109), channel_id=1, source_target_pairs={{1,0},{2,1},{3,2},{4,3},{5,4},{6,5},{7,6},{8,7},{9,8},{10,9},{11,1... | collective-permute-start | bytes 4616 | tf_op jit(solution)/shard_map/ppermute | solution.py:16
  60.5 5.2 %collective-permute-start.6 = (f32[3,1,128]{2,1,0:T(1,128)S(1)}, f32[3,1,128]{2,1,0:T(1,128)S(1)}, u32[]{:S(2)}, u32[]{:S(2)}) collective-permute-start(f32[3,1,128]{2,1,0:T(1,128)S(1)} %get-tuple-element.108), channel_id=1, source_target_pairs={{0,1},{1,2},{2,3},{3,4},{4,5},{5,6},{6,7},{7,8},{8,9},{9,10},{10,1... | collective-permute-start | bytes 4616 | tf_op jit(solution)/shard_map/ppermute | solution.py:16
  66.9 4.4 %multiply_bitcast_fusion.1 = f32[4,256,3,128]{3,2,1,0:T(4,128)S(1)} fusion(f32[4,128]{1,0:T(4,128)S(1)} %pad_maximum_fusion.19, f32[3,3,4,1]{1,0,2,3:T(4,128)S(1)} %reshape.1038, f32[4,256,3,128]{3,1,2,0:T(8,128)S(1)} %pad_maximum_fusion.1), kind=kOutput, calls=%fused_computation.7 | convolution fusion | flops 14548992 | bytes 3147920 | tf_op jit(solution)/shard_map/abj,jwbs->jwas/dot_general | solution.py:70
  71.3 1.6 %copy.46 = f32[4,256,3,128]{1,3,2,0:T(8,128)} copy(f32[4,256,3,128]{3,2,1,0:T(4,128)S(1)} %multiply_bitcast_fusion.1) | data formatting | bytes 3145728 | tf_op jit(solution)/shard_map/mul | solution.py:73
  73.1 2.5 %fusion.52 = f32[4,64,256]{2,1,0:T(8,128)S(1)} fusion(f32[4,256,384]{1,2,0:T(8,128)} %bitcast.206, f32[4,64,1,128]{3,1,2,0:T(8,128)S(1)} %get-tuple-element.119, f32[4,64,1,128]{3,1,2,0:T(8,128)S(1)} %get-tuple-element.120, f32[4,64,1,128]{3,1,2,0:T(8,128)S(1)} %get-tuple-element.118), kind=kOutput, calls=%fused_computation.94 | convolution fusion | flops 302186496 | bytes 2228224 | tf_op jit(solution)/shard_map/jhk,jwk->jhw/dot_general | solution.py:74
  76.6 1.9 %collective-permute-start.9 = (f32[15,2048]{1,0:T(8,128)S(1)}, f32[15,2048]{1,0:T(8,128)S(1)}, u32[]{:S(2)}, u32[]{:S(2)}) collective-permute-start(f32[15,2048]{1,0:T(8,128)S(1)} %get-tuple-element.97), channel_id=1, source_target_pairs={{1,0},{2,1},{3,2},{4,3},{5,4},{6,5},{7,6},{8,7},{9,8},{10,9},{11,1... | collective-permute-start | bytes 368648 | tf_op jit(solution)/shard_map/ppermute | solution.py:27
  78.5 5.3 %collective-permute-start.8 = (f32[15,2048]{1,0:T(8,128)S(1)}, f32[15,2048]{1,0:T(8,128)S(1)}, u32[]{:S(2)}, u32[]{:S(2)}) collective-permute-start(f32[15,2048]{1,0:T(8,128)S(1)} %get-tuple-element.96), channel_id=1, source_target_pairs={{0,1},{1,2},{2,3},{3,4},{4,5},{5,6},{6,7},{7,8},{8,9},{9,10},{10,1... | collective-permute-start | bytes 368648 | tf_op jit(solution)/shard_map/ppermute | solution.py:24
  84.4 1.1 %collective-permute-done.8 = f32[15,2048]{1,0:T(8,128)S(1)} collective-permute-done((f32[15,2048]{1,0:T(8,128)S(1)}, f32[15,2048]{1,0:T(8,128)S(1)}, u32[]{:S(2)}, u32[]{:S(2)}) %collective-permute-start.8) | collective-permute-done | bytes 122912 | tf_op jit(solution)/shard_map/ppermute | solution.py:24
  86.8 0.8 fusion.167
  88.0 1.8 %convolution_bitcast_fusion = f32[2,3,3,128]{1,2,3,0:T(4,128)S(1)} fusion(f32[2,94,3,128]{1,2,3,0:T(4,128)S(1)} %copy.50, f32[2,94,3,128]{1,2,3,0:T(4,128)S(1)} %copy-done.3), kind=kOutput, calls=%fused_computation.29 | convolution fusion | flops 2598912 | bytes 586752 | tf_op jit(solution)/shard_map/jhas,jhbs->jabs/dot_general | solution.py:100
  90.4 2.8 %collective-permute-start.11 = (f32[3,1,128]{2,1,0:T(1,128)S(1)}, f32[3,1,128]{2,1,0:T(1,128)S(1)}, u32[]{:S(2)}, u32[]{:S(2)}) collective-permute-start(f32[3,1,128]{2,1,0:T(1,128)S(1)} %get-tuple-element.104), channel_id=1, source_target_pairs={{1,0},{2,1},{3,2},{4,3},{5,4},{6,5},{7,6},{8,7},{9,8},{10,9},{11,1... | collective-permute-start | bytes 4616 | tf_op jit(solution)/shard_map/ppermute | solution.py:16
  93.2 4.4 %collective-permute-start.10 = (f32[3,1,128]{2,1,0:T(1,128)S(1)}, f32[3,1,128]{2,1,0:T(1,128)S(1)}, u32[]{:S(2)}, u32[]{:S(2)}) collective-permute-start(f32[3,1,128]{2,1,0:T(1,128)S(1)} %get-tuple-element.103), channel_id=1, source_target_pairs={{0,1},{1,2},{2,3},{3,4},{4,5},{5,6},{6,7},{7,8},{8,9},{9,10},{10,1... | collective-permute-start | bytes 4616 | tf_op jit(solution)/shard_map/ppermute | solution.py:16
  98.8 4.4 %multiply_bitcast_fusion = f32[4,256,3,128]{3,2,1,0:T(4,128)S(1)} fusion(f32[4,128]{1,0:T(4,128)S(1)} %pad_maximum_fusion.20, f32[3,3,4,1]{1,0,2,3:T(4,128)S(1)} %reshape.1038, f32[4,256,3,128]{3,1,2,0:T(8,128)S(1)} %pad_maximum_fusion.2), kind=kOutput, calls=%fused_computation.6 | convolution fusion | flops 14548992 | bytes 3147920 | tf_op jit(solution)/shard_map/abj,jwbs->jwas/dot_general | solution.py:70
  103.2 1.6 %copy.54 = f32[4,256,3,128]{1,3,2,0:T(8,128)} copy(f32[4,256,3,128]{3,2,1,0:T(4,128)S(1)} %multiply_bitcast_fusion) | data formatting | bytes 3145728 | tf_op jit(solution)/shard_map/mul | solution.py:73
  104.9 2.5 %fusion.49 = f32[4,64,256]{2,1,0:T(8,128)S(1)} fusion(f32[4,256,384]{1,2,0:T(8,128)} %bitcast.205, f32[4,64,1,128]{3,1,2,0:T(8,128)S(1)} %get-tuple-element.116, f32[4,64,1,128]{3,1,2,0:T(8,128)S(1)} %get-tuple-element.117, f32[4,64,1,128]{3,1,2,0:T(8,128)S(1)} %get-tuple-element.115), kind=kOutput, calls=%fused_computation.91 | convolution fusion | flops 302186496 | bytes 2228224 | tf_op jit(solution)/shard_map/jhk,jwk->jhw/dot_general | solution.py:74
  108.2 1.0 slice_subtract_fusion
  (128 shorter events, 21.8 us)
Async XLA Ops:
  0.6 14.6 %copy-start = (f32[9,256]{1,0:T(8,128)S(1)}, f32[9,256]{1,0:T(8,128)}, u32[]{:S(2)}) copy-start(f32[9,256]{1,0:T(8,128)} %param.15) | copy-start | bytes 27652
  7.9 26.9 %collective-permute-start.1 = (f32[3,1,128]{2,1,0:T(1,128)S(1)}, f32[3,1,128]{2,1,0:T(1,128)S(1)}, u32[]{:S(2)}, u32[]{:S(2)}) collective-permute-start(f32[3,1,128]{2,1,0:T(1,128)S(1)} %get-tuple-element.114), channel_id=1, source_target_pairs={{1,0},{2,1},{3,2},{4,3},{5,4},{6,5},{7,6},{8,7},{9,8},{10,9},{11,1... | collective-permute-start | bytes 4616 | tf_op jit(solution)/shard_map/ppermute | solution.py:16
  10.5 24.3 %collective-permute-start = (f32[3,1,128]{2,1,0:T(1,128)S(1)}, f32[3,1,128]{2,1,0:T(1,128)S(1)}, u32[]{:S(2)}, u32[]{:S(2)}) collective-permute-start(f32[3,1,128]{2,1,0:T(1,128)S(1)} %get-tuple-element.113), channel_id=1, source_target_pairs={{0,1},{1,2},{2,3},{3,4},{4,5},{5,6},{6,7},{7,8},{8,9},{9,10},{10,1... | collective-permute-start | bytes 4616 | tf_op jit(solution)/shard_map/ppermute | solution.py:16
  16.2 15.9 %collective-permute-start.3 = (f32[10,1]{0,1:T(1,128)S(1)}, f32[10,1]{0,1:T(1,128)S(1)}, u32[]{:S(2)}, u32[]{:S(2)}) collective-permute-start(f32[10,1]{0,1:T(1,128)S(1)} %get-tuple-element.155), channel_id=1, source_target_pairs={{1,0},{2,1},{3,2},{4,3},{5,4},{6,5},{7,6},{8,7},{9,8},{10,9},{11,1... | collective-permute-start | bytes 128 | tf_op jit(solution)/shard_map/ppermute | solution.py:16
  18.1 15.2 %collective-permute-start.2 = (f32[10,1]{0,1:T(1,128)S(1)}, f32[10,1]{0,1:T(1,128)S(1)}, u32[]{:S(2)}, u32[]{:S(2)}) collective-permute-start(f32[10,1]{0,1:T(1,128)S(1)} %get-tuple-element.154), channel_id=1, source_target_pairs={{0,1},{1,2},{2,3},{3,4},{4,5},{5,6},{6,7},{7,8},{8,9},{9,10},{10,1... | collective-permute-start | bytes 128 | tf_op jit(solution)/shard_map/ppermute | solution.py:16
  26.4 2.2 %copy-start.10 = (s32[2]{0:T(128)S(1)}, s32[2]{0:T(128)}, u32[]{:S(2)}) copy-start(s32[2]{0:T(128)} %param.10) | copy-start | bytes 28
  26.4 2.3 %copy-start.7 = (f32[2,128]{1,0:T(2,128)S(1)}, f32[2,128]{1,0:T(2,128)}, u32[]{:S(2)}) copy-start(f32[2,128]{1,0:T(2,128)} %param.13) | copy-start | bytes 3076
  30.3 5.0 %copy-start.8 = (f32[2,128]{1,0:T(2,128)S(1)}, f32[2,128]{1,0:T(2,128)}, u32[]{:S(2)}) copy-start(f32[2,128]{1,0:T(2,128)} %param.14) | copy-start | bytes 3076
  44.0 1.0 copy-start.1
  44.7 7.2 %copy-start.4 = (f32[2,256,1,128]{1,3,2,0:T(8,128)S(1)}, f32[2,256,1,128]{1,3,2,0:T(8,128)}, u32[]{:S(2)}) copy-start(f32[2,256,1,128]{1,3,2,0:T(8,128)} %get-tuple-element.130) | copy-start | bytes 786436
  44.7 7.2 %copy-start.5 = (f32[2,256,1,128]{1,3,2,0:T(8,128)S(1)}, f32[2,256,1,128]{1,3,2,0:T(8,128)}, u32[]{:S(2)}) copy-start(f32[2,256,1,128]{1,3,2,0:T(8,128)} %get-tuple-element.131) | copy-start | bytes 786436
  44.7 7.2 %copy-start.6 = (f32[2,256,1,128]{1,3,2,0:T(8,128)S(1)}, f32[2,256,1,128]{1,3,2,0:T(8,128)}, u32[]{:S(2)}) copy-start(f32[2,256,1,128]{1,3,2,0:T(8,128)} %get-tuple-element.132) | copy-start | bytes 786436
  45.3 7.3 %collective-permute-start.5 = (f32[15,2048]{1,0:T(8,128)S(1)}, f32[15,2048]{1,0:T(8,128)S(1)}, u32[]{:S(2)}, u32[]{:S(2)}) collective-permute-start(f32[15,2048]{1,0:T(8,128)S(1)} %get-tuple-element.99), channel_id=1, source_target_pairs={{1,0},{2,1},{3,2},{4,3},{5,4},{6,5},{7,6},{8,7},{9,8},{10,9},{11,1... | collective-permute-start | bytes 368648 | tf_op jit(solution)/shard_map/ppermute | solution.py:27
  47.2 6.5 %collective-permute-start.4 = (f32[15,2048]{1,0:T(8,128)S(1)}, f32[15,2048]{1,0:T(8,128)S(1)}, u32[]{:S(2)}, u32[]{:S(2)}) collective-permute-start(f32[15,2048]{1,0:T(8,128)S(1)} %get-tuple-element.98), channel_id=1, source_target_pairs={{0,1},{1,2},{2,3},{3,4},{4,5},{5,6},{6,7},{7,8},{8,9},{9,10},{10,1... | collective-permute-start | bytes 368648 | tf_op jit(solution)/shard_map/ppermute | solution.py:24
  54.8 1.4 %copy-start.2 = (f32[2,94,3,128]{1,2,3,0:T(4,128)S(1)}, f32[2,94,3,128]{1,2,3,0:T(4,128)}, u32[]{:S(2)}) copy-start(f32[2,94,3,128]{1,2,3,0:T(4,128)} %copy.36) | copy-start | bytes 866308
  58.5 7.2 %collective-permute-start.7 = (f32[3,1,128]{2,1,0:T(1,128)S(1)}, f32[3,1,128]{2,1,0:T(1,128)S(1)}, u32[]{:S(2)}, u32[]{:S(2)}) collective-permute-start(f32[3,1,128]{2,1,0:T(1,128)S(1)} %get-tuple-element.109), channel_id=1, source_target_pairs={{1,0},{2,1},{3,2},{4,3},{5,4},{6,5},{7,6},{8,7},{9,8},{10,9},{11,1... | collective-permute-start | bytes 4616 | tf_op jit(solution)/shard_map/ppermute | solution.py:16
  60.5 5.9 %collective-permute-start.6 = (f32[3,1,128]{2,1,0:T(1,128)S(1)}, f32[3,1,128]{2,1,0:T(1,128)S(1)}, u32[]{:S(2)}, u32[]{:S(2)}) collective-permute-start(f32[3,1,128]{2,1,0:T(1,128)S(1)} %get-tuple-element.108), channel_id=1, source_target_pairs={{0,1},{1,2},{2,3},{3,4},{4,5},{5,6},{6,7},{7,8},{8,9},{9,10},{10,1... | collective-permute-start | bytes 4616 | tf_op jit(solution)/shard_map/ppermute | solution.py:16
  76.6 7.8 %collective-permute-start.9 = (f32[15,2048]{1,0:T(8,128)S(1)}, f32[15,2048]{1,0:T(8,128)S(1)}, u32[]{:S(2)}, u32[]{:S(2)}) collective-permute-start(f32[15,2048]{1,0:T(8,128)S(1)} %get-tuple-element.97), channel_id=1, source_target_pairs={{1,0},{2,1},{3,2},{4,3},{5,4},{6,5},{7,6},{8,7},{9,8},{10,9},{11,1... | collective-permute-start | bytes 368648 | tf_op jit(solution)/shard_map/ppermute | solution.py:27
  78.5 7.0 %collective-permute-start.8 = (f32[15,2048]{1,0:T(8,128)S(1)}, f32[15,2048]{1,0:T(8,128)S(1)}, u32[]{:S(2)}, u32[]{:S(2)}) collective-permute-start(f32[15,2048]{1,0:T(8,128)S(1)} %get-tuple-element.96), channel_id=1, source_target_pairs={{0,1},{1,2},{2,3},{3,4},{4,5},{5,6},{6,7},{7,8},{8,9},{9,10},{10,1... | collective-permute-start | bytes 368648 | tf_op jit(solution)/shard_map/ppermute | solution.py:24
  86.6 1.4 %copy-start.3 = (f32[2,94,3,128]{1,2,3,0:T(4,128)S(1)}, f32[2,94,3,128]{1,2,3,0:T(4,128)}, u32[]{:S(2)}) copy-start(f32[2,94,3,128]{1,2,3,0:T(4,128)} %copy.36) | copy-start | bytes 866308
  90.3 8.5 %copy-start.9 = (f32[2,128]{1,0:T(2,128)}, f32[2,128]{1,0:T(2,128)S(1)}, u32[]{:S(2)}) copy-start(f32[2,128]{1,0:T(2,128)S(1)} %divide_add_fusion) | copy-start | bytes 3076
  90.4 7.2 %collective-permute-start.11 = (f32[3,1,128]{2,1,0:T(1,128)S(1)}, f32[3,1,128]{2,1,0:T(1,128)S(1)}, u32[]{:S(2)}, u32[]{:S(2)}) collective-permute-start(f32[3,1,128]{2,1,0:T(1,128)S(1)} %get-tuple-element.104), channel_id=1, source_target_pairs={{1,0},{2,1},{3,2},{4,3},{5,4},{6,5},{7,6},{8,7},{9,8},{10,9},{11,1... | collective-permute-start | bytes 4616 | tf_op jit(solution)/shard_map/ppermute | solution.py:16
  93.2 5.1 %collective-permute-start.10 = (f32[3,1,128]{2,1,0:T(1,128)S(1)}, f32[3,1,128]{2,1,0:T(1,128)S(1)}, u32[]{:S(2)}, u32[]{:S(2)}) collective-permute-start(f32[3,1,128]{2,1,0:T(1,128)S(1)} %get-tuple-element.103), channel_id=1, source_target_pairs={{0,1},{1,2},{2,3},{3,4},{4,5},{5,6},{6,7},{7,8},{8,9},{9,10},{10,1... | collective-permute-start | bytes 4616 | tf_op jit(solution)/shard_map/ppermute | solution.py:16
where the time goes:
time: 111 us; the launch traced here: 109 us
  starting transfers between devices  41.1 us (37%)
  matrix products  34.2 us (31%)
  local copies, waits for them, and re-layouts  11.5 us (10%)
  other arithmetic  11 us (10%)
  between operations  6.63 us (6%)
  waiting for transfers between devices  4.72 us (4%)
    ppermute x8, starting transfers between devices, from_behind(): return lax.ppermute(shard, axis, pairs)  27.3 us
    dot_general x3, matrix products, render(): jnp.einsum('abj,jwbs->jwas', coefs.reshape(3, 3, block_count), cols_profi...  13.1 us
    ppermute x2, starting transfers between devices, padded_2(): lax.ppermute(lax.slice_in_dim(block, block.shape[dim] - width, None, axis...  10 us
    dot_general x3, matrix products, render(): jnp.einsum('jhk,jwk->jhw', rows_profile.reshape(block_count, row_count, 3...  7.44 us
    mul x3, local copies, waits for them, and re-layouts, render(): mixed = mixed * fluxes[:, None, None, :]  4.83 us
    ppermute x2, starting transfers between devices, padded_2(): lax.ppermute(lax.slice_in_dim(block, 0, width, axis=dim), axis, backward)  3.84 us
    mul x9, other arithmetic, profile(): core_part = jnp.exp(-0.5 * scaled * scaled) * tapered  3.79 us
    dot_general x2, matrix products, fit_terms(): jnp.einsum('jhas,jhbs->jabs', rows_profile, across, precision=HIGHEST)  3.64 us
  transfers between devices with their start and end apart: 12, of which 6 were waited for; matrix products, arithmetic and copies ran while one was open for 11% of the time, Pallas kernels for 0%

commit v1 on v0

v1 whole, which is shorter than its diff:
```python
import functools

import jax
import jax.numpy as jnp
from jax import lax
from jax.experimental import pallas as pl
from jax.experimental.pallas import tpu as pltpu
from jax.sharding import PartitionSpec as P

REACH = 15
ITERS = 2
HALO = 16
LANES = 128
WIN = 384
SLOTS = 8


HIGHEST = lax.Precision.HIGHEST


def profile(dist):
    tapered = jnp.maximum(0.0, 1.0 - dist / 15.5 * (dist / 15.5))
    scaled = dist / 1.7
    core_part = jnp.exp(-0.5 * scaled * scaled) * tapered
    wing_part = jnp.exp(-dist * dist / 72.0) * tapered
    return jnp.stack([core_part, scaled * core_part, wing_part], axis=-2)


def profile3(dist):
    tapered = jnp.maximum(0.0, 1.0 - dist / 15.5 * (dist / 15.5))
    scaled = dist / 1.7
    core_part = jnp.exp(-0.5 * scaled * scaled) * tapered
    wing_part = jnp.exp(-dist * dist / 72.0) * tapered
    return core_part, scaled * core_part, wing_part


def block_coefs(psf_coef, cell_index):
    cell_ids = jnp.arange(psf_coef.shape[1])
    picker = (cell_ids[:, None] == cell_index[None, :]).astype(psf_coef.dtype)
    return jnp.dot(psf_coef, picker, precision=HIGHEST)


def norms(ylocal, xoff, coefs):
    block_count = ylocal.shape[0]
    offsets = jnp.arange(-15, 17).astype(ylocal.dtype)
    rows_profile = profile(
        jnp.floor(ylocal)[:, None, :] + offsets[None, :, None] - ylocal[:, None, :]
    )
    cols_profile = profile(jnp.floor(xoff)[:, None, :] + offsets[None, :, None] - xoff[:, None, :])
    gram_rows = jnp.einsum("jkas,jkcs->acjs", rows_profile, rows_profile, precision=HIGHEST)
    gram_cols = jnp.einsum("jkbs,jkds->bdjs", cols_profile, cols_profile, precision=HIGHEST)
    shaped = coefs.reshape(3, 3, block_count)
    return jnp.einsum(
        "abj,cdj,acjs,bdjs->js", shaped, shaped, gram_rows, gram_cols, precision=HIGHEST
    )


def exchange(to_above, to_below):
    count = lax.axis_size("ty")
    forward = [(i, i + 1) for i in range(count - 1)]
    backward = [(i + 1, i) for i in range(count - 1)]
    from_above = lax.ppermute(to_below, "ty", forward)
    from_below = lax.ppermute(to_above, "ty", backward)
    return from_above, from_below


def phase_kernel(
    final, own, blocks, cols_ref, coef_ref, y_ref, x_ref, f_ref, w_ref, above_ref, img_ref,
    below_ref, mask_ref, out_ref, canvas
):
    ext_rows, pad_width = canvas.shape
    strip_rows, width = img_ref.shape
    canvas[...] = jnp.zeros_like(canvas)
    hpos = lax.broadcasted_iota(jnp.int32, (ext_rows, LANES), 0).astype(jnp.float32) - HALO
    wpos = lax.broadcasted_iota(jnp.int32, (WIN, LANES), 0).astype(jnp.float32) - LANES
    keep_above = hpos < REACH
    dims_nt = (((1,), (1,)), ((), ()))
    saved = []
    for j in range(blocks):
        rows = profile3(hpos - y_ref[j : j + 1, :])
        if j == own:
            rows_model = tuple(jnp.where(keep_above, r, 0.0) for r in rows)
        else:
            rows_model = rows
        cols = profile3(wpos - x_ref[j : j + 1, :])
        flux = f_ref[j : j + 1, :]
        stamp = None
        for a in range(3):
            base = 9 * j + 3 * a
            mixed = (
                coef_ref[base] * cols[0] + coef_ref[base + 1] * cols[1] + coef_ref[base + 2] * cols[2]
            ) * flux
            part = lax.dot_general(
                rows_model[a], mixed, dims_nt, precision=HIGHEST,
                preferred_element_type=jnp.float32,
            )
            stamp = part if stamp is None else stamp + part
        start = pl.multiple_of(cols_ref[j] * LANES, LANES)
        canvas[:, pl.ds(start, WIN)] += stamp
        if j < own:
            saved.append((rows, cols))
    if final:
        out_ref[...] = img_ref[...] - canvas[HALO : HALO + strip_rows, LANES : LANES + width]
        return
    top = (above_ref[...] - canvas[0:HALO, LANES : LANES + width]) * mask_ref[0:HALO, :]
    mid = (img_ref[...] - canvas[HALO : HALO + strip_rows, LANES : LANES + width]) * mask_ref[
        HALO : HALO + strip_rows, :
    ]
    bot = (below_ref[...] - canvas[HALO + strip_rows :, LANES : LANES + width]) * mask_ref[
        HALO + strip_rows :, :
    ]
    canvas[0:HALO, LANES : LANES + width] = top
    canvas[HALO : HALO + strip_rows, LANES : LANES + width] = mid
    canvas[HALO + strip_rows :, LANES : LANES + width] = bot
    canvas[:, 0:LANES] = jnp.zeros((ext_rows, LANES), jnp.float32)
    canvas[:, LANES + width :] = jnp.zeros((ext_rows, pad_width - LANES - width), jnp.float32)
    out_ref[...] = jnp.zeros_like(out_ref)
    for j in range(own):
        rows, cols = saved[j]
        start = pl.multiple_of(cols_ref[j] * LANES, LANES)
        window = canvas[:, pl.ds(start, WIN)]
        across = [
            jnp.dot(window, cols[b], precision=HIGHEST, preferred_element_type=jnp.float32)
            for b in range(3)
        ]
        grad = None
        for a in range(3):
            for b in range(3):
                paired = jnp.sum(rows[a] * across[b], axis=0, keepdims=True)
                term = coef_ref[9 * j + 3 * a + b] * paired
                grad = term if grad is None else grad + term
        out_ref[j : j + 1, :] = f_ref[j : j + 1, :] + 0.5 * grad / w_ref[j : j + 1, :]


def run_phase(final, own, blocks, cols, coef_flat, ys, xs, fs, ws, above, image, below, mask):
    strip_rows, width = image.shape
    ext_rows = strip_rows + 2 * HALO
    smem = pl.BlockSpec(memory_space=pltpu.SMEM)
    vmem = pl.BlockSpec(memory_space=pltpu.VMEM)
    if final:
        out_shape = jax.ShapeDtypeStruct((strip_rows, width), jnp.float32)
    else:
        out_shape = jax.ShapeDtypeStruct((SLOTS, LANES), jnp.float32)
    matmul_flops = 2 * 3 * ext_rows * WIN * LANES * (blocks + (0 if final else own))
    return pl.pallas_call(
        functools.partial(phase_kernel, final, own, blocks),
        out_shape=out_shape,
        in_specs=[smem, smem] + [vmem] * 8,
        out_specs=vmem,
        scratch_shapes=[pltpu.VMEM((ext_rows, width + 2 * LANES), jnp.float32)],
        cost_estimate=pl.CostEstimate(
            flops=6 * matmul_flops, transcendentals=blocks * 2 * (ext_rows + WIN) * LANES,
            bytes_accessed=4 * (ext_rows * width * (1 if final else 2)),
        ),
    )(cols, coef_flat, ys, xs, fs, ws, above, image, below, mask)


def local(image, band_row, col_block, cell_index, offset_y, offset_x, flux_start, psf_coef):
    strip_rows, strip_width = image.shape
    own = band_row.shape[0]
    coefs = block_coefs(psf_coef, cell_index)
    ylocal = band_row.astype(jnp.float32)[:, None] + offset_y
    weight = norms(ylocal, offset_x, coefs)

    top = (band_row[1] < band_row[0]).astype(jnp.int32)
    pick_top = top == 0

    def edge(values, axis):
        first = lax.index_in_dim(values, 0, axis, keepdims=False)
        second = lax.index_in_dim(values, 1, axis, keepdims=False)
        return jnp.where(pick_top, first, second), jnp.where(pick_top, second, first)

    y_top, y_bot = edge(ylocal, 0)
    x_top, x_bot = edge(offset_x, 0)
    f_top, f_bot = edge(flux_start, 0)
    c_top, c_bot = edge(coefs, 1)
    col_f = col_block.astype(jnp.float32)
    k_top, k_bot = edge(col_f, 0)

    def star_row(y, x, f, c, k):
        meta = jnp.concatenate([c, k[None], jnp.zeros((LANES - 10,), jnp.float32)])
        row = jnp.concatenate([y, x, f, meta, jnp.zeros((strip_width - 4 * LANES,), jnp.float32)])
        return row[None, :]

    send_up = jnp.concatenate(
        [image[:REACH], star_row(y_top, x_top, f_top, c_top, k_top)], axis=0
    )
    send_down = jnp.concatenate(
        [star_row(y_bot, x_bot, f_bot, c_bot, k_bot), image[strip_rows - REACH :]], axis=0
    )
    got_above, got_below = exchange(send_up, send_down)

    def unpack(row):
        return (
            row[0:LANES],
            row[LANES : 2 * LANES],
            row[2 * LANES : 3 * LANES],
            row[3 * LANES : 3 * LANES + 9],
            row[3 * LANES + 9],
        )

    ya, xa, fa, ca, ka = unpack(got_above[0])
    yb, xb, fb, cb, kb = unpack(got_below[REACH])

    ext_rows = strip_rows + 2 * HALO
    me = lax.axis_index("ty")
    last = lax.axis_size("ty") - 1
    h_ids = jnp.arange(ext_rows)
    row_ok = (h_ids >= HALO - REACH) & (h_ids < HALO + strip_rows + REACH)
    row_ok = row_ok & ((h_ids >= HALO) | (me > 0)) & ((h_ids < HALO + strip_rows) | (me < last))
    mask = row_ok.astype(jnp.float32)[:, None]

    blocks = own + 2
    spare = jnp.zeros((SLOTS - blocks, LANES), jnp.float32)
    ys = jnp.concatenate(
        [ylocal, (ya - strip_rows)[None], (yb + strip_rows)[None], spare], axis=0
    )
    xs = jnp.concatenate([offset_x, xa[None], xb[None], spare], axis=0)
    all_c = jnp.concatenate([coefs, ca[:, None], cb[:, None]], axis=1)
    coef_flat = all_c.T.reshape(-1)
    cols = jnp.concatenate(
        [col_block, ka.astype(jnp.int32)[None], kb.astype(jnp.int32)[None]]
    )
    ws = jnp.concatenate([weight, jnp.ones((SLOTS - own, LANES), jnp.float32)], axis=0)

    phase = functools.partial(
        run_phase, own=own, blocks=blocks, cols=cols, coef_flat=coef_flat, ys=ys, xs=xs, ws=ws,
        above=got_above, image=image, below=got_below, mask=mask,
    )
    fluxes = flux_start
    f_above, f_below = fa, fb
    for iteration in range(ITERS):
        fs = jnp.concatenate([fluxes, f_above[None], f_below[None], spare], axis=0)
        fluxes = phase(False, fs=fs)[:own]
        new_top, new_bot = edge(fluxes, 0)
        f_above, f_below = exchange(new_top, new_bot)
    fs = jnp.concatenate([fluxes, f_above[None], f_below[None], spare], axis=0)
    residual = phase(True, fs=fs)
    return (fluxes, residual)


def solution(mesh):
    return jax.shard_map(
        local,
        mesh=mesh,
        in_specs=(
            P(("groups", "ty"), None),
            P(("groups", "ty")),
            P(("groups", "ty")),
            P(("groups", "ty")),
            P(("groups", "ty"), None),
            P(("groups", "ty"), None),
            P(("groups", "ty"), None),
            P(),
        ),
        out_specs=(P(("groups", "ty"), None), P(("groups", "ty"), None)),
        check_vma=False,
    )
```

time: 111 us -> 67.1 us (0.60); the launches traced: 109 us -> 66.5 us
  matrix products: 34.2 us -> 4.5 us
  starting transfers between devices: 41.1 us -> 16.6 us
  Pallas kernels: 0 us -> 17.6 us
  other arithmetic: 11 us -> 4.99 us
  waiting for transfers between devices: 4.72 us -> 6.39 us
    dot_general x17 -> x0, matrix products: 29 us -> none  [the longest x3 13.1 us: render(): jnp.einsum('abj,jwbs->jwas', coefs.reshape(3, 3, block_count), cols_profi...]
    ppermute x12 -> x6, starting transfers between devices: 41.1 us -> 16.6 us  [the longest x3 10.3 us: exchange(): from_above = lax.ppermute(to_below, 'ty', forward)]
    pallas_call x0 -> x3, Pallas kernels: none -> 17.6 us  [run_phase(): pl.pallas_call(functools.partial(phase_kernel, final, own, blocks), out_s...]
    mul x3 -> x0, local copies, waits for them, and re-layouts: 4.83 us -> none  [render(): mixed = mixed * fluxes[:, None, None, :]]
    mul x9 -> x1, other arithmetic: 3.79 us -> 0.12 us  [profile(): core_part = jnp.exp(-0.5 * scaled * scaled) * tapered]
    slice x5 -> x8, local copies, waits for them, and re-layouts: 1.79 us -> 5.4 us  [the longest x1 1.34 us: local(): top = (band_row[1] < band_row[0]).astype(jnp.int32)]
    unnamed x25 -> x20, local copies, waits for them, and re-layouts: 0.57 us -> 2.71 us
    concatenate x12 -> x6, other arithmetic: 0.8 us -> 2.61 us  [the longest x3 1.98 us: local(): fs = jnp.concatenate([fluxes, f_above[None], f_below[None], spare], axis=0)]
  transfers between devices with their start and end apart: 12 -> 6, of which waited for: 6 -> 2; matrix products, arithmetic and copies ran while one was open for 11% -> 11% of each run, Pallas kernels for 0% -> 0%
where the time goes in v1:
time: 67.1 us; the launch traced here: 66.5 us
  Pallas kernels  17.6 us (26%)
  starting transfers between devices  16.6 us (25%)
  local copies, waits for them, and re-layouts  10.4 us (15%)
  waiting for transfers between devices  6.39 us (10%)
  between operations  6.03 us (9%)
  other arithmetic  4.99 us (7%)
  matrix products  4.5 us (7%)
    pallas_call x3, Pallas kernels, run_phase(): pl.pallas_call(functools.partial(phase_kernel, final, own, blocks), out_s...  17.6 us
    ppermute x3, starting transfers between devices, exchange(): from_above = lax.ppermute(to_below, 'ty', forward)  10.3 us
    ppermute x3, waiting for transfers between devices, exchange(): from_below = lax.ppermute(to_above, 'ty', backward)  6.38 us
    ppermute x3, starting transfers between devices, exchange(): from_below = lax.ppermute(to_above, 'ty', backward)  6.35 us
    unnamed x20, local copies, waits for them, and re-layouts  2.71 us
    concatenate x3, other arithmetic, local(): fs = jnp.concatenate([fluxes, f_above[None], f_below[None], spare], axis=0)  1.98 us
    dot_general x1, matrix products, norms(): jnp.einsum('jkas,jkcs->acjs', rows_profile, rows_profile, precision=HIGHEST)  1.77 us
    dot_general x1, matrix products, norms(): jnp.einsum('jkbs,jkds->bdjs', cols_profile, cols_profile, precision=HIGHEST)  1.77 us
  transfers between devices with their start and end apart: 6, of which 2 were waited for; matrix products, arithmetic and copies ran while one was open for 11% of the time, Pallas kernels for 0%

profile of v1, /device:TPU:11, one launch (start us, length us, event | category | flops | bytes accessed | tf_op | source)
XLA Modules:
  0.0 66.5 jit_solution(11475951965382040244)
XLA Ops:
  0.7 1.3 %fusion.43 = (s32[1]{0:T(128)}, s32[1]{0:T(128)}) fusion(s32[2]{0:T(128)} %param.9), kind=kLoop, calls=%fused_computation.87 | loop fusion | bytes 16 | tf_op jit(solution)/shard_map/slice | solution.py:165
  3.3 0.6 copy-done.6
  4.0 0.6 fusion.42
  4.6 0.7 copy-done.9
  5.4 0.7 %copy-done.2 = f32[2,128]{1,0:T(2,128)S(1)} copy-done((f32[2,128]{1,0:T(2,128)S(1)}, f32[2,128]{1,0:T(2,128)}, u32[]{:S(2)}) %copy-start.2) | copy-done | bytes 1048
  6.1 1.0 %fusion.39 = (f32[15,2048]{1,0:T(8,128)S(1)}, f32[15,2048]{1,0:T(8,128)S(1)}) fusion(f32[64,2048]{1,0:T(8,128)} %img_ref.5), kind=kLoop, calls=%fused_computation.83 | loop fusion | bytes 491520 | tf_op jit(solution)/shard_map/slice | solution.py:189
  7.2 0.7 %copy-done.1 = f32[2,128]{1,0:T(2,128)S(1)} copy-done((f32[2,128]{1,0:T(2,128)S(1)}, f32[2,128]{1,0:T(2,128)}, u32[]{:S(2)}) %copy-start.1) | copy-done | bytes 1048
  9.3 3.7 %collective-permute-start = (f32[16,2048]{1,0:T(8,128)S(1)}, f32[16,2048]{1,0:T(8,128)S(1)}, u32[]{:S(2)}, u32[]{:S(2)}) collective-permute-start(f32[16,2048]{1,0:T(8,128)S(1)} %pad_maximum_fusion), channel_id=1, source_target_pairs={{0,1},{1,2},{2,3},{3,4},{4,5},{5,6},{6,7},{7,8},{8,9},{9,10},{10,1... | collective-permute-start | bytes 393224 | tf_op jit(solution)/shard_map/ppermute | solution.py:62
  14.4 1.9 %collective-permute-start.1 = (f32[16,2048]{1,0:T(8,128)S(1)}, f32[16,2048]{1,0:T(8,128)S(1)}, u32[]{:S(2)}, u32[]{:S(2)}) collective-permute-start(f32[16,2048]{1,0:T(8,128)S(1)} %pad_maximum_fusion.1), channel_id=1, source_target_pairs={{1,0},{2,1},{3,2},{4,3},{5,4},{6,5},{7,6},{8,7},{9,8},{10,9},{11,1... | collective-permute-start | bytes 393224 | tf_op jit(solution)/shard_map/ppermute | solution.py:63
  16.9 1.8 %convolution_bitcast_fusion.1 = f32[3,3,2,128]{0,1,3,2:T(4,128)S(1)} fusion(f32[2,32,3,128]{1,2,3,0:T(4,128)S(1)} %copy.10), kind=kOutput, calls=%fused_computation.1 | convolution fusion | flops 884736 | bytes 107520 | tf_op jit(solution)/shard_map/jkas,jkcs->acjs/dot_general | solution.py:50
  19.0 1.8 %convolution_bitcast_fusion = f32[3,3,2,128]{0,1,3,2:T(4,128)S(1)} fusion(f32[2,32,3,128]{1,2,3,0:T(4,128)S(1)} %copy.14), kind=kOutput, calls=%fused_computation | convolution fusion | flops 884736 | bytes 107520 | tf_op jit(solution)/shard_map/jkbs,jkds->bdjs/dot_general | solution.py:51
  21.8 0.6 concatenate.45.w_ref
  22.4 0.6 fusion.9.mask_ref
  23.0 0.7 reshape.216.coef_ref
  24.9 0.6 slice.147
  26.2 0.6 pad_add_fusion.cols_ref
  26.7 0.7 %maximum_maximum_fusion.2 = (f32[8,128]{1,0:T(8,128)}, f32[8,128]{1,0:T(8,128)}, f32[8,128]{1,0:T(8,128)}) fusion(f32[1,128]{1,0:T(1,128)S(1)} %get-tuple-element.9, f32[1,128]{1,0:T(1,128)S(1)} %get-tuple-element.6, f32[2,128]{1,0:T(2,128)S(1)} %copy-done.2, f32[8]{0:T(128)S(1)} %pad.26.clone, f32[1,128]{1,0:T(1,128)S(1)} %get-tuple-element.10, ...), kind=kLoop, calls=%fused_computation.45 | loop fusion | flops 9216 | bytes 18464 | tf_op jit(solution)/shard_map/concatenate | solution.py:233
  27.4 6.0 %shard_map.95 = f32[8,128]{1,0:T(8,128)} custom-call(s32[4]{0:T(128)} %pad_add_fusion.cols_ref, f32[36]{0:T(128)} %reshape.216.coef_ref, f32[8,128]{1,0:T(8,128)} %get-tuple-element.35.y_ref, f32[8,128]{1,0:T(8,128)} %get-tuple-element.34.x_ref, f32[8,128]{1,0:T(8,128)} %get-tuple-element.33.f_ref, f32[8,128]{1,0:T(8,128)} %concatenate.45.w_ref, ...), custom_call_target="tpu_custom_call" | custom-call | flops 1019215872 | bytes 1572864 | tf_op jit(solution)/shard_map/pallas_call | solution.py:145
  33.4 0.8 %fusion.32 = (f32[128]{0:T(128)S(1)}, f32[128]{0:T(128)S(1)}) fusion(pred[]{:T(512)} %bitcast.2, f32[8,128]{1,0:T(8,128)} %shard_map.95), kind=kLoop, calls=%fused_computation.69 | loop fusion | flops 256 | bytes 2049 | tf_op jit(solution)/shard_map/jit(_where)/select_n | solution.py:171
  34.2 4.5 %collective-permute-start.2 = (f32[128]{0:T(128)S(1)}, f32[128]{0:T(128)S(1)}, u32[]{:S(2)}, u32[]{:S(2)}) collective-permute-start(f32[128]{0:T(128)S(1)} %get-tuple-element.14), channel_id=1, source_target_pairs={{0,1},{1,2},{2,3},{3,4},{4,5},{5,6},{6,7},{7,8},{8,9},{9,10},{10,1... | collective-permute-start | bytes 1544 | tf_op jit(solution)/shard_map/ppermute | solution.py:62
  38.7 2.1 %collective-permute-start.3 = (f32[128]{0:T(128)S(1)}, f32[128]{0:T(128)S(1)}, u32[]{:S(2)}, u32[]{:S(2)}) collective-permute-start(f32[128]{0:T(128)S(1)} %get-tuple-element.15), channel_id=1, source_target_pairs={{1,0},{2,1},{3,2},{4,3},{5,4},{6,5},{7,6},{8,7},{9,8},{10,9},{11,1... | collective-permute-start | bytes 1544 | tf_op jit(solution)/shard_map/ppermute | solution.py:63
  40.9 3.6 %collective-permute-done.3 = f32[128]{0:T(128)S(1)} collective-permute-done((f32[128]{0:T(128)S(1)}, f32[128]{0:T(128)S(1)}, u32[]{:S(2)}, u32[]{:S(2)}) %collective-permute-start.3) | collective-permute-done | bytes 544 | tf_op jit(solution)/shard_map/ppermute | solution.py:63
  44.5 0.6 slice-done
  45.1 0.7 maximum_maximum_fusion.3.f_ref
  45.8 6.0 %shard_map.96 = f32[8,128]{1,0:T(8,128)} custom-call(s32[4]{0:T(128)} %pad_add_fusion.cols_ref, f32[36]{0:T(128)} %reshape.216.coef_ref, f32[8,128]{1,0:T(8,128)} %get-tuple-element.35.y_ref, f32[8,128]{1,0:T(8,128)} %get-tuple-element.34.x_ref, f32[8,128]{1,0:T(8,128)} %maximum_maximum_fusion.3.f_ref, f32[8,128]{1,0:T(8,128)} %concatenate.45.w_ref, ...), custom_call_target="tpu_custom_call" | custom-call | flops 1019215872 | bytes 1572864 | tf_op jit(solution)/shard_map/pallas_call | solution.py:145
  51.8 0.8 %fusion.34 = (f32[128]{0:T(128)S(1)}, f32[128]{0:T(128)S(1)}) fusion(pred[]{:T(512)} %bitcast.2, f32[8,128]{1,0:T(8,128)} %shard_map.96), kind=kLoop, calls=%fused_computation.71 | loop fusion | flops 256 | bytes 2049 | tf_op jit(solution)/shard_map/jit(_where)/select_n | solution.py:171
  52.6 2.0 %collective-permute-start.4 = (f32[128]{0:T(128)S(1)}, f32[128]{0:T(128)S(1)}, u32[]{:S(2)}, u32[]{:S(2)}) collective-permute-start(f32[128]{0:T(128)S(1)} %get-tuple-element.12), channel_id=1, source_target_pairs={{0,1},{1,2},{2,3},{3,4},{4,5},{5,6},{6,7},{7,8},{8,9},{9,10},{10,1... | collective-permute-start | bytes 1544 | tf_op jit(solution)/shard_map/ppermute | solution.py:62
  54.5 2.3 %collective-permute-start.5 = (f32[128]{0:T(128)S(1)}, f32[128]{0:T(128)S(1)}, u32[]{:S(2)}, u32[]{:S(2)}) collective-permute-start(f32[128]{0:T(128)S(1)} %get-tuple-element.13), channel_id=1, source_target_pairs={{1,0},{2,1},{3,2},{4,3},{5,4},{6,5},{7,6},{8,7},{9,8},{10,9},{11,1... | collective-permute-start | bytes 1544 | tf_op jit(solution)/shard_map/ppermute | solution.py:63
  56.9 0.7 %slice.143 = f32[2,128]{1,0:T(2,128)S(1)} slice(f32[8,128]{1,0:T(8,128)} %shard_map.96), slice={[0:2], [0:128]} | slice | bytes 2048 | tf_op jit(solution)/shard_map/slice | solution.py:234
  57.6 2.7 %collective-permute-done.5 = f32[128]{0:T(128)S(1)} collective-permute-done((f32[128]{0:T(128)S(1)}, f32[128]{0:T(128)S(1)}, u32[]{:S(2)}, u32[]{:S(2)}) %collective-permute-start.5) | collective-permute-done | bytes 544 | tf_op jit(solution)/shard_map/ppermute | solution.py:63
  60.3 0.7 maximum_maximum_fusion.4.f_ref
  61.0 5.6 %shard_map.97 = f32[64,2048]{1,0:T(8,128)} custom-call(s32[4]{0:T(128)} %pad_add_fusion.cols_ref, f32[36]{0:T(128)} %reshape.216.coef_ref, f32[8,128]{1,0:T(8,128)} %get-tuple-element.35.y_ref, f32[8,128]{1,0:T(8,128)} %get-tuple-element.34.x_ref, f32[8,128]{1,0:T(8,128)} %maximum_maximum_fusion.4.f_ref, f32[8,128]{1,0:T(8,128)} %concatenate.45.w_ref, ...), custom_call_target="tpu_custom_call" | custom-call | flops 679477248 | bytes 786432 | tf_op jit(solution)/shard_map/pallas_call | solution.py:145
  (53 shorter events, 3.0 us)
Async XLA Ops:
  0.6 3.9 %copy-start = (f32[9,256]{1,0:T(8,128)S(1)}, f32[9,256]{1,0:T(8,128)}, u32[]{:S(2)}) copy-start(f32[9,256]{1,0:T(8,128)} %param.15) | copy-start | bytes 27652
  0.6 1.3 %copy-start.4 = (s32[2]{0:T(128)S(1)}, s32[2]{0:T(128)}, u32[]{:S(2)}) copy-start(s32[2]{0:T(128)} %param.9) | copy-start | bytes 28
  3.3 0.7 copy-start.6
  4.5 0.7 copy-start.9
  5.4 0.7 %copy-start.2 = (f32[2,128]{1,0:T(2,128)S(1)}, f32[2,128]{1,0:T(2,128)}, u32[]{:S(2)}) copy-start(f32[2,128]{1,0:T(2,128)} %param.14) | copy-start | bytes 3076
  6.1 1.0 %copy-start.5 = (f32[2,128]{1,0:T(2,128)S(1)}, f32[2,128]{1,0:T(2,128)}, u32[]{:S(2)}) copy-start(f32[2,128]{1,0:T(2,128)} %param.12) | copy-start | bytes 3076
  7.2 0.7 %copy-start.1 = (f32[2,128]{1,0:T(2,128)S(1)}, f32[2,128]{1,0:T(2,128)}, u32[]{:S(2)}) copy-start(f32[2,128]{1,0:T(2,128)} %param.13) | copy-start | bytes 3076
  9.3 13.7 %collective-permute-start = (f32[16,2048]{1,0:T(8,128)S(1)}, f32[16,2048]{1,0:T(8,128)S(1)}, u32[]{:S(2)}, u32[]{:S(2)}) collective-permute-start(f32[16,2048]{1,0:T(8,128)S(1)} %pad_maximum_fusion), channel_id=1, source_target_pairs={{0,1},{1,2},{2,3},{3,4},{4,5},{5,6},{6,7},{7,8},{8,9},{9,10},{10,1... | collective-permute-start | bytes 393224 | tf_op jit(solution)/shard_map/ppermute | solution.py:62
  14.4 8.6 %collective-permute-start.1 = (f32[16,2048]{1,0:T(8,128)S(1)}, f32[16,2048]{1,0:T(8,128)S(1)}, u32[]{:S(2)}, u32[]{:S(2)}) collective-permute-start(f32[16,2048]{1,0:T(8,128)S(1)} %pad_maximum_fusion.1), channel_id=1, source_target_pairs={{1,0},{2,1},{3,2},{4,3},{5,4},{6,5},{7,6},{8,7},{9,8},{10,9},{11,1... | collective-permute-start | bytes 393224 | tf_op jit(solution)/shard_map/ppermute | solution.py:63
  23.0 4.4 %copy-start.7 = (f32[16,2048]{1,0:T(8,128)}, f32[16,2048]{1,0:T(8,128)S(1)}, u32[]{:S(2)}) copy-start(f32[16,2048]{1,0:T(8,128)S(1)} %collective-permute-done.above_ref) | copy-start | bytes 393220
  23.0 4.4 %copy-start.8 = (f32[16,2048]{1,0:T(8,128)}, f32[16,2048]{1,0:T(8,128)S(1)}, u32[]{:S(2)}) copy-start(f32[16,2048]{1,0:T(8,128)S(1)} %collective-permute-done.1.below_ref) | copy-start | bytes 393220
  34.2 6.7 %collective-permute-start.2 = (f32[128]{0:T(128)S(1)}, f32[128]{0:T(128)S(1)}, u32[]{:S(2)}, u32[]{:S(2)}) collective-permute-start(f32[128]{0:T(128)S(1)} %get-tuple-element.14), channel_id=1, source_target_pairs={{0,1},{1,2},{2,3},{3,4},{4,5},{5,6},{6,7},{7,8},{8,9},{9,10},{10,1... | collective-permute-start | bytes 1544 | tf_op jit(solution)/shard_map/ppermute | solution.py:62
  38.7 5.8 %collective-permute-start.3 = (f32[128]{0:T(128)S(1)}, f32[128]{0:T(128)S(1)}, u32[]{:S(2)}, u32[]{:S(2)}) collective-permute-start(f32[128]{0:T(128)S(1)} %get-tuple-element.15), channel_id=1, source_target_pairs={{1,0},{2,1},{3,2},{4,3},{5,4},{6,5},{7,6},{8,7},{9,8},{10,9},{11,1... | collective-permute-start | bytes 1544 | tf_op jit(solution)/shard_map/ppermute | solution.py:63
  44.5 0.6 slice-start
  52.6 5.0 %collective-permute-start.4 = (f32[128]{0:T(128)S(1)}, f32[128]{0:T(128)S(1)}, u32[]{:S(2)}, u32[]{:S(2)}) collective-permute-start(f32[128]{0:T(128)S(1)} %get-tuple-element.12), channel_id=1, source_target_pairs={{0,1},{1,2},{2,3},{3,4},{4,5},{5,6},{6,7},{7,8},{8,9},{9,10},{10,1... | collective-permute-start | bytes 1544 | tf_op jit(solution)/shard_map/ppermute | solution.py:62
  54.5 5.8 %collective-permute-start.5 = (f32[128]{0:T(128)S(1)}, f32[128]{0:T(128)S(1)}, u32[]{:S(2)}, u32[]{:S(2)}) collective-permute-start(f32[128]{0:T(128)S(1)} %get-tuple-element.13), channel_id=1, source_target_pairs={{1,0},{2,1},{3,2},{4,3},{5,4},{6,5},{7,6},{8,7},{9,8},{10,9},{11,1... | collective-permute-start | bytes 1544 | tf_op jit(solution)/shard_map/ppermute | solution.py:63
  57.6 2.7 %copy-start.3 = (f32[2,128]{1,0:T(2,128)}, f32[2,128]{1,0:T(2,128)S(1)}, u32[]{:S(2)}) copy-start(f32[2,128]{1,0:T(2,128)S(1)} %slice.143) | copy-start | bytes 3076

commit v2 on v1

v2 whole, which is shorter than its diff:
```python
import functools

import jax
import jax.numpy as jnp
from jax import lax
from jax.experimental import pallas as pl
from jax.experimental.pallas import tpu as pltpu
from jax.sharding import PartitionSpec as P

REACH = 15
ITERS = 2
HALO = 16
LANES = 128
WIN = 384
META = 8
PACKET = HALO + META


HIGHEST = lax.Precision.HIGHEST
DIMS_NT = (((1,), (1,)), ((), ()))


def profile3(dist):
    tapered = jnp.maximum(0.0, 1.0 - dist / 15.5 * (dist / 15.5))
    scaled = dist / 1.7
    core_part = jnp.exp(-0.5 * scaled * scaled) * tapered
    wing_part = jnp.exp(-dist * dist / 72.0) * tapered
    return core_part, scaled * core_part, wing_part


def exchange(to_above, to_below):
    count = lax.axis_size("ty")
    forward = [(i, i + 1) for i in range(count - 1)]
    backward = [(i + 1, i) for i in range(count - 1)]
    from_above = lax.ppermute(to_below, "ty", forward)
    from_below = lax.ppermute(to_above, "ty", backward)
    return from_above, from_below


def own_coefs(psf_ref, cell_ref, j):
    cell = cell_ref[j]
    return [psf_ref[k, cell] for k in range(9)]


def setup_kernel(
    band_ref, col_ref, cell_ref, psf_ref, img_ref, oy_ref, ox_ref, f_ref, up_ref, down_ref, w_ref
):
    strip_rows = img_ref.shape[0]
    own = oy_ref.shape[0]
    offs = lax.broadcasted_iota(jnp.int32, (32, LANES), 0).astype(jnp.float32) - 15.0
    lane = lax.broadcasted_iota(jnp.int32, (1, LANES), 1)
    ys, metas = [], []
    for j in range(own):
        y = band_ref[j].astype(jnp.float32) + oy_ref[j : j + 1, :]
        x = ox_ref[j : j + 1, :]
        c = own_coefs(psf_ref, cell_ref, j)
        rows = profile3(jnp.floor(y) + offs - y)
        cols = profile3(jnp.floor(x) + offs - x)
        gram_r = [[jnp.sum(rows[a] * rows[b], axis=0, keepdims=True) for b in range(3)] for a in range(3)]
        gram_c = [[jnp.sum(cols[a] * cols[b], axis=0, keepdims=True) for b in range(3)] for a in range(3)]
        weight = None
        for a in range(3):
            for cc in range(3):
                inner = None
                for b in range(3):
                    for d in range(3):
                        term = (c[3 * a + b] * c[3 * cc + d]) * gram_c[b][d]
                        inner = term if inner is None else inner + term
                term = gram_r[a][cc] * inner
                weight = term if weight is None else weight + term
        w_ref[j : j + 1, :] = weight
        meta = jnp.zeros((1, LANES), jnp.float32)
        for k in range(9):
            meta = jnp.where(lane == k, c[k], meta)
        meta = jnp.where(lane == 9, col_ref[j].astype(jnp.float32), meta)
        ys.append(y)
        metas.append(meta)
    top_first = band_ref[0] <= band_ref[1]

    def pick(first, second):
        return jnp.where(top_first, first, second), jnp.where(top_first, second, first)

    y_top, y_bot = pick(ys[0], ys[1])
    x_top, x_bot = pick(ox_ref[0:1, :], ox_ref[1:2, :])
    f_top, f_bot = pick(f_ref[0:1, :], f_ref[1:2, :])
    m_top, m_bot = pick(metas[0], metas[1])
    up_ref[...] = jnp.zeros_like(up_ref)
    down_ref[...] = jnp.zeros_like(down_ref)
    up_ref[0:HALO, :] = img_ref[0:HALO, :]
    for r, v in enumerate((y_top, x_top, f_top, m_top)):
        up_ref[HALO + r : HALO + r + 1, 0:LANES] = v
    for r, v in enumerate((y_bot, x_bot, f_bot, m_bot)):
        down_ref[r : r + 1, 0:LANES] = v
    down_ref[META:PACKET, :] = img_ref[strip_rows - HALO : strip_rows, :]


def phase_kernel(
    final, above_row, below_row,
    band_ref, col_ref, cell_ref, psf_ref, nbm_ref, flag_ref,
    oy_ref, ox_ref, f_ref, w_ref, above_ref, img_ref, below_ref, fa_ref, fb_ref,
    *rest,
):
    if final:
        out_ref, canvas = rest
    else:
        fout_ref, up_ref, down_ref, canvas = rest
    ext_rows, pad_width = canvas.shape
    strip_rows, width = img_ref.shape
    own = oy_ref.shape[0]
    canvas[...] = jnp.zeros_like(canvas)
    hpos = lax.broadcasted_iota(jnp.int32, (ext_rows, LANES), 0).astype(jnp.float32) - HALO
    wpos = lax.broadcasted_iota(jnp.int32, (WIN, LANES), 0).astype(jnp.float32) - LANES
    keep_above = hpos < REACH

    specs = []
    for j in range(own):
        y = band_ref[j].astype(jnp.float32) + oy_ref[j : j + 1, :]
        specs.append((y, ox_ref[j : j + 1, :], f_ref[j : j + 1, :],
                      own_coefs(psf_ref, cell_ref, j), col_ref[j]))
    specs.append((
        above_ref[0:1, 0:LANES] - strip_rows, above_ref[1:2, 0:LANES],
        fa_ref[above_row : above_row + 1, 0:LANES],
        [nbm_ref[k] for k in range(9)], nbm_ref[9].astype(jnp.int32),
    ))
    specs.append((
        below_ref[HALO : HALO + 1, 0:LANES] + strip_rows, below_ref[HALO + 1 : HALO + 2, 0:LANES],
        fb_ref[below_row : below_row + 1, 0:LANES],
        [nbm_ref[16 + k] for k in range(9)], nbm_ref[16 + 9].astype(jnp.int32),
    ))

    saved = []
    for j, (y, x, flux, c, col) in enumerate(specs):
        rows = profile3(hpos - y)
        if j == own:
            rows_model = tuple(jnp.where(keep_above, r, 0.0) for r in rows)
        else:
            rows_model = rows
        cols = profile3(wpos - x)
        stamp = None
        for a in range(3):
            mixed = (c[3 * a] * cols[0] + c[3 * a + 1] * cols[1] + c[3 * a + 2] * cols[2]) * flux
            part = lax.dot_general(
                rows_model[a], mixed, DIMS_NT, precision=HIGHEST,
                preferred_element_type=jnp.float32,
            )
            stamp = part if stamp is None else stamp + part
        start = pl.multiple_of(col * LANES, LANES)
        canvas[:, pl.ds(start, WIN)] += stamp
        if j < own:
            saved.append((rows, cols, c, start))
    inner = slice(LANES, LANES + width)
    if final:
        out_ref[...] = img_ref[...] - canvas[HALO : HALO + strip_rows, inner]
        return
    edge_ids = lax.broadcasted_iota(jnp.int32, (HALO, width), 0)
    top_ok = (edge_ids >= HALO - REACH) & (flag_ref[0] > 0)
    bot_ok = (edge_ids < REACH) & (flag_ref[1] > 0)
    top = jnp.where(top_ok, above_ref[META:PACKET, :] - canvas[0:HALO, inner], 0.0)
    bot = jnp.where(bot_ok, below_ref[0:HALO, :] - canvas[HALO + strip_rows :, inner], 0.0)
    mid = img_ref[...] - canvas[HALO : HALO + strip_rows, inner]
    canvas[0:HALO, inner] = top
    canvas[HALO : HALO + strip_rows, inner] = mid
    canvas[HALO + strip_rows :, inner] = bot
    canvas[:, 0:LANES] = jnp.zeros((ext_rows, LANES), jnp.float32)
    canvas[:, LANES + width :] = jnp.zeros((ext_rows, pad_width - LANES - width), jnp.float32)
    news = []
    for j in range(own):
        rows, cols, c, start = saved[j]
        window = canvas[:, pl.ds(start, WIN)]
        across = [
            jnp.dot(window, cols[b], precision=HIGHEST, preferred_element_type=jnp.float32)
            for b in range(3)
        ]
        grad = None
        for a in range(3):
            for b in range(3):
                paired = jnp.sum(rows[a] * across[b], axis=0, keepdims=True)
                term = c[3 * a + b] * paired
                grad = term if grad is None else grad + term
        new = f_ref[j : j + 1, :] + 0.5 * grad / w_ref[j : j + 1, :]
        fout_ref[j : j + 1, :] = new
        news.append(new)
    top_first = band_ref[0] <= band_ref[1]
    up_ref[...] = jnp.where(top_first, news[0], news[1])
    down_ref[...] = jnp.where(top_first, news[1], news[0])


def local(image, band_row, col_block, cell_index, offset_y, offset_x, flux_start, psf_coef):
    strip_rows, strip_width = image.shape
    own = band_row.shape[0]
    f32 = jnp.float32
    smem = pl.BlockSpec(memory_space=pltpu.SMEM)
    vmem = pl.BlockSpec(memory_space=pltpu.VMEM)
    packet = jax.ShapeDtypeStruct((PACKET, strip_width), f32)
    send_up, send_down, weight = pl.pallas_call(
        setup_kernel,
        out_shape=(packet, packet, jax.ShapeDtypeStruct((own, LANES), f32)),
        in_specs=[smem] * 4 + [vmem] * 4,
        out_specs=(vmem, vmem, vmem),
    )(band_row, col_block, cell_index, psf_coef, image, offset_y, offset_x, flux_start)
    got_above, got_below = exchange(send_up, send_down)

    me = lax.axis_index("ty")
    last = lax.axis_size("ty") - 1
    flags = jnp.stack([me > 0, me < last]).astype(jnp.int32)
    nbm = jnp.concatenate([got_above[3, :16], got_below[HALO + 3, :16]])

    ext_rows = strip_rows + 2 * HALO
    blocks = own + 2
    flops = 6 * 2 * 3 * ext_rows * WIN * LANES * (blocks + own)
    flux_shape = jax.ShapeDtypeStruct((own, LANES), f32)
    edge_shape = jax.ShapeDtypeStruct((1, LANES), f32)
    common = (band_row, col_block, cell_index, psf_coef, nbm, flags,
              offset_y, offset_x)

    def phase(final, fluxes, fa, fb, above_row, below_row):
        kernel = functools.partial(phase_kernel, final, above_row, below_row)
        if final:
            out_shape = jax.ShapeDtypeStruct((strip_rows, strip_width), f32)
            out_specs = vmem
        else:
            out_shape = (flux_shape, edge_shape, edge_shape)
            out_specs = (vmem, vmem, vmem)
        return pl.pallas_call(
            kernel,
            out_shape=out_shape,
            in_specs=[smem] * 6 + [vmem] * 9,
            out_specs=out_specs,
            scratch_shapes=[pltpu.VMEM((ext_rows, strip_width + 2 * LANES), f32)],
            cost_estimate=pl.CostEstimate(
                flops=flops, transcendentals=blocks * 2 * (ext_rows + WIN) * LANES,
                bytes_accessed=4 * ext_rows * strip_width * 2,
            ),
        )(*common, fluxes, weight, got_above, image, got_below, fa, fb)

    fluxes = flux_start
    fa, fb = got_above, got_below
    above_row, below_row = 2, HALO + 2
    for iteration in range(ITERS):
        fluxes, new_top, new_bot = phase(False, fluxes, fa, fb, above_row, below_row)
        fa, fb = exchange(new_top, new_bot)
        above_row, below_row = 0, 0
    residual = phase(True, fluxes, fa, fb, above_row, below_row)
    return (fluxes, residual)


def solution(mesh):
    return jax.shard_map(
        local,
        mesh=mesh,
        in_specs=(
            P(("groups", "ty"), None),
            P(("groups", "ty")),
            P(("groups", "ty")),
            P(("groups", "ty")),
            P(("groups", "ty"), None),
            P(("groups", "ty"), None),
            P(("groups", "ty"), None),
            P(),
        ),
        out_specs=(P(("groups", "ty"), None), P(("groups", "ty"), None)),
        check_vma=False,
    )
```

time: 67.1 us -> 51.2 us (0.76)
  local copies, waits for them, and re-layouts: 10.4 us -> 2.3 us
  waiting for transfers between devices: 6.39 us -> 12.1 us
  between operations: 6.03 us -> 0.75 us
  matrix products: 4.5 us -> 0 us
  other arithmetic: 4.99 us -> 1.22 us
  Pallas kernels: 17.6 us -> 19.8 us
  starting transfers between devices: 16.6 us -> 14.7 us
    slice x8 -> x0, local copies, waits for them, and re-layouts: 5.4 us -> none  [the longest x1 1.34 us: local(): top = (band_row[1] < band_row[0]).astype(jnp.int32)]
    ppermute x3, waiting for transfers between devices: 6.38 us -> 11.7 us  [exchange(): from_below = lax.ppermute(to_above, 'ty', backward)]
    dot_general x5 -> x0, matrix products: 4.5 us -> none  [the longest x1 1.77 us: norms(): jnp.einsum('jkas,jkcs->acjs', rows_profile, rows_profile, precision=HIGHEST)]
    ppermute x3, starting transfers between devices: 10.3 us -> 7.88 us  [exchange(): from_above = lax.ppermute(to_below, 'ty', forward)]
    pallas_call x3 -> x4, Pallas kernels: 17.6 us -> 19.8 us  [the longest x3 17.9 us: phase(): pl.pallas_call(kernel, out_shape=out_shape, in_specs=[smem] * 6 + [vmem]...]
    concatenate x6 -> x1, other arithmetic: 2.61 us -> 0.6 us  [local(): nbm = jnp.concatenate([got_above[3, :16], got_below[HALO + 3, :16]])]
    select_n x5 -> x0, other arithmetic: 1.52 us -> none  [edge(): jnp.where(pick_top, second, first)]
    concatenate x4 -> x0, local copies, waits for them, and re-layouts: 0.84 us -> none  [the longest x1 0.59 us: local(): jnp.concatenate([weight, jnp.ones((SLOTS - own, LANES), jnp.float32)], ax...]
  transfers between devices with their start and end apart: 6 -> 6, of which waited for: 2 -> 4; matrix products, arithmetic and copies ran while one was open for 11% -> 1% of each run, Pallas kernels for 0% -> 0%
where the time goes in v2:
time: 51.2 us; the launch traced here: 50.9 us
  Pallas kernels  19.8 us (39%)
  starting transfers between devices  14.7 us (29%)
  waiting for transfers between devices  12.1 us (24%)
  local copies, waits for them, and re-layouts  2.3 us (4%)
  other arithmetic  1.22 us (2%)
  between operations  0.75 us (1%)
    pallas_call x3, Pallas kernels, phase(): pl.pallas_call(kernel, out_shape=out_shape, in_specs=[smem] * 6 + [vmem]...  17.9 us
    ppermute x3, waiting for transfers between devices, exchange(): from_below = lax.ppermute(to_above, 'ty', backward)  11.7 us
    ppermute x3, starting transfers between devices, exchange(): from_above = lax.ppermute(to_below, 'ty', forward)  7.88 us
    ppermute x3, starting transfers between devices, exchange(): from_below = lax.ppermute(to_above, 'ty', backward)  6.83 us
    unnamed x20, local copies, waits for them, and re-layouts  2.29 us
    pallas_call x1, Pallas kernels, local(): pl.pallas_call(setup_kernel, out_shape=(packet, packet, jax.ShapeDtypeStr...  1.92 us
  transfers between devices with their start and end apart: 6, of which 4 were waited for; matrix products, arithmetic and copies ran while one was open for 1% of the time, Pallas kernels for 0%

profile of v2, /device:TPU:11, one launch (start us, length us, event | category | flops | bytes accessed | tf_op | source)
XLA Modules:
  0.0 50.9 jit_solution(16920505681406160657)
XLA Ops:
  0.6 1.9 %shard_map.95 = (f32[24,2048]{1,0:T(8,128)}, f32[24,2048]{1,0:T(8,128)}, f32[2,128]{1,0:T(2,128)}) custom-call(s32[2]{0:T(128)} %band_ref.7, s32[2]{0:T(128)} %col_ref.7, s32[2]{0:T(128)} %cell_ref.7, f32[9,256]{1,0:T(8,128)} %psf_ref.7, f32[64,2048]{1,0:T(8,128)} %img_ref.7, f32[2,128]{1,0:T(2,128)} %oy_ref.7, f32[2,128]{1,0:T(2,128)} %ox_ref.7, f32[2,128]{1,0:T(2,128)} %f_ref.3), custom_call_target="tpu_custom_call" | custom-call | tf_op jit(solution)/shard_map/pallas_call | solution.py:195
  2.5 3.7 %collective-permute-start = (f32[24,2048]{1,0:T(8,128)}, f32[24,2048]{1,0:T(8,128)S(1)}, u32[]{:S(2)}, u32[]{:S(2)}) collective-permute-start(f32[24,2048]{1,0:T(8,128)} %get-tuple-element.11), channel_id=1, source_target_pairs={{0,1},{1,2},{2,3},{3,4},{4,5},{5,6},{6,7},{7,8},{8,9},{9,10},{10,1... | collective-permute-start | bytes 589832 | tf_op jit(solution)/shard_map/ppermute | solution.py:35
  6.3 1.9 %collective-permute-start.1 = (f32[24,2048]{1,0:T(8,128)}, f32[24,2048]{1,0:T(8,128)S(1)}, u32[]{:S(2)}, u32[]{:S(2)}) collective-permute-start(f32[24,2048]{1,0:T(8,128)} %get-tuple-element.12), channel_id=1, source_target_pairs={{1,0},{2,1},{3,2},{4,3},{5,4},{6,5},{7,6},{8,7},{9,8},{10,9},{11,1... | collective-permute-start | bytes 589832 | tf_op jit(solution)/shard_map/ppermute | solution.py:36
  8.2 0.6 %add_convert_fusion.flag_ref = s32[2]{0:T(128)} fusion(pred[1]{0:T(512)(128)(4,1)} %bitcast.3, pred[1]{0:T(512)(128)(4,1)} %bitcast.2), kind=kLoop, calls=%fused_computation | loop fusion | flops 4 | bytes 10 | tf_op jit(solution)/shard_map/convert_element_type | solution.py:205
  8.8 0.4 collective-permute-done.above_ref.fa_ref
  9.2 0.0 copy-start
  9.2 5.2 %collective-permute-done.1.below_ref.fb_ref = f32[24,2048]{1,0:T(8,128)S(1)} collective-permute-done((f32[24,2048]{1,0:T(8,128)}, f32[24,2048]{1,0:T(8,128)S(1)}, u32[]{:S(2)}, u32[]{:S(2)}) %collective-permute-start.1) | collective-permute-done | bytes 196640 | tf_op jit(solution)/shard_map/ppermute | solution.py:36
  14.4 0.0 copy-start.1
  14.4 0.6 %pad_maximum_fusion.nbm_ref = f32[32]{0:T(128)} fusion(f32[16]{0:T(128)S(1)} %slice_bitcast_fusion, f32[16]{0:T(128)S(1)} %slice_bitcast_fusion.1), kind=kLoop, calls=%fused_computation.3 | loop fusion | flops 32 | bytes 256 | tf_op jit(solution)/shard_map/concatenate | solution.py:206
  15.0 0.0 copy-done
  15.0 0.1 copy-done.1
  15.1 6.2 %shard_map.96 = (f32[2,128]{1,0:T(2,128)}, f32[1,128]{1,0:T(1,128)}, f32[1,128]{1,0:T(1,128)}) custom-call(s32[2]{0:T(128)} %band_ref.7, s32[2]{0:T(128)} %col_ref.7, s32[2]{0:T(128)} %cell_ref.7, f32[9,256]{1,0:T(8,128)} %psf_ref.7, f32[32]{0:T(128)} %pad_maximum_fusion.nbm_ref, s32[2]{0:T(128)} %add_convert_fusion.flag_ref, f32[2,128]{1,0:T(2,128)} %oy_ref.7, ...), custom_call_target="tpu_custom_call" | custom-call | flops 1019215872 | bytes 1572864 | tf_op jit(solution)/shard_map/pallas_call | solution.py:224
  21.2 0.7 %copy-done.9 = f32[1,128]{1,0:T(1,128)S(1)} copy-done((f32[1,128]{1,0:T(1,128)S(1)}, f32[1,128]{1,0:T(1,128)}, u32[]{:S(2)}) %copy-start.9) | copy-done | bytes 536
  21.9 2.0 %collective-permute-start.2 = (f32[1,128]{1,0:T(1,128)S(1)}, f32[1,128]{1,0:T(1,128)S(1)}, u32[]{:S(2)}, u32[]{:S(2)}) collective-permute-start(f32[1,128]{1,0:T(1,128)S(1)} %copy-done.9), channel_id=1, source_target_pairs={{0,1},{1,2},{2,3},{3,4},{4,5},{5,6},{6,7},{7,8},{8,9},{9,10},{10,1... | collective-permute-start | bytes 1544 | tf_op jit(solution)/shard_map/ppermute | solution.py:35
  23.9 0.0 copy-done.7
  24.0 2.4 %collective-permute-start.3 = (f32[1,128]{1,0:T(1,128)S(1)}, f32[1,128]{1,0:T(1,128)S(1)}, u32[]{:S(2)}, u32[]{:S(2)}) collective-permute-start(f32[1,128]{1,0:T(1,128)S(1)} %copy-done.7), channel_id=1, source_target_pairs={{1,0},{2,1},{3,2},{4,3},{5,4},{6,5},{7,6},{8,7},{9,8},{10,9},{11,1... | collective-permute-start | bytes 1544 | tf_op jit(solution)/shard_map/ppermute | solution.py:36
  26.4 0.0 collective-permute-done.2.fa_ref
  26.4 0.0 copy-start.3
  26.4 3.3 %collective-permute-done.3.fb_ref = f32[1,128]{1,0:T(1,128)S(1)} collective-permute-done((f32[1,128]{1,0:T(1,128)S(1)}, f32[1,128]{1,0:T(1,128)S(1)}, u32[]{:S(2)}, u32[]{:S(2)}) %collective-permute-start.3) | collective-permute-done | bytes 544 | tf_op jit(solution)/shard_map/ppermute | solution.py:36
  29.7 0.0 copy-done.3
  29.7 0.5 copy-done.6
  30.2 6.0 %shard_map.97 = (f32[2,128]{1,0:T(2,128)}, f32[1,128]{1,0:T(1,128)}, f32[1,128]{1,0:T(1,128)}) custom-call(s32[2]{0:T(128)} %band_ref.7, s32[2]{0:T(128)} %col_ref.7, s32[2]{0:T(128)} %cell_ref.7, f32[9,256]{1,0:T(8,128)} %psf_ref.7, f32[32]{0:T(128)} %pad_maximum_fusion.nbm_ref, s32[2]{0:T(128)} %add_convert_fusion.flag_ref, f32[2,128]{1,0:T(2,128)} %oy_ref.7, ...), custom_call_target="tpu_custom_call" | custom-call | flops 1019215872 | bytes 1572864 | tf_op jit(solution)/shard_map/pallas_call | solution.py:224
  36.2 0.6 %copy-done.8 = f32[1,128]{1,0:T(1,128)S(1)} copy-done((f32[1,128]{1,0:T(1,128)S(1)}, f32[1,128]{1,0:T(1,128)}, u32[]{:S(2)}) %copy-start.8) | copy-done | bytes 536
  36.8 2.1 %collective-permute-start.4 = (f32[1,128]{1,0:T(1,128)S(1)}, f32[1,128]{1,0:T(1,128)S(1)}, u32[]{:S(2)}, u32[]{:S(2)}) collective-permute-start(f32[1,128]{1,0:T(1,128)S(1)} %copy-done.8), channel_id=1, source_target_pairs={{0,1},{1,2},{2,3},{3,4},{4,5},{5,6},{6,7},{7,8},{8,9},{9,10},{10,1... | collective-permute-start | bytes 1544 | tf_op jit(solution)/shard_map/ppermute | solution.py:35
  38.9 0.0 copy-done.4
  39.0 2.5 %collective-permute-start.5 = (f32[1,128]{1,0:T(1,128)S(1)}, f32[1,128]{1,0:T(1,128)S(1)}, u32[]{:S(2)}, u32[]{:S(2)}) collective-permute-start(f32[1,128]{1,0:T(1,128)S(1)} %copy-done.4), channel_id=1, source_target_pairs={{1,0},{2,1},{3,2},{4,3},{5,4},{6,5},{7,6},{8,7},{9,8},{10,9},{11,1... | collective-permute-start | bytes 1544 | tf_op jit(solution)/shard_map/ppermute | solution.py:36
  41.5 0.0 collective-permute-done.4.fa_ref
  41.5 0.0 copy-start.2
  41.5 3.2 %collective-permute-done.5.fb_ref = f32[1,128]{1,0:T(1,128)S(1)} collective-permute-done((f32[1,128]{1,0:T(1,128)S(1)}, f32[1,128]{1,0:T(1,128)S(1)}, u32[]{:S(2)}, u32[]{:S(2)}) %collective-permute-start.5) | collective-permute-done | bytes 544 | tf_op jit(solution)/shard_map/ppermute | solution.py:36
  44.7 0.0 copy-done.2
  44.7 0.5 copy-done.5
  45.2 5.7 %shard_map.98 = f32[64,2048]{1,0:T(8,128)} custom-call(s32[2]{0:T(128)} %band_ref.7, s32[2]{0:T(128)} %col_ref.7, s32[2]{0:T(128)} %cell_ref.7, f32[9,256]{1,0:T(8,128)} %psf_ref.7, f32[32]{0:T(128)} %pad_maximum_fusion.nbm_ref, s32[2]{0:T(128)} %add_convert_fusion.flag_ref, f32[2,128]{1,0:T(2,128)} %oy_ref.7, f32[2,128]{1,0:T(2,128)} %ox_ref.7, ...), custom_call_target="tpu_custom_call" | custom-call | flops 1019215872 | bytes 1572864 | tf_op jit(solution)/shard_map/pallas_call | solution.py:224
  (8 shorter events, 0.0 us)
Async XLA Ops:
  2.5 6.6 %collective-permute-start = (f32[24,2048]{1,0:T(8,128)}, f32[24,2048]{1,0:T(8,128)S(1)}, u32[]{:S(2)}, u32[]{:S(2)}) collective-permute-start(f32[24,2048]{1,0:T(8,128)} %get-tuple-element.11), channel_id=1, source_target_pairs={{0,1},{1,2},{2,3},{3,4},{4,5},{5,6},{6,7},{7,8},{8,9},{9,10},{10,1... | collective-permute-start | bytes 589832 | tf_op jit(solution)/shard_map/ppermute | solution.py:35
  6.3 8.1 %collective-permute-start.1 = (f32[24,2048]{1,0:T(8,128)}, f32[24,2048]{1,0:T(8,128)S(1)}, u32[]{:S(2)}, u32[]{:S(2)}) collective-permute-start(f32[24,2048]{1,0:T(8,128)} %get-tuple-element.12), channel_id=1, source_target_pairs={{1,0},{2,1},{3,2},{4,3},{5,4},{6,5},{7,6},{8,7},{9,8},{10,9},{11,1... | collective-permute-start | bytes 589832 | tf_op jit(solution)/shard_map/ppermute | solution.py:36
  9.2 5.8 %copy-start = (f32[24,2048]{1,0:T(8,128)}, f32[24,2048]{1,0:T(8,128)S(1)}, u32[]{:S(2)}) copy-start(f32[24,2048]{1,0:T(8,128)S(1)} %collective-permute-done.above_ref.fa_ref) | copy-start | bytes 589828
  14.4 0.7 %copy-start.1 = (f32[24,2048]{1,0:T(8,128)}, f32[24,2048]{1,0:T(8,128)S(1)}, u32[]{:S(2)}) copy-start(f32[24,2048]{1,0:T(8,128)S(1)} %collective-permute-done.1.below_ref.fb_ref) | copy-start | bytes 589828
  21.2 0.7 %copy-start.9 = (f32[1,128]{1,0:T(1,128)S(1)}, f32[1,128]{1,0:T(1,128)}, u32[]{:S(2)}) copy-start(f32[1,128]{1,0:T(1,128)} %get-tuple-element.15) | copy-start | bytes 1540
  21.9 2.1 %copy-start.7 = (f32[1,128]{1,0:T(1,128)S(1)}, f32[1,128]{1,0:T(1,128)}, u32[]{:S(2)}) copy-start(f32[1,128]{1,0:T(1,128)} %get-tuple-element.16) | copy-start | bytes 1540
  21.9 4.5 %collective-permute-start.2 = (f32[1,128]{1,0:T(1,128)S(1)}, f32[1,128]{1,0:T(1,128)S(1)}, u32[]{:S(2)}, u32[]{:S(2)}) collective-permute-start(f32[1,128]{1,0:T(1,128)S(1)} %copy-done.9), channel_id=1, source_target_pairs={{0,1},{1,2},{2,3},{3,4},{4,5},{5,6},{6,7},{7,8},{8,9},{9,10},{10,1... | collective-permute-start | bytes 1544 | tf_op jit(solution)/shard_map/ppermute | solution.py:35
  24.0 5.8 %collective-permute-start.3 = (f32[1,128]{1,0:T(1,128)S(1)}, f32[1,128]{1,0:T(1,128)S(1)}, u32[]{:S(2)}, u32[]{:S(2)}) collective-permute-start(f32[1,128]{1,0:T(1,128)S(1)} %copy-done.7), channel_id=1, source_target_pairs={{1,0},{2,1},{3,2},{4,3},{5,4},{6,5},{7,6},{8,7},{9,8},{10,9},{11,1... | collective-permute-start | bytes 1544 | tf_op jit(solution)/shard_map/ppermute | solution.py:36
  26.4 3.3 %copy-start.3 = (f32[1,128]{1,0:T(1,128)}, f32[1,128]{1,0:T(1,128)S(1)}, u32[]{:S(2)}) copy-start(f32[1,128]{1,0:T(1,128)S(1)} %collective-permute-done.2.fa_ref) | copy-start | bytes 1540
  29.7 0.5 copy-start.6
  36.2 0.6 %copy-start.8 = (f32[1,128]{1,0:T(1,128)S(1)}, f32[1,128]{1,0:T(1,128)}, u32[]{:S(2)}) copy-start(f32[1,128]{1,0:T(1,128)} %get-tuple-element.18) | copy-start | bytes 1540
  36.8 2.1 %copy-start.4 = (f32[1,128]{1,0:T(1,128)S(1)}, f32[1,128]{1,0:T(1,128)}, u32[]{:S(2)}) copy-start(f32[1,128]{1,0:T(1,128)} %get-tuple-element.19) | copy-start | bytes 1540
  36.8 4.7 %collective-permute-start.4 = (f32[1,128]{1,0:T(1,128)S(1)}, f32[1,128]{1,0:T(1,128)S(1)}, u32[]{:S(2)}, u32[]{:S(2)}) collective-permute-start(f32[1,128]{1,0:T(1,128)S(1)} %copy-done.8), channel_id=1, source_target_pairs={{0,1},{1,2},{2,3},{3,4},{4,5},{5,6},{6,7},{7,8},{8,9},{9,10},{10,1... | collective-permute-start | bytes 1544 | tf_op jit(solution)/shard_map/ppermute | solution.py:35
  39.0 5.8 %collective-permute-start.5 = (f32[1,128]{1,0:T(1,128)S(1)}, f32[1,128]{1,0:T(1,128)S(1)}, u32[]{:S(2)}, u32[]{:S(2)}) collective-permute-start(f32[1,128]{1,0:T(1,128)S(1)} %copy-done.4), channel_id=1, source_target_pairs={{1,0},{2,1},{3,2},{4,3},{5,4},{6,5},{7,6},{8,7},{9,8},{10,9},{11,1... | collective-permute-start | bytes 1544 | tf_op jit(solution)/shard_map/ppermute | solution.py:36
  41.5 3.2 %copy-start.2 = (f32[1,128]{1,0:T(1,128)}, f32[1,128]{1,0:T(1,128)S(1)}, u32[]{:S(2)}) copy-start(f32[1,128]{1,0:T(1,128)S(1)} %collective-permute-done.4.fa_ref) | copy-start | bytes 1540
  44.7 0.5 copy-start.5

commit v3 on v2

--- a/solution.py
+++ b/solution.py
@@ -12,8 +12,7 @@
 HALO = 16
 LANES = 128
 WIN = 384
-META = 8
-PACKET = HALO + META
+PACKET = HALO
 
 
 HIGHEST = lax.Precision.HIGHEST
@@ -21,10 +20,11 @@
 
 
 def profile3(dist):
-    tapered = jnp.maximum(0.0, 1.0 - dist / 15.5 * (dist / 15.5))
-    scaled = dist / 1.7
+    tapered_arg = dist * (1.0 / 15.5)
+    tapered = jnp.maximum(0.0, 1.0 - tapered_arg * tapered_arg)
+    scaled = dist * (1.0 / 1.7)
     core_part = jnp.exp(-0.5 * scaled * scaled) * tapered
-    wing_part = jnp.exp(-dist * dist / 72.0) * tapered
+    wing_part = jnp.exp(dist * dist * (-1.0 / 72.0)) * tapered
     return core_part, scaled * core_part, wing_part
 
 
@@ -84,18 +84,16 @@
     x_top, x_bot = pick(ox_ref[0:1, :], ox_ref[1:2, :])
     f_top, f_bot = pick(f_ref[0:1, :], f_ref[1:2, :])
     m_top, m_bot = pick(metas[0], metas[1])
-    up_ref[...] = jnp.zeros_like(up_ref)
-    down_ref[...] = jnp.zeros_like(down_ref)
-    up_ref[0:HALO, :] = img_ref[0:HALO, :]
+    up_ref[...] = img_ref[0:HALO, :]
     for r, v in enumerate((y_top, x_top, f_top, m_top)):
-        up_ref[HALO + r : HALO + r + 1, 0:LANES] = v
+        up_ref[HALO - 1 : HALO, r * LANES : (r + 1) * LANES] = v
+    down_ref[...] = img_ref[strip_rows - HALO : strip_rows, :]
     for r, v in enumerate((y_bot, x_bot, f_bot, m_bot)):
-        down_ref[r : r + 1, 0:LANES] = v
-    down_ref[META:PACKET, :] = img_ref[strip_rows - HALO : strip_rows, :]
+        down_ref[0:1, r * LANES : (r + 1) * LANES] = v
 
 
 def phase_kernel(
-    final, above_row, below_row,
+    final, above_col, below_row, below_col,
     band_ref, col_ref, cell_ref, psf_ref, nbm_ref, flag_ref,
     oy_ref, ox_ref, f_ref, w_ref, above_ref, img_ref, below_ref, fa_ref, fb_ref,
     *rest,
@@ -118,13 +116,14 @@
         specs.append((y, ox_ref[j : j + 1, :], f_ref[j : j + 1, :],
                       own_coefs(psf_ref, cell_ref, j), col_ref[j]))
     specs.append((
-        above_ref[0:1, 0:LANES] - strip_rows, above_ref[1:2, 0:LANES],
-        fa_ref[above_row : above_row + 1, 0:LANES],
+        above_ref[0:1, 0:LANES] - strip_rows, above_ref[0:1, LANES : 2 * LANES],
+        fa_ref[0:1, above_col : above_col + LANES],
         [nbm_ref[k] for k in range(9)], nbm_ref[9].astype(jnp.int32),
     ))
     specs.append((
-        below_ref[HALO : HALO + 1, 0:LANES] + strip_rows, below_ref[HALO + 1 : HALO + 2, 0:LANES],
-        fb_ref[below_row : below_row + 1, 0:LANES],
+        below_ref[HALO - 1 : HALO, 0:LANES] + strip_rows,
+        below_ref[HALO - 1 : HALO, LANES : 2 * LANES],
+        fb_ref[below_row : below_row + 1, below_col : below_col + LANES],
         [nbm_ref[16 + k] for k in range(9)], nbm_ref[16 + 9].astype(jnp.int32),
     ))
 
@@ -155,7 +154,7 @@
     edge_ids = lax.broadcasted_iota(jnp.int32, (HALO, width), 0)
     top_ok = (edge_ids >= HALO - REACH) & (flag_ref[0] > 0)
     bot_ok = (edge_ids < REACH) & (flag_ref[1] > 0)
-    top = jnp.where(top_ok, above_ref[META:PACKET, :] - canvas[0:HALO, inner], 0.0)
+    top = jnp.where(top_ok, above_ref[...] - canvas[0:HALO, inner], 0.0)
     bot = jnp.where(bot_ok, below_ref[0:HALO, :] - canvas[HALO + strip_rows :, inner], 0.0)
     mid = img_ref[...] - canvas[HALO : HALO + strip_rows, inner]
     canvas[0:HALO, inner] = top
@@ -203,7 +202,9 @@
     me = lax.axis_index("ty")
     last = lax.axis_size("ty") - 1
     flags = jnp.stack([me > 0, me < last]).astype(jnp.int32)
-    nbm = jnp.concatenate([got_above[3, :16], got_below[HALO + 3, :16]])
+    nbm = jnp.concatenate(
+        [got_above[0, 3 * LANES : 3 * LANES + 16], got_below[HALO - 1, 3 * LANES : 3 * LANES + 16]]
+    )
 
     ext_rows = strip_rows + 2 * HALO
     blocks = own + 2
@@ -213,8 +214,8 @@
     common = (band_row, col_block, cell_index, psf_coef, nbm, flags,
               offset_y, offset_x)
 
-    def phase(final, fluxes, fa, fb, above_row, below_row):
-        kernel = functools.partial(phase_kernel, final, above_row, below_row)
+    def phase(final, fluxes, fa, fb, flux_at):
+        kernel = functools.partial(phase_kernel, final, *flux_at)
         if final:
             out_shape = jax.ShapeDtypeStruct((strip_rows, strip_width), f32)
             out_specs = vmem
@@ -235,12 +236,12 @@
 
     fluxes = flux_start
     fa, fb = got_above, got_below
-    above_row, below_row = 2, HALO + 2
+    flux_at = (2 * LANES, HALO - 1, 2 * LANES)
     for iteration in range(ITERS):
-        fluxes, new_top, new_bot = phase(False, fluxes, fa, fb, above_row, below_row)
+        fluxes, new_top, new_bot = phase(False, fluxes, fa, fb, flux_at)
         fa, fb = exchange(new_top, new_bot)
-        above_row, below_row = 0, 0
-    residual = phase(True, fluxes, fa, fb, above_row, below_row)
+        flux_at = (0, 0, 0)
+    residual = phase(True, fluxes, fa, fb, flux_at)
     return (fluxes, residual)
 
 

time: 51.2 us -> 50.3 us (0.982)
  waiting for transfers between devices: 12.1 us -> 11.4 us
  transfers between devices with their start and end apart: 6 -> 6, of which waited for: 4 -> 3; matrix products, arithmetic and copies ran while one was open for 1% -> 1% of each run, Pallas kernels for 0% -> 0%
where the time goes in v3:
time: 50.3 us; the launch traced here: 50 us
  Pallas kernels  19.5 us (39%)
  starting transfers between devices  14.7 us (29%)
  waiting for transfers between devices  11.4 us (23%)
  local copies, waits for them, and re-layouts  2.35 us (5%)
  other arithmetic  1.23 us (2%)
  between operations  0.75 us (1%)
    pallas_call x3, Pallas kernels, phase(): pl.pallas_call(kernel, out_shape=out_shape, in_specs=[smem] * 6 + [vmem]...  17.6 us
    ppermute x3, waiting for transfers between devices, exchange(): from_below = lax.ppermute(to_above, 'ty', backward)  11.4 us
    ppermute x3, starting transfers between devices, exchange(): from_above = lax.ppermute(to_below, 'ty', forward)  7.88 us
    ppermute x3, starting transfers between devices, exchange(): from_below = lax.ppermute(to_above, 'ty', backward)  6.84 us
    unnamed x20, local copies, waits for them, and re-layouts  2.34 us
    pallas_call x1, Pallas kernels, local(): pl.pallas_call(setup_kernel, out_shape=(packet, packet, jax.ShapeDtypeStr...  1.9 us
  transfers between devices with their start and end apart: 6, of which 3 were waited for; matrix products, arithmetic and copies ran while one was open for 1% of the time, Pallas kernels for 0%

profile of v3, /device:TPU:11, one launch (start us, length us, event | category | flops | bytes accessed | tf_op | source)
XLA Modules:
  0.0 50.0 jit_solution(2736177578349945255)
XLA Ops:
  0.6 1.9 %shard_map.95 = (f32[16,2048]{1,0:T(8,128)}, f32[16,2048]{1,0:T(8,128)}, f32[2,128]{1,0:T(2,128)}) custom-call(s32[2]{0:T(128)} %band_ref.7, s32[2]{0:T(128)} %col_ref.7, s32[2]{0:T(128)} %cell_ref.7, f32[9,256]{1,0:T(8,128)} %psf_ref.7, f32[64,2048]{1,0:T(8,128)} %img_ref.7, f32[2,128]{1,0:T(2,128)} %oy_ref.7, f32[2,128]{1,0:T(2,128)} %ox_ref.7, f32[2,128]{1,0:T(2,128)} %f_ref.3), custom_call_target="tpu_custom_call" | custom-call | tf_op jit(solution)/shard_map/pallas_call | solution.py:194
  2.5 3.7 %collective-permute-start = (f32[16,2048]{1,0:T(8,128)}, f32[16,2048]{1,0:T(8,128)S(1)}, u32[]{:S(2)}, u32[]{:S(2)}) collective-permute-start(f32[16,2048]{1,0:T(8,128)} %get-tuple-element.11), channel_id=1, source_target_pairs={{0,1},{1,2},{2,3},{3,4},{4,5},{5,6},{6,7},{7,8},{8,9},{9,10},{10,1... | collective-permute-start | bytes 393224 | tf_op jit(solution)/shard_map/ppermute | solution.py:35
  6.3 1.9 %collective-permute-start.1 = (f32[16,2048]{1,0:T(8,128)}, f32[16,2048]{1,0:T(8,128)S(1)}, u32[]{:S(2)}, u32[]{:S(2)}) collective-permute-start(f32[16,2048]{1,0:T(8,128)} %get-tuple-element.12), channel_id=1, source_target_pairs={{1,0},{2,1},{3,2},{4,3},{5,4},{6,5},{7,6},{8,7},{9,8},{10,9},{11,1... | collective-permute-start | bytes 393224 | tf_op jit(solution)/shard_map/ppermute | solution.py:36
  8.2 0.6 %add_convert_fusion.flag_ref = s32[2]{0:T(128)} fusion(pred[1]{0:T(512)(128)(4,1)} %bitcast.3, pred[1]{0:T(512)(128)(4,1)} %bitcast.2), kind=kLoop, calls=%fused_computation | loop fusion | flops 4 | bytes 10 | tf_op jit(solution)/shard_map/convert_element_type | solution.py:204
  8.8 0.0 collective-permute-done.above_ref.fa_ref
  8.8 0.0 copy-start
  8.8 4.9 %collective-permute-done.1.below_ref.fb_ref = f32[16,2048]{1,0:T(8,128)S(1)} collective-permute-done((f32[16,2048]{1,0:T(8,128)}, f32[16,2048]{1,0:T(8,128)S(1)}, u32[]{:S(2)}, u32[]{:S(2)}) %collective-permute-start.1) | collective-permute-done | bytes 131104 | tf_op jit(solution)/shard_map/ppermute | solution.py:36
  13.7 0.0 copy-start.1
  13.7 0.7 %pad_maximum_fusion.nbm_ref = f32[32]{0:T(128)} fusion(f32[16]{0:T(128)S(1)} %slice_bitcast_fusion, f32[16]{0:T(128)S(1)} %slice_bitcast_fusion.1), kind=kLoop, calls=%fused_computation.3 | loop fusion | flops 32 | bytes 256 | tf_op jit(solution)/shard_map/concatenate | solution.py:205
  14.3 0.0 copy-done
  14.3 0.0 copy-done.1
  14.3 6.0 %shard_map.96 = (f32[2,128]{1,0:T(2,128)}, f32[1,128]{1,0:T(1,128)}, f32[1,128]{1,0:T(1,128)}) custom-call(s32[2]{0:T(128)} %band_ref.7, s32[2]{0:T(128)} %col_ref.7, s32[2]{0:T(128)} %cell_ref.7, f32[9,256]{1,0:T(8,128)} %psf_ref.7, f32[32]{0:T(128)} %pad_maximum_fusion.nbm_ref, s32[2]{0:T(128)} %add_convert_fusion.flag_ref, f32[2,128]{1,0:T(2,128)} %oy_ref.7, ...), custom_call_target="tpu_custom_call" | custom-call | flops 1019215872 | bytes 1572864 | tf_op jit(solution)/shard_map/pallas_call | solution.py:225
  20.4 0.7 %copy-done.9 = f32[1,128]{1,0:T(1,128)S(1)} copy-done((f32[1,128]{1,0:T(1,128)S(1)}, f32[1,128]{1,0:T(1,128)}, u32[]{:S(2)}) %copy-start.9) | copy-done | bytes 536
  21.0 2.0 %collective-permute-start.2 = (f32[1,128]{1,0:T(1,128)S(1)}, f32[1,128]{1,0:T(1,128)S(1)}, u32[]{:S(2)}, u32[]{:S(2)}) collective-permute-start(f32[1,128]{1,0:T(1,128)S(1)} %copy-done.9), channel_id=1, source_target_pairs={{0,1},{1,2},{2,3},{3,4},{4,5},{5,6},{6,7},{7,8},{8,9},{9,10},{10,1... | collective-permute-start | bytes 1544 | tf_op jit(solution)/shard_map/ppermute | solution.py:35
  23.1 0.0 copy-done.7
  23.1 2.4 %collective-permute-start.3 = (f32[1,128]{1,0:T(1,128)S(1)}, f32[1,128]{1,0:T(1,128)S(1)}, u32[]{:S(2)}, u32[]{:S(2)}) collective-permute-start(f32[1,128]{1,0:T(1,128)S(1)} %copy-done.7), channel_id=1, source_target_pairs={{1,0},{2,1},{3,2},{4,3},{5,4},{6,5},{7,6},{8,7},{9,8},{10,9},{11,1... | collective-permute-start | bytes 1544 | tf_op jit(solution)/shard_map/ppermute | solution.py:36
  25.5 0.0 collective-permute-done.2.fa_ref
  25.5 0.0 copy-start.3
  25.5 3.3 %collective-permute-done.3.fb_ref = f32[1,128]{1,0:T(1,128)S(1)} collective-permute-done((f32[1,128]{1,0:T(1,128)S(1)}, f32[1,128]{1,0:T(1,128)S(1)}, u32[]{:S(2)}, u32[]{:S(2)}) %collective-permute-start.3) | collective-permute-done | bytes 544 | tf_op jit(solution)/shard_map/ppermute | solution.py:36
  28.9 0.0 copy-done.3
  28.9 0.5 copy-done.6
  29.4 6.0 %shard_map.97 = (f32[2,128]{1,0:T(2,128)}, f32[1,128]{1,0:T(1,128)}, f32[1,128]{1,0:T(1,128)}) custom-call(s32[2]{0:T(128)} %band_ref.7, s32[2]{0:T(128)} %col_ref.7, s32[2]{0:T(128)} %cell_ref.7, f32[9,256]{1,0:T(8,128)} %psf_ref.7, f32[32]{0:T(128)} %pad_maximum_fusion.nbm_ref, s32[2]{0:T(128)} %add_convert_fusion.flag_ref, f32[2,128]{1,0:T(2,128)} %oy_ref.7, ...), custom_call_target="tpu_custom_call" | custom-call | flops 1019215872 | bytes 1572864 | tf_op jit(solution)/shard_map/pallas_call | solution.py:225
  35.3 0.7 %copy-done.8 = f32[1,128]{1,0:T(1,128)S(1)} copy-done((f32[1,128]{1,0:T(1,128)S(1)}, f32[1,128]{1,0:T(1,128)}, u32[]{:S(2)}) %copy-start.8) | copy-done | bytes 536
  36.0 2.1 %collective-permute-start.4 = (f32[1,128]{1,0:T(1,128)S(1)}, f32[1,128]{1,0:T(1,128)S(1)}, u32[]{:S(2)}, u32[]{:S(2)}) collective-permute-start(f32[1,128]{1,0:T(1,128)S(1)} %copy-done.8), channel_id=1, source_target_pairs={{0,1},{1,2},{2,3},{3,4},{4,5},{5,6},{6,7},{7,8},{8,9},{9,10},{10,1... | collective-permute-start | bytes 1544 | tf_op jit(solution)/shard_map/ppermute | solution.py:35
  38.1 0.0 copy-done.4
  38.1 2.5 %collective-permute-start.5 = (f32[1,128]{1,0:T(1,128)S(1)}, f32[1,128]{1,0:T(1,128)S(1)}, u32[]{:S(2)}, u32[]{:S(2)}) collective-permute-start(f32[1,128]{1,0:T(1,128)S(1)} %copy-done.4), channel_id=1, source_target_pairs={{1,0},{2,1},{3,2},{4,3},{5,4},{6,5},{7,6},{8,7},{9,8},{10,9},{11,1... | collective-permute-start | bytes 1544 | tf_op jit(solution)/shard_map/ppermute | solution.py:36
  40.6 0.0 collective-permute-done.4.fa_ref
  40.6 0.0 copy-start.2
  40.7 3.2 %collective-permute-done.5.fb_ref = f32[1,128]{1,0:T(1,128)S(1)} collective-permute-done((f32[1,128]{1,0:T(1,128)S(1)}, f32[1,128]{1,0:T(1,128)S(1)}, u32[]{:S(2)}, u32[]{:S(2)}) %collective-permute-start.5) | collective-permute-done | bytes 544 | tf_op jit(solution)/shard_map/ppermute | solution.py:36
  43.9 0.0 copy-done.2
  43.9 0.5 copy-done.5
  44.4 5.6 %shard_map.98 = f32[64,2048]{1,0:T(8,128)} custom-call(s32[2]{0:T(128)} %band_ref.7, s32[2]{0:T(128)} %col_ref.7, s32[2]{0:T(128)} %cell_ref.7, f32[9,256]{1,0:T(8,128)} %psf_ref.7, f32[32]{0:T(128)} %pad_maximum_fusion.nbm_ref, s32[2]{0:T(128)} %add_convert_fusion.flag_ref, f32[2,128]{1,0:T(2,128)} %oy_ref.7, f32[2,128]{1,0:T(2,128)} %ox_ref.7, ...), custom_call_target="tpu_custom_call" | custom-call | flops 1019215872 | bytes 1572864 | tf_op jit(solution)/shard_map/pallas_call | solution.py:225
  (8 shorter events, 0.0 us)
Async XLA Ops:
  2.5 6.2 %collective-permute-start = (f32[16,2048]{1,0:T(8,128)}, f32[16,2048]{1,0:T(8,128)S(1)}, u32[]{:S(2)}, u32[]{:S(2)}) collective-permute-start(f32[16,2048]{1,0:T(8,128)} %get-tuple-element.11), channel_id=1, source_target_pairs={{0,1},{1,2},{2,3},{3,4},{4,5},{5,6},{6,7},{7,8},{8,9},{9,10},{10,1... | collective-permute-start | bytes 393224 | tf_op jit(solution)/shard_map/ppermute | solution.py:35
  6.3 7.4 %collective-permute-start.1 = (f32[16,2048]{1,0:T(8,128)}, f32[16,2048]{1,0:T(8,128)S(1)}, u32[]{:S(2)}, u32[]{:S(2)}) collective-permute-start(f32[16,2048]{1,0:T(8,128)} %get-tuple-element.12), channel_id=1, source_target_pairs={{1,0},{2,1},{3,2},{4,3},{5,4},{6,5},{7,6},{8,7},{9,8},{10,9},{11,1... | collective-permute-start | bytes 393224 | tf_op jit(solution)/shard_map/ppermute | solution.py:36
  8.8 5.5 %copy-start = (f32[16,2048]{1,0:T(8,128)}, f32[16,2048]{1,0:T(8,128)S(1)}, u32[]{:S(2)}) copy-start(f32[16,2048]{1,0:T(8,128)S(1)} %collective-permute-done.above_ref.fa_ref) | copy-start | bytes 393220
  13.7 0.7 %copy-start.1 = (f32[16,2048]{1,0:T(8,128)}, f32[16,2048]{1,0:T(8,128)S(1)}, u32[]{:S(2)}) copy-start(f32[16,2048]{1,0:T(8,128)S(1)} %collective-permute-done.1.below_ref.fb_ref) | copy-start | bytes 393220
  20.4 0.7 %copy-start.9 = (f32[1,128]{1,0:T(1,128)S(1)}, f32[1,128]{1,0:T(1,128)}, u32[]{:S(2)}) copy-start(f32[1,128]{1,0:T(1,128)} %get-tuple-element.15) | copy-start | bytes 1540
  21.0 2.1 %copy-start.7 = (f32[1,128]{1,0:T(1,128)S(1)}, f32[1,128]{1,0:T(1,128)}, u32[]{:S(2)}) copy-start(f32[1,128]{1,0:T(1,128)} %get-tuple-element.16) | copy-start | bytes 1540
  21.0 4.5 %collective-permute-start.2 = (f32[1,128]{1,0:T(1,128)S(1)}, f32[1,128]{1,0:T(1,128)S(1)}, u32[]{:S(2)}, u32[]{:S(2)}) collective-permute-start(f32[1,128]{1,0:T(1,128)S(1)} %copy-done.9), channel_id=1, source_target_pairs={{0,1},{1,2},{2,3},{3,4},{4,5},{5,6},{6,7},{7,8},{8,9},{9,10},{10,1... | collective-permute-start | bytes 1544 | tf_op jit(solution)/shard_map/ppermute | solution.py:35
  23.1 5.8 %collective-permute-start.3 = (f32[1,128]{1,0:T(1,128)S(1)}, f32[1,128]{1,0:T(1,128)S(1)}, u32[]{:S(2)}, u32[]{:S(2)}) collective-permute-start(f32[1,128]{1,0:T(1,128)S(1)} %copy-done.7), channel_id=1, source_target_pairs={{1,0},{2,1},{3,2},{4,3},{5,4},{6,5},{7,6},{8,7},{9,8},{10,9},{11,1... | collective-permute-start | bytes 1544 | tf_op jit(solution)/shard_map/ppermute | solution.py:36
  25.5 3.3 %copy-start.3 = (f32[1,128]{1,0:T(1,128)}, f32[1,128]{1,0:T(1,128)S(1)}, u32[]{:S(2)}) copy-start(f32[1,128]{1,0:T(1,128)S(1)} %collective-permute-done.2.fa_ref) | copy-start | bytes 1540
  28.8 0.5 %copy-start.6 = (f32[1,128]{1,0:T(1,128)}, f32[1,128]{1,0:T(1,128)S(1)}, u32[]{:S(2)}) copy-start(f32[1,128]{1,0:T(1,128)S(1)} %collective-permute-done.3.fb_ref) | copy-start | bytes 1540
  35.3 0.7 %copy-start.8 = (f32[1,128]{1,0:T(1,128)S(1)}, f32[1,128]{1,0:T(1,128)}, u32[]{:S(2)}) copy-start(f32[1,128]{1,0:T(1,128)} %get-tuple-element.18) | copy-start | bytes 1540
  36.0 2.1 %copy-start.4 = (f32[1,128]{1,0:T(1,128)S(1)}, f32[1,128]{1,0:T(1,128)}, u32[]{:S(2)}) copy-start(f32[1,128]{1,0:T(1,128)} %get-tuple-element.19) | copy-start | bytes 1540
  36.0 4.7 %collective-permute-start.4 = (f32[1,128]{1,0:T(1,128)S(1)}, f32[1,128]{1,0:T(1,128)S(1)}, u32[]{:S(2)}, u32[]{:S(2)}) collective-permute-start(f32[1,128]{1,0:T(1,128)S(1)} %copy-done.8), channel_id=1, source_target_pairs={{0,1},{1,2},{2,3},{3,4},{4,5},{5,6},{6,7},{7,8},{8,9},{9,10},{10,1... | collective-permute-start | bytes 1544 | tf_op jit(solution)/shard_map/ppermute | solution.py:35
  38.1 5.8 %collective-permute-start.5 = (f32[1,128]{1,0:T(1,128)S(1)}, f32[1,128]{1,0:T(1,128)S(1)}, u32[]{:S(2)}, u32[]{:S(2)}) collective-permute-start(f32[1,128]{1,0:T(1,128)S(1)} %copy-done.4), channel_id=1, source_target_pairs={{1,0},{2,1},{3,2},{4,3},{5,4},{6,5},{7,6},{8,7},{9,8},{10,9},{11,1... | collective-permute-start | bytes 1544 | tf_op jit(solution)/shard_map/ppermute | solution.py:36
  40.6 3.2 %copy-start.2 = (f32[1,128]{1,0:T(1,128)}, f32[1,128]{1,0:T(1,128)S(1)}, u32[]{:S(2)}) copy-start(f32[1,128]{1,0:T(1,128)S(1)} %collective-permute-done.4.fa_ref) | copy-start | bytes 1540
  43.9 0.5 %copy-start.5 = (f32[1,128]{1,0:T(1,128)}, f32[1,128]{1,0:T(1,128)S(1)}, u32[]{:S(2)}) copy-start(f32[1,128]{1,0:T(1,128)S(1)} %collective-permute-done.5.fb_ref) | copy-start | bytes 1540

commit v4 on v3

--- a/solution.py
+++ b/solution.py
@@ -92,10 +92,37 @@
         down_ref[0:1, r * LANES : (r + 1) * LANES] = v
 
 
+def add_stamp(canvas, y, x, flux, c, col, keep_rows=None):
+    ext_rows = canvas.shape[0]
+    hpos = lax.broadcasted_iota(jnp.int32, (ext_rows, LANES), 0).astype(jnp.float32) - HALO
+    wpos = lax.broadcasted_iota(jnp.int32, (WIN, LANES), 0).astype(jnp.float32) - LANES
+    rows = profile3(hpos - y)
+    if keep_rows is not None:
+        rows = tuple(jnp.where(hpos < keep_rows, r, 0.0) for r in rows)
+    cols = profile3(wpos - x)
+    stamp = None
+    for a in range(3):
+        mixed = (c[3 * a] * cols[0] + c[3 * a + 1] * cols[1] + c[3 * a + 2] * cols[2]) * flux
+        part = lax.dot_general(
+            rows[a], mixed, DIMS_NT, precision=HIGHEST, preferred_element_type=jnp.float32,
+        )
+        stamp = part if stamp is None else stamp + part
+    start = pl.multiple_of(col * LANES, LANES)
+    canvas[:, pl.ds(start, WIN)] += stamp
+
+
+def own_kernel(band_ref, col_ref, cell_ref, psf_ref, oy_ref, ox_ref, f_ref, canvas):
+    canvas[...] = jnp.zeros_like(canvas)
+    for j in range(oy_ref.shape[0]):
+        y = band_ref[j].astype(jnp.float32) + oy_ref[j : j + 1, :]
+        add_stamp(canvas, y, ox_ref[j : j + 1, :], f_ref[j : j + 1, :],
+                  own_coefs(psf_ref, cell_ref, j), col_ref[j])
+
+
 def phase_kernel(
     final, above_col, below_row, below_col,
     band_ref, col_ref, cell_ref, psf_ref, nbm_ref, flag_ref,
-    oy_ref, ox_ref, f_ref, w_ref, above_ref, img_ref, below_ref, fa_ref, fb_ref,
+    oy_ref, ox_ref, f_ref, w_ref, above_ref, img_ref, below_ref, fa_ref, fb_ref, own_ref,
     *rest,
 ):
     if final:
@@ -105,48 +132,18 @@
     ext_rows, pad_width = canvas.shape
     strip_rows, width = img_ref.shape
     own = oy_ref.shape[0]
-    canvas[...] = jnp.zeros_like(canvas)
-    hpos = lax.broadcasted_iota(jnp.int32, (ext_rows, LANES), 0).astype(jnp.float32) - HALO
-    wpos = lax.broadcasted_iota(jnp.int32, (WIN, LANES), 0).astype(jnp.float32) - LANES
-    keep_above = hpos < REACH
-
-    specs = []
-    for j in range(own):
-        y = band_ref[j].astype(jnp.float32) + oy_ref[j : j + 1, :]
-        specs.append((y, ox_ref[j : j + 1, :], f_ref[j : j + 1, :],
-                      own_coefs(psf_ref, cell_ref, j), col_ref[j]))
-    specs.append((
-        above_ref[0:1, 0:LANES] - strip_rows, above_ref[0:1, LANES : 2 * LANES],
+    canvas[...] = own_ref[...]
+    add_stamp(
+        canvas, above_ref[0:1, 0:LANES] - strip_rows, above_ref[0:1, LANES : 2 * LANES],
         fa_ref[0:1, above_col : above_col + LANES],
-        [nbm_ref[k] for k in range(9)], nbm_ref[9].astype(jnp.int32),
-    ))
-    specs.append((
-        below_ref[HALO - 1 : HALO, 0:LANES] + strip_rows,
+        [nbm_ref[k] for k in range(9)], nbm_ref[9].astype(jnp.int32), keep_rows=REACH,
+    )
+    add_stamp(
+        canvas, below_ref[HALO - 1 : HALO, 0:LANES] + strip_rows,
         below_ref[HALO - 1 : HALO, LANES : 2 * LANES],
         fb_ref[below_row : below_row + 1, below_col : below_col + LANES],
         [nbm_ref[16 + k] for k in range(9)], nbm_ref[16 + 9].astype(jnp.int32),
-    ))
-
-    saved = []
-    for j, (y, x, flux, c, col) in enumerate(specs):
-        rows = profile3(hpos - y)
-        if j == own:
-            rows_model = tuple(jnp.where(keep_above, r, 0.0) for r in rows)
-        else:
-            rows_model = rows
-        cols = profile3(wpos - x)
-        stamp = None
-        for a in range(3):
-            mixed = (c[3 * a] * cols[0] + c[3 * a + 1] * cols[1] + c[3 * a + 2] * cols[2]) * flux
-            part = lax.dot_general(
-                rows_model[a], mixed, DIMS_NT, precision=HIGHEST,
-                preferred_element_type=jnp.float32,
-            )
-            stamp = part if stamp is None else stamp + part
-        start = pl.multiple_of(col * LANES, LANES)
-        canvas[:, pl.ds(start, WIN)] += stamp
-        if j < own:
-            saved.append((rows, cols, c, start))
+    )
     inner = slice(LANES, LANES + width)
     if final:
         out_ref[...] = img_ref[...] - canvas[HALO : HALO + strip_rows, inner]
@@ -162,9 +159,15 @@
     canvas[HALO + strip_rows :, inner] = bot
     canvas[:, 0:LANES] = jnp.zeros((ext_rows, LANES), jnp.float32)
     canvas[:, LANES + width :] = jnp.zeros((ext_rows, pad_width - LANES - width), jnp.float32)
+    hpos = lax.broadcasted_iota(jnp.int32, (ext_rows, LANES), 0).astype(jnp.float32) - HALO
+    wpos = lax.broadcasted_iota(jnp.int32, (WIN, LANES), 0).astype(jnp.float32) - LANES
     news = []
     for j in range(own):
-        rows, cols, c, start = saved[j]
+        y = band_ref[j].astype(jnp.float32) + oy_ref[j : j + 1, :]
+        rows = profile3(hpos - y)
+        cols = profile3(wpos - ox_ref[j : j + 1, :])
+        c = own_coefs(psf_ref, cell_ref, j)
+        start = pl.multiple_of(col_ref[j] * LANES, LANES)
         window = canvas[:, pl.ds(start, WIN)]
         across = [
             jnp.dot(window, cols[b], precision=HIGHEST, preferred_element_type=jnp.float32)
@@ -214,6 +217,20 @@
     common = (band_row, col_block, cell_index, psf_coef, nbm, flags,
               offset_y, offset_x)
 
+    canvas_shape = jax.ShapeDtypeStruct((ext_rows, strip_width + 2 * LANES), f32)
+
+    def own_part(fluxes):
+        return pl.pallas_call(
+            own_kernel,
+            out_shape=canvas_shape,
+            in_specs=[smem] * 4 + [vmem] * 3,
+            out_specs=vmem,
+            cost_estimate=pl.CostEstimate(
+                flops=flops * own // (blocks + own), transcendentals=own * 2 * (ext_rows + WIN) * LANES,
+                bytes_accessed=4 * ext_rows * (strip_width + 2 * LANES),
+            ),
+        )(band_row, col_block, cell_index, psf_coef, offset_y, offset_x, fluxes)
+
     def phase(final, fluxes, fa, fb, flux_at):
         kernel = functools.partial(phase_kernel, final, *flux_at)
         if final:
@@ -225,14 +242,14 @@
         return pl.pallas_call(
             kernel,
             out_shape=out_shape,
-            in_specs=[smem] * 6 + [vmem] * 9,
+            in_specs=[smem] * 6 + [vmem] * 10,
             out_specs=out_specs,
             scratch_shapes=[pltpu.VMEM((ext_rows, strip_width + 2 * LANES), f32)],
             cost_estimate=pl.CostEstimate(
                 flops=flops, transcendentals=blocks * 2 * (ext_rows + WIN) * LANES,
                 bytes_accessed=4 * ext_rows * strip_width * 2,
             ),
-        )(*common, fluxes, weight, got_above, image, got_below, fa, fb)
+        )(*common, fluxes, weight, got_above, image, got_below, fa, fb, own_part(fluxes))
 
     fluxes = flux_start
     fa, fb = got_above, got_below

time: 50.3 us -> 53.8 us (1.070)
  the two profiles are of different devices: /device:TPU:11 before, /device:TPU:24 now
where the time goes in v4:
time: 53.8 us; the launch traced here: 53.2 us
  Pallas kernels  27.9 us (52%)
  starting transfers between devices  19.8 us (37%)
  local copies, waits for them, and re-layouts  3.52 us (7%)
  other arithmetic  1.25 us (2%)
  between operations  0.74 us (1%)
    pallas_call x3, Pallas kernels, phase(): pl.pallas_call(kernel, out_shape=out_shape, in_specs=[smem] * 6 + [vmem]...  14.2 us
    ppermute x3, starting transfers between devices, exchange(): from_below = lax.ppermute(to_above, 'ty', backward)  13.8 us
    pallas_call x3, Pallas kernels, own_part(): pl.pallas_call(own_kernel, out_shape=canvas_shape, in_specs=[smem] * 4 +...  11.8 us
    ppermute x3, starting transfers between devices, exchange(): from_above = lax.ppermute(to_below, 'ty', forward)  5.99 us
    unnamed x20, local copies, waits for them, and re-layouts  3.51 us
    pallas_call x1, Pallas kernels, local(): pl.pallas_call(setup_kernel, out_shape=(packet, packet, jax.ShapeDtypeStr...  1.9 us
  transfers between devices with their start and end apart: 6, of which 0 were waited for; matrix products, arithmetic and copies ran while one was open for 1% of the time, Pallas kernels for 22%

profile of v4, /device:TPU:24, one launch (start us, length us, event | category | flops | bytes accessed | tf_op | source)
XLA Modules:
  0.0 53.2 jit_solution(15436747702943950592)
XLA Ops:
  0.6 1.9 %shard_map.95 = (f32[16,2048]{1,0:T(8,128)}, f32[16,2048]{1,0:T(8,128)}, f32[2,128]{1,0:T(2,128)}) custom-call(s32[2]{0:T(128)} %band_ref.13, s32[2]{0:T(128)} %col_ref.13, s32[2]{0:T(128)} %cell_ref.13, f32[9,256]{1,0:T(8,128)} %psf_ref.13, f32[64,2048]{1,0:T(8,128)} %img_ref.7, f32[2,128]{1,0:T(2,128)} %oy_ref.13, f32[2,128]{1,0:T(2,128)} %ox_ref.13, ...), custom_call_target="tpu_custom_call" | custom-call | tf_op jit(solution)/shard_map/pallas_call | solution.py:197
  2.5 1.9 %collective-permute-start = (f32[16,2048]{1,0:T(8,128)}, f32[16,2048]{1,0:T(8,128)S(1)}, u32[]{:S(2)}, u32[]{:S(2)}) collective-permute-start(f32[16,2048]{1,0:T(8,128)} %get-tuple-element.11), channel_id=1, source_target_pairs={{0,1},{1,2},{2,3},{3,4},{4,5},{5,6},{6,7},{7,8},{8,9},{9,10},{10,1... | collective-permute-start | bytes 393224 | tf_op jit(solution)/shard_map/ppermute | solution.py:35
  4.4 4.5 %collective-permute-start.1 = (f32[16,2048]{1,0:T(8,128)}, f32[16,2048]{1,0:T(8,128)S(1)}, u32[]{:S(2)}, u32[]{:S(2)}) collective-permute-start(f32[16,2048]{1,0:T(8,128)} %get-tuple-element.12), channel_id=1, source_target_pairs={{1,0},{2,1},{3,2},{4,3},{5,4},{6,5},{7,6},{8,7},{9,8},{10,9},{11,1... | collective-permute-start | bytes 393224 | tf_op jit(solution)/shard_map/ppermute | solution.py:36
  9.0 3.9 %shard_map.96.own_ref = f32[96,2304]{1,0:T(8,128)} custom-call(s32[2]{0:T(128)} %band_ref.13, s32[2]{0:T(128)} %col_ref.13, s32[2]{0:T(128)} %cell_ref.13, f32[9,256]{1,0:T(8,128)} %psf_ref.13, f32[2,128]{1,0:T(2,128)} %oy_ref.13, f32[2,128]{1,0:T(2,128)} %ox_ref.13, f32[2,128]{1,0:T(2,128)} %f_ref.5), custom_call_target="tpu_custom_call" | custom-call | flops 339738624 | bytes 884736 | tf_op jit(solution)/shard_map/pallas_call | solution.py:223
  12.9 0.6 %add_convert_fusion.flag_ref = s32[2]{0:T(128)} fusion(pred[1]{0:T(512)(128)(4,1)} %bitcast.3, pred[1]{0:T(512)(128)(4,1)} %bitcast.2), kind=kLoop, calls=%fused_computation | loop fusion | flops 4 | bytes 10 | tf_op jit(solution)/shard_map/convert_element_type | solution.py:207
  13.5 0.0 collective-permute-done.above_ref.fa_ref
  13.5 0.0 collective-permute-done.1.below_ref.fb_ref
  13.5 0.0 copy-start.1
  13.6 0.6 %pad_maximum_fusion.nbm_ref = f32[32]{0:T(128)} fusion(f32[16]{0:T(128)S(1)} %slice_bitcast_fusion, f32[16]{0:T(128)S(1)} %slice_bitcast_fusion.1), kind=kLoop, calls=%fused_computation.3 | loop fusion | flops 32 | bytes 256 | tf_op jit(solution)/shard_map/concatenate | solution.py:208
  14.2 0.0 copy-done
  14.2 0.0 copy-done.1
  14.3 5.0 %shard_map.97 = (f32[2,128]{1,0:T(2,128)}, f32[1,128]{1,0:T(1,128)}, f32[1,128]{1,0:T(1,128)}) custom-call(s32[2]{0:T(128)} %band_ref.13, s32[2]{0:T(128)} %col_ref.13, s32[2]{0:T(128)} %cell_ref.13, f32[9,256]{1,0:T(8,128)} %psf_ref.13, f32[32]{0:T(128)} %pad_maximum_fusion.nbm_ref, s32[2]{0:T(128)} %add_convert_fusion.flag_ref, f32[2,128]{1,0:T(2,128)} %oy_ref.13, ...), custom_call_target="tpu_custom_call" | custom-call | flops 1019215872 | bytes 1572864 | tf_op jit(solution)/shard_map/pallas_call | solution.py:242
  19.3 0.7 %copy-done.9 = f32[1,128]{1,0:T(1,128)S(1)} copy-done((f32[1,128]{1,0:T(1,128)S(1)}, f32[1,128]{1,0:T(1,128)}, u32[]{:S(2)}) %copy-start.9) | copy-done | bytes 536
  19.9 2.0 %collective-permute-start.2 = (f32[1,128]{1,0:T(1,128)S(1)}, f32[1,128]{1,0:T(1,128)S(1)}, u32[]{:S(2)}, u32[]{:S(2)}) collective-permute-start(f32[1,128]{1,0:T(1,128)S(1)} %copy-done.9), channel_id=1, source_target_pairs={{0,1},{1,2},{2,3},{3,4},{4,5},{5,6},{6,7},{7,8},{8,9},{9,10},{10,1... | collective-permute-start | bytes 1544 | tf_op jit(solution)/shard_map/ppermute | solution.py:35
  22.0 0.0 copy-done.6
  22.0 4.5 %collective-permute-start.3 = (f32[1,128]{1,0:T(1,128)S(1)}, f32[1,128]{1,0:T(1,128)S(1)}, u32[]{:S(2)}, u32[]{:S(2)}) collective-permute-start(f32[1,128]{1,0:T(1,128)S(1)} %copy-done.6), channel_id=1, source_target_pairs={{1,0},{2,1},{3,2},{4,3},{5,4},{6,5},{7,6},{8,7},{9,8},{10,9},{11,1... | collective-permute-start | bytes 1544 | tf_op jit(solution)/shard_map/ppermute | solution.py:36
  26.6 3.9 %shard_map.98.own_ref = f32[96,2304]{1,0:T(8,128)} custom-call(s32[2]{0:T(128)} %band_ref.13, s32[2]{0:T(128)} %col_ref.13, s32[2]{0:T(128)} %cell_ref.13, f32[9,256]{1,0:T(8,128)} %psf_ref.13, f32[2,128]{1,0:T(2,128)} %oy_ref.13, f32[2,128]{1,0:T(2,128)} %ox_ref.13, f32[2,128]{1,0:T(2,128)} %get-tuple-element.14.f_ref), custom_call_target="tpu_custom_call" | custom-call | flops 339738624 | bytes 884736 | tf_op jit(solution)/shard_map/pallas_call | solution.py:223
  30.5 0.0 collective-permute-done.2.fa_ref
  30.5 0.0 collective-permute-done.3.fb_ref
  30.5 0.6 %copy-done.3 = f32[1,128]{1,0:T(1,128)} copy-done((f32[1,128]{1,0:T(1,128)}, f32[1,128]{1,0:T(1,128)S(1)}, u32[]{:S(2)}) %copy-start.3) | copy-done | bytes 536
  31.1 0.5 %copy-done.7 = f32[1,128]{1,0:T(1,128)} copy-done((f32[1,128]{1,0:T(1,128)}, f32[1,128]{1,0:T(1,128)S(1)}, u32[]{:S(2)}) %copy-start.7) | copy-done | bytes 536
  31.6 4.9 %shard_map.99 = (f32[2,128]{1,0:T(2,128)}, f32[1,128]{1,0:T(1,128)}, f32[1,128]{1,0:T(1,128)}) custom-call(s32[2]{0:T(128)} %band_ref.13, s32[2]{0:T(128)} %col_ref.13, s32[2]{0:T(128)} %cell_ref.13, f32[9,256]{1,0:T(8,128)} %psf_ref.13, f32[32]{0:T(128)} %pad_maximum_fusion.nbm_ref, s32[2]{0:T(128)} %add_convert_fusion.flag_ref, f32[2,128]{1,0:T(2,128)} %oy_ref.13, ...), custom_call_target="tpu_custom_call" | custom-call | flops 1019215872 | bytes 1572864 | tf_op jit(solution)/shard_map/pallas_call | solution.py:242
  36.5 0.6 %copy-done.8 = f32[1,128]{1,0:T(1,128)S(1)} copy-done((f32[1,128]{1,0:T(1,128)S(1)}, f32[1,128]{1,0:T(1,128)}, u32[]{:S(2)}) %copy-start.8) | copy-done | bytes 536
  37.1 2.0 %collective-permute-start.4 = (f32[1,128]{1,0:T(1,128)S(1)}, f32[1,128]{1,0:T(1,128)S(1)}, u32[]{:S(2)}, u32[]{:S(2)}) collective-permute-start(f32[1,128]{1,0:T(1,128)S(1)} %copy-done.8), channel_id=1, source_target_pairs={{0,1},{1,2},{2,3},{3,4},{4,5},{5,6},{6,7},{7,8},{8,9},{9,10},{10,1... | collective-permute-start | bytes 1544 | tf_op jit(solution)/shard_map/ppermute | solution.py:35
  39.2 0.0 copy-done.4
  39.2 4.7 %collective-permute-start.5 = (f32[1,128]{1,0:T(1,128)S(1)}, f32[1,128]{1,0:T(1,128)S(1)}, u32[]{:S(2)}, u32[]{:S(2)}) collective-permute-start(f32[1,128]{1,0:T(1,128)S(1)} %copy-done.4), channel_id=1, source_target_pairs={{1,0},{2,1},{3,2},{4,3},{5,4},{6,5},{7,6},{8,7},{9,8},{10,9},{11,1... | collective-permute-start | bytes 1544 | tf_op jit(solution)/shard_map/ppermute | solution.py:36
  43.9 3.9 %shard_map.100.own_ref = f32[96,2304]{1,0:T(8,128)} custom-call(s32[2]{0:T(128)} %band_ref.13, s32[2]{0:T(128)} %col_ref.13, s32[2]{0:T(128)} %cell_ref.13, f32[9,256]{1,0:T(8,128)} %psf_ref.13, f32[2,128]{1,0:T(2,128)} %oy_ref.13, f32[2,128]{1,0:T(2,128)} %ox_ref.13, f32[2,128]{1,0:T(2,128)} %get-tuple-element.9.f_ref), custom_call_target="tpu_custom_call" | custom-call | flops 339738624 | bytes 884736 | tf_op jit(solution)/shard_map/pallas_call | solution.py:223
  47.9 0.0 collective-permute-done.4.fa_ref
  47.9 0.0 collective-permute-done.5.fb_ref
  47.9 0.6 %copy-done.2 = f32[1,128]{1,0:T(1,128)} copy-done((f32[1,128]{1,0:T(1,128)}, f32[1,128]{1,0:T(1,128)S(1)}, u32[]{:S(2)}) %copy-start.2) | copy-done | bytes 536
  48.4 0.5 %copy-done.5 = f32[1,128]{1,0:T(1,128)} copy-done((f32[1,128]{1,0:T(1,128)}, f32[1,128]{1,0:T(1,128)S(1)}, u32[]{:S(2)}) %copy-start.5) | copy-done | bytes 536
  49.0 4.2 %shard_map.101 = f32[64,2048]{1,0:T(8,128)} custom-call(s32[2]{0:T(128)} %band_ref.13, s32[2]{0:T(128)} %col_ref.13, s32[2]{0:T(128)} %cell_ref.13, f32[9,256]{1,0:T(8,128)} %psf_ref.13, f32[32]{0:T(128)} %pad_maximum_fusion.nbm_ref, s32[2]{0:T(128)} %add_convert_fusion.flag_ref, f32[2,128]{1,0:T(2,128)} %oy_ref.13, f32[2,128]{1,0:T(2,128)} %ox_ref.13, ...), custom_call_target="tpu_custom_call" | custom-call | flops 1019215872 | bytes 1572864 | tf_op jit(solution)/shard_map/pallas_call | solution.py:242
  (11 shorter events, 0.0 us)
Async XLA Ops:
  2.5 11.0 %collective-permute-start = (f32[16,2048]{1,0:T(8,128)}, f32[16,2048]{1,0:T(8,128)S(1)}, u32[]{:S(2)}, u32[]{:S(2)}) collective-permute-start(f32[16,2048]{1,0:T(8,128)} %get-tuple-element.11), channel_id=1, source_target_pairs={{0,1},{1,2},{2,3},{3,4},{4,5},{5,6},{6,7},{7,8},{8,9},{9,10},{10,1... | collective-permute-start | bytes 393224 | tf_op jit(solution)/shard_map/ppermute | solution.py:35
  4.4 9.1 %collective-permute-start.1 = (f32[16,2048]{1,0:T(8,128)}, f32[16,2048]{1,0:T(8,128)S(1)}, u32[]{:S(2)}, u32[]{:S(2)}) collective-permute-start(f32[16,2048]{1,0:T(8,128)} %get-tuple-element.12), channel_id=1, source_target_pairs={{1,0},{2,1},{3,2},{4,3},{5,4},{6,5},{7,6},{8,7},{9,8},{10,9},{11,1... | collective-permute-start | bytes 393224 | tf_op jit(solution)/shard_map/ppermute | solution.py:36
  13.5 0.7 %copy-start = (f32[16,2048]{1,0:T(8,128)}, f32[16,2048]{1,0:T(8,128)S(1)}, u32[]{:S(2)}) copy-start(f32[16,2048]{1,0:T(8,128)S(1)} %collective-permute-done.above_ref.fa_ref) | copy-start | bytes 393220
  13.5 0.7 %copy-start.1 = (f32[16,2048]{1,0:T(8,128)}, f32[16,2048]{1,0:T(8,128)S(1)}, u32[]{:S(2)}) copy-start(f32[16,2048]{1,0:T(8,128)S(1)} %collective-permute-done.1.below_ref.fb_ref) | copy-start | bytes 393220
  19.3 0.7 %copy-start.9 = (f32[1,128]{1,0:T(1,128)S(1)}, f32[1,128]{1,0:T(1,128)}, u32[]{:S(2)}) copy-start(f32[1,128]{1,0:T(1,128)} %get-tuple-element.15) | copy-start | bytes 1540
  19.9 2.1 %copy-start.6 = (f32[1,128]{1,0:T(1,128)S(1)}, f32[1,128]{1,0:T(1,128)}, u32[]{:S(2)}) copy-start(f32[1,128]{1,0:T(1,128)} %get-tuple-element.16) | copy-start | bytes 1540
  19.9 10.5 %collective-permute-start.2 = (f32[1,128]{1,0:T(1,128)S(1)}, f32[1,128]{1,0:T(1,128)S(1)}, u32[]{:S(2)}, u32[]{:S(2)}) collective-permute-start(f32[1,128]{1,0:T(1,128)S(1)} %copy-done.9), channel_id=1, source_target_pairs={{0,1},{1,2},{2,3},{3,4},{4,5},{5,6},{6,7},{7,8},{8,9},{9,10},{10,1... | collective-permute-start | bytes 1544 | tf_op jit(solution)/shard_map/ppermute | solution.py:35
  22.0 8.5 %collective-permute-start.3 = (f32[1,128]{1,0:T(1,128)S(1)}, f32[1,128]{1,0:T(1,128)S(1)}, u32[]{:S(2)}, u32[]{:S(2)}) collective-permute-start(f32[1,128]{1,0:T(1,128)S(1)} %copy-done.6), channel_id=1, source_target_pairs={{1,0},{2,1},{3,2},{4,3},{5,4},{6,5},{7,6},{8,7},{9,8},{10,9},{11,1... | collective-permute-start | bytes 1544 | tf_op jit(solution)/shard_map/ppermute | solution.py:36
  30.5 0.6 %copy-start.3 = (f32[1,128]{1,0:T(1,128)}, f32[1,128]{1,0:T(1,128)S(1)}, u32[]{:S(2)}) copy-start(f32[1,128]{1,0:T(1,128)S(1)} %collective-permute-done.2.fa_ref) | copy-start | bytes 1540
  31.1 0.5 %copy-start.7 = (f32[1,128]{1,0:T(1,128)}, f32[1,128]{1,0:T(1,128)S(1)}, u32[]{:S(2)}) copy-start(f32[1,128]{1,0:T(1,128)S(1)} %collective-permute-done.3.fb_ref) | copy-start | bytes 1540
  36.5 0.6 %copy-start.8 = (f32[1,128]{1,0:T(1,128)S(1)}, f32[1,128]{1,0:T(1,128)}, u32[]{:S(2)}) copy-start(f32[1,128]{1,0:T(1,128)} %get-tuple-element.18) | copy-start | bytes 1540
  37.1 2.1 %copy-start.4 = (f32[1,128]{1,0:T(1,128)S(1)}, f32[1,128]{1,0:T(1,128)}, u32[]{:S(2)}) copy-start(f32[1,128]{1,0:T(1,128)} %get-tuple-element.19) | copy-start | bytes 1540
  37.1 10.7 %collective-permute-start.4 = (f32[1,128]{1,0:T(1,128)S(1)}, f32[1,128]{1,0:T(1,128)S(1)}, u32[]{:S(2)}, u32[]{:S(2)}) collective-permute-start(f32[1,128]{1,0:T(1,128)S(1)} %copy-done.8), channel_id=1, source_target_pairs={{0,1},{1,2},{2,3},{3,4},{4,5},{5,6},{6,7},{7,8},{8,9},{9,10},{10,1... | collective-permute-start | bytes 1544 | tf_op jit(solution)/shard_map/ppermute | solution.py:35
  39.2 8.7 %collective-permute-start.5 = (f32[1,128]{1,0:T(1,128)S(1)}, f32[1,128]{1,0:T(1,128)S(1)}, u32[]{:S(2)}, u32[]{:S(2)}) collective-permute-start(f32[1,128]{1,0:T(1,128)S(1)} %copy-done.4), channel_id=1, source_target_pairs={{1,0},{2,1},{3,2},{4,3},{5,4},{6,5},{7,6},{8,7},{9,8},{10,9},{11,1... | collective-permute-start | bytes 1544 | tf_op jit(solution)/shard_map/ppermute | solution.py:36
  47.9 0.6 %copy-start.2 = (f32[1,128]{1,0:T(1,128)}, f32[1,128]{1,0:T(1,128)S(1)}, u32[]{:S(2)}) copy-start(f32[1,128]{1,0:T(1,128)S(1)} %collective-permute-done.4.fa_ref) | copy-start | bytes 1540
  48.4 0.5 %copy-start.5 = (f32[1,128]{1,0:T(1,128)}, f32[1,128]{1,0:T(1,128)S(1)}, u32[]{:S(2)}) copy-start(f32[1,128]{1,0:T(1,128)S(1)} %collective-permute-done.5.fb_ref) | copy-start | bytes 1540

commit v5 on v3

--- a/solution.py
+++ b/solution.py
@@ -26,6 +26,21 @@
     core_part = jnp.exp(-0.5 * scaled * scaled) * tapered
     wing_part = jnp.exp(dist * dist * (-1.0 / 72.0)) * tapered
     return core_part, scaled * core_part, wing_part
+
+
+def split_dot(lhs, rhs, dims):
+    lhs_hi = lhs.astype(jnp.bfloat16)
+    lhs_lo = (lhs - lhs_hi.astype(jnp.float32)).astype(jnp.bfloat16)
+    rhs_hi = rhs.astype(jnp.bfloat16)
+    rhs_lo = (rhs - rhs_hi.astype(jnp.float32)).astype(jnp.bfloat16)
+
+    def one(a, b):
+        return lax.dot_general(a, b, dims, preferred_element_type=jnp.float32)
+
+    return one(lhs_hi, rhs_hi) + (one(lhs_hi, rhs_lo) + one(lhs_lo, rhs_hi))
+
+
+DIMS_NN = (((1,), (0,)), ((), ()))
 
 
 def exchange(to_above, to_below):
@@ -135,14 +150,13 @@
         else:
             rows_model = rows
         cols = profile3(wpos - x)
-        stamp = None
-        for a in range(3):
-            mixed = (c[3 * a] * cols[0] + c[3 * a + 1] * cols[1] + c[3 * a + 2] * cols[2]) * flux
-            part = lax.dot_general(
-                rows_model[a], mixed, DIMS_NT, precision=HIGHEST,
-                preferred_element_type=jnp.float32,
-            )
-            stamp = part if stamp is None else stamp + part
+        mixed = [
+            (c[3 * a] * cols[0] + c[3 * a + 1] * cols[1] + c[3 * a + 2] * cols[2]) * flux
+            for a in range(3)
+        ]
+        stamp = split_dot(
+            jnp.concatenate(rows_model, axis=1), jnp.concatenate(mixed, axis=1), DIMS_NT
+        )
         start = pl.multiple_of(col * LANES, LANES)
         canvas[:, pl.ds(start, WIN)] += stamp
         if j < own:
@@ -166,10 +180,8 @@
     for j in range(own):
         rows, cols, c, start = saved[j]
         window = canvas[:, pl.ds(start, WIN)]
-        across = [
-            jnp.dot(window, cols[b], precision=HIGHEST, preferred_element_type=jnp.float32)
-            for b in range(3)
-        ]
+        across_all = split_dot(window, jnp.concatenate(cols, axis=1), DIMS_NN)
+        across = [across_all[:, b * LANES : (b + 1) * LANES] for b in range(3)]
         grad = None
         for a in range(3):
             for b in range(3):

time: 50.3 us -> 45.4 us (0.903)
  Pallas kernels: 19.5 us -> 14.6 us
    pallas_call x3, Pallas kernels: 17.6 us -> 12.7 us  [phase(): pl.pallas_call(kernel, out_shape=out_shape, in_specs=[smem] * 6 + [vmem]...]
where the time goes in v5:
time: 45.4 us; the launch traced here: 45 us
  Pallas kernels  14.6 us (32%)
  starting transfers between devices  14.5 us (32%)
  waiting for transfers between devices  11.6 us (26%)
  local copies, waits for them, and re-layouts  2.35 us (5%)
  other arithmetic  1.23 us (3%)
  between operations  0.74 us (2%)
    pallas_call x3, Pallas kernels, phase(): pl.pallas_call(kernel, out_shape=out_shape, in_specs=[smem] * 6 + [vmem]...  12.7 us
    ppermute x3, waiting for transfers between devices, exchange(): from_below = lax.ppermute(to_above, 'ty', backward)  11.6 us
    ppermute x3, starting transfers between devices, exchange(): from_above = lax.ppermute(to_below, 'ty', forward)  7.86 us
    ppermute x3, starting transfers between devices, exchange(): from_below = lax.ppermute(to_above, 'ty', backward)  6.67 us
    unnamed x20, local copies, waits for them, and re-layouts  2.34 us
    pallas_call x1, Pallas kernels, local(): pl.pallas_call(setup_kernel, out_shape=(packet, packet, jax.ShapeDtypeStr...  1.9 us
  transfers between devices with their start and end apart: 6, of which 3 were waited for; matrix products, arithmetic and copies ran while one was open for 1% of the time, Pallas kernels for 0%

profile of v5, /device:TPU:11, one launch (start us, length us, event | category | flops | bytes accessed | tf_op | source)
XLA Modules:
  0.0 45.0 jit_solution(3581401493774736019)
XLA Ops:
  0.6 1.9 %shard_map.95 = (f32[16,2048]{1,0:T(8,128)}, f32[16,2048]{1,0:T(8,128)}, f32[2,128]{1,0:T(2,128)}) custom-call(s32[2]{0:T(128)} %band_ref.7, s32[2]{0:T(128)} %col_ref.7, s32[2]{0:T(128)} %cell_ref.7, f32[9,256]{1,0:T(8,128)} %psf_ref.7, f32[64,2048]{1,0:T(8,128)} %img_ref.7, f32[2,128]{1,0:T(2,128)} %oy_ref.7, f32[2,128]{1,0:T(2,128)} %ox_ref.7, f32[2,128]{1,0:T(2,128)} %f_ref.3), custom_call_target="tpu_custom_call" | custom-call | tf_op jit(solution)/shard_map/pallas_call | solution.py:206
  2.5 3.7 %collective-permute-start = (f32[16,2048]{1,0:T(8,128)}, f32[16,2048]{1,0:T(8,128)S(1)}, u32[]{:S(2)}, u32[]{:S(2)}) collective-permute-start(f32[16,2048]{1,0:T(8,128)} %get-tuple-element.11), channel_id=1, source_target_pairs={{0,1},{1,2},{2,3},{3,4},{4,5},{5,6},{6,7},{7,8},{8,9},{9,10},{10,1... | collective-permute-start | bytes 393224 | tf_op jit(solution)/shard_map/ppermute | solution.py:50
  6.3 1.9 %collective-permute-start.1 = (f32[16,2048]{1,0:T(8,128)}, f32[16,2048]{1,0:T(8,128)S(1)}, u32[]{:S(2)}, u32[]{:S(2)}) collective-permute-start(f32[16,2048]{1,0:T(8,128)} %get-tuple-element.12), channel_id=1, source_target_pairs={{1,0},{2,1},{3,2},{4,3},{5,4},{6,5},{7,6},{8,7},{9,8},{10,9},{11,1... | collective-permute-start | bytes 393224 | tf_op jit(solution)/shard_map/ppermute | solution.py:51
  8.2 0.6 %add_convert_fusion.flag_ref = s32[2]{0:T(128)} fusion(pred[1]{0:T(512)(128)(4,1)} %bitcast.3, pred[1]{0:T(512)(128)(4,1)} %bitcast.2), kind=kLoop, calls=%fused_computation | loop fusion | flops 4 | bytes 10 | tf_op jit(solution)/shard_map/convert_element_type | solution.py:216
  8.8 0.0 collective-permute-done.above_ref.fa_ref
  8.8 0.0 copy-start
  8.8 4.9 %collective-permute-done.1.below_ref.fb_ref = f32[16,2048]{1,0:T(8,128)S(1)} collective-permute-done((f32[16,2048]{1,0:T(8,128)}, f32[16,2048]{1,0:T(8,128)S(1)}, u32[]{:S(2)}, u32[]{:S(2)}) %collective-permute-start.1) | collective-permute-done | bytes 131104 | tf_op jit(solution)/shard_map/ppermute | solution.py:51
  13.7 0.0 copy-start.1
  13.7 0.7 %pad_maximum_fusion.nbm_ref = f32[32]{0:T(128)} fusion(f32[16]{0:T(128)S(1)} %slice_bitcast_fusion, f32[16]{0:T(128)S(1)} %slice_bitcast_fusion.1), kind=kLoop, calls=%fused_computation.3 | loop fusion | flops 32 | bytes 256 | tf_op jit(solution)/shard_map/concatenate | solution.py:217
  14.3 0.0 copy-done
  14.3 0.0 copy-done.1
  14.3 4.4 %shard_map.96 = (f32[2,128]{1,0:T(2,128)}, f32[1,128]{1,0:T(1,128)}, f32[1,128]{1,0:T(1,128)}) custom-call(s32[2]{0:T(128)} %band_ref.7, s32[2]{0:T(128)} %col_ref.7, s32[2]{0:T(128)} %cell_ref.7, f32[9,256]{1,0:T(8,128)} %psf_ref.7, f32[32]{0:T(128)} %pad_maximum_fusion.nbm_ref, s32[2]{0:T(128)} %add_convert_fusion.flag_ref, f32[2,128]{1,0:T(2,128)} %oy_ref.7, ...), custom_call_target="tpu_custom_call" | custom-call | flops 1019215872 | bytes 1572864 | tf_op jit(solution)/shard_map/pallas_call | solution.py:237
  18.7 0.7 %copy-done.9 = f32[1,128]{1,0:T(1,128)S(1)} copy-done((f32[1,128]{1,0:T(1,128)S(1)}, f32[1,128]{1,0:T(1,128)}, u32[]{:S(2)}) %copy-start.9) | copy-done | bytes 536
  19.4 2.0 %collective-permute-start.2 = (f32[1,128]{1,0:T(1,128)S(1)}, f32[1,128]{1,0:T(1,128)S(1)}, u32[]{:S(2)}, u32[]{:S(2)}) collective-permute-start(f32[1,128]{1,0:T(1,128)S(1)} %copy-done.9), channel_id=1, source_target_pairs={{0,1},{1,2},{2,3},{3,4},{4,5},{5,6},{6,7},{7,8},{8,9},{9,10},{10,1... | collective-permute-start | bytes 1544 | tf_op jit(solution)/shard_map/ppermute | solution.py:50
  21.4 0.0 copy-done.7
  21.4 2.4 %collective-permute-start.3 = (f32[1,128]{1,0:T(1,128)S(1)}, f32[1,128]{1,0:T(1,128)S(1)}, u32[]{:S(2)}, u32[]{:S(2)}) collective-permute-start(f32[1,128]{1,0:T(1,128)S(1)} %copy-done.7), channel_id=1, source_target_pairs={{1,0},{2,1},{3,2},{4,3},{5,4},{6,5},{7,6},{8,7},{9,8},{10,9},{11,1... | collective-permute-start | bytes 1544 | tf_op jit(solution)/shard_map/ppermute | solution.py:51
  23.8 0.0 collective-permute-done.2.fa_ref
  23.9 0.0 copy-start.3
  23.9 3.3 %collective-permute-done.3.fb_ref = f32[1,128]{1,0:T(1,128)S(1)} collective-permute-done((f32[1,128]{1,0:T(1,128)S(1)}, f32[1,128]{1,0:T(1,128)S(1)}, u32[]{:S(2)}, u32[]{:S(2)}) %collective-permute-start.3) | collective-permute-done | bytes 544 | tf_op jit(solution)/shard_map/ppermute | solution.py:51
  27.2 0.0 copy-done.3
  27.2 0.5 %copy-done.6 = f32[1,128]{1,0:T(1,128)} copy-done((f32[1,128]{1,0:T(1,128)}, f32[1,128]{1,0:T(1,128)S(1)}, u32[]{:S(2)}) %copy-start.6) | copy-done | bytes 536
  27.7 4.3 %shard_map.97 = (f32[2,128]{1,0:T(2,128)}, f32[1,128]{1,0:T(1,128)}, f32[1,128]{1,0:T(1,128)}) custom-call(s32[2]{0:T(128)} %band_ref.7, s32[2]{0:T(128)} %col_ref.7, s32[2]{0:T(128)} %cell_ref.7, f32[9,256]{1,0:T(8,128)} %psf_ref.7, f32[32]{0:T(128)} %pad_maximum_fusion.nbm_ref, s32[2]{0:T(128)} %add_convert_fusion.flag_ref, f32[2,128]{1,0:T(2,128)} %oy_ref.7, ...), custom_call_target="tpu_custom_call" | custom-call | flops 1019215872 | bytes 1572864 | tf_op jit(solution)/shard_map/pallas_call | solution.py:237
  32.0 0.7 %copy-done.8 = f32[1,128]{1,0:T(1,128)S(1)} copy-done((f32[1,128]{1,0:T(1,128)S(1)}, f32[1,128]{1,0:T(1,128)}, u32[]{:S(2)}) %copy-start.8) | copy-done | bytes 536
  32.7 2.1 %collective-permute-start.4 = (f32[1,128]{1,0:T(1,128)S(1)}, f32[1,128]{1,0:T(1,128)S(1)}, u32[]{:S(2)}, u32[]{:S(2)}) collective-permute-start(f32[1,128]{1,0:T(1,128)S(1)} %copy-done.8), channel_id=1, source_target_pairs={{0,1},{1,2},{2,3},{3,4},{4,5},{5,6},{6,7},{7,8},{8,9},{9,10},{10,1... | collective-permute-start | bytes 1544 | tf_op jit(solution)/shard_map/ppermute | solution.py:50
  34.8 0.0 copy-done.4
  34.8 2.3 %collective-permute-start.5 = (f32[1,128]{1,0:T(1,128)S(1)}, f32[1,128]{1,0:T(1,128)S(1)}, u32[]{:S(2)}, u32[]{:S(2)}) collective-permute-start(f32[1,128]{1,0:T(1,128)S(1)} %copy-done.4), channel_id=1, source_target_pairs={{1,0},{2,1},{3,2},{4,3},{5,4},{6,5},{7,6},{8,7},{9,8},{10,9},{11,1... | collective-permute-start | bytes 1544 | tf_op jit(solution)/shard_map/ppermute | solution.py:51
  37.2 0.0 collective-permute-done.4.fa_ref
  37.2 0.0 copy-start.2
  37.2 3.4 %collective-permute-done.5.fb_ref = f32[1,128]{1,0:T(1,128)S(1)} collective-permute-done((f32[1,128]{1,0:T(1,128)S(1)}, f32[1,128]{1,0:T(1,128)S(1)}, u32[]{:S(2)}, u32[]{:S(2)}) %collective-permute-start.5) | collective-permute-done | bytes 544 | tf_op jit(solution)/shard_map/ppermute | solution.py:51
  40.6 0.0 copy-done.2
  40.6 0.5 %copy-done.5 = f32[1,128]{1,0:T(1,128)} copy-done((f32[1,128]{1,0:T(1,128)}, f32[1,128]{1,0:T(1,128)S(1)}, u32[]{:S(2)}) %copy-start.5) | copy-done | bytes 536
  41.1 3.9 %shard_map.98 = f32[64,2048]{1,0:T(8,128)} custom-call(s32[2]{0:T(128)} %band_ref.7, s32[2]{0:T(128)} %col_ref.7, s32[2]{0:T(128)} %cell_ref.7, f32[9,256]{1,0:T(8,128)} %psf_ref.7, f32[32]{0:T(128)} %pad_maximum_fusion.nbm_ref, s32[2]{0:T(128)} %add_convert_fusion.flag_ref, f32[2,128]{1,0:T(2,128)} %oy_ref.7, f32[2,128]{1,0:T(2,128)} %ox_ref.7, ...), custom_call_target="tpu_custom_call" | custom-call | flops 1019215872 | bytes 1572864 | tf_op jit(solution)/shard_map/pallas_call | solution.py:237
  (8 shorter events, 0.0 us)
Async XLA Ops:
  2.5 6.2 %collective-permute-start = (f32[16,2048]{1,0:T(8,128)}, f32[16,2048]{1,0:T(8,128)S(1)}, u32[]{:S(2)}, u32[]{:S(2)}) collective-permute-start(f32[16,2048]{1,0:T(8,128)} %get-tuple-element.11), channel_id=1, source_target_pairs={{0,1},{1,2},{2,3},{3,4},{4,5},{5,6},{6,7},{7,8},{8,9},{9,10},{10,1... | collective-permute-start | bytes 393224 | tf_op jit(solution)/shard_map/ppermute | solution.py:50
  6.3 7.4 %collective-permute-start.1 = (f32[16,2048]{1,0:T(8,128)}, f32[16,2048]{1,0:T(8,128)S(1)}, u32[]{:S(2)}, u32[]{:S(2)}) collective-permute-start(f32[16,2048]{1,0:T(8,128)} %get-tuple-element.12), channel_id=1, source_target_pairs={{1,0},{2,1},{3,2},{4,3},{5,4},{6,5},{7,6},{8,7},{9,8},{10,9},{11,1... | collective-permute-start | bytes 393224 | tf_op jit(solution)/shard_map/ppermute | solution.py:51
  8.8 5.5 %copy-start = (f32[16,2048]{1,0:T(8,128)}, f32[16,2048]{1,0:T(8,128)S(1)}, u32[]{:S(2)}) copy-start(f32[16,2048]{1,0:T(8,128)S(1)} %collective-permute-done.above_ref.fa_ref) | copy-start | bytes 393220
  13.7 0.7 %copy-start.1 = (f32[16,2048]{1,0:T(8,128)}, f32[16,2048]{1,0:T(8,128)S(1)}, u32[]{:S(2)}) copy-start(f32[16,2048]{1,0:T(8,128)S(1)} %collective-permute-done.1.below_ref.fb_ref) | copy-start | bytes 393220
  18.7 0.7 %copy-start.9 = (f32[1,128]{1,0:T(1,128)S(1)}, f32[1,128]{1,0:T(1,128)}, u32[]{:S(2)}) copy-start(f32[1,128]{1,0:T(1,128)} %get-tuple-element.15) | copy-start | bytes 1540
  19.4 2.1 %copy-start.7 = (f32[1,128]{1,0:T(1,128)S(1)}, f32[1,128]{1,0:T(1,128)}, u32[]{:S(2)}) copy-start(f32[1,128]{1,0:T(1,128)} %get-tuple-element.16) | copy-start | bytes 1540
  19.4 4.5 %collective-permute-start.2 = (f32[1,128]{1,0:T(1,128)S(1)}, f32[1,128]{1,0:T(1,128)S(1)}, u32[]{:S(2)}, u32[]{:S(2)}) collective-permute-start(f32[1,128]{1,0:T(1,128)S(1)} %copy-done.9), channel_id=1, source_target_pairs={{0,1},{1,2},{2,3},{3,4},{4,5},{5,6},{6,7},{7,8},{8,9},{9,10},{10,1... | collective-permute-start | bytes 1544 | tf_op jit(solution)/shard_map/ppermute | solution.py:50
  21.4 5.8 %collective-permute-start.3 = (f32[1,128]{1,0:T(1,128)S(1)}, f32[1,128]{1,0:T(1,128)S(1)}, u32[]{:S(2)}, u32[]{:S(2)}) collective-permute-start(f32[1,128]{1,0:T(1,128)S(1)} %copy-done.7), channel_id=1, source_target_pairs={{1,0},{2,1},{3,2},{4,3},{5,4},{6,5},{7,6},{8,7},{9,8},{10,9},{11,1... | collective-permute-start | bytes 1544 | tf_op jit(solution)/shard_map/ppermute | solution.py:51
  23.9 3.3 %copy-start.3 = (f32[1,128]{1,0:T(1,128)}, f32[1,128]{1,0:T(1,128)S(1)}, u32[]{:S(2)}) copy-start(f32[1,128]{1,0:T(1,128)S(1)} %collective-permute-done.2.fa_ref) | copy-start | bytes 1540
  27.2 0.5 %copy-start.6 = (f32[1,128]{1,0:T(1,128)}, f32[1,128]{1,0:T(1,128)S(1)}, u32[]{:S(2)}) copy-start(f32[1,128]{1,0:T(1,128)S(1)} %collective-permute-done.3.fb_ref) | copy-start | bytes 1540
  32.0 0.7 %copy-start.8 = (f32[1,128]{1,0:T(1,128)S(1)}, f32[1,128]{1,0:T(1,128)}, u32[]{:S(2)}) copy-start(f32[1,128]{1,0:T(1,128)} %get-tuple-element.18) | copy-start | bytes 1540
  32.7 2.1 %copy-start.4 = (f32[1,128]{1,0:T(1,128)S(1)}, f32[1,128]{1,0:T(1,128)}, u32[]{:S(2)}) copy-start(f32[1,128]{1,0:T(1,128)} %get-tuple-element.19) | copy-start | bytes 1540
  32.7 4.5 %collective-permute-start.4 = (f32[1,128]{1,0:T(1,128)S(1)}, f32[1,128]{1,0:T(1,128)S(1)}, u32[]{:S(2)}, u32[]{:S(2)}) collective-permute-start(f32[1,128]{1,0:T(1,128)S(1)} %copy-done.8), channel_id=1, source_target_pairs={{0,1},{1,2},{2,3},{3,4},{4,5},{5,6},{6,7},{7,8},{8,9},{9,10},{10,1... | collective-permute-start | bytes 1544 | tf_op jit(solution)/shard_map/ppermute | solution.py:50
  34.8 5.8 %collective-permute-start.5 = (f32[1,128]{1,0:T(1,128)S(1)}, f32[1,128]{1,0:T(1,128)S(1)}, u32[]{:S(2)}, u32[]{:S(2)}) collective-permute-start(f32[1,128]{1,0:T(1,128)S(1)} %copy-done.4), channel_id=1, source_target_pairs={{1,0},{2,1},{3,2},{4,3},{5,4},{6,5},{7,6},{8,7},{9,8},{10,9},{11,1... | collective-permute-start | bytes 1544 | tf_op jit(solution)/shard_map/ppermute | solution.py:51
  37.2 3.4 %copy-start.2 = (f32[1,128]{1,0:T(1,128)}, f32[1,128]{1,0:T(1,128)S(1)}, u32[]{:S(2)}) copy-start(f32[1,128]{1,0:T(1,128)S(1)} %collective-permute-done.4.fa_ref) | copy-start | bytes 1540
  40.6 0.5 %copy-start.5 = (f32[1,128]{1,0:T(1,128)}, f32[1,128]{1,0:T(1,128)S(1)}, u32[]{:S(2)}) copy-start(f32[1,128]{1,0:T(1,128)S(1)} %collective-permute-done.5.fb_ref) | copy-start | bytes 1540

commit v6 on v5

v6 whole, which is shorter than its diff:
```python
import functools

import jax
import jax.numpy as jnp
from jax import lax
from jax.experimental import pallas as pl
from jax.experimental.pallas import tpu as pltpu
from jax.sharding import PartitionSpec as P

REACH = 15
ITERS = 2
LANES = 128
WIN = 384
SLOTS = 8

DIMS_NT = (((1,), (1,)), ((), ()))
DIMS_NN = (((1,), (0,)), ((), ()))


def profile3(dist):
    tapered_arg = dist * (1.0 / 15.5)
    tapered = jnp.maximum(0.0, 1.0 - tapered_arg * tapered_arg)
    scaled = dist * (1.0 / 1.7)
    core_part = jnp.exp(-0.5 * scaled * scaled) * tapered
    wing_part = jnp.exp(dist * dist * (-1.0 / 72.0)) * tapered
    return core_part, scaled * core_part, wing_part


def split_dot(lhs, rhs, dims):
    lhs_hi = lhs.astype(jnp.bfloat16)
    lhs_lo = (lhs - lhs_hi.astype(jnp.float32)).astype(jnp.bfloat16)
    rhs_hi = rhs.astype(jnp.bfloat16)
    rhs_lo = (rhs - rhs_hi.astype(jnp.float32)).astype(jnp.bfloat16)

    def one(a, b):
        return lax.dot_general(a, b, dims, preferred_element_type=jnp.float32)

    return one(lhs_hi, rhs_hi) + (one(lhs_hi, rhs_lo) + one(lhs_lo, rhs_hi))


def exchange(to_above, to_below):
    count = lax.axis_size("ty")
    forward = [(i, i + 1) for i in range(count - 1)]
    backward = [(i + 1, i) for i in range(count - 1)]
    from_above = lax.ppermute(to_below, "ty", forward)
    from_below = lax.ppermute(to_above, "ty", backward)
    return from_above, from_below


def own_coefs(psf_ref, cell_ref, j):
    cell = cell_ref[j]
    return [psf_ref[k, cell] for k in range(9)]


def setup_kernel(band_ref, col_ref, cell_ref, psf_ref, oy_ref, ox_ref, f_ref, up_ref, down_ref, w_ref):
    own = oy_ref.shape[0]
    offs = lax.broadcasted_iota(jnp.int32, (32, LANES), 0).astype(jnp.float32) - 15.0
    lane = lax.broadcasted_iota(jnp.int32, (1, LANES), 1)
    ys, metas, weights = [], [], []
    for j in range(own):
        y = band_ref[j].astype(jnp.float32) + oy_ref[j : j + 1, :]
        x = ox_ref[j : j + 1, :]
        c = own_coefs(psf_ref, cell_ref, j)
        rows = profile3(jnp.floor(y) + offs - y)
        cols = profile3(jnp.floor(x) + offs - x)
        gram_r = [[jnp.sum(rows[a] * rows[b], axis=0, keepdims=True) for b in range(3)] for a in range(3)]
        gram_c = [[jnp.sum(cols[a] * cols[b], axis=0, keepdims=True) for b in range(3)] for a in range(3)]
        weight = None
        for a in range(3):
            for cc in range(3):
                inner = None
                for b in range(3):
                    for d in range(3):
                        term = (c[3 * a + b] * c[3 * cc + d]) * gram_c[b][d]
                        inner = term if inner is None else inner + term
                term = gram_r[a][cc] * inner
                weight = term if weight is None else weight + term
        w_ref[j : j + 1, :] = weight
        meta = jnp.zeros((1, LANES), jnp.float32)
        for k in range(9):
            meta = jnp.where(lane == k, c[k], meta)
        meta = jnp.where(lane == 9, col_ref[j].astype(jnp.float32), meta)
        ys.append(y)
        metas.append(meta)
        weights.append(weight)
    top_first = band_ref[0] <= band_ref[1]

    def pick(first, second):
        return jnp.where(top_first, first, second), jnp.where(top_first, second, first)

    tops, bots = zip(*[
        pick(*pair) for pair in (
            (ys[0], ys[1]), (ox_ref[0:1, :], ox_ref[1:2, :]), (f_ref[0:1, :], f_ref[1:2, :]),
            (weights[0], weights[1]), (metas[0], metas[1]),
        )
    ])
    up_ref[...] = jnp.zeros_like(up_ref)
    down_ref[...] = jnp.zeros_like(down_ref)
    for r in range(5):
        up_ref[r : r + 1, :] = tops[r]
        down_ref[r : r + 1, :] = bots[r]


def phase_kernel(
    final, first,
    band_ref, col_ref, cell_ref, psf_ref, pas_ref, pbs_ref,
    oy_ref, ox_ref, w_ref, pa_ref, pb_ref, img_ref, f_ref, l_ref, ra_ref, rb_ref,
    *rest,
):
    if final:
        out_ref, fluxout_ref, canvas = rest
    else:
        fout_ref, lout_ref, up_ref, down_ref, canvas = rest
    rows_n, pad_width = canvas.shape
    strip_rows, width = img_ref.shape
    own = oy_ref.shape[0]
    top_first = band_ref[0] <= band_ref[1]

    if first:
        fluxes = [f_ref[0:1, :], f_ref[1:2, :], pa_ref[2:3, :], pb_ref[2:3, :]]
    else:
        weights = [w_ref[0:1, :], w_ref[1:2, :], pa_ref[3:4, :], pb_ref[3:4, :]]
        from_above = ra_ref[0:1, :]
        from_below = rb_ref[0:1, :]
        extra = [
            jnp.where(top_first, from_above, from_below),
            jnp.where(top_first, from_below, from_above),
            ra_ref[1:2, :],
            rb_ref[1:2, :],
        ]
        fluxes = []
        for j in range(own + 2):
            grad = l_ref[j : j + 1, :] + extra[j]
            safe = jnp.where(weights[j] == 0.0, 1.0, weights[j])
            fluxes.append(f_ref[j : j + 1, :] + 0.5 * grad / safe)

    specs = []
    for j in range(own):
        y = band_ref[j].astype(jnp.float32) + oy_ref[j : j + 1, :]
        specs.append((y, ox_ref[j : j + 1, :], own_coefs(psf_ref, cell_ref, j), col_ref[j], None))
    specs.append((
        pa_ref[0:1, :] - strip_rows, pa_ref[1:2, :], [pas_ref[4, k] for k in range(9)],
        pas_ref[4, 9].astype(jnp.int32), REACH,
    ))
    specs.append((
        pb_ref[0:1, :] + strip_rows, pb_ref[1:2, :], [pbs_ref[4, k] for k in range(9)],
        pbs_ref[4, 9].astype(jnp.int32), None,
    ))

    canvas[...] = jnp.zeros_like(canvas)
    hpos = lax.broadcasted_iota(jnp.int32, (rows_n, LANES), 0).astype(jnp.float32)
    wpos = lax.broadcasted_iota(jnp.int32, (WIN, LANES), 0).astype(jnp.float32) - LANES
    saved = []
    for j, (y, x, c, col, keep) in enumerate(specs):
        rows = profile3(hpos - y)
        if keep is not None:
            rows = tuple(jnp.where(hpos < keep, r, 0.0) for r in rows)
        cols = profile3(wpos - x)
        mixed = [
            (c[3 * a] * cols[0] + c[3 * a + 1] * cols[1] + c[3 * a + 2] * cols[2]) * fluxes[j]
            for a in range(3)
        ]
        stamp = split_dot(jnp.concatenate(rows, axis=1), jnp.concatenate(mixed, axis=1), DIMS_NT)
        start = pl.multiple_of(col * LANES, LANES)
        canvas[:, pl.ds(start, WIN)] += stamp
        saved.append((rows, cols, c, start))
    inner = slice(LANES, LANES + width)
    if final:
        out_ref[...] = img_ref[...] - canvas[:, inner]
        for j in range(own):
            fluxout_ref[j : j + 1, :] = fluxes[j]
        return
    canvas[:, inner] = img_ref[...] - canvas[:, inner]
    canvas[:, 0:LANES] = jnp.zeros((rows_n, LANES), jnp.float32)
    canvas[:, LANES + width :] = jnp.zeros((rows_n, pad_width - LANES - width), jnp.float32)
    fout_ref[...] = jnp.zeros_like(fout_ref)
    lout_ref[...] = jnp.zeros_like(lout_ref)
    partial = []
    for j, (rows, cols, c, start) in enumerate(saved):
        window = canvas[:, pl.ds(start, WIN)]
        across_all = split_dot(window, jnp.concatenate(cols, axis=1), DIMS_NN)
        grad = None
        for a in range(3):
            for b in range(3):
                paired = jnp.sum(rows[a] * across_all[:, b * LANES : (b + 1) * LANES], axis=0,
                                 keepdims=True)
                term = c[3 * a + b] * paired
                grad = term if grad is None else grad + term
        partial.append(grad)
        fout_ref[j : j + 1, :] = fluxes[j]
        lout_ref[j : j + 1, :] = grad
    top_part = jnp.where(top_first, partial[0], partial[1])
    bot_part = jnp.where(top_first, partial[1], partial[0])
    up_ref[0:1, :] = partial[own]
    up_ref[1:2, :] = top_part
    down_ref[0:1, :] = partial[own + 1]
    down_ref[1:2, :] = bot_part


def local(image, band_row, col_block, cell_index, offset_y, offset_x, flux_start, psf_coef):
    strip_rows, strip_width = image.shape
    own = band_row.shape[0]
    f32 = jnp.float32
    smem = pl.BlockSpec(memory_space=pltpu.SMEM)
    vmem = pl.BlockSpec(memory_space=pltpu.VMEM)
    packet = jax.ShapeDtypeStruct((SLOTS, LANES), f32)
    send_up, send_down, weight = pl.pallas_call(
        setup_kernel,
        out_shape=(packet, packet, jax.ShapeDtypeStruct((own, LANES), f32)),
        in_specs=[smem] * 4 + [vmem] * 3,
        out_specs=(vmem, vmem, vmem),
    )(band_row, col_block, cell_index, psf_coef, offset_y, offset_x, flux_start)
    got_above, got_below = exchange(send_up, send_down)

    blocks = own + 2
    flops = 2 * 3 * 2 * strip_rows * WIN * 3 * LANES * blocks
    state_shape = jax.ShapeDtypeStruct((SLOTS, LANES), f32)
    part_shape = jax.ShapeDtypeStruct((2, LANES), f32)
    common = (band_row, col_block, cell_index, psf_coef, got_above, got_below,
              offset_y, offset_x, weight, got_above, got_below, image)

    def phase(final, first, fluxes, partials, from_above, from_below):
        kernel = functools.partial(phase_kernel, final, first)
        if final:
            out_shape = (jax.ShapeDtypeStruct((strip_rows, strip_width), f32),
                         jax.ShapeDtypeStruct((own, LANES), f32))
            out_specs = (vmem, vmem)
        else:
            out_shape = (state_shape, state_shape, part_shape, part_shape)
            out_specs = (vmem, vmem, vmem, vmem)
        return pl.pallas_call(
            kernel,
            out_shape=out_shape,
            in_specs=[smem] * 6 + [vmem] * 10,
            out_specs=out_specs,
            scratch_shapes=[pltpu.VMEM((strip_rows, strip_width + 2 * LANES), f32)],
            cost_estimate=pl.CostEstimate(
                flops=flops, transcendentals=blocks * 2 * (strip_rows + WIN) * LANES,
                bytes_accessed=4 * strip_rows * strip_width * 2,
            ),
        )(*common, fluxes, partials, from_above, from_below)

    state, partials, up, down = phase(False, True, flux_start, flux_start, flux_start, flux_start)
    for iteration in range(1, ITERS):
        from_above, from_below = exchange(up, down)
        state, partials, up, down = phase(False, False, state, partials, from_above, from_below)
    from_above, from_below = exchange(up, down)
    residual, fluxes = phase(True, False, state, partials, from_above, from_below)
    return (fluxes, residual)


def solution(mesh):
    return jax.shard_map(
        local,
        mesh=mesh,
        in_specs=(
            P(("groups", "ty"), None),
            P(("groups", "ty")),
            P(("groups", "ty")),
            P(("groups", "ty")),
            P(("groups", "ty"), None),
            P(("groups", "ty"), None),
            P(("groups", "ty"), None),
            P(),
        ),
        out_specs=(P(("groups", "ty"), None), P(("groups", "ty"), None)),
        check_vma=False,
    )
```

time: 45.4 us -> 44.4 us (0.978)
  other arithmetic: 1.23 us -> 0 us
  local copies, waits for them, and re-layouts: 2.35 us -> 3.09 us
  waiting for transfers between devices: 11.6 us -> 10.9 us
    unnamed x20, local copies, waits for them, and re-layouts: 2.34 us -> 3.09 us
    ppermute x3, waiting for transfers between devices: 11.6 us -> 10.9 us  [exchange(): from_below = lax.ppermute(to_above, 'ty', backward)]
    concatenate x1 -> x0, other arithmetic: 0.65 us -> none  [local(): jnp.concatenate([got_above[0, 3 * LANES:3 * LANES + 16], got_below[HALO -...]
    convert_element_type x1 -> x0, other arithmetic: 0.58 us -> none  [local(): flags = jnp.stack([me > 0, me < last]).astype(jnp.int32)]
  transfers between devices with their start and end apart: 6 -> 6, of which waited for: 3 -> 3; matrix products, arithmetic and copies ran while one was open for 1% -> 0% of each run, Pallas kernels for 0% -> 0%
where the time goes in v6:
time: 44.4 us; the launch traced here: 43.9 us
  Pallas kernels  14.7 us (33%)
  starting transfers between devices  14.5 us (33%)
  waiting for transfers between devices  10.9 us (25%)
  local copies, waits for them, and re-layouts  3.09 us (7%)
  between operations  0.76 us (2%)
    pallas_call x3, Pallas kernels, phase(): pl.pallas_call(kernel, out_shape=out_shape, in_specs=[smem] * 6 + [vmem]...  12.9 us
    ppermute x3, waiting for transfers between devices, exchange(): from_below = lax.ppermute(to_above, 'ty', backward)  10.9 us
    ppermute x3, starting transfers between devices, exchange(): from_above = lax.ppermute(to_below, 'ty', forward)  7.87 us
    ppermute x3, starting transfers between devices, exchange(): from_below = lax.ppermute(to_above, 'ty', backward)  6.67 us
    unnamed x20, local copies, waits for them, and re-layouts  3.09 us
    pallas_call x1, Pallas kernels, local(): pl.pallas_call(setup_kernel, out_shape=(packet, packet, jax.ShapeDtypeStr...  1.83 us
  transfers between devices with their start and end apart: 6, of which 3 were waited for; matrix products, arithmetic and copies ran while one was open for 0% of the time, Pallas kernels for 0%

profile of v6, /device:TPU:11, one launch (start us, length us, event | category | flops | bytes accessed | tf_op | source)
XLA Modules:
  0.0 43.9 jit_solution(4545133808870476171)
XLA Ops:
  0.6 1.8 %shard_map.95 = (f32[8,128]{1,0:T(8,128)}, f32[8,128]{1,0:T(8,128)}, f32[2,128]{1,0:T(2,128)}) custom-call(s32[2]{0:T(128)} %band_ref.7, s32[2]{0:T(128)} %col_ref.7, s32[2]{0:T(128)} %cell_ref.7, f32[9,256]{1,0:T(8,128)} %psf_ref.7, f32[2,128]{1,0:T(2,128)} %oy_ref.7, f32[2,128]{1,0:T(2,128)} %ox_ref.7, f32[2,128]{1,0:T(2,128)} %rb_ref.1), custom_call_target="tpu_custom_call" | custom-call | tf_op jit(solution)/shard_map/pallas_call | solution.py:207
  2.5 3.7 %collective-permute-start = (f32[8,128]{1,0:T(8,128)}, f32[8,128]{1,0:T(8,128)S(1)}, u32[]{:S(2)}, u32[]{:S(2)}) collective-permute-start(f32[8,128]{1,0:T(8,128)} %get-tuple-element.15), channel_id=1, source_target_pairs={{0,1},{1,2},{2,3},{3,4},{4,5},{5,6},{6,7},{7,8},{8,9},{9,10},{10,1... | collective-permute-start | bytes 12296 | tf_op jit(solution)/shard_map/ppermute | solution.py:45
  6.2 1.9 %collective-permute-start.1 = (f32[8,128]{1,0:T(8,128)}, f32[8,128]{1,0:T(8,128)S(1)}, u32[]{:S(2)}, u32[]{:S(2)}) collective-permute-start(f32[8,128]{1,0:T(8,128)} %get-tuple-element.16), channel_id=1, source_target_pairs={{1,0},{2,1},{3,2},{4,3},{5,4},{6,5},{7,6},{8,7},{9,8},{10,9},{11,1... | collective-permute-start | bytes 12296 | tf_op jit(solution)/shard_map/ppermute | solution.py:46
  8.1 0.0 collective-permute-done.pas_ref.pa_ref
  8.1 0.0 copy-start
  8.1 4.1 %collective-permute-done.1.pbs_ref.pb_ref = f32[8,128]{1,0:T(8,128)S(1)} collective-permute-done((f32[8,128]{1,0:T(8,128)}, f32[8,128]{1,0:T(8,128)S(1)}, u32[]{:S(2)}, u32[]{:S(2)}) %collective-permute-start.1) | collective-permute-done | bytes 4128 | tf_op jit(solution)/shard_map/ppermute | solution.py:46
  12.2 0.0 copy-start.1
  12.2 0.0 copy-done
  12.2 0.6 %copy-done.1 = f32[8,128]{1,0:T(8,128)} copy-done((f32[8,128]{1,0:T(8,128)}, f32[8,128]{1,0:T(8,128)S(1)}, u32[]{:S(2)}) %copy-start.1) | copy-done | bytes 4120
  12.8 4.5 %shard_map.96 = (f32[8,128]{1,0:T(8,128)}, f32[8,128]{1,0:T(8,128)}, f32[2,128]{1,0:T(2,128)}, f32[2,128]{1,0:T(2,128)}) custom-call(s32[2]{0:T(128)} %band_ref.7, s32[2]{0:T(128)} %col_ref.7, s32[2]{0:T(128)} %cell_ref.7, f32[9,256]{1,0:T(8,128)} %psf_ref.7, f32[8,128]{1,0:T(8,128)} %copy-done, f32[8,128]{1,0:T(8,128)} %copy-done.1, f32[2,128]{1,0:T(2,128)} %oy_ref.7, ...), custom_call_target="tpu_custom_call" | custom-call | flops 452984832 | bytes 1048576 | tf_op jit(solution)/shard_map/pallas_call | solution.py:231
  17.3 0.0 copy-start.9
  17.3 0.6 %copy-done.9 = f32[2,128]{1,0:T(2,128)S(1)} copy-done((f32[2,128]{1,0:T(2,128)S(1)}, f32[2,128]{1,0:T(2,128)}, u32[]{:S(2)}) %copy-start.9) | copy-done | bytes 1048
  17.9 0.0 copy-start.8
  17.9 2.1 %collective-permute-start.2 = (f32[2,128]{1,0:T(2,128)S(1)}, f32[2,128]{1,0:T(2,128)S(1)}, u32[]{:S(2)}, u32[]{:S(2)}) collective-permute-start(f32[2,128]{1,0:T(2,128)S(1)} %copy-done.9), channel_id=1, source_target_pairs={{0,1},{1,2},{2,3},{3,4},{4,5},{5,6},{6,7},{7,8},{8,9},{9,10},{10,1... | collective-permute-start | bytes 3080 | tf_op jit(solution)/shard_map/ppermute | solution.py:45
  20.0 0.0 copy-done.8
  20.0 2.4 %collective-permute-start.3 = (f32[2,128]{1,0:T(2,128)S(1)}, f32[2,128]{1,0:T(2,128)S(1)}, u32[]{:S(2)}, u32[]{:S(2)}) collective-permute-start(f32[2,128]{1,0:T(2,128)S(1)} %copy-done.8), channel_id=1, source_target_pairs={{1,0},{2,1},{3,2},{4,3},{5,4},{6,5},{7,6},{8,7},{9,8},{10,9},{11,1... | collective-permute-start | bytes 3080 | tf_op jit(solution)/shard_map/ppermute | solution.py:46
  22.4 0.0 collective-permute-done.2.ra_ref
  22.4 0.0 copy-start.3
  22.4 3.4 %collective-permute-done.3.rb_ref = f32[2,128]{1,0:T(2,128)S(1)} collective-permute-done((f32[2,128]{1,0:T(2,128)S(1)}, f32[2,128]{1,0:T(2,128)S(1)}, u32[]{:S(2)}, u32[]{:S(2)}) %collective-permute-start.3) | collective-permute-done | bytes 1056 | tf_op jit(solution)/shard_map/ppermute | solution.py:46
  25.8 0.0 copy-done.3
  25.8 0.6 %copy-done.6 = f32[2,128]{1,0:T(2,128)} copy-done((f32[2,128]{1,0:T(2,128)}, f32[2,128]{1,0:T(2,128)S(1)}, u32[]{:S(2)}) %copy-start.6) | copy-done | bytes 1048
  26.4 4.5 %shard_map.97 = (f32[8,128]{1,0:T(8,128)}, f32[8,128]{1,0:T(8,128)}, f32[2,128]{1,0:T(2,128)}, f32[2,128]{1,0:T(2,128)}) custom-call(s32[2]{0:T(128)} %band_ref.7, s32[2]{0:T(128)} %col_ref.7, s32[2]{0:T(128)} %cell_ref.7, f32[9,256]{1,0:T(8,128)} %psf_ref.7, f32[8,128]{1,0:T(8,128)} %copy-done, f32[8,128]{1,0:T(8,128)} %copy-done.1, f32[2,128]{1,0:T(2,128)} %oy_ref.7, ...), custom_call_target="tpu_custom_call" | custom-call | flops 452984832 | bytes 1048576 | tf_op jit(solution)/shard_map/pallas_call | solution.py:231
  30.9 0.7 %copy-done.7 = f32[2,128]{1,0:T(2,128)S(1)} copy-done((f32[2,128]{1,0:T(2,128)S(1)}, f32[2,128]{1,0:T(2,128)}, u32[]{:S(2)}) %copy-start.7) | copy-done | bytes 1048
  31.5 2.1 %collective-permute-start.4 = (f32[2,128]{1,0:T(2,128)S(1)}, f32[2,128]{1,0:T(2,128)S(1)}, u32[]{:S(2)}, u32[]{:S(2)}) collective-permute-start(f32[2,128]{1,0:T(2,128)S(1)} %copy-done.7), channel_id=1, source_target_pairs={{0,1},{1,2},{2,3},{3,4},{4,5},{5,6},{6,7},{7,8},{8,9},{9,10},{10,1... | collective-permute-start | bytes 3080 | tf_op jit(solution)/shard_map/ppermute | solution.py:45
  33.6 0.0 copy-done.4
  33.6 2.4 %collective-permute-start.5 = (f32[2,128]{1,0:T(2,128)S(1)}, f32[2,128]{1,0:T(2,128)S(1)}, u32[]{:S(2)}, u32[]{:S(2)}) collective-permute-start(f32[2,128]{1,0:T(2,128)S(1)} %copy-done.4), channel_id=1, source_target_pairs={{1,0},{2,1},{3,2},{4,3},{5,4},{6,5},{7,6},{8,7},{9,8},{10,9},{11,1... | collective-permute-start | bytes 3080 | tf_op jit(solution)/shard_map/ppermute | solution.py:46
  36.0 0.0 collective-permute-done.4.ra_ref
  36.0 0.0 copy-start.2
  36.0 3.4 %collective-permute-done.5.rb_ref = f32[2,128]{1,0:T(2,128)S(1)} collective-permute-done((f32[2,128]{1,0:T(2,128)S(1)}, f32[2,128]{1,0:T(2,128)S(1)}, u32[]{:S(2)}, u32[]{:S(2)}) %collective-permute-start.5) | collective-permute-done | bytes 1056 | tf_op jit(solution)/shard_map/ppermute | solution.py:46
  39.4 0.0 copy-done.2
  39.4 0.6 %copy-done.5 = f32[2,128]{1,0:T(2,128)} copy-done((f32[2,128]{1,0:T(2,128)}, f32[2,128]{1,0:T(2,128)S(1)}, u32[]{:S(2)}) %copy-start.5) | copy-done | bytes 1048
  40.0 3.9 %shard_map.98 = (f32[64,2048]{1,0:T(8,128)}, f32[2,128]{1,0:T(2,128)}) custom-call(s32[2]{0:T(128)} %band_ref.7, s32[2]{0:T(128)} %col_ref.7, s32[2]{0:T(128)} %cell_ref.7, f32[9,256]{1,0:T(8,128)} %psf_ref.7, f32[8,128]{1,0:T(8,128)} %copy-done, f32[8,128]{1,0:T(8,128)} %copy-done.1, f32[2,128]{1,0:T(2,128)} %oy_ref.7, f32[2,128]{1,0:T(2,128)} %ox_ref.7, ...), custom_call_target="tpu_custom_call" | custom-call | flops 452984832 | bytes 1048576 | tf_op jit(solution)/shard_map/pallas_call | solution.py:231
  (4 shorter events, 0.0 us)
Async XLA Ops:
  2.5 5.7 %collective-permute-start = (f32[8,128]{1,0:T(8,128)}, f32[8,128]{1,0:T(8,128)S(1)}, u32[]{:S(2)}, u32[]{:S(2)}) collective-permute-start(f32[8,128]{1,0:T(8,128)} %get-tuple-element.15), channel_id=1, source_target_pairs={{0,1},{1,2},{2,3},{3,4},{4,5},{5,6},{6,7},{7,8},{8,9},{9,10},{10,1... | collective-permute-start | bytes 12296 | tf_op jit(solution)/shard_map/ppermute | solution.py:45
  6.2 6.0 %collective-permute-start.1 = (f32[8,128]{1,0:T(8,128)}, f32[8,128]{1,0:T(8,128)S(1)}, u32[]{:S(2)}, u32[]{:S(2)}) collective-permute-start(f32[8,128]{1,0:T(8,128)} %get-tuple-element.16), channel_id=1, source_target_pairs={{1,0},{2,1},{3,2},{4,3},{5,4},{6,5},{7,6},{8,7},{9,8},{10,9},{11,1... | collective-permute-start | bytes 12296 | tf_op jit(solution)/shard_map/ppermute | solution.py:46
  8.1 4.1 %copy-start = (f32[8,128]{1,0:T(8,128)}, f32[8,128]{1,0:T(8,128)S(1)}, u32[]{:S(2)}) copy-start(f32[8,128]{1,0:T(8,128)S(1)} %collective-permute-done.pas_ref.pa_ref) | copy-start | bytes 12292
  12.2 0.6 %copy-start.1 = (f32[8,128]{1,0:T(8,128)}, f32[8,128]{1,0:T(8,128)S(1)}, u32[]{:S(2)}) copy-start(f32[8,128]{1,0:T(8,128)S(1)} %collective-permute-done.1.pbs_ref.pb_ref) | copy-start | bytes 12292
  17.3 0.6 %copy-start.9 = (f32[2,128]{1,0:T(2,128)S(1)}, f32[2,128]{1,0:T(2,128)}, u32[]{:S(2)}) copy-start(f32[2,128]{1,0:T(2,128)} %get-tuple-element.20) | copy-start | bytes 3076
  17.9 2.1 %copy-start.8 = (f32[2,128]{1,0:T(2,128)S(1)}, f32[2,128]{1,0:T(2,128)}, u32[]{:S(2)}) copy-start(f32[2,128]{1,0:T(2,128)} %get-tuple-element.21) | copy-start | bytes 3076
  17.9 4.5 %collective-permute-start.2 = (f32[2,128]{1,0:T(2,128)S(1)}, f32[2,128]{1,0:T(2,128)S(1)}, u32[]{:S(2)}, u32[]{:S(2)}) collective-permute-start(f32[2,128]{1,0:T(2,128)S(1)} %copy-done.9), channel_id=1, source_target_pairs={{0,1},{1,2},{2,3},{3,4},{4,5},{5,6},{6,7},{7,8},{8,9},{9,10},{10,1... | collective-permute-start | bytes 3080 | tf_op jit(solution)/shard_map/ppermute | solution.py:45
  20.0 5.8 %collective-permute-start.3 = (f32[2,128]{1,0:T(2,128)S(1)}, f32[2,128]{1,0:T(2,128)S(1)}, u32[]{:S(2)}, u32[]{:S(2)}) collective-permute-start(f32[2,128]{1,0:T(2,128)S(1)} %copy-done.8), channel_id=1, source_target_pairs={{1,0},{2,1},{3,2},{4,3},{5,4},{6,5},{7,6},{8,7},{9,8},{10,9},{11,1... | collective-permute-start | bytes 3080 | tf_op jit(solution)/shard_map/ppermute | solution.py:46
  22.4 3.4 %copy-start.3 = (f32[2,128]{1,0:T(2,128)}, f32[2,128]{1,0:T(2,128)S(1)}, u32[]{:S(2)}) copy-start(f32[2,128]{1,0:T(2,128)S(1)} %collective-permute-done.2.ra_ref) | copy-start | bytes 3076
  25.8 0.6 %copy-start.6 = (f32[2,128]{1,0:T(2,128)}, f32[2,128]{1,0:T(2,128)S(1)}, u32[]{:S(2)}) copy-start(f32[2,128]{1,0:T(2,128)S(1)} %collective-permute-done.3.rb_ref) | copy-start | bytes 3076
  30.9 0.7 %copy-start.7 = (f32[2,128]{1,0:T(2,128)S(1)}, f32[2,128]{1,0:T(2,128)}, u32[]{:S(2)}) copy-start(f32[2,128]{1,0:T(2,128)} %get-tuple-element.24) | copy-start | bytes 3076
  31.5 2.1 %copy-start.4 = (f32[2,128]{1,0:T(2,128)S(1)}, f32[2,128]{1,0:T(2,128)}, u32[]{:S(2)}) copy-start(f32[2,128]{1,0:T(2,128)} %get-tuple-element.25) | copy-start | bytes 3076
  31.5 4.5 %collective-permute-start.4 = (f32[2,128]{1,0:T(2,128)S(1)}, f32[2,128]{1,0:T(2,128)S(1)}, u32[]{:S(2)}, u32[]{:S(2)}) collective-permute-start(f32[2,128]{1,0:T(2,128)S(1)} %copy-done.7), channel_id=1, source_target_pairs={{0,1},{1,2},{2,3},{3,4},{4,5},{5,6},{6,7},{7,8},{8,9},{9,10},{10,1... | collective-permute-start | bytes 3080 | tf_op jit(solution)/shard_map/ppermute | solution.py:45
  33.6 5.8 %collective-permute-start.5 = (f32[2,128]{1,0:T(2,128)S(1)}, f32[2,128]{1,0:T(2,128)S(1)}, u32[]{:S(2)}, u32[]{:S(2)}) collective-permute-start(f32[2,128]{1,0:T(2,128)S(1)} %copy-done.4), channel_id=1, source_target_pairs={{1,0},{2,1},{3,2},{4,3},{5,4},{6,5},{7,6},{8,7},{9,8},{10,9},{11,1... | collective-permute-start | bytes 3080 | tf_op jit(solution)/shard_map/ppermute | solution.py:46
  36.0 3.4 %copy-start.2 = (f32[2,128]{1,0:T(2,128)}, f32[2,128]{1,0:T(2,128)S(1)}, u32[]{:S(2)}) copy-start(f32[2,128]{1,0:T(2,128)S(1)} %collective-permute-done.4.ra_ref) | copy-start | bytes 3076
  39.4 0.6 %copy-start.5 = (f32[2,128]{1,0:T(2,128)}, f32[2,128]{1,0:T(2,128)S(1)}, u32[]{:S(2)}) copy-start(f32[2,128]{1,0:T(2,128)S(1)} %collective-permute-done.5.rb_ref) | copy-start | bytes 3076

commit v7 on v6

--- a/solution.py
+++ b/solution.py
@@ -197,6 +197,10 @@
     down_ref[1:2, :] = bot_part
 
 
+def vmem_operands(*arrays):
+    return [pltpu.with_memory_space_constraint(a, pltpu.VMEM) for a in arrays]
+
+
 def local(image, band_row, col_block, cell_index, offset_y, offset_x, flux_start, psf_coef):
     strip_rows, strip_width = image.shape
     own = band_row.shape[0]
@@ -215,7 +219,7 @@
     blocks = own + 2
     flops = 2 * 3 * 2 * strip_rows * WIN * 3 * LANES * blocks
     state_shape = jax.ShapeDtypeStruct((SLOTS, LANES), f32)
-    part_shape = jax.ShapeDtypeStruct((2, LANES), f32)
+    part_shape = pltpu.VMEM((2, LANES), f32)
     common = (band_row, col_block, cell_index, psf_coef, got_above, got_below,
               offset_y, offset_x, weight, got_above, got_below, image)
 
@@ -238,7 +242,7 @@
                 flops=flops, transcendentals=blocks * 2 * (strip_rows + WIN) * LANES,
                 bytes_accessed=4 * strip_rows * strip_width * 2,
             ),
-        )(*common, fluxes, partials, from_above, from_below)
+        )(*common, fluxes, partials, *vmem_operands(from_above, from_below))
 
     state, partials, up, down = phase(False, True, flux_start, flux_start, flux_start, flux_start)
     for iteration in range(1, ITERS):

time: 44.4 us -> 41.6 us (0.937)
  local copies, waits for them, and re-layouts: 3.09 us -> 0.59 us
    unnamed x20 -> x6, local copies, waits for them, and re-layouts: 3.09 us -> 0.59 us
where the time goes in v7:
time: 41.6 us; the launch traced here: 41.2 us
  Pallas kernels  14.7 us (35%)
  starting transfers between devices  14.3 us (34%)
  waiting for transfers between devices  10.9 us (26%)
  between operations  0.72 us (2%)
  local copies, waits for them, and re-layouts  0.59 us (1%)
    pallas_call x3, Pallas kernels, phase(): pl.pallas_call(kernel, out_shape=out_shape, in_specs=[smem] * 6 + [vmem]...  12.9 us
    ppermute x3, waiting for transfers between devices, exchange(): from_below = lax.ppermute(to_above, 'ty', backward)  10.9 us
    ppermute x3, starting transfers between devices, exchange(): from_above = lax.ppermute(to_below, 'ty', forward)  7.62 us
    ppermute x3, starting transfers between devices, exchange(): from_below = lax.ppermute(to_above, 'ty', backward)  6.65 us
    pallas_call x1, Pallas kernels, local(): pl.pallas_call(setup_kernel, out_shape=(packet, packet, jax.ShapeDtypeStr...  1.83 us
  transfers between devices with their start and end apart: 6, of which 3 were waited for; matrix products, arithmetic and copies ran while one was open for 0% of the time, Pallas kernels for 0%

profile of v7, /device:TPU:11, one launch (start us, length us, event | category | flops | bytes accessed | tf_op | source)
XLA Modules:
  0.0 41.2 jit_solution(5680108119730021624)
XLA Ops:
  0.6 1.8 %shard_map.95 = (f32[8,128]{1,0:T(8,128)}, f32[8,128]{1,0:T(8,128)}, f32[2,128]{1,0:T(2,128)}) custom-call(s32[2]{0:T(128)} %band_ref.7, s32[2]{0:T(128)} %col_ref.7, s32[2]{0:T(128)} %cell_ref.7, f32[9,256]{1,0:T(8,128)} %psf_ref.7, f32[2,128]{1,0:T(2,128)} %oy_ref.7, f32[2,128]{1,0:T(2,128)} %ox_ref.7, f32[2,128]{1,0:T(2,128)} %rb_ref.1), custom_call_target="tpu_custom_call" | custom-call | tf_op jit(solution)/shard_map/pallas_call | solution.py:211
  2.5 3.7 %collective-permute-start = (f32[8,128]{1,0:T(8,128)}, f32[8,128]{1,0:T(8,128)S(1)}, u32[]{:S(2)}, u32[]{:S(2)}) collective-permute-start(f32[8,128]{1,0:T(8,128)} %get-tuple-element.15), channel_id=1, source_target_pairs={{0,1},{1,2},{2,3},{3,4},{4,5},{5,6},{6,7},{7,8},{8,9},{9,10},{10,1... | collective-permute-start | bytes 12296 | tf_op jit(solution)/shard_map/ppermute | solution.py:45
  6.2 0.0 copy-start
  6.2 1.9 %collective-permute-start.1 = (f32[8,128]{1,0:T(8,128)}, f32[8,128]{1,0:T(8,128)S(1)}, u32[]{:S(2)}, u32[]{:S(2)}) collective-permute-start(f32[8,128]{1,0:T(8,128)} %get-tuple-element.16), channel_id=1, source_target_pairs={{1,0},{2,1},{3,2},{4,3},{5,4},{6,5},{7,6},{8,7},{9,8},{10,9},{11,1... | collective-permute-start | bytes 12296 | tf_op jit(solution)/shard_map/ppermute | solution.py:46
  8.1 0.0 collective-permute-done.pas_ref.pa_ref
  8.1 0.0 copy-start.1
  8.2 4.1 %collective-permute-done.1.pbs_ref.pb_ref = f32[8,128]{1,0:T(8,128)S(1)} collective-permute-done((f32[8,128]{1,0:T(8,128)}, f32[8,128]{1,0:T(8,128)S(1)}, u32[]{:S(2)}, u32[]{:S(2)}) %collective-permute-start.1) | collective-permute-done | bytes 4128 | tf_op jit(solution)/shard_map/ppermute | solution.py:46
  12.2 0.0 copy-start.2
  12.2 0.0 copy-done.1
  12.2 0.6 %copy-done.2 = f32[8,128]{1,0:T(8,128)} copy-done((f32[8,128]{1,0:T(8,128)}, f32[8,128]{1,0:T(8,128)S(1)}, u32[]{:S(2)}) %copy-start.2) | copy-done | bytes 4120
  12.8 0.0 copy-done
  12.8 4.5 %shard_map.96 = (f32[8,128]{1,0:T(8,128)}, f32[8,128]{1,0:T(8,128)}, f32[2,128]{1,0:T(2,128)S(1)}, f32[2,128]{1,0:T(2,128)S(1)}) custom-call(s32[2]{0:T(128)} %band_ref.7, s32[2]{0:T(128)} %col_ref.7, s32[2]{0:T(128)} %cell_ref.7, f32[9,256]{1,0:T(8,128)} %psf_ref.7, f32[8,128]{1,0:T(8,128)} %copy-done.1, f32[8,128]{1,0:T(8,128)} %copy-done.2, ...), custom_call_target="tpu_custom_call" | custom-call | flops 452984832 | bytes 1048576 | tf_op jit(solution)/shard_map/pallas_call | solution.py:235
  17.3 1.9 %collective-permute-start.2 = (f32[2,128]{1,0:T(2,128)S(1)}, f32[2,128]{1,0:T(2,128)S(1)}, u32[]{:S(2)}, u32[]{:S(2)}) collective-permute-start(f32[2,128]{1,0:T(2,128)S(1)} %get-tuple-element.20), channel_id=1, source_target_pairs={{0,1},{1,2},{2,3},{3,4},{4,5},{5,6},{6,7},{7,8},{8,9},{9,10},{10,1... | collective-permute-start | bytes 3080 | tf_op jit(solution)/shard_map/ppermute | solution.py:45
  19.3 2.4 %collective-permute-start.3 = (f32[2,128]{1,0:T(2,128)S(1)}, f32[2,128]{1,0:T(2,128)S(1)}, u32[]{:S(2)}, u32[]{:S(2)}) collective-permute-start(f32[2,128]{1,0:T(2,128)S(1)} %get-tuple-element.21), channel_id=1, source_target_pairs={{1,0},{2,1},{3,2},{4,3},{5,4},{6,5},{7,6},{8,7},{9,8},{10,9},{11,1... | collective-permute-start | bytes 3080 | tf_op jit(solution)/shard_map/ppermute | solution.py:46
  21.6 0.0 collective-permute-done.2.ra_ref
  21.7 3.4 %collective-permute-done.3.rb_ref = f32[2,128]{1,0:T(2,128)S(1)} collective-permute-done((f32[2,128]{1,0:T(2,128)S(1)}, f32[2,128]{1,0:T(2,128)S(1)}, u32[]{:S(2)}, u32[]{:S(2)}) %collective-permute-start.3) | collective-permute-done | bytes 1056 | tf_op jit(solution)/shard_map/ppermute | solution.py:46
  25.0 4.5 %shard_map.97 = (f32[8,128]{1,0:T(8,128)}, f32[8,128]{1,0:T(8,128)}, f32[2,128]{1,0:T(2,128)S(1)}, f32[2,128]{1,0:T(2,128)S(1)}) custom-call(s32[2]{0:T(128)} %band_ref.7, s32[2]{0:T(128)} %col_ref.7, s32[2]{0:T(128)} %cell_ref.7, f32[9,256]{1,0:T(8,128)} %psf_ref.7, f32[8,128]{1,0:T(8,128)} %copy-done.1, f32[8,128]{1,0:T(8,128)} %copy-done.2, ...), custom_call_target="tpu_custom_call" | custom-call | flops 452984832 | bytes 1048576 | tf_op jit(solution)/shard_map/pallas_call | solution.py:235
  29.5 2.0 %collective-permute-start.4 = (f32[2,128]{1,0:T(2,128)S(1)}, f32[2,128]{1,0:T(2,128)S(1)}, u32[]{:S(2)}, u32[]{:S(2)}) collective-permute-start(f32[2,128]{1,0:T(2,128)S(1)} %get-tuple-element.24), channel_id=1, source_target_pairs={{0,1},{1,2},{2,3},{3,4},{4,5},{5,6},{6,7},{7,8},{8,9},{9,10},{10,1... | collective-permute-start | bytes 3080 | tf_op jit(solution)/shard_map/ppermute | solution.py:45
  31.5 2.4 %collective-permute-start.5 = (f32[2,128]{1,0:T(2,128)S(1)}, f32[2,128]{1,0:T(2,128)S(1)}, u32[]{:S(2)}, u32[]{:S(2)}) collective-permute-start(f32[2,128]{1,0:T(2,128)S(1)} %get-tuple-element.25), channel_id=1, source_target_pairs={{1,0},{2,1},{3,2},{4,3},{5,4},{6,5},{7,6},{8,7},{9,8},{10,9},{11,1... | collective-permute-start | bytes 3080 | tf_op jit(solution)/shard_map/ppermute | solution.py:46
  33.9 0.0 collective-permute-done.4.ra_ref
  33.9 3.4 %collective-permute-done.5.rb_ref = f32[2,128]{1,0:T(2,128)S(1)} collective-permute-done((f32[2,128]{1,0:T(2,128)S(1)}, f32[2,128]{1,0:T(2,128)S(1)}, u32[]{:S(2)}, u32[]{:S(2)}) %collective-permute-start.5) | collective-permute-done | bytes 1056 | tf_op jit(solution)/shard_map/ppermute | solution.py:46
  37.3 3.9 %shard_map.98 = (f32[64,2048]{1,0:T(8,128)}, f32[2,128]{1,0:T(2,128)}) custom-call(s32[2]{0:T(128)} %band_ref.7, s32[2]{0:T(128)} %col_ref.7, s32[2]{0:T(128)} %cell_ref.7, f32[9,256]{1,0:T(8,128)} %psf_ref.7, f32[8,128]{1,0:T(8,128)} %copy-done.1, f32[8,128]{1,0:T(8,128)} %copy-done.2, f32[2,128]{1,0:T(2,128)} %oy_ref.7, f32[2,128]{1,0:T(2,128)} %ox_ref.7, ...), custom_call_target="tpu_custom_call" | custom-call | flops 452984832 | bytes 1048576 | tf_op jit(solution)/shard_map/pallas_call | solution.py:235
Async XLA Ops:
  2.5 5.7 %collective-permute-start = (f32[8,128]{1,0:T(8,128)}, f32[8,128]{1,0:T(8,128)S(1)}, u32[]{:S(2)}, u32[]{:S(2)}) collective-permute-start(f32[8,128]{1,0:T(8,128)} %get-tuple-element.15), channel_id=1, source_target_pairs={{0,1},{1,2},{2,3},{3,4},{4,5},{5,6},{6,7},{7,8},{8,9},{9,10},{10,1... | collective-permute-start | bytes 12296 | tf_op jit(solution)/shard_map/ppermute | solution.py:45
  6.2 6.6 %copy-start = (f32[2,128]{1,0:T(2,128)S(1)}, f32[2,128]{1,0:T(2,128)}, u32[]{:S(2)}) copy-start(f32[2,128]{1,0:T(2,128)} %rb_ref.1) | copy-start | bytes 3076
  6.2 6.0 %collective-permute-start.1 = (f32[8,128]{1,0:T(8,128)}, f32[8,128]{1,0:T(8,128)S(1)}, u32[]{:S(2)}, u32[]{:S(2)}) collective-permute-start(f32[8,128]{1,0:T(8,128)} %get-tuple-element.16), channel_id=1, source_target_pairs={{1,0},{2,1},{3,2},{4,3},{5,4},{6,5},{7,6},{8,7},{9,8},{10,9},{11,1... | collective-permute-start | bytes 12296 | tf_op jit(solution)/shard_map/ppermute | solution.py:46
  8.1 4.1 %copy-start.1 = (f32[8,128]{1,0:T(8,128)}, f32[8,128]{1,0:T(8,128)S(1)}, u32[]{:S(2)}) copy-start(f32[8,128]{1,0:T(8,128)S(1)} %collective-permute-done.pas_ref.pa_ref) | copy-start | bytes 12292
  12.2 0.6 %copy-start.2 = (f32[8,128]{1,0:T(8,128)}, f32[8,128]{1,0:T(8,128)S(1)}, u32[]{:S(2)}) copy-start(f32[8,128]{1,0:T(8,128)S(1)} %collective-permute-done.1.pbs_ref.pb_ref) | copy-start | bytes 12292
  17.3 4.3 %collective-permute-start.2 = (f32[2,128]{1,0:T(2,128)S(1)}, f32[2,128]{1,0:T(2,128)S(1)}, u32[]{:S(2)}, u32[]{:S(2)}) collective-permute-start(f32[2,128]{1,0:T(2,128)S(1)} %get-tuple-element.20), channel_id=1, source_target_pairs={{0,1},{1,2},{2,3},{3,4},{4,5},{5,6},{6,7},{7,8},{8,9},{9,10},{10,1... | collective-permute-start | bytes 3080 | tf_op jit(solution)/shard_map/ppermute | solution.py:45
  19.3 5.8 %collective-permute-start.3 = (f32[2,128]{1,0:T(2,128)S(1)}, f32[2,128]{1,0:T(2,128)S(1)}, u32[]{:S(2)}, u32[]{:S(2)}) collective-permute-start(f32[2,128]{1,0:T(2,128)S(1)} %get-tuple-element.21), channel_id=1, source_target_pairs={{1,0},{2,1},{3,2},{4,3},{5,4},{6,5},{7,6},{8,7},{9,8},{10,9},{11,1... | collective-permute-start | bytes 3080 | tf_op jit(solution)/shard_map/ppermute | solution.py:46
  29.5 4.3 %collective-permute-start.4 = (f32[2,128]{1,0:T(2,128)S(1)}, f32[2,128]{1,0:T(2,128)S(1)}, u32[]{:S(2)}, u32[]{:S(2)}) collective-permute-start(f32[2,128]{1,0:T(2,128)S(1)} %get-tuple-element.24), channel_id=1, source_target_pairs={{0,1},{1,2},{2,3},{3,4},{4,5},{5,6},{6,7},{7,8},{8,9},{9,10},{10,1... | collective-permute-start | bytes 3080 | tf_op jit(solution)/shard_map/ppermute | solution.py:45
  31.5 5.8 %collective-permute-start.5 = (f32[2,128]{1,0:T(2,128)S(1)}, f32[2,128]{1,0:T(2,128)S(1)}, u32[]{:S(2)}, u32[]{:S(2)}) collective-permute-start(f32[2,128]{1,0:T(2,128)S(1)} %get-tuple-element.25), channel_id=1, source_target_pairs={{1,0},{2,1},{3,2},{4,3},{5,4},{6,5},{7,6},{8,7},{9,8},{10,9},{11,1... | collective-permute-start | bytes 3080 | tf_op jit(solution)/shard_map/ppermute | solution.py:46

commit v8 on v7

--- a/solution.py
+++ b/solution.py
@@ -11,6 +11,7 @@
 ITERS = 2
 LANES = 128
 WIN = 384
+SPAN = 256
 SLOTS = 8
 
 DIMS_NT = (((1,), (1,)), ((), ()))
@@ -149,7 +150,8 @@
 
     canvas[...] = jnp.zeros_like(canvas)
     hpos = lax.broadcasted_iota(jnp.int32, (rows_n, LANES), 0).astype(jnp.float32)
-    wpos = lax.broadcasted_iota(jnp.int32, (WIN, LANES), 0).astype(jnp.float32) - LANES
+    wpos = lax.broadcasted_iota(jnp.int32, (SPAN, LANES), 0).astype(jnp.float32) - LANES // 2
+    spare = jnp.zeros((rows_n, WIN - SPAN), jnp.float32)
     saved = []
     for j, (y, x, c, col, keep) in enumerate(specs):
         rows = profile3(hpos - y)
@@ -162,7 +164,9 @@
         ]
         stamp = split_dot(jnp.concatenate(rows, axis=1), jnp.concatenate(mixed, axis=1), DIMS_NT)
         start = pl.multiple_of(col * LANES, LANES)
-        canvas[:, pl.ds(start, WIN)] += stamp
+        canvas[:, pl.ds(start, WIN)] += pltpu.roll(
+            jnp.concatenate([stamp, spare], axis=1), LANES // 2, 1
+        )
         saved.append((rows, cols, c, start))
     inner = slice(LANES, LANES + width)
     if final:
@@ -177,7 +181,7 @@
     lout_ref[...] = jnp.zeros_like(lout_ref)
     partial = []
     for j, (rows, cols, c, start) in enumerate(saved):
-        window = canvas[:, pl.ds(start, WIN)]
+        window = pltpu.roll(canvas[:, pl.ds(start, WIN)], WIN - LANES // 2, 1)[:, :SPAN]
         across_all = split_dot(window, jnp.concatenate(cols, axis=1), DIMS_NN)
         grad = None
         for a in range(3):

time: 41.6 us -> 40.2 us (0.966)
  Pallas kernels: 14.7 us -> 13.3 us
    pallas_call x3, Pallas kernels: 12.9 us -> 11.5 us  [phase(): pl.pallas_call(kernel, out_shape=out_shape, in_specs=[smem] * 6 + [vmem]...]
where the time goes in v8:
time: 40.2 us; the launch traced here: 39.8 us
  starting transfers between devices  14.3 us (36%)
  Pallas kernels  13.3 us (33%)
  waiting for transfers between devices  10.9 us (27%)
  between operations  0.72 us (2%)
  local copies, waits for them, and re-layouts  0.59 us (1%)
    pallas_call x3, Pallas kernels, phase(): pl.pallas_call(kernel, out_shape=out_shape, in_specs=[smem] * 6 + [vmem]...  11.5 us
    ppermute x3, waiting for transfers between devices, exchange(): from_below = lax.ppermute(to_above, 'ty', backward)  10.9 us
    ppermute x3, starting transfers between devices, exchange(): from_above = lax.ppermute(to_below, 'ty', forward)  7.6 us
    ppermute x3, starting transfers between devices, exchange(): from_below = lax.ppermute(to_above, 'ty', backward)  6.68 us
    pallas_call x1, Pallas kernels, local(): pl.pallas_call(setup_kernel, out_shape=(packet, packet, jax.ShapeDtypeStr...  1.83 us
  transfers between devices with their start and end apart: 6, of which 3 were waited for; matrix products, arithmetic and copies ran while one was open for 0% of the time, Pallas kernels for 0%

profile of v8, /device:TPU:11, one launch (start us, length us, event | category | flops | bytes accessed | tf_op | source)
XLA Modules:
  0.0 39.8 jit_solution(3448651248857711574)
XLA Ops:
  0.6 1.8 %shard_map.95 = (f32[8,128]{1,0:T(8,128)}, f32[8,128]{1,0:T(8,128)}, f32[2,128]{1,0:T(2,128)}) custom-call(s32[2]{0:T(128)} %band_ref.7, s32[2]{0:T(128)} %col_ref.7, s32[2]{0:T(128)} %cell_ref.7, f32[9,256]{1,0:T(8,128)} %psf_ref.7, f32[2,128]{1,0:T(2,128)} %oy_ref.7, f32[2,128]{1,0:T(2,128)} %ox_ref.7, f32[2,128]{1,0:T(2,128)} %rb_ref.1), custom_call_target="tpu_custom_call" | custom-call | tf_op jit(solution)/shard_map/pallas_call | solution.py:215
  2.5 3.7 %collective-permute-start = (f32[8,128]{1,0:T(8,128)}, f32[8,128]{1,0:T(8,128)S(1)}, u32[]{:S(2)}, u32[]{:S(2)}) collective-permute-start(f32[8,128]{1,0:T(8,128)} %get-tuple-element.15), channel_id=1, source_target_pairs={{0,1},{1,2},{2,3},{3,4},{4,5},{5,6},{6,7},{7,8},{8,9},{9,10},{10,1... | collective-permute-start | bytes 12296 | tf_op jit(solution)/shard_map/ppermute | solution.py:46
  6.2 0.0 copy-start
  6.2 1.9 %collective-permute-start.1 = (f32[8,128]{1,0:T(8,128)}, f32[8,128]{1,0:T(8,128)S(1)}, u32[]{:S(2)}, u32[]{:S(2)}) collective-permute-start(f32[8,128]{1,0:T(8,128)} %get-tuple-element.16), channel_id=1, source_target_pairs={{1,0},{2,1},{3,2},{4,3},{5,4},{6,5},{7,6},{8,7},{9,8},{10,9},{11,1... | collective-permute-start | bytes 12296 | tf_op jit(solution)/shard_map/ppermute | solution.py:47
  8.1 0.0 collective-permute-done.pas_ref.pa_ref
  8.1 0.0 copy-start.1
  8.2 4.1 %collective-permute-done.1.pbs_ref.pb_ref = f32[8,128]{1,0:T(8,128)S(1)} collective-permute-done((f32[8,128]{1,0:T(8,128)}, f32[8,128]{1,0:T(8,128)S(1)}, u32[]{:S(2)}, u32[]{:S(2)}) %collective-permute-start.1) | collective-permute-done | bytes 4128 | tf_op jit(solution)/shard_map/ppermute | solution.py:47
  12.2 0.0 copy-start.2
  12.2 0.0 copy-done.1
  12.2 0.6 %copy-done.2 = f32[8,128]{1,0:T(8,128)} copy-done((f32[8,128]{1,0:T(8,128)}, f32[8,128]{1,0:T(8,128)S(1)}, u32[]{:S(2)}) %copy-start.2) | copy-done | bytes 4120
  12.8 0.0 copy-done
  12.8 4.0 %shard_map.96 = (f32[8,128]{1,0:T(8,128)}, f32[8,128]{1,0:T(8,128)}, f32[2,128]{1,0:T(2,128)S(1)}, f32[2,128]{1,0:T(2,128)S(1)}) custom-call(s32[2]{0:T(128)} %band_ref.7, s32[2]{0:T(128)} %col_ref.7, s32[2]{0:T(128)} %cell_ref.7, f32[9,256]{1,0:T(8,128)} %psf_ref.7, f32[8,128]{1,0:T(8,128)} %copy-done.1, f32[8,128]{1,0:T(8,128)} %copy-done.2, ...), custom_call_target="tpu_custom_call" | custom-call | flops 452984832 | bytes 1048576 | tf_op jit(solution)/shard_map/pallas_call | solution.py:239
  16.8 1.9 %collective-permute-start.2 = (f32[2,128]{1,0:T(2,128)S(1)}, f32[2,128]{1,0:T(2,128)S(1)}, u32[]{:S(2)}, u32[]{:S(2)}) collective-permute-start(f32[2,128]{1,0:T(2,128)S(1)} %get-tuple-element.20), channel_id=1, source_target_pairs={{0,1},{1,2},{2,3},{3,4},{4,5},{5,6},{6,7},{7,8},{8,9},{9,10},{10,1... | collective-permute-start | bytes 3080 | tf_op jit(solution)/shard_map/ppermute | solution.py:46
  18.7 2.4 %collective-permute-start.3 = (f32[2,128]{1,0:T(2,128)S(1)}, f32[2,128]{1,0:T(2,128)S(1)}, u32[]{:S(2)}, u32[]{:S(2)}) collective-permute-start(f32[2,128]{1,0:T(2,128)S(1)} %get-tuple-element.21), channel_id=1, source_target_pairs={{1,0},{2,1},{3,2},{4,3},{5,4},{6,5},{7,6},{8,7},{9,8},{10,9},{11,1... | collective-permute-start | bytes 3080 | tf_op jit(solution)/shard_map/ppermute | solution.py:47
  21.1 0.0 collective-permute-done.2.ra_ref
  21.1 3.4 %collective-permute-done.3.rb_ref = f32[2,128]{1,0:T(2,128)S(1)} collective-permute-done((f32[2,128]{1,0:T(2,128)S(1)}, f32[2,128]{1,0:T(2,128)S(1)}, u32[]{:S(2)}, u32[]{:S(2)}) %collective-permute-start.3) | collective-permute-done | bytes 1056 | tf_op jit(solution)/shard_map/ppermute | solution.py:47
  24.5 4.0 %shard_map.97 = (f32[8,128]{1,0:T(8,128)}, f32[8,128]{1,0:T(8,128)}, f32[2,128]{1,0:T(2,128)S(1)}, f32[2,128]{1,0:T(2,128)S(1)}) custom-call(s32[2]{0:T(128)} %band_ref.7, s32[2]{0:T(128)} %col_ref.7, s32[2]{0:T(128)} %cell_ref.7, f32[9,256]{1,0:T(8,128)} %psf_ref.7, f32[8,128]{1,0:T(8,128)} %copy-done.1, f32[8,128]{1,0:T(8,128)} %copy-done.2, ...), custom_call_target="tpu_custom_call" | custom-call | flops 452984832 | bytes 1048576 | tf_op jit(solution)/shard_map/pallas_call | solution.py:239
  28.5 1.9 %collective-permute-start.4 = (f32[2,128]{1,0:T(2,128)S(1)}, f32[2,128]{1,0:T(2,128)S(1)}, u32[]{:S(2)}, u32[]{:S(2)}) collective-permute-start(f32[2,128]{1,0:T(2,128)S(1)} %get-tuple-element.24), channel_id=1, source_target_pairs={{0,1},{1,2},{2,3},{3,4},{4,5},{5,6},{6,7},{7,8},{8,9},{9,10},{10,1... | collective-permute-start | bytes 3080 | tf_op jit(solution)/shard_map/ppermute | solution.py:46
  30.4 2.4 %collective-permute-start.5 = (f32[2,128]{1,0:T(2,128)S(1)}, f32[2,128]{1,0:T(2,128)S(1)}, u32[]{:S(2)}, u32[]{:S(2)}) collective-permute-start(f32[2,128]{1,0:T(2,128)S(1)} %get-tuple-element.25), channel_id=1, source_target_pairs={{1,0},{2,1},{3,2},{4,3},{5,4},{6,5},{7,6},{8,7},{9,8},{10,9},{11,1... | collective-permute-start | bytes 3080 | tf_op jit(solution)/shard_map/ppermute | solution.py:47
  32.8 0.0 collective-permute-done.4.ra_ref
  32.8 3.4 %collective-permute-done.5.rb_ref = f32[2,128]{1,0:T(2,128)S(1)} collective-permute-done((f32[2,128]{1,0:T(2,128)S(1)}, f32[2,128]{1,0:T(2,128)S(1)}, u32[]{:S(2)}, u32[]{:S(2)}) %collective-permute-start.5) | collective-permute-done | bytes 1056 | tf_op jit(solution)/shard_map/ppermute | solution.py:47
  36.2 3.6 %shard_map.98 = (f32[64,2048]{1,0:T(8,128)}, f32[2,128]{1,0:T(2,128)}) custom-call(s32[2]{0:T(128)} %band_ref.7, s32[2]{0:T(128)} %col_ref.7, s32[2]{0:T(128)} %cell_ref.7, f32[9,256]{1,0:T(8,128)} %psf_ref.7, f32[8,128]{1,0:T(8,128)} %copy-done.1, f32[8,128]{1,0:T(8,128)} %copy-done.2, f32[2,128]{1,0:T(2,128)} %oy_ref.7, f32[2,128]{1,0:T(2,128)} %ox_ref.7, ...), custom_call_target="tpu_custom_call" | custom-call | flops 452984832 | bytes 1048576 | tf_op jit(solution)/shard_map/pallas_call | solution.py:239
Async XLA Ops:
  2.5 5.7 %collective-permute-start = (f32[8,128]{1,0:T(8,128)}, f32[8,128]{1,0:T(8,128)S(1)}, u32[]{:S(2)}, u32[]{:S(2)}) collective-permute-start(f32[8,128]{1,0:T(8,128)} %get-tuple-element.15), channel_id=1, source_target_pairs={{0,1},{1,2},{2,3},{3,4},{4,5},{5,6},{6,7},{7,8},{8,9},{9,10},{10,1... | collective-permute-start | bytes 12296 | tf_op jit(solution)/shard_map/ppermute | solution.py:46
  6.2 6.6 %copy-start = (f32[2,128]{1,0:T(2,128)S(1)}, f32[2,128]{1,0:T(2,128)}, u32[]{:S(2)}) copy-start(f32[2,128]{1,0:T(2,128)} %rb_ref.1) | copy-start | bytes 3076
  6.2 6.0 %collective-permute-start.1 = (f32[8,128]{1,0:T(8,128)}, f32[8,128]{1,0:T(8,128)S(1)}, u32[]{:S(2)}, u32[]{:S(2)}) collective-permute-start(f32[8,128]{1,0:T(8,128)} %get-tuple-element.16), channel_id=1, source_target_pairs={{1,0},{2,1},{3,2},{4,3},{5,4},{6,5},{7,6},{8,7},{9,8},{10,9},{11,1... | collective-permute-start | bytes 12296 | tf_op jit(solution)/shard_map/ppermute | solution.py:47
  8.1 4.1 %copy-start.1 = (f32[8,128]{1,0:T(8,128)}, f32[8,128]{1,0:T(8,128)S(1)}, u32[]{:S(2)}) copy-start(f32[8,128]{1,0:T(8,128)S(1)} %collective-permute-done.pas_ref.pa_ref) | copy-start | bytes 12292
  12.2 0.6 %copy-start.2 = (f32[8,128]{1,0:T(8,128)}, f32[8,128]{1,0:T(8,128)S(1)}, u32[]{:S(2)}) copy-start(f32[8,128]{1,0:T(8,128)S(1)} %collective-permute-done.1.pbs_ref.pb_ref) | copy-start | bytes 12292
  16.8 4.3 %collective-permute-start.2 = (f32[2,128]{1,0:T(2,128)S(1)}, f32[2,128]{1,0:T(2,128)S(1)}, u32[]{:S(2)}, u32[]{:S(2)}) collective-permute-start(f32[2,128]{1,0:T(2,128)S(1)} %get-tuple-element.20), channel_id=1, source_target_pairs={{0,1},{1,2},{2,3},{3,4},{4,5},{5,6},{6,7},{7,8},{8,9},{9,10},{10,1... | collective-permute-start | bytes 3080 | tf_op jit(solution)/shard_map/ppermute | solution.py:46
  18.7 5.8 %collective-permute-start.3 = (f32[2,128]{1,0:T(2,128)S(1)}, f32[2,128]{1,0:T(2,128)S(1)}, u32[]{:S(2)}, u32[]{:S(2)}) collective-permute-start(f32[2,128]{1,0:T(2,128)S(1)} %get-tuple-element.21), channel_id=1, source_target_pairs={{1,0},{2,1},{3,2},{4,3},{5,4},{6,5},{7,6},{8,7},{9,8},{10,9},{11,1... | collective-permute-start | bytes 3080 | tf_op jit(solution)/shard_map/ppermute | solution.py:47
  28.5 4.3 %collective-permute-start.4 = (f32[2,128]{1,0:T(2,128)S(1)}, f32[2,128]{1,0:T(2,128)S(1)}, u32[]{:S(2)}, u32[]{:S(2)}) collective-permute-start(f32[2,128]{1,0:T(2,128)S(1)} %get-tuple-element.24), channel_id=1, source_target_pairs={{0,1},{1,2},{2,3},{3,4},{4,5},{5,6},{6,7},{7,8},{8,9},{9,10},{10,1... | collective-permute-start | bytes 3080 | tf_op jit(solution)/shard_map/ppermute | solution.py:46
  30.4 5.8 %collective-permute-start.5 = (f32[2,128]{1,0:T(2,128)S(1)}, f32[2,128]{1,0:T(2,128)S(1)}, u32[]{:S(2)}, u32[]{:S(2)}) collective-permute-start(f32[2,128]{1,0:T(2,128)S(1)} %get-tuple-element.25), channel_id=1, source_target_pairs={{1,0},{2,1},{3,2},{4,3},{5,4},{6,5},{7,6},{8,7},{9,8},{10,9},{11,1... | collective-permute-start | bytes 3080 | tf_op jit(solution)/shard_map/ppermute | solution.py:47

commit v9 on v8

--- a/solution.py
+++ b/solution.py
@@ -32,6 +32,20 @@
     lhs_lo = (lhs - lhs_hi.astype(jnp.float32)).astype(jnp.bfloat16)
     rhs_hi = rhs.astype(jnp.bfloat16)
     rhs_lo = (rhs - rhs_hi.astype(jnp.float32)).astype(jnp.bfloat16)
+
+    def one(a, b):
+        return lax.dot_general(a, b, dims, preferred_element_type=jnp.float32)
+
+    return one(lhs_hi, rhs_hi) + (one(lhs_hi, rhs_lo) + one(lhs_lo, rhs_hi))
+
+
+def split_bf16(value):
+    hi = value.astype(jnp.bfloat16)
+    return hi, (value - hi.astype(jnp.float32)).astype(jnp.bfloat16)
+
+
+def presplit_dot(lhs, rhs_hi, rhs_lo, dims):
+    lhs_hi, lhs_lo = split_bf16(lhs)
 
     def one(a, b):
         return lax.dot_general(a, b, dims, preferred_element_type=jnp.float32)
@@ -108,10 +122,16 @@
     oy_ref, ox_ref, w_ref, pa_ref, pb_ref, img_ref, f_ref, l_ref, ra_ref, rb_ref,
     *rest,
 ):
+    rest = list(rest)
+    if not first:
+        pre_refs, rest = rest[:5], rest[5:]
     if final:
-        out_ref, fluxout_ref, canvas = rest
+        (out_ref, fluxout_ref), rest = rest[:2], rest[2:]
     else:
-        fout_ref, lout_ref, up_ref, down_ref, canvas = rest
+        (fout_ref, lout_ref, up_ref, down_ref), rest = rest[:4], rest[4:]
+    if first:
+        pre_refs, rest = rest[:5], rest[5:]
+    (canvas,) = rest
     rows_n, pad_width = canvas.shape
     strip_rows, width = img_ref.shape
     own = oy_ref.shape[0]
@@ -154,20 +174,30 @@
     spare = jnp.zeros((rows_n, WIN - SPAN), jnp.float32)
     saved = []
     for j, (y, x, c, col, keep) in enumerate(specs):
-        rows = profile3(hpos - y)
-        if keep is not None:
-            rows = tuple(jnp.where(hpos < keep, r, 0.0) for r in rows)
-        cols = profile3(wpos - x)
-        mixed = [
-            (c[3 * a] * cols[0] + c[3 * a + 1] * cols[1] + c[3 * a + 2] * cols[2]) * fluxes[j]
-            for a in range(3)
-        ]
-        stamp = split_dot(jnp.concatenate(rows, axis=1), jnp.concatenate(mixed, axis=1), DIMS_NT)
+        if first:
+            rows = profile3(hpos - y)
+            if keep is not None:
+                rows = tuple(jnp.where(hpos < keep, r, 0.0) for r in rows)
+            cols = profile3(wpos - x)
+            mixed = [c[3 * a] * cols[0] + c[3 * a + 1] * cols[1] + c[3 * a + 2] * cols[2]
+                     for a in range(3)]
+            rows_all = jnp.concatenate(rows, axis=1)
+            mixed_hi, mixed_lo = split_bf16(jnp.concatenate(mixed, axis=1))
+            cols_hi, cols_lo = split_bf16(jnp.concatenate(cols, axis=1))
+            for ref, value in zip(pre_refs, (rows_all, mixed_hi, mixed_lo, cols_hi, cols_lo)):
+                ref[j] = value
+        else:
+            rows_all = pre_refs[0][j]
+            mixed_hi, mixed_lo = pre_refs[1][j], pre_refs[2][j]
+            cols_hi, cols_lo = pre_refs[3][j], pre_refs[4][j]
+        flux = fluxes[j]
+        scaled = rows_all * jnp.concatenate([flux, flux, flux], axis=1)
+        stamp = presplit_dot(scaled, mixed_hi, mixed_lo, DIMS_NT)
         start = pl.multiple_of(col * LANES, LANES)
         canvas[:, pl.ds(start, WIN)] += pltpu.roll(
             jnp.concatenate([stamp, spare], axis=1), LANES // 2, 1
         )
-        saved.append((rows, cols, c, start))
+        saved.append((rows_all, cols_hi, cols_lo, c, start))
     inner = slice(LANES, LANES + width)
     if final:
         out_ref[...] = img_ref[...] - canvas[:, inner]
@@ -180,14 +210,15 @@
     fout_ref[...] = jnp.zeros_like(fout_ref)
     lout_ref[...] = jnp.zeros_like(lout_ref)
     partial = []
-    for j, (rows, cols, c, start) in enumerate(saved):
+    for j, (rows_all, cols_hi, cols_lo, c, start) in enumerate(saved):
         window = pltpu.roll(canvas[:, pl.ds(start, WIN)], WIN - LANES // 2, 1)[:, :SPAN]
-        across_all = split_dot(window, jnp.concatenate(cols, axis=1), DIMS_NN)
+        across_all = presplit_dot(window, cols_hi, cols_lo, DIMS_NN)
         grad = None
         for a in range(3):
             for b in range(3):
-                paired = jnp.sum(rows[a] * across_all[:, b * LANES : (b + 1) * LANES], axis=0,
-                                 keepdims=True)
+                paired = jnp.sum(
+                    rows_all[:, a * LANES : (a + 1) * LANES]
+                    * across_all[:, b * LANES : (b + 1) * LANES], axis=0, keepdims=True)
                 term = c[3 * a + b] * paired
                 grad = term if grad is None else grad + term
         partial.append(grad)
@@ -227,33 +258,40 @@
     common = (band_row, col_block, cell_index, psf_coef, got_above, got_below,
               offset_y, offset_x, weight, got_above, got_below, image)
 
-    def phase(final, first, fluxes, partials, from_above, from_below):
+    pre_shapes = [pltpu.VMEM((blocks, strip_rows, 3 * LANES), f32)] + [
+        pltpu.VMEM((blocks, SPAN, 3 * LANES), jnp.bfloat16)] * 4
+
+    def phase(final, first, fluxes, partials, from_above, from_below, pre=()):
         kernel = functools.partial(phase_kernel, final, first)
         if final:
-            out_shape = (jax.ShapeDtypeStruct((strip_rows, strip_width), f32),
-                         jax.ShapeDtypeStruct((own, LANES), f32))
-            out_specs = (vmem, vmem)
+            out_shape = [jax.ShapeDtypeStruct((strip_rows, strip_width), f32),
+                         jax.ShapeDtypeStruct((own, LANES), f32)]
         else:
-            out_shape = (state_shape, state_shape, part_shape, part_shape)
-            out_specs = (vmem, vmem, vmem, vmem)
+            out_shape = [state_shape, state_shape, part_shape, part_shape]
+        if first:
+            out_shape = out_shape + pre_shapes
         return pl.pallas_call(
             kernel,
-            out_shape=out_shape,
-            in_specs=[smem] * 6 + [vmem] * 10,
-            out_specs=out_specs,
+            out_shape=tuple(out_shape),
+            in_specs=[smem] * 6 + [vmem] * (10 + len(pre)),
+            out_specs=tuple([vmem] * len(out_shape)),
             scratch_shapes=[pltpu.VMEM((strip_rows, strip_width + 2 * LANES), f32)],
             cost_estimate=pl.CostEstimate(
                 flops=flops, transcendentals=blocks * 2 * (strip_rows + WIN) * LANES,
                 bytes_accessed=4 * strip_rows * strip_width * 2,
             ),
-        )(*common, fluxes, partials, *vmem_operands(from_above, from_below))
-
-    state, partials, up, down = phase(False, True, flux_start, flux_start, flux_start, flux_start)
+        )(*common, fluxes, partials, *vmem_operands(from_above, from_below, *pre))
+
+    state, partials, up, down, *pre = phase(
+        False, True, flux_start, flux_start, flux_start, flux_start
+    )
     for iteration in range(1, ITERS):
         from_above, from_below = exchange(up, down)
-        state, partials, up, down = phase(False, False, state, partials, from_above, from_below)
+        state, partials, up, down = phase(
+            False, False, state, partials, from_above, from_below, pre
+        )
     from_above, from_below = exchange(up, down)
-    residual, fluxes = phase(True, False, state, partials, from_above, from_below)
+    residual, fluxes = phase(True, False, state, partials, from_above, from_below, pre)
     return (fluxes, residual)
 
 

time: 40.2 us -> 51.3 us (1.28)
  local copies, waits for them, and re-layouts: 0.59 us -> 12.3 us
  Pallas kernels: 13.3 us -> 12.3 us
    unnamed x6 -> x38, local copies, waits for them, and re-layouts: 0.59 us -> 12.3 us
    pallas_call x3, Pallas kernels: 11.5 us -> 10.5 us  [phase(): pl.pallas_call(kernel, out_shape=tuple(out_shape), in_specs=[smem] * 6 +...]
where the time goes in v9:
time: 51.3 us; the launch traced here: 50.6 us
  starting transfers between devices  14.4 us (28%)
  Pallas kernels  12.3 us (24%)
  local copies, waits for them, and re-layouts  12.3 us (24%)
  waiting for transfers between devices  10.9 us (21%)
  between operations  0.75 us (1%)
    unnamed x38, local copies, waits for them, and re-layouts  12.3 us
    ppermute x3, waiting for transfers between devices, exchange(): from_below = lax.ppermute(to_above, 'ty', backward)  10.9 us
    pallas_call x3, Pallas kernels, phase(): pl.pallas_call(kernel, out_shape=tuple(out_shape), in_specs=[smem] * 6 +...  10.5 us
    ppermute x3, starting transfers between devices, exchange(): from_above = lax.ppermute(to_below, 'ty', forward)  7.73 us
    ppermute x3, starting transfers between devices, exchange(): from_below = lax.ppermute(to_above, 'ty', backward)  6.68 us
    pallas_call x1, Pallas kernels, local(): pl.pallas_call(setup_kernel, out_shape=(packet, packet, jax.ShapeDtypeStr...  1.84 us
  transfers between devices with their start and end apart: 6, of which 3 were waited for; matrix products, arithmetic and copies ran while one was open for 0% of the time, Pallas kernels for 0%

profile of v9, /device:TPU:11, one launch (start us, length us, event | category | flops | bytes accessed | tf_op | source)
XLA Modules:
  0.0 50.6 jit_solution(6372016718084139924)
XLA Ops:
  0.6 1.8 %shard_map.95 = (f32[8,128]{1,0:T(8,128)}, f32[8,128]{1,0:T(8,128)}, f32[2,128]{1,0:T(2,128)}) custom-call(s32[2]{0:T(128)} %band_ref.7, s32[2]{0:T(128)} %col_ref.7, s32[2]{0:T(128)} %cell_ref.7, f32[9,256]{1,0:T(8,128)} %psf_ref.7, f32[2,128]{1,0:T(2,128)} %oy_ref.7, f32[2,128]{1,0:T(2,128)} %ox_ref.7, f32[2,128]{1,0:T(2,128)} %rb_ref.1), custom_call_target="tpu_custom_call" | custom-call | tf_op jit(solution)/shard_map/pallas_call | solution.py:246
  2.5 3.7 %collective-permute-start = (f32[8,128]{1,0:T(8,128)}, f32[8,128]{1,0:T(8,128)S(1)}, u32[]{:S(2)}, u32[]{:S(2)}) collective-permute-start(f32[8,128]{1,0:T(8,128)} %get-tuple-element.20), channel_id=1, source_target_pairs={{0,1},{1,2},{2,3},{3,4},{4,5},{5,6},{6,7},{7,8},{8,9},{9,10},{10,1... | collective-permute-start | bytes 12296 | tf_op jit(solution)/shard_map/ppermute | solution.py:60
  6.2 0.0 copy-start.14
  6.2 1.9 %collective-permute-start.1 = (f32[8,128]{1,0:T(8,128)}, f32[8,128]{1,0:T(8,128)S(1)}, u32[]{:S(2)}, u32[]{:S(2)}) collective-permute-start(f32[8,128]{1,0:T(8,128)} %get-tuple-element.21), channel_id=1, source_target_pairs={{1,0},{2,1},{3,2},{4,3},{5,4},{6,5},{7,6},{8,7},{9,8},{10,9},{11,1... | collective-permute-start | bytes 12296 | tf_op jit(solution)/shard_map/ppermute | solution.py:61
  8.1 0.0 collective-permute-done.pas_ref.pa_ref
  8.2 4.1 %collective-permute-done.1.pbs_ref.pb_ref = f32[8,128]{1,0:T(8,128)S(1)} collective-permute-done((f32[8,128]{1,0:T(8,128)}, f32[8,128]{1,0:T(8,128)S(1)}, u32[]{:S(2)}, u32[]{:S(2)}) %collective-permute-start.1) | collective-permute-done | bytes 4128 | tf_op jit(solution)/shard_map/ppermute | solution.py:61
  12.2 0.6 %copy-done.18 = f32[8,128]{1,0:T(8,128)} copy-done((f32[8,128]{1,0:T(8,128)}, f32[8,128]{1,0:T(8,128)S(1)}, u32[]{:S(2)}) %copy-start.18) | copy-done | bytes 4120
  12.8 4.0 %shard_map.96 = (f32[8,128]{1,0:T(8,128)}, f32[8,128]{1,0:T(8,128)}, f32[2,128]{1,0:T(2,128)S(1)}, f32[2,128]{1,0:T(2,128)S(1)}, f32[4,64,384]{2,1,0:T(8,128)S(1...) custom-call(s32[2]{0:T(128)} %band_ref.7, ...), custom_call_target="tpu_custom_call" | custom-call | flops 452984832 | bytes 1048576 | tf_op jit(solution)/shard_map/pallas_call | solution.py:273
  16.9 0.9 %copy-done = bf16[4,256,384]{2,1,0:T(8,128)(2,1)} copy-done((bf16[4,256,384]{2,1,0:T(8,128)(2,1)}, bf16[4,256,384]{2,1,0:T(8,128)(2,1)S(1)}, u32[]{:S(2)}) %copy-start) | copy-done | bytes 786456
  17.8 0.9 %copy-done.2 = bf16[4,256,384]{2,1,0:T(8,128)(2,1)} copy-done((bf16[4,256,384]{2,1,0:T(8,128)(2,1)}, bf16[4,256,384]{2,1,0:T(8,128)(2,1)S(1)}, u32[]{:S(2)}) %copy-start.2) | copy-done | bytes 786456
  18.7 0.9 %copy-done.4 = bf16[4,256,384]{2,1,0:T(8,128)(2,1)} copy-done((bf16[4,256,384]{2,1,0:T(8,128)(2,1)}, bf16[4,256,384]{2,1,0:T(8,128)(2,1)S(1)}, u32[]{:S(2)}) %copy-start.4) | copy-done | bytes 786456
  19.6 0.9 %copy-done.6 = bf16[4,256,384]{2,1,0:T(8,128)(2,1)} copy-done((bf16[4,256,384]{2,1,0:T(8,128)(2,1)}, bf16[4,256,384]{2,1,0:T(8,128)(2,1)S(1)}, u32[]{:S(2)}) %copy-start.6) | copy-done | bytes 786456
  20.5 0.7 %copy-done.8 = f32[4,64,384]{2,1,0:T(8,128)} copy-done((f32[4,64,384]{2,1,0:T(8,128)}, f32[4,64,384]{2,1,0:T(8,128)S(1)}, u32[]{:S(2)}) %copy-start.8) | copy-done | bytes 393240
  21.2 1.9 %collective-permute-start.2 = (f32[2,128]{1,0:T(2,128)S(1)}, f32[2,128]{1,0:T(2,128)S(1)}, u32[]{:S(2)}, u32[]{:S(2)}) collective-permute-start(f32[2,128]{1,0:T(2,128)S(1)} %get-tuple-element.25), channel_id=1, source_target_pairs={{0,1},{1,2},{2,3},{3,4},{4,5},{5,6},{6,7},{7,8},{8,9},{9,10},{10,1... | collective-permute-start | bytes 3080 | tf_op jit(solution)/shard_map/ppermute | solution.py:60
  23.2 2.4 %collective-permute-start.3 = (f32[2,128]{1,0:T(2,128)S(1)}, f32[2,128]{1,0:T(2,128)S(1)}, u32[]{:S(2)}, u32[]{:S(2)}) collective-permute-start(f32[2,128]{1,0:T(2,128)S(1)} %get-tuple-element.26), channel_id=1, source_target_pairs={{1,0},{2,1},{3,2},{4,3},{5,4},{6,5},{7,6},{8,7},{9,8},{10,9},{11,1... | collective-permute-start | bytes 3080 | tf_op jit(solution)/shard_map/ppermute | solution.py:61
  25.6 0.0 copy-start.10
  25.6 3.4 %collective-permute-done.3.rb_ref = f32[2,128]{1,0:T(2,128)S(1)} collective-permute-done((f32[2,128]{1,0:T(2,128)S(1)}, f32[2,128]{1,0:T(2,128)S(1)}, u32[]{:S(2)}, u32[]{:S(2)}) %collective-permute-start.3) | collective-permute-done | bytes 1056 | tf_op jit(solution)/shard_map/ppermute | solution.py:61
  29.0 0.6 %copy-done.12 = f32[2,128]{1,0:T(2,128)} copy-done((f32[2,128]{1,0:T(2,128)}, f32[2,128]{1,0:T(2,128)S(1)}, u32[]{:S(2)}) %copy-start.12) | copy-done | bytes 1048
  29.6 0.7 %copy-done.13 = f32[2,128]{1,0:T(2,128)S(1)} copy-done((f32[2,128]{1,0:T(2,128)S(1)}, f32[2,128]{1,0:T(2,128)}, u32[]{:S(2)}) %copy-start.13) | copy-done | bytes 1048
  30.2 0.0 copy-done.11
  30.2 1.1 %copy-done.1 = bf16[4,256,384]{2,1,0:T(8,128)(2,1)S(1)} copy-done((bf16[4,256,384]{2,1,0:T(8,128)(2,1)S(1)}, bf16[4,256,384]{2,1,0:T(8,128)(2,1)}, u32[]{:S(2)}) %copy-start.1) | copy-done | bytes 786456
  31.4 1.1 %copy-done.3 = bf16[4,256,384]{2,1,0:T(8,128)(2,1)S(1)} copy-done((bf16[4,256,384]{2,1,0:T(8,128)(2,1)S(1)}, bf16[4,256,384]{2,1,0:T(8,128)(2,1)}, u32[]{:S(2)}) %copy-start.3) | copy-done | bytes 786456
  32.5 1.1 %copy-done.5 = bf16[4,256,384]{2,1,0:T(8,128)(2,1)S(1)} copy-done((bf16[4,256,384]{2,1,0:T(8,128)(2,1)S(1)}, bf16[4,256,384]{2,1,0:T(8,128)(2,1)}, u32[]{:S(2)}) %copy-start.5) | copy-done | bytes 786456
  33.6 1.1 %copy-done.7 = bf16[4,256,384]{2,1,0:T(8,128)(2,1)S(1)} copy-done((bf16[4,256,384]{2,1,0:T(8,128)(2,1)S(1)}, bf16[4,256,384]{2,1,0:T(8,128)(2,1)}, u32[]{:S(2)}) %copy-start.7) | copy-done | bytes 786456
  34.8 1.0 %copy-done.9 = f32[4,64,384]{2,1,0:T(8,128)S(1)} copy-done((f32[4,64,384]{2,1,0:T(8,128)S(1)}, f32[4,64,384]{2,1,0:T(8,128)}, u32[]{:S(2)}) %copy-start.9) | copy-done | bytes 393240
  35.8 3.4 %shard_map.97 = (f32[8,128]{1,0:T(8,128)}, f32[8,128]{1,0:T(8,128)}, f32[2,128]{1,0:T(2,128)S(1)}, f32[2,128]{1,0:T(2,128)S(1)}) custom-call(s32[2]{0:T(128)} %band_ref.7, s32[2]{0:T(128)} %col_ref.7, s32[2]{0:T(128)} %cell_ref.7, f32[9,256]{1,0:T(8,128)} %psf_ref.7, f32[8,128]{1,0:T(8,128)} %copy-done.17, f32[8,128]{1,0:T(8,128)} %copy-done.18, ...), custom_call_target="tpu_custom_call" | custom-call | flops 452984832 | bytes 1048576 | tf_op jit(solution)/shard_map/pallas_call | solution.py:273
  39.2 0.6 %copy-done.15 = f32[2,128]{1,0:T(2,128)} copy-done((f32[2,128]{1,0:T(2,128)}, f32[2,128]{1,0:T(2,128)S(1)}, u32[]{:S(2)}) %copy-start.15) | copy-done | bytes 1048
  39.7 2.1 %collective-permute-start.4 = (f32[2,128]{1,0:T(2,128)S(1)}, f32[2,128]{1,0:T(2,128)S(1)}, u32[]{:S(2)}, u32[]{:S(2)}) collective-permute-start(f32[2,128]{1,0:T(2,128)S(1)} %get-tuple-element.34), channel_id=1, source_target_pairs={{0,1},{1,2},{2,3},{3,4},{4,5},{5,6},{6,7},{7,8},{8,9},{9,10},{10,1... | collective-permute-start | bytes 3080 | tf_op jit(solution)/shard_map/ppermute | solution.py:60
  41.8 2.4 %collective-permute-start.5 = (f32[2,128]{1,0:T(2,128)S(1)}, f32[2,128]{1,0:T(2,128)S(1)}, u32[]{:S(2)}, u32[]{:S(2)}) collective-permute-start(f32[2,128]{1,0:T(2,128)S(1)} %copy-done.16), channel_id=1, source_target_pairs={{1,0},{2,1},{3,2},{4,3},{5,4},{6,5},{7,6},{8,7},{9,8},{10,9},{11,1... | collective-permute-start | bytes 3080 | tf_op jit(solution)/shard_map/ppermute | solution.py:61
  44.2 0.0 collective-permute-done.4.ra_ref
  44.2 3.4 %collective-permute-done.5.rb_ref = f32[2,128]{1,0:T(2,128)S(1)} collective-permute-done((f32[2,128]{1,0:T(2,128)S(1)}, f32[2,128]{1,0:T(2,128)S(1)}, u32[]{:S(2)}, u32[]{:S(2)}) %collective-permute-start.5) | collective-permute-done | bytes 1056 | tf_op jit(solution)/shard_map/ppermute | solution.py:61
  47.6 3.0 %shard_map.98 = (f32[64,2048]{1,0:T(8,128)}, f32[2,128]{1,0:T(2,128)}) custom-call(s32[2]{0:T(128)} %band_ref.7, s32[2]{0:T(128)} %col_ref.7, s32[2]{0:T(128)} %cell_ref.7, f32[9,256]{1,0:T(8,128)} %psf_ref.7, f32[8,128]{1,0:T(8,128)} %copy-done.17, f32[8,128]{1,0:T(8,128)} %copy-done.18, f32[2,128]{1,0:T(2,128)} %oy_ref.7, f32[2,128]{1,0:T(2,128)} %ox_ref.7, ...), custom_call_target="tpu_custom_call" | custom-call | flops 452984832 | bytes 1048576 | tf_op jit(solution)/shard_map/pallas_call | solution.py:273
  (22 shorter events, 0.0 us)
Async XLA Ops:
  2.5 5.7 %collective-permute-start = (f32[8,128]{1,0:T(8,128)}, f32[8,128]{1,0:T(8,128)S(1)}, u32[]{:S(2)}, u32[]{:S(2)}) collective-permute-start(f32[8,128]{1,0:T(8,128)} %get-tuple-element.20), channel_id=1, source_target_pairs={{0,1},{1,2},{2,3},{3,4},{4,5},{5,6},{6,7},{7,8},{8,9},{9,10},{10,1... | collective-permute-start | bytes 12296 | tf_op jit(solution)/shard_map/ppermute | solution.py:60
  6.2 6.6 %copy-start.14 = (f32[2,128]{1,0:T(2,128)S(1)}, f32[2,128]{1,0:T(2,128)}, u32[]{:S(2)}) copy-start(f32[2,128]{1,0:T(2,128)} %rb_ref.1) | copy-start | bytes 3076
  6.2 6.0 %collective-permute-start.1 = (f32[8,128]{1,0:T(8,128)}, f32[8,128]{1,0:T(8,128)S(1)}, u32[]{:S(2)}, u32[]{:S(2)}) collective-permute-start(f32[8,128]{1,0:T(8,128)} %get-tuple-element.21), channel_id=1, source_target_pairs={{1,0},{2,1},{3,2},{4,3},{5,4},{6,5},{7,6},{8,7},{9,8},{10,9},{11,1... | collective-permute-start | bytes 12296 | tf_op jit(solution)/shard_map/ppermute | solution.py:61
  8.1 4.7 %copy-start.17 = (f32[8,128]{1,0:T(8,128)}, f32[8,128]{1,0:T(8,128)S(1)}, u32[]{:S(2)}) copy-start(f32[8,128]{1,0:T(8,128)S(1)} %collective-permute-done.pas_ref.pa_ref) | copy-start | bytes 12292
  12.2 0.6 %copy-start.18 = (f32[8,128]{1,0:T(8,128)}, f32[8,128]{1,0:T(8,128)S(1)}, u32[]{:S(2)}) copy-start(f32[8,128]{1,0:T(8,128)S(1)} %collective-permute-done.1.pbs_ref.pb_ref) | copy-start | bytes 12292
  16.9 0.9 %copy-start = (bf16[4,256,384]{2,1,0:T(8,128)(2,1)}, bf16[4,256,384]{2,1,0:T(8,128)(2,1)S(1)}, u32[]{:S(2)}) copy-start(bf16[4,256,384]{2,1,0:T(8,128)(2,1)S(1)} %get-tuple-element.28.rest_1_) | copy-start | bytes 2359300
  17.8 0.9 %copy-start.2 = (bf16[4,256,384]{2,1,0:T(8,128)(2,1)}, bf16[4,256,384]{2,1,0:T(8,128)(2,1)S(1)}, u32[]{:S(2)}) copy-start(bf16[4,256,384]{2,1,0:T(8,128)(2,1)S(1)} %get-tuple-element.29.rest_2_) | copy-start | bytes 2359300
  18.7 0.9 %copy-start.4 = (bf16[4,256,384]{2,1,0:T(8,128)(2,1)}, bf16[4,256,384]{2,1,0:T(8,128)(2,1)S(1)}, u32[]{:S(2)}) copy-start(bf16[4,256,384]{2,1,0:T(8,128)(2,1)S(1)} %get-tuple-element.30.rest_3_) | copy-start | bytes 2359300
  19.6 0.9 %copy-start.6 = (bf16[4,256,384]{2,1,0:T(8,128)(2,1)}, bf16[4,256,384]{2,1,0:T(8,128)(2,1)S(1)}, u32[]{:S(2)}) copy-start(bf16[4,256,384]{2,1,0:T(8,128)(2,1)S(1)} %get-tuple-element.31.rest_4_) | copy-start | bytes 2359300
  20.5 0.7 %copy-start.8 = (f32[4,64,384]{2,1,0:T(8,128)}, f32[4,64,384]{2,1,0:T(8,128)S(1)}, u32[]{:S(2)}) copy-start(f32[4,64,384]{2,1,0:T(8,128)S(1)} %get-tuple-element.27.rest_0_) | copy-start | bytes 1179652
  21.2 4.3 %collective-permute-start.2 = (f32[2,128]{1,0:T(2,128)S(1)}, f32[2,128]{1,0:T(2,128)S(1)}, u32[]{:S(2)}, u32[]{:S(2)}) collective-permute-start(f32[2,128]{1,0:T(2,128)S(1)} %get-tuple-element.25), channel_id=1, source_target_pairs={{0,1},{1,2},{2,3},{3,4},{4,5},{5,6},{6,7},{7,8},{8,9},{9,10},{10,1... | collective-permute-start | bytes 3080 | tf_op jit(solution)/shard_map/ppermute | solution.py:60
  23.2 5.8 %collective-permute-start.3 = (f32[2,128]{1,0:T(2,128)S(1)}, f32[2,128]{1,0:T(2,128)S(1)}, u32[]{:S(2)}, u32[]{:S(2)}) collective-permute-start(f32[2,128]{1,0:T(2,128)S(1)} %get-tuple-element.26), channel_id=1, source_target_pairs={{1,0},{2,1},{3,2},{4,3},{5,4},{6,5},{7,6},{8,7},{9,8},{10,9},{11,1... | collective-permute-start | bytes 3080 | tf_op jit(solution)/shard_map/ppermute | solution.py:61
  25.6 3.4 %copy-start.10 = (f32[2,128]{1,0:T(2,128)}, f32[2,128]{1,0:T(2,128)S(1)}, u32[]{:S(2)}) copy-start(f32[2,128]{1,0:T(2,128)S(1)} %collective-permute-done.2.ra_ref) | copy-start | bytes 3076
  29.0 0.6 %copy-start.12 = (f32[2,128]{1,0:T(2,128)}, f32[2,128]{1,0:T(2,128)S(1)}, u32[]{:S(2)}) copy-start(f32[2,128]{1,0:T(2,128)S(1)} %collective-permute-done.3.rb_ref) | copy-start | bytes 3076
  29.5 0.7 %copy-start.13 = (f32[2,128]{1,0:T(2,128)S(1)}, f32[2,128]{1,0:T(2,128)}, u32[]{:S(2)}) copy-start(f32[2,128]{1,0:T(2,128)} %copy-done.12) | copy-start | bytes 3076
  29.6 0.7 %copy-start.11 = (f32[2,128]{1,0:T(2,128)S(1)}, f32[2,128]{1,0:T(2,128)}, u32[]{:S(2)}) copy-start(f32[2,128]{1,0:T(2,128)} %copy-done.10) | copy-start | bytes 3076
  30.2 1.1 %copy-start.1 = (bf16[4,256,384]{2,1,0:T(8,128)(2,1)S(1)}, bf16[4,256,384]{2,1,0:T(8,128)(2,1)}, u32[]{:S(2)}) copy-start(bf16[4,256,384]{2,1,0:T(8,128)(2,1)} %copy-done) | copy-start | bytes 2359300
  31.4 1.1 %copy-start.3 = (bf16[4,256,384]{2,1,0:T(8,128)(2,1)S(1)}, bf16[4,256,384]{2,1,0:T(8,128)(2,1)}, u32[]{:S(2)}) copy-start(bf16[4,256,384]{2,1,0:T(8,128)(2,1)} %copy-done.2) | copy-start | bytes 2359300
  32.5 1.1 %copy-start.5 = (bf16[4,256,384]{2,1,0:T(8,128)(2,1)S(1)}, bf16[4,256,384]{2,1,0:T(8,128)(2,1)}, u32[]{:S(2)}) copy-start(bf16[4,256,384]{2,1,0:T(8,128)(2,1)} %copy-done.4) | copy-start | bytes 2359300
  33.6 1.1 %copy-start.7 = (bf16[4,256,384]{2,1,0:T(8,128)(2,1)S(1)}, bf16[4,256,384]{2,1,0:T(8,128)(2,1)}, u32[]{:S(2)}) copy-start(bf16[4,256,384]{2,1,0:T(8,128)(2,1)} %copy-done.6) | copy-start | bytes 2359300
  34.8 1.0 %copy-start.9 = (f32[4,64,384]{2,1,0:T(8,128)S(1)}, f32[4,64,384]{2,1,0:T(8,128)}, u32[]{:S(2)}) copy-start(f32[4,64,384]{2,1,0:T(8,128)} %copy-done.8) | copy-start | bytes 1179652
  39.2 0.6 %copy-start.15 = (f32[2,128]{1,0:T(2,128)}, f32[2,128]{1,0:T(2,128)S(1)}, u32[]{:S(2)}) copy-start(f32[2,128]{1,0:T(2,128)S(1)} %get-tuple-element.35) | copy-start | bytes 3076
  39.7 2.1 %copy-start.16 = (f32[2,128]{1,0:T(2,128)S(1)}, f32[2,128]{1,0:T(2,128)}, u32[]{:S(2)}) copy-start(f32[2,128]{1,0:T(2,128)} %copy-done.15) | copy-start | bytes 3076
  39.7 4.5 %collective-permute-start.4 = (f32[2,128]{1,0:T(2,128)S(1)}, f32[2,128]{1,0:T(2,128)S(1)}, u32[]{:S(2)}, u32[]{:S(2)}) collective-permute-start(f32[2,128]{1,0:T(2,128)S(1)} %get-tuple-element.34), channel_id=1, source_target_pairs={{0,1},{1,2},{2,3},{3,4},{4,5},{5,6},{6,7},{7,8},{8,9},{9,10},{10,1... | collective-permute-start | bytes 3080 | tf_op jit(solution)/shard_map/ppermute | solution.py:60
  41.8 5.8 %collective-permute-start.5 = (f32[2,128]{1,0:T(2,128)S(1)}, f32[2,128]{1,0:T(2,128)S(1)}, u32[]{:S(2)}, u32[]{:S(2)}) collective-permute-start(f32[2,128]{1,0:T(2,128)S(1)} %copy-done.16), channel_id=1, source_target_pairs={{1,0},{2,1},{3,2},{4,3},{5,4},{6,5},{7,6},{8,7},{9,8},{10,9},{11,1... | collective-permute-start | bytes 3080 | tf_op jit(solution)/shard_map/ppermute | solution.py:61

commit v10 on v8

--- a/solution.py
+++ b/solution.py
@@ -39,13 +39,17 @@
     return one(lhs_hi, rhs_hi) + (one(lhs_hi, rhs_lo) + one(lhs_lo, rhs_hi))
 
 
-def exchange(to_above, to_below):
+def exchange(first, second):
     count = lax.axis_size("ty")
-    forward = [(i, i + 1) for i in range(count - 1)]
-    backward = [(i + 1, i) for i in range(count - 1)]
-    from_above = lax.ppermute(to_below, "ty", forward)
-    from_below = lax.ppermute(to_above, "ty", backward)
-    return from_above, from_below
+    within = [(i, i ^ 1) for i in range(count) if (i ^ 1) < count]
+    across = [(i, i + 1) for i in range(1, count - 1, 2)] + [
+        (i + 1, i) for i in range(1, count - 1, 2)
+    ]
+    return lax.ppermute(first, "ty", within), lax.ppermute(second, "ty", across)
+
+
+def even_device():
+    return lax.axis_index("ty") % 2 == 0
 
 
 def own_coefs(psf_ref, cell_ref, j):
@@ -95,19 +99,29 @@
             (weights[0], weights[1]), (metas[0], metas[1]),
         )
     ])
-    up_ref[...] = jnp.zeros_like(up_ref)
-    down_ref[...] = jnp.zeros_like(down_ref)
+    even = even_device()
+    first_ref, second_ref = up_ref, down_ref
+    first_ref[...] = jnp.zeros_like(first_ref)
+    second_ref[...] = jnp.zeros_like(second_ref)
     for r in range(5):
-        up_ref[r : r + 1, :] = tops[r]
-        down_ref[r : r + 1, :] = bots[r]
+        first_ref[r : r + 1, :] = jnp.where(even, bots[r], tops[r])
+        second_ref[r : r + 1, :] = jnp.where(even, tops[r], bots[r])
 
 
 def phase_kernel(
     final, first,
-    band_ref, col_ref, cell_ref, psf_ref, pas_ref, pbs_ref,
-    oy_ref, ox_ref, w_ref, pa_ref, pb_ref, img_ref, f_ref, l_ref, ra_ref, rb_ref,
+    band_ref, col_ref, cell_ref, psf_ref, xs1_ref, xs2_ref,
+    oy_ref, ox_ref, w_ref, x1_ref, x2_ref, img_ref, f_ref, l_ref, q1_ref, q2_ref,
     *rest,
 ):
+    even = even_device()
+
+    def above(ref1, ref2, row):
+        return jnp.where(even, ref2[row : row + 1, :], ref1[row : row + 1, :])
+
+    def below(ref1, ref2, row):
+        return jnp.where(even, ref1[row : row + 1, :], ref2[row : row + 1, :])
+
     if final:
         out_ref, fluxout_ref, canvas = rest
     else:
@@ -118,16 +132,16 @@
     top_first = band_ref[0] <= band_ref[1]
 
     if first:
-        fluxes = [f_ref[0:1, :], f_ref[1:2, :], pa_ref[2:3, :], pb_ref[2:3, :]]
+        fluxes = [f_ref[0:1, :], f_ref[1:2, :], above(x1_ref, x2_ref, 2), below(x1_ref, x2_ref, 2)]
     else:
-        weights = [w_ref[0:1, :], w_ref[1:2, :], pa_ref[3:4, :], pb_ref[3:4, :]]
-        from_above = ra_ref[0:1, :]
-        from_below = rb_ref[0:1, :]
+        weights = [w_ref[0:1, :], w_ref[1:2, :], above(x1_ref, x2_ref, 3), below(x1_ref, x2_ref, 3)]
+        from_above = above(q1_ref, q2_ref, 0)
+        from_below = below(q1_ref, q2_ref, 0)
         extra = [
             jnp.where(top_first, from_above, from_below),
             jnp.where(top_first, from_below, from_above),
-            ra_ref[1:2, :],
-            rb_ref[1:2, :],
+            above(q1_ref, q2_ref, 1),
+            below(q1_ref, q2_ref, 1),
         ]
         fluxes = []
         for j in range(own + 2):
@@ -140,12 +154,14 @@
         y = band_ref[j].astype(jnp.float32) + oy_ref[j : j + 1, :]
         specs.append((y, ox_ref[j : j + 1, :], own_coefs(psf_ref, cell_ref, j), col_ref[j], None))
     specs.append((
-        pa_ref[0:1, :] - strip_rows, pa_ref[1:2, :], [pas_ref[4, k] for k in range(9)],
-        pas_ref[4, 9].astype(jnp.int32), REACH,
+        above(x1_ref, x2_ref, 0) - strip_rows, above(x1_ref, x2_ref, 1),
+        [jnp.where(even, xs2_ref[4, k], xs1_ref[4, k]) for k in range(9)],
+        jnp.where(even, xs2_ref[4, 9], xs1_ref[4, 9]).astype(jnp.int32), REACH,
     ))
     specs.append((
-        pb_ref[0:1, :] + strip_rows, pb_ref[1:2, :], [pbs_ref[4, k] for k in range(9)],
-        pbs_ref[4, 9].astype(jnp.int32), None,
+        below(x1_ref, x2_ref, 0) + strip_rows, below(x1_ref, x2_ref, 1),
+        [jnp.where(even, xs1_ref[4, k], xs2_ref[4, k]) for k in range(9)],
+        jnp.where(even, xs1_ref[4, 9], xs2_ref[4, 9]).astype(jnp.int32), None,
     ))
 
     canvas[...] = jnp.zeros_like(canvas)
@@ -195,10 +211,11 @@
         lout_ref[j : j + 1, :] = grad
     top_part = jnp.where(top_first, partial[0], partial[1])
     bot_part = jnp.where(top_first, partial[1], partial[0])
-    up_ref[0:1, :] = partial[own]
-    up_ref[1:2, :] = top_part
-    down_ref[0:1, :] = partial[own + 1]
-    down_ref[1:2, :] = bot_part
+    first_ref, second_ref = up_ref, down_ref
+    first_ref[0:1, :] = jnp.where(even, partial[own + 1], partial[own])
+    first_ref[1:2, :] = jnp.where(even, bot_part, top_part)
+    second_ref[0:1, :] = jnp.where(even, partial[own], partial[own + 1])
+    second_ref[1:2, :] = jnp.where(even, top_part, bot_part)
 
 
 def vmem_operands(*arrays):
@@ -212,22 +229,22 @@
     smem = pl.BlockSpec(memory_space=pltpu.SMEM)
     vmem = pl.BlockSpec(memory_space=pltpu.VMEM)
     packet = jax.ShapeDtypeStruct((SLOTS, LANES), f32)
-    send_up, send_down, weight = pl.pallas_call(
+    send_within, send_across, weight = pl.pallas_call(
         setup_kernel,
         out_shape=(packet, packet, jax.ShapeDtypeStruct((own, LANES), f32)),
         in_specs=[smem] * 4 + [vmem] * 3,
         out_specs=(vmem, vmem, vmem),
     )(band_row, col_block, cell_index, psf_coef, offset_y, offset_x, flux_start)
-    got_above, got_below = exchange(send_up, send_down)
+    got_within, got_across = exchange(send_within, send_across)
 
     blocks = own + 2
     flops = 2 * 3 * 2 * strip_rows * WIN * 3 * LANES * blocks
     state_shape = jax.ShapeDtypeStruct((SLOTS, LANES), f32)
     part_shape = pltpu.VMEM((2, LANES), f32)
-    common = (band_row, col_block, cell_index, psf_coef, got_above, got_below,
-              offset_y, offset_x, weight, got_above, got_below, image)
-
-    def phase(final, first, fluxes, partials, from_above, from_below):
+    common = (band_row, col_block, cell_index, psf_coef, got_within, got_across,
+              offset_y, offset_x, weight, got_within, got_across, image)
+
+    def phase(final, first, fluxes, partials, swap_within, swap_across):
         kernel = functools.partial(phase_kernel, final, first)
         if final:
             out_shape = (jax.ShapeDtypeStruct((strip_rows, strip_width), f32),
@@ -246,14 +263,14 @@
                 flops=flops, transcendentals=blocks * 2 * (strip_rows + WIN) * LANES,
                 bytes_accessed=4 * strip_rows * strip_width * 2,
             ),
-        )(*common, fluxes, partials, *vmem_operands(from_above, from_below))
-
-    state, partials, up, down = phase(False, True, flux_start, flux_start, flux_start, flux_start)
+        )(*common, fluxes, partials, *vmem_operands(swap_within, swap_across))
+
+    state, partials, within, across = phase(False, True, flux_start, flux_start, flux_start, flux_start)
     for iteration in range(1, ITERS):
-        from_above, from_below = exchange(up, down)
-        state, partials, up, down = phase(False, False, state, partials, from_above, from_below)
-    from_above, from_below = exchange(up, down)
-    residual, fluxes = phase(True, False, state, partials, from_above, from_below)
+        swap_within, swap_across = exchange(within, across)
+        state, partials, within, across = phase(False, False, state, partials, swap_within, swap_across)
+    swap_within, swap_across = exchange(within, across)
+    residual, fluxes = phase(True, False, state, partials, swap_within, swap_across)
     return (fluxes, residual)
 
 

time: 40.2 us -> 33.3 us (0.83)
  starting transfers between devices: 14.3 us -> 9.67 us
  waiting for transfers between devices: 10.9 us -> 8.68 us
    ppermute x6, starting transfers between devices: 14.3 us -> 9.67 us  [the longest x3 8.99 us: exchange(): lax.ppermute(second, 'ty', across)]
    ppermute x6, waiting for transfers between devices: 10.9 us -> 8.68 us  [the longest x3 8.67 us: exchange(): lax.ppermute(second, 'ty', across)]
where the time goes in v10:
time: 33.3 us; the launch traced here: 32.9 us
  Pallas kernels  13.3 us (40%)
  starting transfers between devices  9.67 us (29%)
  waiting for transfers between devices  8.68 us (26%)
  between operations  0.69 us (2%)
  local copies, waits for them, and re-layouts  0.59 us (2%)
    pallas_call x3, Pallas kernels, phase(): pl.pallas_call(kernel, out_shape=out_shape, in_specs=[smem] * 6 + [vmem]...  11.5 us
    ppermute x3, starting transfers between devices, exchange(): lax.ppermute(second, 'ty', across)  8.99 us
    ppermute x3, waiting for transfers between devices, exchange(): lax.ppermute(second, 'ty', across)  8.67 us
    pallas_call x1, Pallas kernels, local(): pl.pallas_call(setup_kernel, out_shape=(packet, packet, jax.ShapeDtypeStr...  1.84 us
    ppermute x3, starting transfers between devices, exchange(): lax.ppermute(first, 'ty', within)  0.68 us
  transfers between devices with their start and end apart: 6, of which 3 were waited for; matrix products, arithmetic and copies ran while one was open for 0% of the time, Pallas kernels for 0%

profile of v10, /device:TPU:11, one launch (start us, length us, event | category | flops | bytes accessed | tf_op | source)
XLA Modules:
  0.0 32.9 jit_solution(3945151366742609380)
XLA Ops:
  0.6 1.8 %shard_map.95 = (f32[8,128]{1,0:T(8,128)}, f32[8,128]{1,0:T(8,128)}, f32[2,128]{1,0:T(2,128)}) custom-call(s32[2]{0:T(128)} %band_ref.7, s32[2]{0:T(128)} %col_ref.7, s32[2]{0:T(128)} %cell_ref.7, f32[9,256]{1,0:T(8,128)} %psf_ref.7, f32[2,128]{1,0:T(2,128)} %oy_ref.7, f32[2,128]{1,0:T(2,128)} %ox_ref.7, f32[2,128]{1,0:T(2,128)} %q2_ref.1), custom_call_target="tpu_custom_call" | custom-call | tf_op jit(solution)/shard_map/pallas_call | solution.py:232
  2.5 0.7 %collective-permute-start = (f32[8,128]{1,0:T(8,128)}, f32[8,128]{1,0:T(8,128)S(1)}, u32[]{:S(2)}, u32[]{:S(2)}) collective-permute-start(f32[8,128]{1,0:T(8,128)} %get-tuple-element.15), channel_id=1, source_target_pairs={{0,1},{1,0},{2,3},{3,2},{4,5},{5,4},{6,7},{7,6},{8,9},{9,8},{10,11... | collective-permute-start | bytes 12296 | tf_op jit(solution)/shard_map/ppermute | solution.py:48
  3.1 0.0 copy-start
  3.1 3.1 %collective-permute-start.1 = (f32[8,128]{1,0:T(8,128)}, f32[8,128]{1,0:T(8,128)S(1)}, u32[]{:S(2)}, u32[]{:S(2)}) collective-permute-start(f32[8,128]{1,0:T(8,128)} %get-tuple-element.16), channel_id=1, source_target_pairs={{1,2},{3,4},{5,6},{7,8},{9,10},{11,12},{13,14},{2,1},{4,3},{6,5},{... | collective-permute-start | bytes 12296 | tf_op jit(solution)/shard_map/ppermute | solution.py:48
  6.2 0.0 collective-permute-done.xs1_ref.x1_ref
  6.2 0.0 copy-start.1
  6.2 3.1 %collective-permute-done.1.xs2_ref.x2_ref = f32[8,128]{1,0:T(8,128)S(1)} collective-permute-done((f32[8,128]{1,0:T(8,128)}, f32[8,128]{1,0:T(8,128)S(1)}, u32[]{:S(2)}, u32[]{:S(2)}) %collective-permute-start.1) | collective-permute-done | bytes 4128 | tf_op jit(solution)/shard_map/ppermute | solution.py:48
  9.3 0.0 copy-start.2
  9.3 0.0 copy-done.1
  9.3 0.6 %copy-done.2 = f32[8,128]{1,0:T(8,128)} copy-done((f32[8,128]{1,0:T(8,128)}, f32[8,128]{1,0:T(8,128)S(1)}, u32[]{:S(2)}) %copy-start.2) | copy-done | bytes 4120
  9.9 0.0 copy-done
  9.9 4.0 %shard_map.96 = (f32[8,128]{1,0:T(8,128)}, f32[8,128]{1,0:T(8,128)}, f32[2,128]{1,0:T(2,128)S(1)}, f32[2,128]{1,0:T(2,128)S(1)}) custom-call(s32[2]{0:T(128)} %band_ref.7, s32[2]{0:T(128)} %col_ref.7, s32[2]{0:T(128)} %cell_ref.7, f32[9,256]{1,0:T(8,128)} %psf_ref.7, f32[8,128]{1,0:T(8,128)} %copy-done.1, f32[8,128]{1,0:T(8,128)} %copy-done.2, ...), custom_call_target="tpu_custom_call" | custom-call | flops 452984832 | bytes 1048576 | tf_op jit(solution)/shard_map/pallas_call | solution.py:256
  13.9 0.0 collective-permute-start.2
  13.9 3.0 %collective-permute-start.3 = (f32[2,128]{1,0:T(2,128)S(1)}, f32[2,128]{1,0:T(2,128)S(1)}, u32[]{:S(2)}, u32[]{:S(2)}) collective-permute-start(f32[2,128]{1,0:T(2,128)S(1)} %get-tuple-element.21), channel_id=1, source_target_pairs={{1,2},{3,4},{5,6},{7,8},{9,10},{11,12},{13,14},{2,1},{4,3},{6,5},{... | collective-permute-start | bytes 3080 | tf_op jit(solution)/shard_map/ppermute | solution.py:48
  16.8 0.0 collective-permute-done.2.q1_ref
  16.8 2.8 %collective-permute-done.3.q2_ref = f32[2,128]{1,0:T(2,128)S(1)} collective-permute-done((f32[2,128]{1,0:T(2,128)S(1)}, f32[2,128]{1,0:T(2,128)S(1)}, u32[]{:S(2)}, u32[]{:S(2)}) %collective-permute-start.3) | collective-permute-done | bytes 1056 | tf_op jit(solution)/shard_map/ppermute | solution.py:48
  19.6 4.0 %shard_map.97 = (f32[8,128]{1,0:T(8,128)}, f32[8,128]{1,0:T(8,128)}, f32[2,128]{1,0:T(2,128)S(1)}, f32[2,128]{1,0:T(2,128)S(1)}) custom-call(s32[2]{0:T(128)} %band_ref.7, s32[2]{0:T(128)} %col_ref.7, s32[2]{0:T(128)} %cell_ref.7, f32[9,256]{1,0:T(8,128)} %psf_ref.7, f32[8,128]{1,0:T(8,128)} %copy-done.1, f32[8,128]{1,0:T(8,128)} %copy-done.2, ...), custom_call_target="tpu_custom_call" | custom-call | flops 452984832 | bytes 1048576 | tf_op jit(solution)/shard_map/pallas_call | solution.py:256
  23.6 0.0 collective-permute-start.4
  23.6 3.0 %collective-permute-start.5 = (f32[2,128]{1,0:T(2,128)S(1)}, f32[2,128]{1,0:T(2,128)S(1)}, u32[]{:S(2)}, u32[]{:S(2)}) collective-permute-start(f32[2,128]{1,0:T(2,128)S(1)} %get-tuple-element.25), channel_id=1, source_target_pairs={{1,2},{3,4},{5,6},{7,8},{9,10},{11,12},{13,14},{2,1},{4,3},{6,5},{... | collective-permute-start | bytes 3080 | tf_op jit(solution)/shard_map/ppermute | solution.py:48
  26.6 0.0 collective-permute-done.4.q1_ref
  26.6 2.8 %collective-permute-done.5.q2_ref = f32[2,128]{1,0:T(2,128)S(1)} collective-permute-done((f32[2,128]{1,0:T(2,128)S(1)}, f32[2,128]{1,0:T(2,128)S(1)}, u32[]{:S(2)}, u32[]{:S(2)}) %collective-permute-start.5) | collective-permute-done | bytes 1056 | tf_op jit(solution)/shard_map/ppermute | solution.py:48
  29.4 3.6 %shard_map.98 = (f32[64,2048]{1,0:T(8,128)}, f32[2,128]{1,0:T(2,128)}) custom-call(s32[2]{0:T(128)} %band_ref.7, s32[2]{0:T(128)} %col_ref.7, s32[2]{0:T(128)} %cell_ref.7, f32[9,256]{1,0:T(8,128)} %psf_ref.7, f32[8,128]{1,0:T(8,128)} %copy-done.1, f32[8,128]{1,0:T(8,128)} %copy-done.2, f32[2,128]{1,0:T(2,128)} %oy_ref.7, f32[2,128]{1,0:T(2,128)} %ox_ref.7, ...), custom_call_target="tpu_custom_call" | custom-call | flops 452984832 | bytes 1048576 | tf_op jit(solution)/shard_map/pallas_call | solution.py:256
Async XLA Ops:
  2.5 3.8 %collective-permute-start = (f32[8,128]{1,0:T(8,128)}, f32[8,128]{1,0:T(8,128)S(1)}, u32[]{:S(2)}, u32[]{:S(2)}) collective-permute-start(f32[8,128]{1,0:T(8,128)} %get-tuple-element.15), channel_id=1, source_target_pairs={{0,1},{1,0},{2,3},{3,2},{4,5},{5,4},{6,7},{7,6},{8,9},{9,8},{10,11... | collective-permute-start | bytes 12296 | tf_op jit(solution)/shard_map/ppermute | solution.py:48
  3.1 6.7 %copy-start = (f32[2,128]{1,0:T(2,128)S(1)}, f32[2,128]{1,0:T(2,128)}, u32[]{:S(2)}) copy-start(f32[2,128]{1,0:T(2,128)} %q2_ref.1) | copy-start | bytes 3076
  3.1 6.2 %collective-permute-start.1 = (f32[8,128]{1,0:T(8,128)}, f32[8,128]{1,0:T(8,128)S(1)}, u32[]{:S(2)}, u32[]{:S(2)}) collective-permute-start(f32[8,128]{1,0:T(8,128)} %get-tuple-element.16), channel_id=1, source_target_pairs={{1,2},{3,4},{5,6},{7,8},{9,10},{11,12},{13,14},{2,1},{4,3},{6,5},{... | collective-permute-start | bytes 12296 | tf_op jit(solution)/shard_map/ppermute | solution.py:48
  6.2 3.1 %copy-start.1 = (f32[8,128]{1,0:T(8,128)}, f32[8,128]{1,0:T(8,128)S(1)}, u32[]{:S(2)}) copy-start(f32[8,128]{1,0:T(8,128)S(1)} %collective-permute-done.xs1_ref.x1_ref) | copy-start | bytes 12292
  9.3 0.6 %copy-start.2 = (f32[8,128]{1,0:T(8,128)}, f32[8,128]{1,0:T(8,128)S(1)}, u32[]{:S(2)}) copy-start(f32[8,128]{1,0:T(8,128)S(1)} %collective-permute-done.1.xs2_ref.x2_ref) | copy-start | bytes 12292
  13.9 3.0 %collective-permute-start.2 = (f32[2,128]{1,0:T(2,128)S(1)}, f32[2,128]{1,0:T(2,128)S(1)}, u32[]{:S(2)}, u32[]{:S(2)}) collective-permute-start(f32[2,128]{1,0:T(2,128)S(1)} %get-tuple-element.20), channel_id=1, source_target_pairs={{0,1},{1,0},{2,3},{3,2},{4,5},{5,4},{6,7},{7,6},{8,9},{9,8},{10,11... | collective-permute-start | bytes 3080 | tf_op jit(solution)/shard_map/ppermute | solution.py:48
  13.9 5.8 %collective-permute-start.3 = (f32[2,128]{1,0:T(2,128)S(1)}, f32[2,128]{1,0:T(2,128)S(1)}, u32[]{:S(2)}, u32[]{:S(2)}) collective-permute-start(f32[2,128]{1,0:T(2,128)S(1)} %get-tuple-element.21), channel_id=1, source_target_pairs={{1,2},{3,4},{5,6},{7,8},{9,10},{11,12},{13,14},{2,1},{4,3},{6,5},{... | collective-permute-start | bytes 3080 | tf_op jit(solution)/shard_map/ppermute | solution.py:48
  23.6 3.0 %collective-permute-start.4 = (f32[2,128]{1,0:T(2,128)S(1)}, f32[2,128]{1,0:T(2,128)S(1)}, u32[]{:S(2)}, u32[]{:S(2)}) collective-permute-start(f32[2,128]{1,0:T(2,128)S(1)} %get-tuple-element.24), channel_id=1, source_target_pairs={{0,1},{1,0},{2,3},{3,2},{4,5},{5,4},{6,7},{7,6},{8,9},{9,8},{10,11... | collective-permute-start | bytes 3080 | tf_op jit(solution)/shard_map/ppermute | solution.py:48
  23.6 5.8 %collective-permute-start.5 = (f32[2,128]{1,0:T(2,128)S(1)}, f32[2,128]{1,0:T(2,128)S(1)}, u32[]{:S(2)}, u32[]{:S(2)}) collective-permute-start(f32[2,128]{1,0:T(2,128)S(1)} %get-tuple-element.25), channel_id=1, source_target_pairs={{1,2},{3,4},{5,6},{7,8},{9,10},{11,12},{13,14},{2,1},{4,3},{6,5},{... | collective-permute-start | bytes 3080 | tf_op jit(solution)/shard_map/ppermute | solution.py:48

commit v11 on v10

--- a/solution.py
+++ b/solution.py
@@ -32,6 +32,20 @@
     lhs_lo = (lhs - lhs_hi.astype(jnp.float32)).astype(jnp.bfloat16)
     rhs_hi = rhs.astype(jnp.bfloat16)
     rhs_lo = (rhs - rhs_hi.astype(jnp.float32)).astype(jnp.bfloat16)
+
+    def one(a, b):
+        return lax.dot_general(a, b, dims, preferred_element_type=jnp.float32)
+
+    return one(lhs_hi, rhs_hi) + (one(lhs_hi, rhs_lo) + one(lhs_lo, rhs_hi))
+
+
+def split_bf16(value):
+    hi = value.astype(jnp.bfloat16)
+    return hi, (value - hi.astype(jnp.float32)).astype(jnp.bfloat16)
+
+
+def presplit_dot(lhs, rhs_hi, rhs_lo, dims):
+    lhs_hi, lhs_lo = split_bf16(lhs)
 
     def one(a, b):
         return lax.dot_general(a, b, dims, preferred_element_type=jnp.float32)
@@ -173,17 +187,17 @@
         rows = profile3(hpos - y)
         if keep is not None:
             rows = tuple(jnp.where(hpos < keep, r, 0.0) for r in rows)
-        cols = profile3(wpos - x)
+        cols_hi, cols_lo = split_bf16(jnp.concatenate(profile3(wpos - x), axis=1))
         mixed = [
-            (c[3 * a] * cols[0] + c[3 * a + 1] * cols[1] + c[3 * a + 2] * cols[2]) * fluxes[j]
-            for a in range(3)
+            (c[b] * rows[0] + c[3 + b] * rows[1] + c[6 + b] * rows[2]) * fluxes[j]
+            for b in range(3)
         ]
-        stamp = split_dot(jnp.concatenate(rows, axis=1), jnp.concatenate(mixed, axis=1), DIMS_NT)
+        stamp = presplit_dot(jnp.concatenate(mixed, axis=1), cols_hi, cols_lo, DIMS_NT)
         start = pl.multiple_of(col * LANES, LANES)
         canvas[:, pl.ds(start, WIN)] += pltpu.roll(
             jnp.concatenate([stamp, spare], axis=1), LANES // 2, 1
         )
-        saved.append((rows, cols, c, start))
+        saved.append((rows, cols_hi, cols_lo, c, start))
     inner = slice(LANES, LANES + width)
     if final:
         out_ref[...] = img_ref[...] - canvas[:, inner]
@@ -196,9 +210,9 @@
     fout_ref[...] = jnp.zeros_like(fout_ref)
     lout_ref[...] = jnp.zeros_like(lout_ref)
     partial = []
-    for j, (rows, cols, c, start) in enumerate(saved):
+    for j, (rows, cols_hi, cols_lo, c, start) in enumerate(saved):
         window = pltpu.roll(canvas[:, pl.ds(start, WIN)], WIN - LANES // 2, 1)[:, :SPAN]
-        across_all = split_dot(window, jnp.concatenate(cols, axis=1), DIMS_NN)
+        across_all = presplit_dot(window, cols_hi, cols_lo, DIMS_NN)
         grad = None
         for a in range(3):
             for b in range(3):

time: 33.3 us -> 32.5 us (0.976)
  Pallas kernels: 13.3 us -> 12.5 us
    pallas_call x3, Pallas kernels: 11.5 us -> 10.7 us  [phase(): pl.pallas_call(kernel, out_shape=out_shape, in_specs=[smem] * 6 + [vmem]...]
where the time goes in v11:
time: 32.5 us; the launch traced here: 32.2 us
  Pallas kernels  12.5 us (38%)
  starting transfers between devices  9.68 us (30%)
  waiting for transfers between devices  8.67 us (27%)
  between operations  0.69 us (2%)
  local copies, waits for them, and re-layouts  0.59 us (2%)
    pallas_call x3, Pallas kernels, phase(): pl.pallas_call(kernel, out_shape=out_shape, in_specs=[smem] * 6 + [vmem]...  10.7 us
    ppermute x3, starting transfers between devices, exchange(): lax.ppermute(second, 'ty', across)  9 us
    ppermute x3, waiting for transfers between devices, exchange(): lax.ppermute(second, 'ty', across)  8.66 us
    pallas_call x1, Pallas kernels, local(): pl.pallas_call(setup_kernel, out_shape=(packet, packet, jax.ShapeDtypeStr...  1.84 us
    ppermute x3, starting transfers between devices, exchange(): lax.ppermute(first, 'ty', within)  0.68 us
  transfers between devices with their start and end apart: 6, of which 3 were waited for; matrix products, arithmetic and copies ran while one was open for 0% of the time, Pallas kernels for 0%

profile of v11, /device:TPU:11, one launch (start us, length us, event | category | flops | bytes accessed | tf_op | source)
XLA Modules:
  0.0 32.2 jit_solution(3258594876052745288)
XLA Ops:
  0.6 1.8 %shard_map.95 = (f32[8,128]{1,0:T(8,128)}, f32[8,128]{1,0:T(8,128)}, f32[2,128]{1,0:T(2,128)}) custom-call(s32[2]{0:T(128)} %band_ref.7, s32[2]{0:T(128)} %col_ref.7, s32[2]{0:T(128)} %cell_ref.7, f32[9,256]{1,0:T(8,128)} %psf_ref.7, f32[2,128]{1,0:T(2,128)} %oy_ref.7, f32[2,128]{1,0:T(2,128)} %ox_ref.7, f32[2,128]{1,0:T(2,128)} %q2_ref.1), custom_call_target="tpu_custom_call" | custom-call | tf_op jit(solution)/shard_map/pallas_call | solution.py:246
  2.5 0.7 %collective-permute-start = (f32[8,128]{1,0:T(8,128)}, f32[8,128]{1,0:T(8,128)S(1)}, u32[]{:S(2)}, u32[]{:S(2)}) collective-permute-start(f32[8,128]{1,0:T(8,128)} %get-tuple-element.15), channel_id=1, source_target_pairs={{0,1},{1,0},{2,3},{3,2},{4,5},{5,4},{6,7},{7,6},{8,9},{9,8},{10,11... | collective-permute-start | bytes 12296 | tf_op jit(solution)/shard_map/ppermute | solution.py:62
  3.1 0.0 copy-start
  3.1 3.1 %collective-permute-start.1 = (f32[8,128]{1,0:T(8,128)}, f32[8,128]{1,0:T(8,128)S(1)}, u32[]{:S(2)}, u32[]{:S(2)}) collective-permute-start(f32[8,128]{1,0:T(8,128)} %get-tuple-element.16), channel_id=1, source_target_pairs={{1,2},{3,4},{5,6},{7,8},{9,10},{11,12},{13,14},{2,1},{4,3},{6,5},{... | collective-permute-start | bytes 12296 | tf_op jit(solution)/shard_map/ppermute | solution.py:62
  6.2 0.0 collective-permute-done.xs1_ref.x1_ref
  6.2 0.0 copy-start.1
  6.2 3.1 %collective-permute-done.1.xs2_ref.x2_ref = f32[8,128]{1,0:T(8,128)S(1)} collective-permute-done((f32[8,128]{1,0:T(8,128)}, f32[8,128]{1,0:T(8,128)S(1)}, u32[]{:S(2)}, u32[]{:S(2)}) %collective-permute-start.1) | collective-permute-done | bytes 4128 | tf_op jit(solution)/shard_map/ppermute | solution.py:62
  9.3 0.0 copy-start.2
  9.3 0.0 copy-done.1
  9.3 0.6 %copy-done.2 = f32[8,128]{1,0:T(8,128)} copy-done((f32[8,128]{1,0:T(8,128)}, f32[8,128]{1,0:T(8,128)S(1)}, u32[]{:S(2)}) %copy-start.2) | copy-done | bytes 4120
  9.9 0.0 copy-done
  9.9 3.7 %shard_map.96 = (f32[8,128]{1,0:T(8,128)}, f32[8,128]{1,0:T(8,128)}, f32[2,128]{1,0:T(2,128)S(1)}, f32[2,128]{1,0:T(2,128)S(1)}) custom-call(s32[2]{0:T(128)} %band_ref.7, s32[2]{0:T(128)} %col_ref.7, s32[2]{0:T(128)} %cell_ref.7, f32[9,256]{1,0:T(8,128)} %psf_ref.7, f32[8,128]{1,0:T(8,128)} %copy-done.1, f32[8,128]{1,0:T(8,128)} %copy-done.2, ...), custom_call_target="tpu_custom_call" | custom-call | flops 452984832 | bytes 1048576 | tf_op jit(solution)/shard_map/pallas_call | solution.py:270
  13.6 0.0 collective-permute-start.2
  13.6 3.0 %collective-permute-start.3 = (f32[2,128]{1,0:T(2,128)S(1)}, f32[2,128]{1,0:T(2,128)S(1)}, u32[]{:S(2)}, u32[]{:S(2)}) collective-permute-start(f32[2,128]{1,0:T(2,128)S(1)} %get-tuple-element.21), channel_id=1, source_target_pairs={{1,2},{3,4},{5,6},{7,8},{9,10},{11,12},{13,14},{2,1},{4,3},{6,5},{... | collective-permute-start | bytes 3080 | tf_op jit(solution)/shard_map/ppermute | solution.py:62
  16.5 0.0 collective-permute-done.2.q1_ref
  16.6 2.8 %collective-permute-done.3.q2_ref = f32[2,128]{1,0:T(2,128)S(1)} collective-permute-done((f32[2,128]{1,0:T(2,128)S(1)}, f32[2,128]{1,0:T(2,128)S(1)}, u32[]{:S(2)}, u32[]{:S(2)}) %collective-permute-start.3) | collective-permute-done | bytes 1056 | tf_op jit(solution)/shard_map/ppermute | solution.py:62
  19.4 3.7 %shard_map.97 = (f32[8,128]{1,0:T(8,128)}, f32[8,128]{1,0:T(8,128)}, f32[2,128]{1,0:T(2,128)S(1)}, f32[2,128]{1,0:T(2,128)S(1)}) custom-call(s32[2]{0:T(128)} %band_ref.7, s32[2]{0:T(128)} %col_ref.7, s32[2]{0:T(128)} %cell_ref.7, f32[9,256]{1,0:T(8,128)} %psf_ref.7, f32[8,128]{1,0:T(8,128)} %copy-done.1, f32[8,128]{1,0:T(8,128)} %copy-done.2, ...), custom_call_target="tpu_custom_call" | custom-call | flops 452984832 | bytes 1048576 | tf_op jit(solution)/shard_map/pallas_call | solution.py:270
  23.1 0.0 collective-permute-start.4
  23.1 3.0 %collective-permute-start.5 = (f32[2,128]{1,0:T(2,128)S(1)}, f32[2,128]{1,0:T(2,128)S(1)}, u32[]{:S(2)}, u32[]{:S(2)}) collective-permute-start(f32[2,128]{1,0:T(2,128)S(1)} %get-tuple-element.25), channel_id=1, source_target_pairs={{1,2},{3,4},{5,6},{7,8},{9,10},{11,12},{13,14},{2,1},{4,3},{6,5},{... | collective-permute-start | bytes 3080 | tf_op jit(solution)/shard_map/ppermute | solution.py:62
  26.0 0.0 collective-permute-done.4.q1_ref
  26.1 2.8 %collective-permute-done.5.q2_ref = f32[2,128]{1,0:T(2,128)S(1)} collective-permute-done((f32[2,128]{1,0:T(2,128)S(1)}, f32[2,128]{1,0:T(2,128)S(1)}, u32[]{:S(2)}, u32[]{:S(2)}) %collective-permute-start.5) | collective-permute-done | bytes 1056 | tf_op jit(solution)/shard_map/ppermute | solution.py:62
  28.9 3.3 %shard_map.98 = (f32[64,2048]{1,0:T(8,128)}, f32[2,128]{1,0:T(2,128)}) custom-call(s32[2]{0:T(128)} %band_ref.7, s32[2]{0:T(128)} %col_ref.7, s32[2]{0:T(128)} %cell_ref.7, f32[9,256]{1,0:T(8,128)} %psf_ref.7, f32[8,128]{1,0:T(8,128)} %copy-done.1, f32[8,128]{1,0:T(8,128)} %copy-done.2, f32[2,128]{1,0:T(2,128)} %oy_ref.7, f32[2,128]{1,0:T(2,128)} %ox_ref.7, ...), custom_call_target="tpu_custom_call" | custom-call | flops 452984832 | bytes 1048576 | tf_op jit(solution)/shard_map/pallas_call | solution.py:270
Async XLA Ops:
  2.5 3.8 %collective-permute-start = (f32[8,128]{1,0:T(8,128)}, f32[8,128]{1,0:T(8,128)S(1)}, u32[]{:S(2)}, u32[]{:S(2)}) collective-permute-start(f32[8,128]{1,0:T(8,128)} %get-tuple-element.15), channel_id=1, source_target_pairs={{0,1},{1,0},{2,3},{3,2},{4,5},{5,4},{6,7},{7,6},{8,9},{9,8},{10,11... | collective-permute-start | bytes 12296 | tf_op jit(solution)/shard_map/ppermute | solution.py:62
  3.1 6.7 %copy-start = (f32[2,128]{1,0:T(2,128)S(1)}, f32[2,128]{1,0:T(2,128)}, u32[]{:S(2)}) copy-start(f32[2,128]{1,0:T(2,128)} %q2_ref.1) | copy-start | bytes 3076
  3.1 6.2 %collective-permute-start.1 = (f32[8,128]{1,0:T(8,128)}, f32[8,128]{1,0:T(8,128)S(1)}, u32[]{:S(2)}, u32[]{:S(2)}) collective-permute-start(f32[8,128]{1,0:T(8,128)} %get-tuple-element.16), channel_id=1, source_target_pairs={{1,2},{3,4},{5,6},{7,8},{9,10},{11,12},{13,14},{2,1},{4,3},{6,5},{... | collective-permute-start | bytes 12296 | tf_op jit(solution)/shard_map/ppermute | solution.py:62
  6.2 3.1 %copy-start.1 = (f32[8,128]{1,0:T(8,128)}, f32[8,128]{1,0:T(8,128)S(1)}, u32[]{:S(2)}) copy-start(f32[8,128]{1,0:T(8,128)S(1)} %collective-permute-done.xs1_ref.x1_ref) | copy-start | bytes 12292
  9.3 0.6 %copy-start.2 = (f32[8,128]{1,0:T(8,128)}, f32[8,128]{1,0:T(8,128)S(1)}, u32[]{:S(2)}) copy-start(f32[8,128]{1,0:T(8,128)S(1)} %collective-permute-done.1.xs2_ref.x2_ref) | copy-start | bytes 12292
  13.6 3.0 %collective-permute-start.2 = (f32[2,128]{1,0:T(2,128)S(1)}, f32[2,128]{1,0:T(2,128)S(1)}, u32[]{:S(2)}, u32[]{:S(2)}) collective-permute-start(f32[2,128]{1,0:T(2,128)S(1)} %get-tuple-element.20), channel_id=1, source_target_pairs={{0,1},{1,0},{2,3},{3,2},{4,5},{5,4},{6,7},{7,6},{8,9},{9,8},{10,11... | collective-permute-start | bytes 3080 | tf_op jit(solution)/shard_map/ppermute | solution.py:62
  13.6 5.8 %collective-permute-start.3 = (f32[2,128]{1,0:T(2,128)S(1)}, f32[2,128]{1,0:T(2,128)S(1)}, u32[]{:S(2)}, u32[]{:S(2)}) collective-permute-start(f32[2,128]{1,0:T(2,128)S(1)} %get-tuple-element.21), channel_id=1, source_target_pairs={{1,2},{3,4},{5,6},{7,8},{9,10},{11,12},{13,14},{2,1},{4,3},{6,5},{... | collective-permute-start | bytes 3080 | tf_op jit(solution)/shard_map/ppermute | solution.py:62
  23.1 3.0 %collective-permute-start.4 = (f32[2,128]{1,0:T(2,128)S(1)}, f32[2,128]{1,0:T(2,128)S(1)}, u32[]{:S(2)}, u32[]{:S(2)}) collective-permute-start(f32[2,128]{1,0:T(2,128)S(1)} %get-tuple-element.24), channel_id=1, source_target_pairs={{0,1},{1,0},{2,3},{3,2},{4,5},{5,4},{6,7},{7,6},{8,9},{9,8},{10,11... | collective-permute-start | bytes 3080 | tf_op jit(solution)/shard_map/ppermute | solution.py:62
  23.1 5.8 %collective-permute-start.5 = (f32[2,128]{1,0:T(2,128)S(1)}, f32[2,128]{1,0:T(2,128)S(1)}, u32[]{:S(2)}, u32[]{:S(2)}) collective-permute-start(f32[2,128]{1,0:T(2,128)S(1)} %get-tuple-element.25), channel_id=1, source_target_pairs={{1,2},{3,4},{5,6},{7,8},{9,10},{11,12},{13,14},{2,1},{4,3},{6,5},{... | collective-permute-start | bytes 3080 | tf_op jit(solution)/shard_map/ppermute | solution.py:62

commit v12 on v11

--- a/solution.py
+++ b/solution.py
@@ -71,11 +71,9 @@
     return [psf_ref[k, cell] for k in range(9)]
 
 
-def setup_kernel(band_ref, col_ref, cell_ref, psf_ref, oy_ref, ox_ref, f_ref, up_ref, down_ref, w_ref):
+def weight_kernel(band_ref, cell_ref, psf_ref, oy_ref, ox_ref, w_ref):
     own = oy_ref.shape[0]
     offs = lax.broadcasted_iota(jnp.int32, (32, LANES), 0).astype(jnp.float32) - 15.0
-    lane = lax.broadcasted_iota(jnp.int32, (1, LANES), 1)
-    ys, metas, weights = [], [], []
     for j in range(own):
         y = band_ref[j].astype(jnp.float32) + oy_ref[j : j + 1, :]
         x = ox_ref[j : j + 1, :]
@@ -95,13 +93,19 @@
                 term = gram_r[a][cc] * inner
                 weight = term if weight is None else weight + term
         w_ref[j : j + 1, :] = weight
+
+
+def setup_kernel(band_ref, col_ref, cell_ref, psf_ref, oy_ref, ox_ref, f_ref, up_ref, down_ref):
+    own = oy_ref.shape[0]
+    lane = lax.broadcasted_iota(jnp.int32, (1, LANES), 1)
+    ys, metas = [], []
+    for j in range(own):
+        ys.append(band_ref[j].astype(jnp.float32) + oy_ref[j : j + 1, :])
+        c = own_coefs(psf_ref, cell_ref, j)
         meta = jnp.zeros((1, LANES), jnp.float32)
         for k in range(9):
             meta = jnp.where(lane == k, c[k], meta)
-        meta = jnp.where(lane == 9, col_ref[j].astype(jnp.float32), meta)
-        ys.append(y)
-        metas.append(meta)
-        weights.append(weight)
+        metas.append(jnp.where(lane == 9, col_ref[j].astype(jnp.float32), meta))
     top_first = band_ref[0] <= band_ref[1]
 
     def pick(first, second):
@@ -110,14 +114,14 @@
     tops, bots = zip(*[
         pick(*pair) for pair in (
             (ys[0], ys[1]), (ox_ref[0:1, :], ox_ref[1:2, :]), (f_ref[0:1, :], f_ref[1:2, :]),
-            (weights[0], weights[1]), (metas[0], metas[1]),
+            (metas[0], metas[1]),
         )
     ])
     even = even_device()
     first_ref, second_ref = up_ref, down_ref
     first_ref[...] = jnp.zeros_like(first_ref)
     second_ref[...] = jnp.zeros_like(second_ref)
-    for r in range(5):
+    for r in range(4):
         first_ref[r : r + 1, :] = jnp.where(even, bots[r], tops[r])
         second_ref[r : r + 1, :] = jnp.where(even, tops[r], bots[r])
 
@@ -148,7 +152,7 @@
     if first:
         fluxes = [f_ref[0:1, :], f_ref[1:2, :], above(x1_ref, x2_ref, 2), below(x1_ref, x2_ref, 2)]
     else:
-        weights = [w_ref[0:1, :], w_ref[1:2, :], above(x1_ref, x2_ref, 3), below(x1_ref, x2_ref, 3)]
+        weights = [w_ref[0:1, :], w_ref[1:2, :], above(q1_ref, q2_ref, 2), below(q1_ref, q2_ref, 2)]
         from_above = above(q1_ref, q2_ref, 0)
         from_below = below(q1_ref, q2_ref, 0)
         extra = [
@@ -169,13 +173,13 @@
         specs.append((y, ox_ref[j : j + 1, :], own_coefs(psf_ref, cell_ref, j), col_ref[j], None))
     specs.append((
         above(x1_ref, x2_ref, 0) - strip_rows, above(x1_ref, x2_ref, 1),
-        [jnp.where(even, xs2_ref[4, k], xs1_ref[4, k]) for k in range(9)],
-        jnp.where(even, xs2_ref[4, 9], xs1_ref[4, 9]).astype(jnp.int32), REACH,
+        [jnp.where(even, xs2_ref[3, k], xs1_ref[3, k]) for k in range(9)],
+        jnp.where(even, xs2_ref[3, 9], xs1_ref[3, 9]).astype(jnp.int32), REACH,
     ))
     specs.append((
         below(x1_ref, x2_ref, 0) + strip_rows, below(x1_ref, x2_ref, 1),
-        [jnp.where(even, xs1_ref[4, k], xs2_ref[4, k]) for k in range(9)],
-        jnp.where(even, xs1_ref[4, 9], xs2_ref[4, 9]).astype(jnp.int32), None,
+        [jnp.where(even, xs1_ref[3, k], xs2_ref[3, k]) for k in range(9)],
+        jnp.where(even, xs1_ref[3, 9], xs2_ref[3, 9]).astype(jnp.int32), None,
     ))
 
     canvas[...] = jnp.zeros_like(canvas)
@@ -225,11 +229,15 @@
         lout_ref[j : j + 1, :] = grad
     top_part = jnp.where(top_first, partial[0], partial[1])
     bot_part = jnp.where(top_first, partial[1], partial[0])
+    top_weight = jnp.where(top_first, w_ref[0:1, :], w_ref[1:2, :])
+    bot_weight = jnp.where(top_first, w_ref[1:2, :], w_ref[0:1, :])
     first_ref, second_ref = up_ref, down_ref
     first_ref[0:1, :] = jnp.where(even, partial[own + 1], partial[own])
     first_ref[1:2, :] = jnp.where(even, bot_part, top_part)
+    first_ref[2:3, :] = jnp.where(even, bot_weight, top_weight)
     second_ref[0:1, :] = jnp.where(even, partial[own], partial[own + 1])
     second_ref[1:2, :] = jnp.where(even, top_part, bot_part)
+    second_ref[2:3, :] = jnp.where(even, top_weight, bot_weight)
 
 
 def vmem_operands(*arrays):
@@ -243,18 +251,28 @@
     smem = pl.BlockSpec(memory_space=pltpu.SMEM)
     vmem = pl.BlockSpec(memory_space=pltpu.VMEM)
     packet = jax.ShapeDtypeStruct((SLOTS, LANES), f32)
-    send_within, send_across, weight = pl.pallas_call(
+    send_within, send_across = pl.pallas_call(
         setup_kernel,
-        out_shape=(packet, packet, jax.ShapeDtypeStruct((own, LANES), f32)),
+        out_shape=(packet, packet),
         in_specs=[smem] * 4 + [vmem] * 3,
-        out_specs=(vmem, vmem, vmem),
+        out_specs=(vmem, vmem),
     )(band_row, col_block, cell_index, psf_coef, offset_y, offset_x, flux_start)
     got_within, got_across = exchange(send_within, send_across)
+    weight = pl.pallas_call(
+        weight_kernel,
+        out_shape=jax.ShapeDtypeStruct((own, LANES), f32),
+        in_specs=[smem] * 3 + [vmem] * 2,
+        out_specs=vmem,
+        cost_estimate=pl.CostEstimate(
+            flops=own * 60 * 32 * LANES * 2, transcendentals=own * 4 * 32 * LANES,
+            bytes_accessed=4 * 4 * own * LANES,
+        ),
+    )(band_row, cell_index, psf_coef, offset_y, offset_x)
 
     blocks = own + 2
     flops = 2 * 3 * 2 * strip_rows * WIN * 3 * LANES * blocks
     state_shape = jax.ShapeDtypeStruct((SLOTS, LANES), f32)
-    part_shape = pltpu.VMEM((2, LANES), f32)
+    part_shape = pltpu.VMEM((4, LANES), f32)
     common = (band_row, col_block, cell_index, psf_coef, got_within, got_across,
               offset_y, offset_x, weight, got_within, got_across, image)
 

time: 32.5 us -> 32.5 us (level)
  waiting for transfers between devices: 8.67 us -> 7.06 us
  Pallas kernels: 12.5 us -> 14.1 us
    ppermute x3, waiting for transfers between devices: 8.66 us -> 7.06 us  [exchange(): lax.ppermute(second, 'ty', across)]
    pallas_call x1 -> x2, Pallas kernels: 1.84 us -> 3.38 us  [the longest x1 1.72 us: local(): pl.pallas_call(setup_kernel, out_shape=(packet, packet), in_specs=[smem]...]
  transfers between devices with their start and end apart: 6 -> 6, of which waited for: 3 -> 3; matrix products, arithmetic and copies ran while one was open for 0% -> 0% of each run, Pallas kernels for 0% -> 5%
where the time goes in v12:
time: 32.5 us; the launch traced here: 32.1 us
  Pallas kernels  14.1 us (43%)
  starting transfers between devices  9.67 us (30%)
  waiting for transfers between devices  7.06 us (22%)
  between operations  0.68 us (2%)
  local copies, waits for them, and re-layouts  0.59 us (2%)
    pallas_call x3, Pallas kernels, phase(): pl.pallas_call(kernel, out_shape=out_shape, in_specs=[smem] * 6 + [vmem]...  10.7 us
    ppermute x3, starting transfers between devices, exchange(): lax.ppermute(second, 'ty', across)  8.99 us
    ppermute x3, waiting for transfers between devices, exchange(): lax.ppermute(second, 'ty', across)  7.06 us
    pallas_call x1, Pallas kernels, local(): pl.pallas_call(setup_kernel, out_shape=(packet, packet), in_specs=[smem]...  1.72 us
    pallas_call x1, Pallas kernels, local(): pl.pallas_call(weight_kernel, out_shape=jax.ShapeDtypeStruct((own, LANES)...  1.66 us
    ppermute x3, starting transfers between devices, exchange(): lax.ppermute(first, 'ty', within)  0.68 us
  transfers between devices with their start and end apart: 6, of which 3 were waited for; matrix products, arithmetic and copies ran while one was open for 0% of the time, Pallas kernels for 5%

profile of v12, /device:TPU:11, one launch (start us, length us, event | category | flops | bytes accessed | tf_op | source)
XLA Modules:
  0.0 32.1 jit_solution(16630383149216337487)
XLA Ops:
  0.6 1.7 %shard_map.95 = (f32[8,128]{1,0:T(8,128)}, f32[8,128]{1,0:T(8,128)}) custom-call(s32[2]{0:T(128)} %band_ref.9, s32[2]{0:T(128)} %col_ref.7, s32[2]{0:T(128)} %cell_ref.9, f32[9,256]{1,0:T(8,128)} %psf_ref.9, f32[2,128]{1,0:T(2,128)} %oy_ref.9, f32[2,128]{1,0:T(2,128)} %ox_ref.9, f32[2,128]{1,0:T(2,128)} %q2_ref.1), custom_call_target="tpu_custom_call" | custom-call | tf_op jit(solution)/shard_map/pallas_call | solution.py:254
  2.3 0.7 %collective-permute-start = (f32[8,128]{1,0:T(8,128)}, f32[8,128]{1,0:T(8,128)S(1)}, u32[]{:S(2)}, u32[]{:S(2)}) collective-permute-start(f32[8,128]{1,0:T(8,128)} %get-tuple-element.14), channel_id=1, source_target_pairs={{0,1},{1,0},{2,3},{3,2},{4,5},{5,4},{6,7},{7,6},{8,9},{9,8},{10,11... | collective-permute-start | bytes 12296 | tf_op jit(solution)/shard_map/ppermute | solution.py:62
  3.0 0.0 copy-start
  3.0 3.1 %collective-permute-start.1 = (f32[8,128]{1,0:T(8,128)}, f32[8,128]{1,0:T(8,128)S(1)}, u32[]{:S(2)}, u32[]{:S(2)}) collective-permute-start(f32[8,128]{1,0:T(8,128)} %get-tuple-element.15), channel_id=1, source_target_pairs={{1,2},{3,4},{5,6},{7,8},{9,10},{11,12},{13,14},{2,1},{4,3},{6,5},{... | collective-permute-start | bytes 12296 | tf_op jit(solution)/shard_map/ppermute | solution.py:62
  6.1 1.7 %shard_map.96.w_ref = f32[2,128]{1,0:T(2,128)} custom-call(s32[2]{0:T(128)} %band_ref.9, s32[2]{0:T(128)} %cell_ref.9, f32[9,256]{1,0:T(8,128)} %psf_ref.9, f32[2,128]{1,0:T(2,128)} %oy_ref.9, f32[2,128]{1,0:T(2,128)} %ox_ref.9), custom_call_target="tpu_custom_call" | custom-call | flops 983040 | bytes 4096 | tf_op jit(solution)/shard_map/pallas_call | solution.py:261
  7.8 0.0 collective-permute-done.xs1_ref.x1_ref
  7.8 0.0 copy-start.1
  7.8 1.4 %collective-permute-done.1.xs2_ref.x2_ref = f32[8,128]{1,0:T(8,128)S(1)} collective-permute-done((f32[8,128]{1,0:T(8,128)}, f32[8,128]{1,0:T(8,128)S(1)}, u32[]{:S(2)}, u32[]{:S(2)}) %collective-permute-start.1) | collective-permute-done | bytes 4128 | tf_op jit(solution)/shard_map/ppermute | solution.py:62
  9.2 0.0 copy-done.1
  9.2 0.0 copy-start.2
  9.2 0.6 %copy-done.2 = f32[8,128]{1,0:T(8,128)} copy-done((f32[8,128]{1,0:T(8,128)}, f32[8,128]{1,0:T(8,128)S(1)}, u32[]{:S(2)}) %copy-start.2) | copy-done | bytes 4120
  9.8 0.0 copy-done
  9.8 3.7 %shard_map.97 = (f32[8,128]{1,0:T(8,128)}, f32[8,128]{1,0:T(8,128)}, f32[4,128]{1,0:T(4,128)S(1)}, f32[4,128]{1,0:T(4,128)S(1)}) custom-call(s32[2]{0:T(128)} %band_ref.9, s32[2]{0:T(128)} %col_ref.7, s32[2]{0:T(128)} %cell_ref.9, f32[9,256]{1,0:T(8,128)} %psf_ref.9, f32[8,128]{1,0:T(8,128)} %copy-done.1, f32[8,128]{1,0:T(8,128)} %copy-done.2, ...), custom_call_target="tpu_custom_call" | custom-call | flops 452984832 | bytes 1048576 | tf_op jit(solution)/shard_map/pallas_call | solution.py:288
  13.5 0.0 collective-permute-start.2
  13.5 3.0 %collective-permute-start.3 = (f32[4,128]{1,0:T(4,128)S(1)}, f32[4,128]{1,0:T(4,128)S(1)}, u32[]{:S(2)}, u32[]{:S(2)}) collective-permute-start(f32[4,128]{1,0:T(4,128)S(1)} %get-tuple-element.19), channel_id=1, source_target_pairs={{1,2},{3,4},{5,6},{7,8},{9,10},{11,12},{13,14},{2,1},{4,3},{6,5},{... | collective-permute-start | bytes 6152 | tf_op jit(solution)/shard_map/ppermute | solution.py:62
  16.4 0.0 collective-permute-done.2.q1_ref
  16.4 2.8 %collective-permute-done.3.q2_ref = f32[4,128]{1,0:T(4,128)S(1)} collective-permute-done((f32[4,128]{1,0:T(4,128)S(1)}, f32[4,128]{1,0:T(4,128)S(1)}, u32[]{:S(2)}, u32[]{:S(2)}) %collective-permute-start.3) | collective-permute-done | bytes 2080 | tf_op jit(solution)/shard_map/ppermute | solution.py:62
  19.3 3.7 %shard_map.98 = (f32[8,128]{1,0:T(8,128)}, f32[8,128]{1,0:T(8,128)}, f32[4,128]{1,0:T(4,128)S(1)}, f32[4,128]{1,0:T(4,128)S(1)}) custom-call(s32[2]{0:T(128)} %band_ref.9, s32[2]{0:T(128)} %col_ref.7, s32[2]{0:T(128)} %cell_ref.9, f32[9,256]{1,0:T(8,128)} %psf_ref.9, f32[8,128]{1,0:T(8,128)} %copy-done.1, f32[8,128]{1,0:T(8,128)} %copy-done.2, ...), custom_call_target="tpu_custom_call" | custom-call | flops 452984832 | bytes 1048576 | tf_op jit(solution)/shard_map/pallas_call | solution.py:288
  23.0 0.0 collective-permute-start.4
  23.0 3.0 %collective-permute-start.5 = (f32[4,128]{1,0:T(4,128)S(1)}, f32[4,128]{1,0:T(4,128)S(1)}, u32[]{:S(2)}, u32[]{:S(2)}) collective-permute-start(f32[4,128]{1,0:T(4,128)S(1)} %get-tuple-element.23), channel_id=1, source_target_pairs={{1,2},{3,4},{5,6},{7,8},{9,10},{11,12},{13,14},{2,1},{4,3},{6,5},{... | collective-permute-start | bytes 6152 | tf_op jit(solution)/shard_map/ppermute | solution.py:62
  25.9 0.0 collective-permute-done.4.q1_ref
  25.9 2.8 %collective-permute-done.5.q2_ref = f32[4,128]{1,0:T(4,128)S(1)} collective-permute-done((f32[4,128]{1,0:T(4,128)S(1)}, f32[4,128]{1,0:T(4,128)S(1)}, u32[]{:S(2)}, u32[]{:S(2)}) %collective-permute-start.5) | collective-permute-done | bytes 2080 | tf_op jit(solution)/shard_map/ppermute | solution.py:62
  28.8 3.3 %shard_map.99 = (f32[64,2048]{1,0:T(8,128)}, f32[2,128]{1,0:T(2,128)}) custom-call(s32[2]{0:T(128)} %band_ref.9, s32[2]{0:T(128)} %col_ref.7, s32[2]{0:T(128)} %cell_ref.9, f32[9,256]{1,0:T(8,128)} %psf_ref.9, f32[8,128]{1,0:T(8,128)} %copy-done.1, f32[8,128]{1,0:T(8,128)} %copy-done.2, f32[2,128]{1,0:T(2,128)} %oy_ref.9, f32[2,128]{1,0:T(2,128)} %ox_ref.9, ...), custom_call_target="tpu_custom_call" | custom-call | flops 452984832 | bytes 1048576 | tf_op jit(solution)/shard_map/pallas_call | solution.py:288
Async XLA Ops:
  2.3 5.4 %collective-permute-start = (f32[8,128]{1,0:T(8,128)}, f32[8,128]{1,0:T(8,128)S(1)}, u32[]{:S(2)}, u32[]{:S(2)}) collective-permute-start(f32[8,128]{1,0:T(8,128)} %get-tuple-element.14), channel_id=1, source_target_pairs={{0,1},{1,0},{2,3},{3,2},{4,5},{5,4},{6,7},{7,6},{8,9},{9,8},{10,11... | collective-permute-start | bytes 12296 | tf_op jit(solution)/shard_map/ppermute | solution.py:62
  3.0 6.8 %copy-start = (f32[2,128]{1,0:T(2,128)S(1)}, f32[2,128]{1,0:T(2,128)}, u32[]{:S(2)}) copy-start(f32[2,128]{1,0:T(2,128)} %q2_ref.1) | copy-start | bytes 3076
  3.0 6.2 %collective-permute-start.1 = (f32[8,128]{1,0:T(8,128)}, f32[8,128]{1,0:T(8,128)S(1)}, u32[]{:S(2)}, u32[]{:S(2)}) collective-permute-start(f32[8,128]{1,0:T(8,128)} %get-tuple-element.15), channel_id=1, source_target_pairs={{1,2},{3,4},{5,6},{7,8},{9,10},{11,12},{13,14},{2,1},{4,3},{6,5},{... | collective-permute-start | bytes 12296 | tf_op jit(solution)/shard_map/ppermute | solution.py:62
  7.8 1.4 %copy-start.1 = (f32[8,128]{1,0:T(8,128)}, f32[8,128]{1,0:T(8,128)S(1)}, u32[]{:S(2)}) copy-start(f32[8,128]{1,0:T(8,128)S(1)} %collective-permute-done.xs1_ref.x1_ref) | copy-start | bytes 12292
  9.2 0.6 %copy-start.2 = (f32[8,128]{1,0:T(8,128)}, f32[8,128]{1,0:T(8,128)S(1)}, u32[]{:S(2)}) copy-start(f32[8,128]{1,0:T(8,128)S(1)} %collective-permute-done.1.xs2_ref.x2_ref) | copy-start | bytes 12292
  13.5 3.0 %collective-permute-start.2 = (f32[4,128]{1,0:T(4,128)S(1)}, f32[4,128]{1,0:T(4,128)S(1)}, u32[]{:S(2)}, u32[]{:S(2)}) collective-permute-start(f32[4,128]{1,0:T(4,128)S(1)} %get-tuple-element.18), channel_id=1, source_target_pairs={{0,1},{1,0},{2,3},{3,2},{4,5},{5,4},{6,7},{7,6},{8,9},{9,8},{10,11... | collective-permute-start | bytes 6152 | tf_op jit(solution)/shard_map/ppermute | solution.py:62
  13.5 5.8 %collective-permute-start.3 = (f32[4,128]{1,0:T(4,128)S(1)}, f32[4,128]{1,0:T(4,128)S(1)}, u32[]{:S(2)}, u32[]{:S(2)}) collective-permute-start(f32[4,128]{1,0:T(4,128)S(1)} %get-tuple-element.19), channel_id=1, source_target_pairs={{1,2},{3,4},{5,6},{7,8},{9,10},{11,12},{13,14},{2,1},{4,3},{6,5},{... | collective-permute-start | bytes 6152 | tf_op jit(solution)/shard_map/ppermute | solution.py:62
  23.0 3.0 %collective-permute-start.4 = (f32[4,128]{1,0:T(4,128)S(1)}, f32[4,128]{1,0:T(4,128)S(1)}, u32[]{:S(2)}, u32[]{:S(2)}) collective-permute-start(f32[4,128]{1,0:T(4,128)S(1)} %get-tuple-element.22), channel_id=1, source_target_pairs={{0,1},{1,0},{2,3},{3,2},{4,5},{5,4},{6,7},{7,6},{8,9},{9,8},{10,11... | collective-permute-start | bytes 6152 | tf_op jit(solution)/shard_map/ppermute | solution.py:62
  23.0 5.8 %collective-permute-start.5 = (f32[4,128]{1,0:T(4,128)S(1)}, f32[4,128]{1,0:T(4,128)S(1)}, u32[]{:S(2)}, u32[]{:S(2)}) collective-permute-start(f32[4,128]{1,0:T(4,128)S(1)} %get-tuple-element.23), channel_id=1, source_target_pairs={{1,2},{3,4},{5,6},{7,8},{9,10},{11,12},{13,14},{2,1},{4,3},{6,5},{... | collective-permute-start | bytes 6152 | tf_op jit(solution)/shard_map/ppermute | solution.py:62

commit v13 on v11

--- a/solution.py
+++ b/solution.py
@@ -242,21 +242,21 @@
     f32 = jnp.float32
     smem = pl.BlockSpec(memory_space=pltpu.SMEM)
     vmem = pl.BlockSpec(memory_space=pltpu.VMEM)
-    packet = jax.ShapeDtypeStruct((SLOTS, LANES), f32)
+    packet = pltpu.VMEM((SLOTS, LANES), f32)
     send_within, send_across, weight = pl.pallas_call(
         setup_kernel,
-        out_shape=(packet, packet, jax.ShapeDtypeStruct((own, LANES), f32)),
+        out_shape=(packet, packet, pltpu.VMEM((own, LANES), f32)),
         in_specs=[smem] * 4 + [vmem] * 3,
         out_specs=(vmem, vmem, vmem),
-    )(band_row, col_block, cell_index, psf_coef, offset_y, offset_x, flux_start)
+    )(band_row, col_block, cell_index, psf_coef, *vmem_operands(offset_y, offset_x, flux_start))
     got_within, got_across = exchange(send_within, send_across)
 
     blocks = own + 2
     flops = 2 * 3 * 2 * strip_rows * WIN * 3 * LANES * blocks
-    state_shape = jax.ShapeDtypeStruct((SLOTS, LANES), f32)
+    state_shape = pltpu.VMEM((SLOTS, LANES), f32)
     part_shape = pltpu.VMEM((2, LANES), f32)
     common = (band_row, col_block, cell_index, psf_coef, got_within, got_across,
-              offset_y, offset_x, weight, got_within, got_across, image)
+              *vmem_operands(offset_y, offset_x, weight, got_within, got_across), image)
 
     def phase(final, first, fluxes, partials, swap_within, swap_across):
         kernel = functools.partial(phase_kernel, final, first)
@@ -277,7 +277,7 @@
                 flops=flops, transcendentals=blocks * 2 * (strip_rows + WIN) * LANES,
                 bytes_accessed=4 * strip_rows * strip_width * 2,
             ),
-        )(*common, fluxes, partials, *vmem_operands(swap_within, swap_across))
+        )(*common, *vmem_operands(fluxes, partials, swap_within, swap_across))
 
     state, partials, within, across = phase(False, True, flux_start, flux_start, flux_start, flux_start)
     for iteration in range(1, ITERS):

time: 32.5 us -> 31.4 us (0.966)
  Pallas kernels: 12.5 us -> 10.1 us
  local copies, waits for them, and re-layouts: 0.59 us -> 2.03 us
  waiting for transfers between devices: 8.67 us -> 8.09 us
  starting transfers between devices: 9.68 us -> 10.1 us
    pallas_call x3, Pallas kernels: 10.7 us -> 8.97 us  [phase(): pl.pallas_call(kernel, out_shape=out_shape, in_specs=[smem] * 6 + [vmem]...]
    unnamed x6, local copies, waits for them, and re-layouts: 0.59 us -> 2.03 us
    pallas_call x1, Pallas kernels: 1.84 us -> 1.09 us  [local(): pl.pallas_call(setup_kernel, out_shape=(packet, packet, pltpu.VMEM((own,...]
    ppermute x3, waiting for transfers between devices: 8.66 us -> 8.08 us  [exchange(): lax.ppermute(second, 'ty', across)]
where the time goes in v13:
time: 31.4 us; the launch traced here: 31 us
  Pallas kernels  10.1 us (32%)
  starting transfers between devices  10.1 us (32%)
  waiting for transfers between devices  8.09 us (26%)
  local copies, waits for them, and re-layouts  2.03 us (6%)
  between operations  0.72 us (2%)
    ppermute x3, starting transfers between devices, exchange(): lax.ppermute(second, 'ty', across)  9.25 us
    pallas_call x3, Pallas kernels, phase(): pl.pallas_call(kernel, out_shape=out_shape, in_specs=[smem] * 6 + [vmem]...  8.97 us
    ppermute x3, waiting for transfers between devices, exchange(): lax.ppermute(second, 'ty', across)  8.08 us
    unnamed x6, local copies, waits for them, and re-layouts  2.03 us
    pallas_call x1, Pallas kernels, local(): pl.pallas_call(setup_kernel, out_shape=(packet, packet, pltpu.VMEM((own,...  1.09 us
    ppermute x3, starting transfers between devices, exchange(): lax.ppermute(first, 'ty', within)  0.88 us
  transfers between devices with their start and end apart: 6, of which 3 were waited for; matrix products, arithmetic and copies ran while one was open for 0% of the time, Pallas kernels for 0%

profile of v13, /device:TPU:11, one launch (start us, length us, event | category | flops | bytes accessed | tf_op | source)
XLA Modules:
  0.0 31.0 jit_solution(11531432820403725641)
XLA Ops:
  0.6 0.0 copy-start
  0.6 0.7 %copy-done = f32[2,128]{1,0:T(2,128)S(1)} copy-done((f32[2,128]{1,0:T(2,128)S(1)}, f32[2,128]{1,0:T(2,128)}, u32[]{:S(2)}) %copy-start) | copy-done | bytes 1048
  1.3 0.0 copy-start.1
  1.3 0.7 %copy-done.1 = f32[2,128]{1,0:T(2,128)S(1)} copy-done((f32[2,128]{1,0:T(2,128)S(1)}, f32[2,128]{1,0:T(2,128)}, u32[]{:S(2)}) %copy-start.1) | copy-done | bytes 1048
  2.0 0.0 copy-start.2
  2.0 0.7 %copy-done.2 = f32[2,128]{1,0:T(2,128)S(1)} copy-done((f32[2,128]{1,0:T(2,128)S(1)}, f32[2,128]{1,0:T(2,128)}, u32[]{:S(2)}) %copy-start.2) | copy-done | bytes 1048
  2.7 1.1 %shard_map.95 = (f32[8,128]{1,0:T(8,128)S(1)}, f32[8,128]{1,0:T(8,128)S(1)}, f32[2,128]{1,0:T(2,128)S(1)}) custom-call(s32[2]{0:T(128)} %band_ref.7, s32[2]{0:T(128)} %col_ref.7, s32[2]{0:T(128)} %cell_ref.7, f32[9,256]{1,0:T(8,128)} %psf_ref.7, f32[2,128]{1,0:T(2,128)S(1)} %copy-done.1, f32[2,128]{1,0:T(2,128)S(1)} %copy-done.2, f32[2,128]{1,0:T(2,128)S(1)} %copy-done), custom_call_target="tpu_custom_call" | custom-call | tf_op jit(solution)/shard_map/pallas_call | solution.py:246
  3.8 0.7 %collective-permute-start = (f32[8,128]{1,0:T(8,128)S(1)}, f32[8,128]{1,0:T(8,128)S(1)}, u32[]{:S(2)}, u32[]{:S(2)}) collective-permute-start(f32[8,128]{1,0:T(8,128)S(1)} %get-tuple-element.15), channel_id=1, source_target_pairs={{0,1},{1,0},{2,3},{3,2},{4,5},{5,4},{6,7},{7,6},{8,9},{9,8},{10,11... | collective-permute-start | bytes 12296 | tf_op jit(solution)/shard_map/ppermute | solution.py:62
  4.5 3.1 %collective-permute-start.1 = (f32[8,128]{1,0:T(8,128)S(1)}, f32[8,128]{1,0:T(8,128)S(1)}, u32[]{:S(2)}, u32[]{:S(2)}) collective-permute-start(f32[8,128]{1,0:T(8,128)S(1)} %get-tuple-element.16), channel_id=1, source_target_pairs={{1,2},{3,4},{5,6},{7,8},{9,10},{11,12},{13,14},{2,1},{4,3},{6,5},{... | collective-permute-start | bytes 12296 | tf_op jit(solution)/shard_map/ppermute | solution.py:62
  7.6 0.0 collective-permute-done.xs1_ref.x1_ref
  7.6 2.7 %collective-permute-done.1.xs2_ref.x2_ref = f32[8,128]{1,0:T(8,128)S(1)} collective-permute-done((f32[8,128]{1,0:T(8,128)S(1)}, f32[8,128]{1,0:T(8,128)S(1)}, u32[]{:S(2)}, u32[]{:S(2)}) %collective-permute-start.1) | collective-permute-done | bytes 4128 | tf_op jit(solution)/shard_map/ppermute | solution.py:62
  10.3 2.9 %shard_map.96 = (f32[8,128]{1,0:T(8,128)S(1)}, f32[8,128]{1,0:T(8,128)S(1)}, f32[2,128]{1,0:T(2,128)S(1)}, f32[2,128]{1,0:T(2,128)S(1)}) custom-call(s32[2]{0:T(128)} %band_ref.7, s32[2]{0:T(128)} %col_ref.7, s32[2]{0:T(128)} %cell_ref.7, f32[9,256]{1,0:T(8,128)} %psf_ref.7, f32[8,128]{1,0:T(8,128)S(1)} %collective-permute-done.xs1_ref.x1_ref, ...), custom_call_target="tpu_custom_call" | custom-call | flops 452984832 | bytes 1048576 | tf_op jit(solution)/shard_map/pallas_call | solution.py:270
  13.2 0.1 collective-permute-start.2
  13.3 3.1 %collective-permute-start.3 = (f32[2,128]{1,0:T(2,128)S(1)}, f32[2,128]{1,0:T(2,128)S(1)}, u32[]{:S(2)}, u32[]{:S(2)}) collective-permute-start(f32[2,128]{1,0:T(2,128)S(1)} %get-tuple-element.21), channel_id=1, source_target_pairs={{1,2},{3,4},{5,6},{7,8},{9,10},{11,12},{13,14},{2,1},{4,3},{6,5},{... | collective-permute-start | bytes 3080 | tf_op jit(solution)/shard_map/ppermute | solution.py:62
  16.4 0.0 collective-permute-done.2.q1_ref
  16.4 2.7 %collective-permute-done.3.q2_ref = f32[2,128]{1,0:T(2,128)S(1)} collective-permute-done((f32[2,128]{1,0:T(2,128)S(1)}, f32[2,128]{1,0:T(2,128)S(1)}, u32[]{:S(2)}, u32[]{:S(2)}) %collective-permute-start.3) | collective-permute-done | bytes 1056 | tf_op jit(solution)/shard_map/ppermute | solution.py:62
  19.1 2.9 %shard_map.97 = (f32[8,128]{1,0:T(8,128)S(1)}, f32[8,128]{1,0:T(8,128)S(1)}, f32[2,128]{1,0:T(2,128)S(1)}, f32[2,128]{1,0:T(2,128)S(1)}) custom-call(s32[2]{0:T(128)} %band_ref.7, s32[2]{0:T(128)} %col_ref.7, s32[2]{0:T(128)} %cell_ref.7, f32[9,256]{1,0:T(8,128)} %psf_ref.7, f32[8,128]{1,0:T(8,128)S(1)} %collective-permute-done.xs1_ref.x1_ref, ...), custom_call_target="tpu_custom_call" | custom-call | flops 452984832 | bytes 1048576 | tf_op jit(solution)/shard_map/pallas_call | solution.py:270
  22.0 0.1 collective-permute-start.4
  22.1 3.1 %collective-permute-start.5 = (f32[2,128]{1,0:T(2,128)S(1)}, f32[2,128]{1,0:T(2,128)S(1)}, u32[]{:S(2)}, u32[]{:S(2)}) collective-permute-start(f32[2,128]{1,0:T(2,128)S(1)} %get-tuple-element.25), channel_id=1, source_target_pairs={{1,2},{3,4},{5,6},{7,8},{9,10},{11,12},{13,14},{2,1},{4,3},{6,5},{... | collective-permute-start | bytes 3080 | tf_op jit(solution)/shard_map/ppermute | solution.py:62
  25.2 0.0 collective-permute-done.4.q1_ref
  25.2 2.7 %collective-permute-done.5.q2_ref = f32[2,128]{1,0:T(2,128)S(1)} collective-permute-done((f32[2,128]{1,0:T(2,128)S(1)}, f32[2,128]{1,0:T(2,128)S(1)}, u32[]{:S(2)}, u32[]{:S(2)}) %collective-permute-start.5) | collective-permute-done | bytes 1056 | tf_op jit(solution)/shard_map/ppermute | solution.py:62
  27.9 3.1 %shard_map.98 = (f32[64,2048]{1,0:T(8,128)}, f32[2,128]{1,0:T(2,128)}) custom-call(s32[2]{0:T(128)} %band_ref.7, s32[2]{0:T(128)} %col_ref.7, s32[2]{0:T(128)} %cell_ref.7, f32[9,256]{1,0:T(8,128)} %psf_ref.7, f32[8,128]{1,0:T(8,128)S(1)} %collective-permute-done.xs1_ref.x1_ref, f32[8,128]{1,0:T(8,128)S(1)} %collective-permute-done.1.xs2_ref.x2_ref, ...), custom_call_target="tpu_custom_call" | custom-call | flops 452984832 | bytes 1048576 | tf_op jit(solution)/shard_map/pallas_call | solution.py:270
Async XLA Ops:
  0.6 0.7 %copy-start = (f32[2,128]{1,0:T(2,128)S(1)}, f32[2,128]{1,0:T(2,128)}, u32[]{:S(2)}) copy-start(f32[2,128]{1,0:T(2,128)} %q2_ref.1) | copy-start | bytes 3076
  1.3 0.7 %copy-start.1 = (f32[2,128]{1,0:T(2,128)S(1)}, f32[2,128]{1,0:T(2,128)}, u32[]{:S(2)}) copy-start(f32[2,128]{1,0:T(2,128)} %oy_ref.7) | copy-start | bytes 3076
  2.0 0.7 %copy-start.2 = (f32[2,128]{1,0:T(2,128)S(1)}, f32[2,128]{1,0:T(2,128)}, u32[]{:S(2)}) copy-start(f32[2,128]{1,0:T(2,128)} %ox_ref.7) | copy-start | bytes 3076
  3.8 3.8 %collective-permute-start = (f32[8,128]{1,0:T(8,128)S(1)}, f32[8,128]{1,0:T(8,128)S(1)}, u32[]{:S(2)}, u32[]{:S(2)}) collective-permute-start(f32[8,128]{1,0:T(8,128)S(1)} %get-tuple-element.15), channel_id=1, source_target_pairs={{0,1},{1,0},{2,3},{3,2},{4,5},{5,4},{6,7},{7,6},{8,9},{9,8},{10,11... | collective-permute-start | bytes 12296 | tf_op jit(solution)/shard_map/ppermute | solution.py:62
  4.5 5.8 %collective-permute-start.1 = (f32[8,128]{1,0:T(8,128)S(1)}, f32[8,128]{1,0:T(8,128)S(1)}, u32[]{:S(2)}, u32[]{:S(2)}) collective-permute-start(f32[8,128]{1,0:T(8,128)S(1)} %get-tuple-element.16), channel_id=1, source_target_pairs={{1,2},{3,4},{5,6},{7,8},{9,10},{11,12},{13,14},{2,1},{4,3},{6,5},{... | collective-permute-start | bytes 12296 | tf_op jit(solution)/shard_map/ppermute | solution.py:62
  13.2 3.2 %collective-permute-start.2 = (f32[2,128]{1,0:T(2,128)S(1)}, f32[2,128]{1,0:T(2,128)S(1)}, u32[]{:S(2)}, u32[]{:S(2)}) collective-permute-start(f32[2,128]{1,0:T(2,128)S(1)} %get-tuple-element.20), channel_id=1, source_target_pairs={{0,1},{1,0},{2,3},{3,2},{4,5},{5,4},{6,7},{7,6},{8,9},{9,8},{10,11... | collective-permute-start | bytes 3080 | tf_op jit(solution)/shard_map/ppermute | solution.py:62
  13.3 5.8 %collective-permute-start.3 = (f32[2,128]{1,0:T(2,128)S(1)}, f32[2,128]{1,0:T(2,128)S(1)}, u32[]{:S(2)}, u32[]{:S(2)}) collective-permute-start(f32[2,128]{1,0:T(2,128)S(1)} %get-tuple-element.21), channel_id=1, source_target_pairs={{1,2},{3,4},{5,6},{7,8},{9,10},{11,12},{13,14},{2,1},{4,3},{6,5},{... | collective-permute-start | bytes 3080 | tf_op jit(solution)/shard_map/ppermute | solution.py:62
  22.0 3.2 %collective-permute-start.4 = (f32[2,128]{1,0:T(2,128)S(1)}, f32[2,128]{1,0:T(2,128)S(1)}, u32[]{:S(2)}, u32[]{:S(2)}) collective-permute-start(f32[2,128]{1,0:T(2,128)S(1)} %get-tuple-element.24), channel_id=1, source_target_pairs={{0,1},{1,0},{2,3},{3,2},{4,5},{5,4},{6,7},{7,6},{8,9},{9,8},{10,11... | collective-permute-start | bytes 3080 | tf_op jit(solution)/shard_map/ppermute | solution.py:62
  22.1 5.8 %collective-permute-start.5 = (f32[2,128]{1,0:T(2,128)S(1)}, f32[2,128]{1,0:T(2,128)S(1)}, u32[]{:S(2)}, u32[]{:S(2)}) collective-permute-start(f32[2,128]{1,0:T(2,128)S(1)} %get-tuple-element.25), channel_id=1, source_target_pairs={{1,2},{3,4},{5,6},{7,8},{9,10},{11,12},{13,14},{2,1},{4,3},{6,5},{... | collective-permute-start | bytes 3080 | tf_op jit(solution)/shard_map/ppermute | solution.py:62

commit v14 on v13

--- a/solution.py
+++ b/solution.py
@@ -248,7 +248,7 @@
         out_shape=(packet, packet, pltpu.VMEM((own, LANES), f32)),
         in_specs=[smem] * 4 + [vmem] * 3,
         out_specs=(vmem, vmem, vmem),
-    )(band_row, col_block, cell_index, psf_coef, *vmem_operands(offset_y, offset_x, flux_start))
+    )(band_row, col_block, cell_index, psf_coef, offset_y, offset_x, flux_start)
     got_within, got_across = exchange(send_within, send_across)
 
     blocks = own + 2

time: 31.4 us -> 29.6 us (0.943)
  local copies, waits for them, and re-layouts: 2.03 us -> 0.01 us
    unnamed x6, local copies, waits for them, and re-layouts: 2.03 us -> 0.01 us
where the time goes in v14:
time: 29.6 us; the launch traced here: 29.3 us
  starting transfers between devices  10.4 us (35%)
  Pallas kernels  10.2 us (34%)
  waiting for transfers between devices  8 us (27%)
  between operations  0.72 us (2%)
    ppermute x3, starting transfers between devices, exchange(): lax.ppermute(second, 'ty', across)  9.48 us
    pallas_call x3, Pallas kernels, phase(): pl.pallas_call(kernel, out_shape=out_shape, in_specs=[smem] * 6 + [vmem]...  8.97 us
    ppermute x3, waiting for transfers between devices, exchange(): lax.ppermute(second, 'ty', across)  7.99 us
    pallas_call x1, Pallas kernels, local(): pl.pallas_call(setup_kernel, out_shape=(packet, packet, pltpu.VMEM((own,...  1.24 us
    ppermute x3, starting transfers between devices, exchange(): lax.ppermute(first, 'ty', within)  0.88 us
  transfers between devices with their start and end apart: 6, of which 3 were waited for; matrix products, arithmetic and copies ran while one was open for 0% of the time, Pallas kernels for 0%

profile of v14, /device:TPU:11, one launch (start us, length us, event | category | flops | bytes accessed | tf_op | source)
XLA Modules:
  0.0 29.3 jit_solution(15770654245134092449)
XLA Ops:
  0.6 1.2 %shard_map.95 = (f32[8,128]{1,0:T(8,128)S(1)}, f32[8,128]{1,0:T(8,128)S(1)}, f32[2,128]{1,0:T(2,128)S(1)}) custom-call(s32[2]{0:T(128)} %band_ref.7, s32[2]{0:T(128)} %col_ref.7, s32[2]{0:T(128)} %cell_ref.7, f32[9,256]{1,0:T(8,128)} %psf_ref.7, f32[2,128]{1,0:T(2,128)} %oy_ref.7, f32[2,128]{1,0:T(2,128)} %ox_ref.7, f32[2,128]{1,0:T(2,128)} %q2_ref.1), custom_call_target="tpu_custom_call" | custom-call | tf_op jit(solution)/shard_map/pallas_call | solution.py:246
  1.9 0.7 %collective-permute-start = (f32[8,128]{1,0:T(8,128)S(1)}, f32[8,128]{1,0:T(8,128)S(1)}, u32[]{:S(2)}, u32[]{:S(2)}) collective-permute-start(f32[8,128]{1,0:T(8,128)S(1)} %get-tuple-element.15), channel_id=1, source_target_pairs={{0,1},{1,0},{2,3},{3,2},{4,5},{5,4},{6,7},{7,6},{8,9},{9,8},{10,11... | collective-permute-start | bytes 12296 | tf_op jit(solution)/shard_map/ppermute | solution.py:62
  2.6 0.0 copy-start.1
  2.6 0.0 copy-start.2
  2.6 0.0 copy-start
  2.6 3.2 %collective-permute-start.1 = (f32[8,128]{1,0:T(8,128)S(1)}, f32[8,128]{1,0:T(8,128)S(1)}, u32[]{:S(2)}, u32[]{:S(2)}) collective-permute-start(f32[8,128]{1,0:T(8,128)S(1)} %get-tuple-element.16), channel_id=1, source_target_pairs={{1,2},{3,4},{5,6},{7,8},{9,10},{11,12},{13,14},{2,1},{4,3},{6,5},{... | collective-permute-start | bytes 12296 | tf_op jit(solution)/shard_map/ppermute | solution.py:62
  5.9 0.0 collective-permute-done.xs1_ref.x1_ref
  5.9 2.7 %collective-permute-done.1.xs2_ref.x2_ref = f32[8,128]{1,0:T(8,128)S(1)} collective-permute-done((f32[8,128]{1,0:T(8,128)S(1)}, f32[8,128]{1,0:T(8,128)S(1)}, u32[]{:S(2)}, u32[]{:S(2)}) %collective-permute-start.1) | collective-permute-done | bytes 4128 | tf_op jit(solution)/shard_map/ppermute | solution.py:62
  8.6 0.0 copy-done.1
  8.6 0.0 copy-done.2
  8.6 0.0 copy-done
  8.6 2.9 %shard_map.96 = (f32[8,128]{1,0:T(8,128)S(1)}, f32[8,128]{1,0:T(8,128)S(1)}, f32[2,128]{1,0:T(2,128)S(1)}, f32[2,128]{1,0:T(2,128)S(1)}) custom-call(s32[2]{0:T(128)} %band_ref.7, s32[2]{0:T(128)} %col_ref.7, s32[2]{0:T(128)} %cell_ref.7, f32[9,256]{1,0:T(8,128)} %psf_ref.7, f32[8,128]{1,0:T(8,128)S(1)} %collective-permute-done.xs1_ref.x1_ref, ...), custom_call_target="tpu_custom_call" | custom-call | flops 452984832 | bytes 1048576 | tf_op jit(solution)/shard_map/pallas_call | solution.py:270
  11.5 0.1 collective-permute-start.2
  11.6 3.1 %collective-permute-start.3 = (f32[2,128]{1,0:T(2,128)S(1)}, f32[2,128]{1,0:T(2,128)S(1)}, u32[]{:S(2)}, u32[]{:S(2)}) collective-permute-start(f32[2,128]{1,0:T(2,128)S(1)} %get-tuple-element.21), channel_id=1, source_target_pairs={{1,2},{3,4},{5,6},{7,8},{9,10},{11,12},{13,14},{2,1},{4,3},{6,5},{... | collective-permute-start | bytes 3080 | tf_op jit(solution)/shard_map/ppermute | solution.py:62
  14.7 0.0 collective-permute-done.2.q1_ref
  14.7 2.6 %collective-permute-done.3.q2_ref = f32[2,128]{1,0:T(2,128)S(1)} collective-permute-done((f32[2,128]{1,0:T(2,128)S(1)}, f32[2,128]{1,0:T(2,128)S(1)}, u32[]{:S(2)}, u32[]{:S(2)}) %collective-permute-start.3) | collective-permute-done | bytes 1056 | tf_op jit(solution)/shard_map/ppermute | solution.py:62
  17.4 2.9 %shard_map.97 = (f32[8,128]{1,0:T(8,128)S(1)}, f32[8,128]{1,0:T(8,128)S(1)}, f32[2,128]{1,0:T(2,128)S(1)}, f32[2,128]{1,0:T(2,128)S(1)}) custom-call(s32[2]{0:T(128)} %band_ref.7, s32[2]{0:T(128)} %col_ref.7, s32[2]{0:T(128)} %cell_ref.7, f32[9,256]{1,0:T(8,128)} %psf_ref.7, f32[8,128]{1,0:T(8,128)S(1)} %collective-permute-done.xs1_ref.x1_ref, ...), custom_call_target="tpu_custom_call" | custom-call | flops 452984832 | bytes 1048576 | tf_op jit(solution)/shard_map/pallas_call | solution.py:270
  20.3 0.1 collective-permute-start.4
  20.4 3.1 %collective-permute-start.5 = (f32[2,128]{1,0:T(2,128)S(1)}, f32[2,128]{1,0:T(2,128)S(1)}, u32[]{:S(2)}, u32[]{:S(2)}) collective-permute-start(f32[2,128]{1,0:T(2,128)S(1)} %get-tuple-element.25), channel_id=1, source_target_pairs={{1,2},{3,4},{5,6},{7,8},{9,10},{11,12},{13,14},{2,1},{4,3},{6,5},{... | collective-permute-start | bytes 3080 | tf_op jit(solution)/shard_map/ppermute | solution.py:62
  23.5 0.0 collective-permute-done.4.q1_ref
  23.5 2.6 %collective-permute-done.5.q2_ref = f32[2,128]{1,0:T(2,128)S(1)} collective-permute-done((f32[2,128]{1,0:T(2,128)S(1)}, f32[2,128]{1,0:T(2,128)S(1)}, u32[]{:S(2)}, u32[]{:S(2)}) %collective-permute-start.5) | collective-permute-done | bytes 1056 | tf_op jit(solution)/shard_map/ppermute | solution.py:62
  26.2 3.1 %shard_map.98 = (f32[64,2048]{1,0:T(8,128)}, f32[2,128]{1,0:T(2,128)}) custom-call(s32[2]{0:T(128)} %band_ref.7, s32[2]{0:T(128)} %col_ref.7, s32[2]{0:T(128)} %cell_ref.7, f32[9,256]{1,0:T(8,128)} %psf_ref.7, f32[8,128]{1,0:T(8,128)S(1)} %collective-permute-done.xs1_ref.x1_ref, f32[8,128]{1,0:T(8,128)S(1)} %collective-permute-done.1.xs2_ref.x2_ref, ...), custom_call_target="tpu_custom_call" | custom-call | flops 452984832 | bytes 1048576 | tf_op jit(solution)/shard_map/pallas_call | solution.py:270
Async XLA Ops:
  1.9 4.0 %collective-permute-start = (f32[8,128]{1,0:T(8,128)S(1)}, f32[8,128]{1,0:T(8,128)S(1)}, u32[]{:S(2)}, u32[]{:S(2)}) collective-permute-start(f32[8,128]{1,0:T(8,128)S(1)} %get-tuple-element.15), channel_id=1, source_target_pairs={{0,1},{1,0},{2,3},{3,2},{4,5},{5,4},{6,7},{7,6},{8,9},{9,8},{10,11... | collective-permute-start | bytes 12296 | tf_op jit(solution)/shard_map/ppermute | solution.py:62
  2.6 6.0 %copy-start.1 = (f32[2,128]{1,0:T(2,128)S(1)}, f32[2,128]{1,0:T(2,128)}, u32[]{:S(2)}) copy-start(f32[2,128]{1,0:T(2,128)} %oy_ref.7) | copy-start | bytes 3076
  2.6 6.0 %copy-start.2 = (f32[2,128]{1,0:T(2,128)S(1)}, f32[2,128]{1,0:T(2,128)}, u32[]{:S(2)}) copy-start(f32[2,128]{1,0:T(2,128)} %ox_ref.7) | copy-start | bytes 3076
  2.6 6.0 %copy-start = (f32[2,128]{1,0:T(2,128)S(1)}, f32[2,128]{1,0:T(2,128)}, u32[]{:S(2)}) copy-start(f32[2,128]{1,0:T(2,128)} %q2_ref.1) | copy-start | bytes 3076
  2.6 5.9 %collective-permute-start.1 = (f32[8,128]{1,0:T(8,128)S(1)}, f32[8,128]{1,0:T(8,128)S(1)}, u32[]{:S(2)}, u32[]{:S(2)}) collective-permute-start(f32[8,128]{1,0:T(8,128)S(1)} %get-tuple-element.16), channel_id=1, source_target_pairs={{1,2},{3,4},{5,6},{7,8},{9,10},{11,12},{13,14},{2,1},{4,3},{6,5},{... | collective-permute-start | bytes 12296 | tf_op jit(solution)/shard_map/ppermute | solution.py:62
  11.5 3.2 %collective-permute-start.2 = (f32[2,128]{1,0:T(2,128)S(1)}, f32[2,128]{1,0:T(2,128)S(1)}, u32[]{:S(2)}, u32[]{:S(2)}) collective-permute-start(f32[2,128]{1,0:T(2,128)S(1)} %get-tuple-element.20), channel_id=1, source_target_pairs={{0,1},{1,0},{2,3},{3,2},{4,5},{5,4},{6,7},{7,6},{8,9},{9,8},{10,11... | collective-permute-start | bytes 3080 | tf_op jit(solution)/shard_map/ppermute | solution.py:62
  11.6 5.8 %collective-permute-start.3 = (f32[2,128]{1,0:T(2,128)S(1)}, f32[2,128]{1,0:T(2,128)S(1)}, u32[]{:S(2)}, u32[]{:S(2)}) collective-permute-start(f32[2,128]{1,0:T(2,128)S(1)} %get-tuple-element.21), channel_id=1, source_target_pairs={{1,2},{3,4},{5,6},{7,8},{9,10},{11,12},{13,14},{2,1},{4,3},{6,5},{... | collective-permute-start | bytes 3080 | tf_op jit(solution)/shard_map/ppermute | solution.py:62
  20.3 3.2 %collective-permute-start.4 = (f32[2,128]{1,0:T(2,128)S(1)}, f32[2,128]{1,0:T(2,128)S(1)}, u32[]{:S(2)}, u32[]{:S(2)}) collective-permute-start(f32[2,128]{1,0:T(2,128)S(1)} %get-tuple-element.24), channel_id=1, source_target_pairs={{0,1},{1,0},{2,3},{3,2},{4,5},{5,4},{6,7},{7,6},{8,9},{9,8},{10,11... | collective-permute-start | bytes 3080 | tf_op jit(solution)/shard_map/ppermute | solution.py:62
  20.4 5.8 %collective-permute-start.5 = (f32[2,128]{1,0:T(2,128)S(1)}, f32[2,128]{1,0:T(2,128)S(1)}, u32[]{:S(2)}, u32[]{:S(2)}) collective-permute-start(f32[2,128]{1,0:T(2,128)S(1)} %get-tuple-element.25), channel_id=1, source_target_pairs={{1,2},{3,4},{5,6},{7,8},{9,10},{11,12},{13,14},{2,1},{4,3},{6,5},{... | collective-permute-start | bytes 3080 | tf_op jit(solution)/shard_map/ppermute | solution.py:62

commit v15 on v14

--- a/solution.py
+++ b/solution.py
@@ -256,7 +256,7 @@
     state_shape = pltpu.VMEM((SLOTS, LANES), f32)
     part_shape = pltpu.VMEM((2, LANES), f32)
     common = (band_row, col_block, cell_index, psf_coef, got_within, got_across,
-              *vmem_operands(offset_y, offset_x, weight, got_within, got_across), image)
+              *vmem_operands(offset_y, offset_x, weight, got_within, got_across, image))
 
     def phase(final, first, fluxes, partials, swap_within, swap_across):
         kernel = functools.partial(phase_kernel, final, first)

time: 29.6 us -> 30.7 us (1.037)
  local copies, waits for them, and re-layouts: 0.01 us -> 1.05 us
    unnamed x6 -> x10, local copies, waits for them, and re-layouts: 0.01 us -> 1.05 us
where the time goes in v15:
time: 30.7 us; the launch traced here: 30.2 us
  starting transfers between devices  10.3 us (34%)
  Pallas kernels  10.1 us (33%)
  waiting for transfers between devices  8 us (26%)
  local copies, waits for them, and re-layouts  1.05 us (3%)
  between operations  0.72 us (2%)
    ppermute x3, starting transfers between devices, exchange(): lax.ppermute(second, 'ty', across)  9.47 us
    pallas_call x3, Pallas kernels, phase(): pl.pallas_call(kernel, out_shape=out_shape, in_specs=[smem] * 6 + [vmem]...  8.83 us
    ppermute x3, waiting for transfers between devices, exchange(): lax.ppermute(second, 'ty', across)  8 us
    pallas_call x1, Pallas kernels, local(): pl.pallas_call(setup_kernel, out_shape=(packet, packet, pltpu.VMEM((own,...  1.24 us
    unnamed x10, local copies, waits for them, and re-layouts  1.05 us
    ppermute x3, starting transfers between devices, exchange(): lax.ppermute(first, 'ty', within)  0.88 us
  transfers between devices with their start and end apart: 6, of which 3 were waited for; matrix products, arithmetic and copies ran while one was open for 0% of the time, Pallas kernels for 0%

profile of v15, /device:TPU:11, one launch (start us, length us, event | category | flops | bytes accessed | tf_op | source)
XLA Modules:
  0.0 30.2 jit_solution(15890438013716326196)
XLA Ops:
  0.6 1.2 %shard_map.95 = (f32[8,128]{1,0:T(8,128)S(1)}, f32[8,128]{1,0:T(8,128)S(1)}, f32[2,128]{1,0:T(2,128)S(1)}) custom-call(s32[2]{0:T(128)} %band_ref.7, s32[2]{0:T(128)} %col_ref.7, s32[2]{0:T(128)} %cell_ref.7, f32[9,256]{1,0:T(8,128)} %psf_ref.7, f32[2,128]{1,0:T(2,128)} %oy_ref.7, f32[2,128]{1,0:T(2,128)} %ox_ref.7, f32[2,128]{1,0:T(2,128)} %q2_ref.1), custom_call_target="tpu_custom_call" | custom-call | tf_op jit(solution)/shard_map/pallas_call | solution.py:246
  1.9 0.7 %collective-permute-start = (f32[8,128]{1,0:T(8,128)S(1)}, f32[8,128]{1,0:T(8,128)S(1)}, u32[]{:S(2)}, u32[]{:S(2)}) collective-permute-start(f32[8,128]{1,0:T(8,128)S(1)} %get-tuple-element.15), channel_id=1, source_target_pairs={{0,1},{1,0},{2,3},{3,2},{4,5},{5,4},{6,7},{7,6},{8,9},{9,8},{10,11... | collective-permute-start | bytes 12296 | tf_op jit(solution)/shard_map/ppermute | solution.py:62
  2.6 0.0 copy-start.1
  2.6 0.0 copy-start.2
  2.6 0.0 copy-start
  2.6 3.2 %collective-permute-start.1 = (f32[8,128]{1,0:T(8,128)S(1)}, f32[8,128]{1,0:T(8,128)S(1)}, u32[]{:S(2)}, u32[]{:S(2)}) collective-permute-start(f32[8,128]{1,0:T(8,128)S(1)} %get-tuple-element.16), channel_id=1, source_target_pairs={{1,2},{3,4},{5,6},{7,8},{9,10},{11,12},{13,14},{2,1},{4,3},{6,5},{... | collective-permute-start | bytes 12296 | tf_op jit(solution)/shard_map/ppermute | solution.py:62
  5.9 0.0 collective-permute-done.xs1_ref.x1_ref
  5.9 2.7 %collective-permute-done.1.xs2_ref.x2_ref = f32[8,128]{1,0:T(8,128)S(1)} collective-permute-done((f32[8,128]{1,0:T(8,128)S(1)}, f32[8,128]{1,0:T(8,128)S(1)}, u32[]{:S(2)}, u32[]{:S(2)}) %collective-permute-start.1) | collective-permute-done | bytes 4128 | tf_op jit(solution)/shard_map/ppermute | solution.py:62
  8.6 0.0 copy-done.1
  8.6 0.0 copy-done.2
  8.6 0.0 copy-done
  8.6 0.0 copy-start.3
  8.6 1.0 %copy-done.3 = f32[64,2048]{1,0:T(8,128)S(1)} copy-done((f32[64,2048]{1,0:T(8,128)S(1)}, f32[64,2048]{1,0:T(8,128)}, u32[]{:S(2)}) %copy-start.3) | copy-done | bytes 524312
  9.6 0.0 copy-start.4
  9.6 3.0 %shard_map.96 = (f32[8,128]{1,0:T(8,128)S(1)}, f32[8,128]{1,0:T(8,128)S(1)}, f32[2,128]{1,0:T(2,128)S(1)}, f32[2,128]{1,0:T(2,128)S(1)}) custom-call(s32[2]{0:T(128)} %band_ref.7, s32[2]{0:T(128)} %col_ref.7, s32[2]{0:T(128)} %cell_ref.7, f32[9,256]{1,0:T(8,128)} %psf_ref.7, f32[8,128]{1,0:T(8,128)S(1)} %collective-permute-done.xs1_ref.x1_ref, ...), custom_call_target="tpu_custom_call" | custom-call | flops 452984832 | bytes 1048576 | tf_op jit(solution)/shard_map/pallas_call | solution.py:270
  12.6 0.1 collective-permute-start.2
  12.7 3.1 %collective-permute-start.3 = (f32[2,128]{1,0:T(2,128)S(1)}, f32[2,128]{1,0:T(2,128)S(1)}, u32[]{:S(2)}, u32[]{:S(2)}) collective-permute-start(f32[2,128]{1,0:T(2,128)S(1)} %get-tuple-element.21), channel_id=1, source_target_pairs={{1,2},{3,4},{5,6},{7,8},{9,10},{11,12},{13,14},{2,1},{4,3},{6,5},{... | collective-permute-start | bytes 3080 | tf_op jit(solution)/shard_map/ppermute | solution.py:62
  15.8 0.0 collective-permute-done.2.q1_ref
  15.8 2.7 %collective-permute-done.3.q2_ref = f32[2,128]{1,0:T(2,128)S(1)} collective-permute-done((f32[2,128]{1,0:T(2,128)S(1)}, f32[2,128]{1,0:T(2,128)S(1)}, u32[]{:S(2)}, u32[]{:S(2)}) %collective-permute-start.3) | collective-permute-done | bytes 1056 | tf_op jit(solution)/shard_map/ppermute | solution.py:62
  18.5 0.0 copy-done.4
  18.5 2.8 %shard_map.97 = (f32[8,128]{1,0:T(8,128)S(1)}, f32[8,128]{1,0:T(8,128)S(1)}, f32[2,128]{1,0:T(2,128)S(1)}, f32[2,128]{1,0:T(2,128)S(1)}) custom-call(s32[2]{0:T(128)} %band_ref.7, s32[2]{0:T(128)} %col_ref.7, s32[2]{0:T(128)} %cell_ref.7, f32[9,256]{1,0:T(8,128)} %psf_ref.7, f32[8,128]{1,0:T(8,128)S(1)} %collective-permute-done.xs1_ref.x1_ref, ...), custom_call_target="tpu_custom_call" | custom-call | flops 452984832 | bytes 1048576 | tf_op jit(solution)/shard_map/pallas_call | solution.py:270
  21.3 0.1 collective-permute-start.4
  21.4 3.1 %collective-permute-start.5 = (f32[2,128]{1,0:T(2,128)S(1)}, f32[2,128]{1,0:T(2,128)S(1)}, u32[]{:S(2)}, u32[]{:S(2)}) collective-permute-start(f32[2,128]{1,0:T(2,128)S(1)} %get-tuple-element.25), channel_id=1, source_target_pairs={{1,2},{3,4},{5,6},{7,8},{9,10},{11,12},{13,14},{2,1},{4,3},{6,5},{... | collective-permute-start | bytes 3080 | tf_op jit(solution)/shard_map/ppermute | solution.py:62
  24.5 0.0 collective-permute-done.4.q1_ref
  24.5 2.7 %collective-permute-done.5.q2_ref = f32[2,128]{1,0:T(2,128)S(1)} collective-permute-done((f32[2,128]{1,0:T(2,128)S(1)}, f32[2,128]{1,0:T(2,128)S(1)}, u32[]{:S(2)}, u32[]{:S(2)}) %collective-permute-start.5) | collective-permute-done | bytes 1056 | tf_op jit(solution)/shard_map/ppermute | solution.py:62
  27.1 3.0 %shard_map.98 = (f32[64,2048]{1,0:T(8,128)}, f32[2,128]{1,0:T(2,128)}) custom-call(s32[2]{0:T(128)} %band_ref.7, s32[2]{0:T(128)} %col_ref.7, s32[2]{0:T(128)} %cell_ref.7, f32[9,256]{1,0:T(8,128)} %psf_ref.7, f32[8,128]{1,0:T(8,128)S(1)} %collective-permute-done.xs1_ref.x1_ref, f32[8,128]{1,0:T(8,128)S(1)} %collective-permute-done.1.xs2_ref.x2_ref, ...), custom_call_target="tpu_custom_call" | custom-call | flops 452984832 | bytes 1048576 | tf_op jit(solution)/shard_map/pallas_call | solution.py:270
Async XLA Ops:
  1.9 4.0 %collective-permute-start = (f32[8,128]{1,0:T(8,128)S(1)}, f32[8,128]{1,0:T(8,128)S(1)}, u32[]{:S(2)}, u32[]{:S(2)}) collective-permute-start(f32[8,128]{1,0:T(8,128)S(1)} %get-tuple-element.15), channel_id=1, source_target_pairs={{0,1},{1,0},{2,3},{3,2},{4,5},{5,4},{6,7},{7,6},{8,9},{9,8},{10,11... | collective-permute-start | bytes 12296 | tf_op jit(solution)/shard_map/ppermute | solution.py:62
  2.6 6.0 %copy-start.1 = (f32[2,128]{1,0:T(2,128)S(1)}, f32[2,128]{1,0:T(2,128)}, u32[]{:S(2)}) copy-start(f32[2,128]{1,0:T(2,128)} %oy_ref.7) | copy-start | bytes 3076
  2.6 6.0 %copy-start.2 = (f32[2,128]{1,0:T(2,128)S(1)}, f32[2,128]{1,0:T(2,128)}, u32[]{:S(2)}) copy-start(f32[2,128]{1,0:T(2,128)} %ox_ref.7) | copy-start | bytes 3076
  2.6 6.0 %copy-start = (f32[2,128]{1,0:T(2,128)S(1)}, f32[2,128]{1,0:T(2,128)}, u32[]{:S(2)}) copy-start(f32[2,128]{1,0:T(2,128)} %q2_ref.1) | copy-start | bytes 3076
  2.6 5.9 %collective-permute-start.1 = (f32[8,128]{1,0:T(8,128)S(1)}, f32[8,128]{1,0:T(8,128)S(1)}, u32[]{:S(2)}, u32[]{:S(2)}) collective-permute-start(f32[8,128]{1,0:T(8,128)S(1)} %get-tuple-element.16), channel_id=1, source_target_pairs={{1,2},{3,4},{5,6},{7,8},{9,10},{11,12},{13,14},{2,1},{4,3},{6,5},{... | collective-permute-start | bytes 12296 | tf_op jit(solution)/shard_map/ppermute | solution.py:62
  8.6 1.0 %copy-start.3 = (f32[64,2048]{1,0:T(8,128)S(1)}, f32[64,2048]{1,0:T(8,128)}, u32[]{:S(2)}) copy-start(f32[64,2048]{1,0:T(8,128)} %img_ref.5) | copy-start | bytes 1572868
  9.6 8.8 %copy-start.4 = (f32[64,2048]{1,0:T(8,128)S(1)}, f32[64,2048]{1,0:T(8,128)}, u32[]{:S(2)}) copy-start(f32[64,2048]{1,0:T(8,128)} %img_ref.5) | copy-start | bytes 1572868
  12.6 3.2 %collective-permute-start.2 = (f32[2,128]{1,0:T(2,128)S(1)}, f32[2,128]{1,0:T(2,128)S(1)}, u32[]{:S(2)}, u32[]{:S(2)}) collective-permute-start(f32[2,128]{1,0:T(2,128)S(1)} %get-tuple-element.20), channel_id=1, source_target_pairs={{0,1},{1,0},{2,3},{3,2},{4,5},{5,4},{6,7},{7,6},{8,9},{9,8},{10,11... | collective-permute-start | bytes 3080 | tf_op jit(solution)/shard_map/ppermute | solution.py:62
  12.7 5.8 %collective-permute-start.3 = (f32[2,128]{1,0:T(2,128)S(1)}, f32[2,128]{1,0:T(2,128)S(1)}, u32[]{:S(2)}, u32[]{:S(2)}) collective-permute-start(f32[2,128]{1,0:T(2,128)S(1)} %get-tuple-element.21), channel_id=1, source_target_pairs={{1,2},{3,4},{5,6},{7,8},{9,10},{11,12},{13,14},{2,1},{4,3},{6,5},{... | collective-permute-start | bytes 3080 | tf_op jit(solution)/shard_map/ppermute | solution.py:62
  21.3 3.2 %collective-permute-start.4 = (f32[2,128]{1,0:T(2,128)S(1)}, f32[2,128]{1,0:T(2,128)S(1)}, u32[]{:S(2)}, u32[]{:S(2)}) collective-permute-start(f32[2,128]{1,0:T(2,128)S(1)} %get-tuple-element.24), channel_id=1, source_target_pairs={{0,1},{1,0},{2,3},{3,2},{4,5},{5,4},{6,7},{7,6},{8,9},{9,8},{10,11... | collective-permute-start | bytes 3080 | tf_op jit(solution)/shard_map/ppermute | solution.py:62
  21.4 5.8 %collective-permute-start.5 = (f32[2,128]{1,0:T(2,128)S(1)}, f32[2,128]{1,0:T(2,128)S(1)}, u32[]{:S(2)}, u32[]{:S(2)}) collective-permute-start(f32[2,128]{1,0:T(2,128)S(1)} %get-tuple-element.25), channel_id=1, source_target_pairs={{1,2},{3,4},{5,6},{7,8},{9,10},{11,12},{13,14},{2,1},{4,3},{6,5},{... | collective-permute-start | bytes 3080 | tf_op jit(solution)/shard_map/ppermute | solution.py:62

commit v16 on v14

--- a/solution.py
+++ b/solution.py
@@ -183,10 +183,13 @@
     wpos = lax.broadcasted_iota(jnp.int32, (SPAN, LANES), 0).astype(jnp.float32) - LANES // 2
     spare = jnp.zeros((rows_n, WIN - SPAN), jnp.float32)
     saved = []
+    bands = [(0, rows_n)] * own + [(0, 16), (rows_n - 16, 16)]
     for j, (y, x, c, col, keep) in enumerate(specs):
-        rows = profile3(hpos - y)
+        row0, count = bands[j]
+        rpos = hpos[row0 : row0 + count]
+        rows = profile3(rpos - y)
         if keep is not None:
-            rows = tuple(jnp.where(hpos < keep, r, 0.0) for r in rows)
+            rows = tuple(jnp.where(rpos < keep, r, 0.0) for r in rows)
         cols_hi, cols_lo = split_bf16(jnp.concatenate(profile3(wpos - x), axis=1))
         mixed = [
             (c[b] * rows[0] + c[3 + b] * rows[1] + c[6 + b] * rows[2]) * fluxes[j]
@@ -194,10 +197,10 @@
         ]
         stamp = presplit_dot(jnp.concatenate(mixed, axis=1), cols_hi, cols_lo, DIMS_NT)
         start = pl.multiple_of(col * LANES, LANES)
-        canvas[:, pl.ds(start, WIN)] += pltpu.roll(
-            jnp.concatenate([stamp, spare], axis=1), LANES // 2, 1
+        canvas[row0 : row0 + count, pl.ds(start, WIN)] += pltpu.roll(
+            jnp.concatenate([stamp, spare[:count]], axis=1), LANES // 2, 1
         )
-        saved.append((rows, cols_hi, cols_lo, c, start))
+        saved.append((rows, cols_hi, cols_lo, c, start, row0, count))
     inner = slice(LANES, LANES + width)
     if final:
         out_ref[...] = img_ref[...] - canvas[:, inner]
@@ -210,8 +213,10 @@
     fout_ref[...] = jnp.zeros_like(fout_ref)
     lout_ref[...] = jnp.zeros_like(lout_ref)
     partial = []
-    for j, (rows, cols_hi, cols_lo, c, start) in enumerate(saved):
-        window = pltpu.roll(canvas[:, pl.ds(start, WIN)], WIN - LANES // 2, 1)[:, :SPAN]
+    for j, (rows, cols_hi, cols_lo, c, start, row0, count) in enumerate(saved):
+        window = pltpu.roll(
+            canvas[row0 : row0 + count, pl.ds(start, WIN)], WIN - LANES // 2, 1
+        )[:, :SPAN]
         across_all = presplit_dot(window, cols_hi, cols_lo, DIMS_NN)
         grad = None
         for a in range(3):

time: 29.6 us -> 29.1 us (0.983)
  Pallas kernels: 10.2 us -> 9.74 us
    pallas_call x3, Pallas kernels: 8.97 us -> 8.5 us  [phase(): pl.pallas_call(kernel, out_shape=out_shape, in_specs=[smem] * 6 + [vmem]...]
where the time goes in v16:
time: 29.1 us; the launch traced here: 28.8 us
  starting transfers between devices  10.4 us (36%)
  Pallas kernels  9.74 us (33%)
  waiting for transfers between devices  8 us (27%)
  between operations  0.72 us (2%)
    ppermute x3, starting transfers between devices, exchange(): lax.ppermute(second, 'ty', across)  9.48 us
    pallas_call x3, Pallas kernels, phase(): pl.pallas_call(kernel, out_shape=out_shape, in_specs=[smem] * 6 + [vmem]...  8.5 us
    ppermute x3, waiting for transfers between devices, exchange(): lax.ppermute(second, 'ty', across)  7.99 us
    pallas_call x1, Pallas kernels, local(): pl.pallas_call(setup_kernel, out_shape=(packet, packet, pltpu.VMEM((own,...  1.24 us
    ppermute x3, starting transfers between devices, exchange(): lax.ppermute(first, 'ty', within)  0.88 us
  transfers between devices with their start and end apart: 6, of which 3 were waited for; matrix products, arithmetic and copies ran while one was open for 0% of the time, Pallas kernels for 0%

profile of v16, /device:TPU:11, one launch (start us, length us, event | category | flops | bytes accessed | tf_op | source)
XLA Modules:
  0.0 28.8 jit_solution(14088309318605288687)
XLA Ops:
  0.6 1.2 %shard_map.95 = (f32[8,128]{1,0:T(8,128)S(1)}, f32[8,128]{1,0:T(8,128)S(1)}, f32[2,128]{1,0:T(2,128)S(1)}) custom-call(s32[2]{0:T(128)} %band_ref.7, s32[2]{0:T(128)} %col_ref.7, s32[2]{0:T(128)} %cell_ref.7, f32[9,256]{1,0:T(8,128)} %psf_ref.7, f32[2,128]{1,0:T(2,128)} %oy_ref.7, f32[2,128]{1,0:T(2,128)} %ox_ref.7, f32[2,128]{1,0:T(2,128)} %q2_ref.1), custom_call_target="tpu_custom_call" | custom-call | tf_op jit(solution)/shard_map/pallas_call | solution.py:251
  1.9 0.7 %collective-permute-start = (f32[8,128]{1,0:T(8,128)S(1)}, f32[8,128]{1,0:T(8,128)S(1)}, u32[]{:S(2)}, u32[]{:S(2)}) collective-permute-start(f32[8,128]{1,0:T(8,128)S(1)} %get-tuple-element.15), channel_id=1, source_target_pairs={{0,1},{1,0},{2,3},{3,2},{4,5},{5,4},{6,7},{7,6},{8,9},{9,8},{10,11... | collective-permute-start | bytes 12296 | tf_op jit(solution)/shard_map/ppermute | solution.py:62
  2.6 0.0 copy-start.1
  2.6 0.0 copy-start.2
  2.6 0.0 copy-start
  2.6 3.2 %collective-permute-start.1 = (f32[8,128]{1,0:T(8,128)S(1)}, f32[8,128]{1,0:T(8,128)S(1)}, u32[]{:S(2)}, u32[]{:S(2)}) collective-permute-start(f32[8,128]{1,0:T(8,128)S(1)} %get-tuple-element.16), channel_id=1, source_target_pairs={{1,2},{3,4},{5,6},{7,8},{9,10},{11,12},{13,14},{2,1},{4,3},{6,5},{... | collective-permute-start | bytes 12296 | tf_op jit(solution)/shard_map/ppermute | solution.py:62
  5.9 0.0 collective-permute-done.xs1_ref.x1_ref
  5.9 2.7 %collective-permute-done.1.xs2_ref.x2_ref = f32[8,128]{1,0:T(8,128)S(1)} collective-permute-done((f32[8,128]{1,0:T(8,128)S(1)}, f32[8,128]{1,0:T(8,128)S(1)}, u32[]{:S(2)}, u32[]{:S(2)}) %collective-permute-start.1) | collective-permute-done | bytes 4128 | tf_op jit(solution)/shard_map/ppermute | solution.py:62
  8.6 0.0 copy-done.1
  8.6 0.0 copy-done.2
  8.6 0.0 copy-done
  8.6 2.8 %shard_map.96 = (f32[8,128]{1,0:T(8,128)S(1)}, f32[8,128]{1,0:T(8,128)S(1)}, f32[2,128]{1,0:T(2,128)S(1)}, f32[2,128]{1,0:T(2,128)S(1)}) custom-call(s32[2]{0:T(128)} %band_ref.7, s32[2]{0:T(128)} %col_ref.7, s32[2]{0:T(128)} %cell_ref.7, f32[9,256]{1,0:T(8,128)} %psf_ref.7, f32[8,128]{1,0:T(8,128)S(1)} %collective-permute-done.xs1_ref.x1_ref, ...), custom_call_target="tpu_custom_call" | custom-call | flops 452984832 | bytes 1048576 | tf_op jit(solution)/shard_map/pallas_call | solution.py:275
  11.3 0.1 collective-permute-start.2
  11.4 3.1 %collective-permute-start.3 = (f32[2,128]{1,0:T(2,128)S(1)}, f32[2,128]{1,0:T(2,128)S(1)}, u32[]{:S(2)}, u32[]{:S(2)}) collective-permute-start(f32[2,128]{1,0:T(2,128)S(1)} %get-tuple-element.21), channel_id=1, source_target_pairs={{1,2},{3,4},{5,6},{7,8},{9,10},{11,12},{13,14},{2,1},{4,3},{6,5},{... | collective-permute-start | bytes 3080 | tf_op jit(solution)/shard_map/ppermute | solution.py:62
  14.5 0.0 collective-permute-done.2.q1_ref
  14.6 2.6 %collective-permute-done.3.q2_ref = f32[2,128]{1,0:T(2,128)S(1)} collective-permute-done((f32[2,128]{1,0:T(2,128)S(1)}, f32[2,128]{1,0:T(2,128)S(1)}, u32[]{:S(2)}, u32[]{:S(2)}) %collective-permute-start.3) | collective-permute-done | bytes 1056 | tf_op jit(solution)/shard_map/ppermute | solution.py:62
  17.2 2.7 %shard_map.97 = (f32[8,128]{1,0:T(8,128)S(1)}, f32[8,128]{1,0:T(8,128)S(1)}, f32[2,128]{1,0:T(2,128)S(1)}, f32[2,128]{1,0:T(2,128)S(1)}) custom-call(s32[2]{0:T(128)} %band_ref.7, s32[2]{0:T(128)} %col_ref.7, s32[2]{0:T(128)} %cell_ref.7, f32[9,256]{1,0:T(8,128)} %psf_ref.7, f32[8,128]{1,0:T(8,128)S(1)} %collective-permute-done.xs1_ref.x1_ref, ...), custom_call_target="tpu_custom_call" | custom-call | flops 452984832 | bytes 1048576 | tf_op jit(solution)/shard_map/pallas_call | solution.py:275
  20.0 0.1 collective-permute-start.4
  20.0 3.1 %collective-permute-start.5 = (f32[2,128]{1,0:T(2,128)S(1)}, f32[2,128]{1,0:T(2,128)S(1)}, u32[]{:S(2)}, u32[]{:S(2)}) collective-permute-start(f32[2,128]{1,0:T(2,128)S(1)} %get-tuple-element.25), channel_id=1, source_target_pairs={{1,2},{3,4},{5,6},{7,8},{9,10},{11,12},{13,14},{2,1},{4,3},{6,5},{... | collective-permute-start | bytes 3080 | tf_op jit(solution)/shard_map/ppermute | solution.py:62
  23.2 0.0 collective-permute-done.4.q1_ref
  23.2 2.6 %collective-permute-done.5.q2_ref = f32[2,128]{1,0:T(2,128)S(1)} collective-permute-done((f32[2,128]{1,0:T(2,128)S(1)}, f32[2,128]{1,0:T(2,128)S(1)}, u32[]{:S(2)}, u32[]{:S(2)}) %collective-permute-start.5) | collective-permute-done | bytes 1056 | tf_op jit(solution)/shard_map/ppermute | solution.py:62
  25.8 3.0 %shard_map.98 = (f32[64,2048]{1,0:T(8,128)}, f32[2,128]{1,0:T(2,128)}) custom-call(s32[2]{0:T(128)} %band_ref.7, s32[2]{0:T(128)} %col_ref.7, s32[2]{0:T(128)} %cell_ref.7, f32[9,256]{1,0:T(8,128)} %psf_ref.7, f32[8,128]{1,0:T(8,128)S(1)} %collective-permute-done.xs1_ref.x1_ref, f32[8,128]{1,0:T(8,128)S(1)} %collective-permute-done.1.xs2_ref.x2_ref, ...), custom_call_target="tpu_custom_call" | custom-call | flops 452984832 | bytes 1048576 | tf_op jit(solution)/shard_map/pallas_call | solution.py:275
Async XLA Ops:
  1.9 4.0 %collective-permute-start = (f32[8,128]{1,0:T(8,128)S(1)}, f32[8,128]{1,0:T(8,128)S(1)}, u32[]{:S(2)}, u32[]{:S(2)}) collective-permute-start(f32[8,128]{1,0:T(8,128)S(1)} %get-tuple-element.15), channel_id=1, source_target_pairs={{0,1},{1,0},{2,3},{3,2},{4,5},{5,4},{6,7},{7,6},{8,9},{9,8},{10,11... | collective-permute-start | bytes 12296 | tf_op jit(solution)/shard_map/ppermute | solution.py:62
  2.6 6.0 %copy-start.1 = (f32[2,128]{1,0:T(2,128)S(1)}, f32[2,128]{1,0:T(2,128)}, u32[]{:S(2)}) copy-start(f32[2,128]{1,0:T(2,128)} %oy_ref.7) | copy-start | bytes 3076
  2.6 6.0 %copy-start.2 = (f32[2,128]{1,0:T(2,128)S(1)}, f32[2,128]{1,0:T(2,128)}, u32[]{:S(2)}) copy-start(f32[2,128]{1,0:T(2,128)} %ox_ref.7) | copy-start | bytes 3076
  2.6 6.0 %copy-start = (f32[2,128]{1,0:T(2,128)S(1)}, f32[2,128]{1,0:T(2,128)}, u32[]{:S(2)}) copy-start(f32[2,128]{1,0:T(2,128)} %q2_ref.1) | copy-start | bytes 3076
  2.6 5.9 %collective-permute-start.1 = (f32[8,128]{1,0:T(8,128)S(1)}, f32[8,128]{1,0:T(8,128)S(1)}, u32[]{:S(2)}, u32[]{:S(2)}) collective-permute-start(f32[8,128]{1,0:T(8,128)S(1)} %get-tuple-element.16), channel_id=1, source_target_pairs={{1,2},{3,4},{5,6},{7,8},{9,10},{11,12},{13,14},{2,1},{4,3},{6,5},{... | collective-permute-start | bytes 12296 | tf_op jit(solution)/shard_map/ppermute | solution.py:62
  11.3 3.2 %collective-permute-start.2 = (f32[2,128]{1,0:T(2,128)S(1)}, f32[2,128]{1,0:T(2,128)S(1)}, u32[]{:S(2)}, u32[]{:S(2)}) collective-permute-start(f32[2,128]{1,0:T(2,128)S(1)} %get-tuple-element.20), channel_id=1, source_target_pairs={{0,1},{1,0},{2,3},{3,2},{4,5},{5,4},{6,7},{7,6},{8,9},{9,8},{10,11... | collective-permute-start | bytes 3080 | tf_op jit(solution)/shard_map/ppermute | solution.py:62
  11.4 5.8 %collective-permute-start.3 = (f32[2,128]{1,0:T(2,128)S(1)}, f32[2,128]{1,0:T(2,128)S(1)}, u32[]{:S(2)}, u32[]{:S(2)}) collective-permute-start(f32[2,128]{1,0:T(2,128)S(1)} %get-tuple-element.21), channel_id=1, source_target_pairs={{1,2},{3,4},{5,6},{7,8},{9,10},{11,12},{13,14},{2,1},{4,3},{6,5},{... | collective-permute-start | bytes 3080 | tf_op jit(solution)/shard_map/ppermute | solution.py:62
  20.0 3.2 %collective-permute-start.4 = (f32[2,128]{1,0:T(2,128)S(1)}, f32[2,128]{1,0:T(2,128)S(1)}, u32[]{:S(2)}, u32[]{:S(2)}) collective-permute-start(f32[2,128]{1,0:T(2,128)S(1)} %get-tuple-element.24), channel_id=1, source_target_pairs={{0,1},{1,0},{2,3},{3,2},{4,5},{5,4},{6,7},{7,6},{8,9},{9,8},{10,11... | collective-permute-start | bytes 3080 | tf_op jit(solution)/shard_map/ppermute | solution.py:62
  20.0 5.8 %collective-permute-start.5 = (f32[2,128]{1,0:T(2,128)S(1)}, f32[2,128]{1,0:T(2,128)S(1)}, u32[]{:S(2)}, u32[]{:S(2)}) collective-permute-start(f32[2,128]{1,0:T(2,128)S(1)} %get-tuple-element.25), channel_id=1, source_target_pairs={{1,2},{3,4},{5,6},{7,8},{9,10},{11,12},{13,14},{2,1},{4,3},{6,5},{... | collective-permute-start | bytes 3080 | tf_op jit(solution)/shard_map/ppermute | solution.py:62

commit v17 on v16

--- a/solution.py
+++ b/solution.py
@@ -183,10 +183,12 @@
     wpos = lax.broadcasted_iota(jnp.int32, (SPAN, LANES), 0).astype(jnp.float32) - LANES // 2
     spare = jnp.zeros((rows_n, WIN - SPAN), jnp.float32)
     saved = []
-    bands = [(0, rows_n)] * own + [(0, 16), (rows_n - 16, 16)]
+    reach_rows = rows_n - 16
+    bands = [(pl.multiple_of(band_ref[j] // 2, 8), reach_rows) for j in range(own)]
+    bands += [(0, 16), (rows_n - 16, 16)]
     for j, (y, x, c, col, keep) in enumerate(specs):
         row0, count = bands[j]
-        rpos = hpos[row0 : row0 + count]
+        rpos = hpos[:count] + (row0 if j >= own else row0.astype(jnp.float32))
         rows = profile3(rpos - y)
         if keep is not None:
             rows = tuple(jnp.where(rpos < keep, r, 0.0) for r in rows)
@@ -197,7 +199,7 @@
         ]
         stamp = presplit_dot(jnp.concatenate(mixed, axis=1), cols_hi, cols_lo, DIMS_NT)
         start = pl.multiple_of(col * LANES, LANES)
-        canvas[row0 : row0 + count, pl.ds(start, WIN)] += pltpu.roll(
+        canvas[pl.ds(row0, count), pl.ds(start, WIN)] += pltpu.roll(
             jnp.concatenate([stamp, spare[:count]], axis=1), LANES // 2, 1
         )
         saved.append((rows, cols_hi, cols_lo, c, start, row0, count))
@@ -215,7 +217,7 @@
     partial = []
     for j, (rows, cols_hi, cols_lo, c, start, row0, count) in enumerate(saved):
         window = pltpu.roll(
-            canvas[row0 : row0 + count, pl.ds(start, WIN)], WIN - LANES // 2, 1
+            canvas[pl.ds(row0, count), pl.ds(start, WIN)], WIN - LANES // 2, 1
         )[:, :SPAN]
         across_all = presplit_dot(window, cols_hi, cols_lo, DIMS_NN)
         grad = None

time: 29.1 us -> 29.1 us (level)
  no operation moved by 1% of the time
where the time goes in v17:
time: 29.1 us; the launch traced here: 28.7 us
  starting transfers between devices  10.4 us (36%)
  Pallas kernels  9.66 us (33%)
  waiting for transfers between devices  7.99 us (27%)
  between operations  0.72 us (2%)
    ppermute x3, starting transfers between devices, exchange(): lax.ppermute(second, 'ty', across)  9.48 us
    pallas_call x3, Pallas kernels, phase(): pl.pallas_call(kernel, out_shape=out_shape, in_specs=[smem] * 6 + [vmem]...  8.42 us
    ppermute x3, waiting for transfers between devices, exchange(): lax.ppermute(second, 'ty', across)  7.99 us
    pallas_call x1, Pallas kernels, local(): pl.pallas_call(setup_kernel, out_shape=(packet, packet, pltpu.VMEM((own,...  1.24 us
    ppermute x3, starting transfers between devices, exchange(): lax.ppermute(first, 'ty', within)  0.88 us
  transfers between devices with their start and end apart: 6, of which 3 were waited for; matrix products, arithmetic and copies ran while one was open for 0% of the time, Pallas kernels for 0%

profile of v17, /device:TPU:11, one launch (start us, length us, event | category | flops | bytes accessed | tf_op | source)
XLA Modules:
  0.0 28.7 jit_solution(2031713902784891565)
XLA Ops:
  0.6 1.2 %shard_map.95 = (f32[8,128]{1,0:T(8,128)S(1)}, f32[8,128]{1,0:T(8,128)S(1)}, f32[2,128]{1,0:T(2,128)S(1)}) custom-call(s32[2]{0:T(128)} %band_ref.7, s32[2]{0:T(128)} %col_ref.7, s32[2]{0:T(128)} %cell_ref.7, f32[9,256]{1,0:T(8,128)} %psf_ref.7, f32[2,128]{1,0:T(2,128)} %oy_ref.7, f32[2,128]{1,0:T(2,128)} %ox_ref.7, f32[2,128]{1,0:T(2,128)} %q2_ref.1), custom_call_target="tpu_custom_call" | custom-call | tf_op jit(solution)/shard_map/pallas_call | solution.py:253
  1.9 0.7 %collective-permute-start = (f32[8,128]{1,0:T(8,128)S(1)}, f32[8,128]{1,0:T(8,128)S(1)}, u32[]{:S(2)}, u32[]{:S(2)}) collective-permute-start(f32[8,128]{1,0:T(8,128)S(1)} %get-tuple-element.15), channel_id=1, source_target_pairs={{0,1},{1,0},{2,3},{3,2},{4,5},{5,4},{6,7},{7,6},{8,9},{9,8},{10,11... | collective-permute-start | bytes 12296 | tf_op jit(solution)/shard_map/ppermute | solution.py:62
  2.6 0.0 copy-start.1
  2.6 0.0 copy-start.2
  2.6 0.0 copy-start
  2.6 3.2 %collective-permute-start.1 = (f32[8,128]{1,0:T(8,128)S(1)}, f32[8,128]{1,0:T(8,128)S(1)}, u32[]{:S(2)}, u32[]{:S(2)}) collective-permute-start(f32[8,128]{1,0:T(8,128)S(1)} %get-tuple-element.16), channel_id=1, source_target_pairs={{1,2},{3,4},{5,6},{7,8},{9,10},{11,12},{13,14},{2,1},{4,3},{6,5},{... | collective-permute-start | bytes 12296 | tf_op jit(solution)/shard_map/ppermute | solution.py:62
  5.9 0.0 collective-permute-done.xs1_ref.x1_ref
  5.9 2.7 %collective-permute-done.1.xs2_ref.x2_ref = f32[8,128]{1,0:T(8,128)S(1)} collective-permute-done((f32[8,128]{1,0:T(8,128)S(1)}, f32[8,128]{1,0:T(8,128)S(1)}, u32[]{:S(2)}, u32[]{:S(2)}) %collective-permute-start.1) | collective-permute-done | bytes 4128 | tf_op jit(solution)/shard_map/ppermute | solution.py:62
  8.6 0.0 copy-done.1
  8.6 0.0 copy-done.2
  8.6 0.0 copy-done
  8.6 2.7 %shard_map.96 = (f32[8,128]{1,0:T(8,128)S(1)}, f32[8,128]{1,0:T(8,128)S(1)}, f32[2,128]{1,0:T(2,128)S(1)}, f32[2,128]{1,0:T(2,128)S(1)}) custom-call(s32[2]{0:T(128)} %band_ref.7, s32[2]{0:T(128)} %col_ref.7, s32[2]{0:T(128)} %cell_ref.7, f32[9,256]{1,0:T(8,128)} %psf_ref.7, f32[8,128]{1,0:T(8,128)S(1)} %collective-permute-done.xs1_ref.x1_ref, ...), custom_call_target="tpu_custom_call" | custom-call | flops 452984832 | bytes 1048576 | tf_op jit(solution)/shard_map/pallas_call | solution.py:277
  11.3 0.1 collective-permute-start.2
  11.4 3.1 %collective-permute-start.3 = (f32[2,128]{1,0:T(2,128)S(1)}, f32[2,128]{1,0:T(2,128)S(1)}, u32[]{:S(2)}, u32[]{:S(2)}) collective-permute-start(f32[2,128]{1,0:T(2,128)S(1)} %get-tuple-element.21), channel_id=1, source_target_pairs={{1,2},{3,4},{5,6},{7,8},{9,10},{11,12},{13,14},{2,1},{4,3},{6,5},{... | collective-permute-start | bytes 3080 | tf_op jit(solution)/shard_map/ppermute | solution.py:62
  14.5 0.0 collective-permute-done.2.q1_ref
  14.5 2.6 %collective-permute-done.3.q2_ref = f32[2,128]{1,0:T(2,128)S(1)} collective-permute-done((f32[2,128]{1,0:T(2,128)S(1)}, f32[2,128]{1,0:T(2,128)S(1)}, u32[]{:S(2)}, u32[]{:S(2)}) %collective-permute-start.3) | collective-permute-done | bytes 1056 | tf_op jit(solution)/shard_map/ppermute | solution.py:62
  17.2 2.7 %shard_map.97 = (f32[8,128]{1,0:T(8,128)S(1)}, f32[8,128]{1,0:T(8,128)S(1)}, f32[2,128]{1,0:T(2,128)S(1)}, f32[2,128]{1,0:T(2,128)S(1)}) custom-call(s32[2]{0:T(128)} %band_ref.7, s32[2]{0:T(128)} %col_ref.7, s32[2]{0:T(128)} %cell_ref.7, f32[9,256]{1,0:T(8,128)} %psf_ref.7, f32[8,128]{1,0:T(8,128)S(1)} %collective-permute-done.xs1_ref.x1_ref, ...), custom_call_target="tpu_custom_call" | custom-call | flops 452984832 | bytes 1048576 | tf_op jit(solution)/shard_map/pallas_call | solution.py:277
  19.9 0.1 collective-permute-start.4
  20.0 3.1 %collective-permute-start.5 = (f32[2,128]{1,0:T(2,128)S(1)}, f32[2,128]{1,0:T(2,128)S(1)}, u32[]{:S(2)}, u32[]{:S(2)}) collective-permute-start(f32[2,128]{1,0:T(2,128)S(1)} %get-tuple-element.25), channel_id=1, source_target_pairs={{1,2},{3,4},{5,6},{7,8},{9,10},{11,12},{13,14},{2,1},{4,3},{6,5},{... | collective-permute-start | bytes 3080 | tf_op jit(solution)/shard_map/ppermute | solution.py:62
  23.1 0.0 collective-permute-done.4.q1_ref
  23.1 2.6 %collective-permute-done.5.q2_ref = f32[2,128]{1,0:T(2,128)S(1)} collective-permute-done((f32[2,128]{1,0:T(2,128)S(1)}, f32[2,128]{1,0:T(2,128)S(1)}, u32[]{:S(2)}, u32[]{:S(2)}) %collective-permute-start.5) | collective-permute-done | bytes 1056 | tf_op jit(solution)/shard_map/ppermute | solution.py:62
  25.7 3.0 %shard_map.98 = (f32[64,2048]{1,0:T(8,128)}, f32[2,128]{1,0:T(2,128)}) custom-call(s32[2]{0:T(128)} %band_ref.7, s32[2]{0:T(128)} %col_ref.7, s32[2]{0:T(128)} %cell_ref.7, f32[9,256]{1,0:T(8,128)} %psf_ref.7, f32[8,128]{1,0:T(8,128)S(1)} %collective-permute-done.xs1_ref.x1_ref, f32[8,128]{1,0:T(8,128)S(1)} %collective-permute-done.1.xs2_ref.x2_ref, ...), custom_call_target="tpu_custom_call" | custom-call | flops 452984832 | bytes 1048576 | tf_op jit(solution)/shard_map/pallas_call | solution.py:277
Async XLA Ops:
  1.9 4.0 %collective-permute-start = (f32[8,128]{1,0:T(8,128)S(1)}, f32[8,128]{1,0:T(8,128)S(1)}, u32[]{:S(2)}, u32[]{:S(2)}) collective-permute-start(f32[8,128]{1,0:T(8,128)S(1)} %get-tuple-element.15), channel_id=1, source_target_pairs={{0,1},{1,0},{2,3},{3,2},{4,5},{5,4},{6,7},{7,6},{8,9},{9,8},{10,11... | collective-permute-start | bytes 12296 | tf_op jit(solution)/shard_map/ppermute | solution.py:62
  2.6 6.0 %copy-start.1 = (f32[2,128]{1,0:T(2,128)S(1)}, f32[2,128]{1,0:T(2,128)}, u32[]{:S(2)}) copy-start(f32[2,128]{1,0:T(2,128)} %oy_ref.7) | copy-start | bytes 3076
  2.6 6.0 %copy-start.2 = (f32[2,128]{1,0:T(2,128)S(1)}, f32[2,128]{1,0:T(2,128)}, u32[]{:S(2)}) copy-start(f32[2,128]{1,0:T(2,128)} %ox_ref.7) | copy-start | bytes 3076
  2.6 6.0 %copy-start = (f32[2,128]{1,0:T(2,128)S(1)}, f32[2,128]{1,0:T(2,128)}, u32[]{:S(2)}) copy-start(f32[2,128]{1,0:T(2,128)} %q2_ref.1) | copy-start | bytes 3076
  2.6 5.9 %collective-permute-start.1 = (f32[8,128]{1,0:T(8,128)S(1)}, f32[8,128]{1,0:T(8,128)S(1)}, u32[]{:S(2)}, u32[]{:S(2)}) collective-permute-start(f32[8,128]{1,0:T(8,128)S(1)} %get-tuple-element.16), channel_id=1, source_target_pairs={{1,2},{3,4},{5,6},{7,8},{9,10},{11,12},{13,14},{2,1},{4,3},{6,5},{... | collective-permute-start | bytes 12296 | tf_op jit(solution)/shard_map/ppermute | solution.py:62
  11.3 3.2 %collective-permute-start.2 = (f32[2,128]{1,0:T(2,128)S(1)}, f32[2,128]{1,0:T(2,128)S(1)}, u32[]{:S(2)}, u32[]{:S(2)}) collective-permute-start(f32[2,128]{1,0:T(2,128)S(1)} %get-tuple-element.20), channel_id=1, source_target_pairs={{0,1},{1,0},{2,3},{3,2},{4,5},{5,4},{6,7},{7,6},{8,9},{9,8},{10,11... | collective-permute-start | bytes 3080 | tf_op jit(solution)/shard_map/ppermute | solution.py:62
  11.4 5.8 %collective-permute-start.3 = (f32[2,128]{1,0:T(2,128)S(1)}, f32[2,128]{1,0:T(2,128)S(1)}, u32[]{:S(2)}, u32[]{:S(2)}) collective-permute-start(f32[2,128]{1,0:T(2,128)S(1)} %get-tuple-element.21), channel_id=1, source_target_pairs={{1,2},{3,4},{5,6},{7,8},{9,10},{11,12},{13,14},{2,1},{4,3},{6,5},{... | collective-permute-start | bytes 3080 | tf_op jit(solution)/shard_map/ppermute | solution.py:62
  19.9 3.2 %collective-permute-start.4 = (f32[2,128]{1,0:T(2,128)S(1)}, f32[2,128]{1,0:T(2,128)S(1)}, u32[]{:S(2)}, u32[]{:S(2)}) collective-permute-start(f32[2,128]{1,0:T(2,128)S(1)} %get-tuple-element.24), channel_id=1, source_target_pairs={{0,1},{1,0},{2,3},{3,2},{4,5},{5,4},{6,7},{7,6},{8,9},{9,8},{10,11... | collective-permute-start | bytes 3080 | tf_op jit(solution)/shard_map/ppermute | solution.py:62
  20.0 5.8 %collective-permute-start.5 = (f32[2,128]{1,0:T(2,128)S(1)}, f32[2,128]{1,0:T(2,128)S(1)}, u32[]{:S(2)}, u32[]{:S(2)}) collective-permute-start(f32[2,128]{1,0:T(2,128)S(1)} %get-tuple-element.25), channel_id=1, source_target_pairs={{1,2},{3,4},{5,6},{7,8},{9,10},{11,12},{13,14},{2,1},{4,3},{6,5},{... | collective-permute-start | bytes 3080 | tf_op jit(solution)/shard_map/ppermute | solution.py:62
